TPU v7x, 128 devices: a whole 4x4x4 slice. The times are simulated.
128 devices in a mesh: dp: 32 (over y, z, core), mp: 4 (over x).
Axes of the slice: x: 4, y: 4, z: 4, core: 2. Of those that a mesh axis runs over, the one named last changes fastest.
Arguments:
- hidden_rows: bfloat16 [16384, 4096], P('dp', 'mp'), may hold values from -3 to 3
- destination: int32 [16384], P('dp'), may hold values from 0 to 16383, as said below
- doc_ids: int32 [16384], P('dp'), may hold values from 0 to 63, never falling along the last dimension, each value on 1 to 8704 neighbouring positions
- norm_gain: float32 [4096], replicated, may hold values from 0.1 to 1.9
- w_query: bfloat16 [4096, 2048], P(None, 'mp'), may hold values from -1 to 1
- w_key: bfloat16 [4096, 512], P(None, 'mp'), may hold values from -1 to 1
- w_value: bfloat16 [4096, 512], P(None, 'mp'), may hold values from -0.09375 to 0.09375
- w_out: bfloat16 [2048, 4096], P('mp'), may hold values from -0.125 to 0.125
Outputs:
- layer_out: bfloat16 [16384, 4096], P('dp', 'mp')
Inputs may be any that keep to these rules, and one draw needn't show every extreme that they name: `destination`: A permutation of the rows. Each aligned block of 512 rows sends exactly 32 rows to each of half of the 512-row blocks of document order and none to the other half, and each block of document order receives exactly 32 rows from each of half of the blocks of token order.
All inputs are finite; a program needn't handle non-finite values.
Results may differ from a plain program's by a relative error of at most 0.011.
Values may be sent and summed in bfloat16 or wider, within the bound.
No kernel may reach another device: no remote copies, remote signals or barrier semaphores. Data moves between devices by JAX's collectives and lax.ppermute only.
A program may use at most 128 MiB of HBM per device.

v0:
```python
import math

import jax
import jax.numpy as jnp
from jax import lax
from jax.sharding import PartitionSpec as P

HD = 128


ROPE_BASE = 500000.0
NORM_EPS = 1e-05
NEG_START = -1e30
key_block = 512


def rope_angles(row_index):
    lane_index = jnp.arange(HD // 2, dtype=jnp.float32)
    frequency = jnp.power(jnp.float32(ROPE_BASE), -2.0 * lane_index / HD)
    return row_index.astype(jnp.float32)[:, None] * frequency[None, :]


def rotate(head_values, angles):
    half_width = head_values.shape[-1] // 2
    first_half = head_values[..., :half_width]
    second_half = head_values[..., half_width:]
    cosine = jnp.cos(angles)[:, None, :]
    sine_part = jnp.sin(angles)[:, None, :]
    return jnp.concatenate(
        [
            first_half * cosine - second_half * sine_part,
            second_half * cosine + first_half * sine_part,
        ],
        axis=-1,
    )


def normalize(routed, norm_gain):
    wide_rows = routed.astype(jnp.float32)
    inv_rms = lax.rsqrt(jnp.mean(wide_rows * wide_rows, axis=1, keepdims=True) + NORM_EPS)
    return (wide_rows * inv_rms * norm_gain[None, :]).astype(jnp.bfloat16)


def local(hidden_rows, destination, doc_ids, norm_gain, w_query, w_key, w_value, w_out):
    owners = lax.axis_size("dp")
    my_index = lax.axis_index("dp")
    tok_dev, columns = hidden_rows.shape
    capacity = 2 * tok_dev // owners
    target = destination // tok_dev
    owner_ids = jnp.arange(owners, dtype=jnp.int32)
    one_hot = (target[:, None] == owner_ids[None, :]).astype(jnp.int32)
    slot_rank = jnp.sum((jnp.cumsum(one_hot, axis=0) - 1) * one_hot, axis=1)
    flat_slot = target * capacity + slot_rank
    outgoing = (
        jnp.zeros((owners * capacity, columns), hidden_rows.dtype).at[flat_slot].set(hidden_rows)
    )
    places = (
        jnp.full((owners * capacity,), tok_dev, jnp.int32).at[flat_slot].set(destination % tok_dev)
    )
    arrived, arrived_rows = (
        lax.all_to_all(
            outgoing.reshape(owners, capacity, columns),
            "dp",
            split_axis=0,
            concat_axis=0,
            tiled=True,
        ),
        lax.all_to_all(
            places.reshape(owners, capacity), "dp", split_axis=0, concat_axis=0, tiled=True
        ),
    )
    arrived_rows = arrived_rows.reshape(-1)
    routed_part = (
        jnp.zeros((tok_dev, columns), hidden_rows.dtype)
        .at[arrived_rows]
        .set(arrived.reshape(-1, columns), mode="drop")
    )
    routed = lax.all_gather(routed_part, "mp", axis=1, tiled=True)
    normed = normalize(routed, norm_gain)
    heads_dev = w_query.shape[1] // HD
    kv_dev = w_key.shape[1] // HD
    group_size = heads_dev // kv_dev
    query_rows = my_index * tok_dev + jnp.arange(tok_dev, dtype=jnp.int32)
    angles = rope_angles(query_rows)
    queries = jnp.dot(normed, w_query, preferred_element_type=jnp.float32).reshape(
        tok_dev, heads_dev, HD
    )
    queries = rotate(queries, angles).astype(jnp.bfloat16).reshape(tok_dev, kv_dev, group_size, HD)
    keys_own = jnp.dot(normed, w_key, preferred_element_type=jnp.float32).reshape(
        tok_dev, kv_dev, HD
    )
    keys_own = rotate(keys_own, angles).astype(jnp.bfloat16)
    values_own = (
        jnp.dot(normed, w_value, preferred_element_type=jnp.float32)
        .astype(jnp.bfloat16)
        .reshape(tok_dev, kv_dev, HD)
    )
    score_scale = HD ** (-0.5)
    query_first = doc_ids[0]
    query_last = doc_ids[tok_dev - 1]
    last_row = query_rows[tok_dev - 1]

    def attend_block(soft_state, block_in):
        keys_blk, values_blk, ids_blk, key_rows = block_in
        row_best, row_total, weighted = soft_state
        scores = (
            jnp.einsum("qgrd,kgd->grqk", queries, keys_blk, preferred_element_type=jnp.float32)
            * score_scale
        )
        allowed = (doc_ids[:, None] == ids_blk[None, :]) & (
            key_rows[None, :] <= query_rows[:, None]
        )
        scores = jnp.where(allowed[None, None], scores, -jnp.inf)
        new_best = jnp.maximum(row_best, jnp.max(scores, axis=-1))
        rescale = jnp.exp(row_best - new_best)
        exp_scores = jnp.exp(scores - new_best[..., None])
        row_total = row_total * rescale + jnp.sum(exp_scores, axis=-1)
        weighted = weighted * rescale[..., None] + jnp.einsum(
            "grqk,kgd->grqd",
            exp_scores.astype(jnp.bfloat16),
            values_blk,
            preferred_element_type=jnp.float32,
        )
        return ((new_best, row_total, weighted), None)

    start_state = (
        jnp.full((kv_dev, group_size, tok_dev), NEG_START, jnp.float32),
        jnp.zeros((kv_dev, group_size, tok_dev), jnp.float32),
        jnp.zeros((kv_dev, group_size, tok_dev, HD), jnp.float32),
    )
    first_row = jnp.int32(0)
    keys_piece = lax.all_gather(keys_own, "dp", axis=0, tiled=True)
    values_piece = lax.all_gather(values_own, "dp", axis=0, tiled=True)
    ids_piece = lax.all_gather(doc_ids, "dp", axis=0, tiled=True)
    key_count = keys_piece.shape[0]
    block_len = math.gcd(key_count, key_block)
    step_count = key_count // block_len
    relevant = (
        (first_row >= 0)
        & (first_row <= last_row)
        & (ids_piece[key_count - 1] >= query_first)
        & (ids_piece[0] <= query_last)
    )

    def run_piece(state_in):
        rows_piece = jnp.arange(key_count, dtype=jnp.int32)
        blocks_in = (
            keys_piece.reshape(step_count, block_len, kv_dev, HD),
            values_piece.reshape(step_count, block_len, kv_dev, HD),
            ids_piece.reshape(step_count, block_len),
            rows_piece.reshape(step_count, block_len),
        )
        return lax.scan(attend_block, state_in, blocks_in)[0]

    def keep_state(state_in):
        return state_in

    soft_state = lax.cond(relevant, run_piece, keep_state, start_state)
    row_best, row_total, weighted = soft_state
    context = (
        jnp.transpose(weighted / row_total[..., None], (2, 0, 1, 3))
        .reshape(tok_dev, heads_dev * HD)
        .astype(jnp.bfloat16)
    )
    partial_out = jnp.dot(context, w_out, preferred_element_type=jnp.float32)
    summed = lax.psum_scatter(partial_out, "mp", scatter_dimension=1, tiled=True)
    attended = (routed_part.astype(jnp.float32) + summed).astype(jnp.bfloat16)
    backward = attended[jnp.minimum(arrived_rows, tok_dev - 1)].reshape(owners, capacity, columns)
    returned = lax.all_to_all(backward, "dp", split_axis=0, concat_axis=0, tiled=True)
    return returned.reshape(owners * capacity, columns)[flat_slot]


def solution(mesh):
    in_specs = (
        P("dp", "mp"),
        P("dp"),
        P("dp"),
        P(),
        P(None, "mp"),
        P(None, "mp"),
        P(None, "mp"),
        P("mp", None),
    )
    out_specs = P("dp", "mp")
    return jax.shard_map(local, mesh=mesh, in_specs=in_specs, out_specs=out_specs, check_vma=False)
```

profile of v0, /device:TPU:1, one launch (start us, length us, event | category | flops | bytes accessed | tf_op | source)
XLA Modules:
  0.0 689.3 jit_solution(14763836879183577752)
XLA Ops:
  12.0 9.6 %all-to-all-start = ((s32[32,1,32]{2,1,0:T(1,128)}), s32[32,1,32]{2,1,0:T(1,128)S(1)}, u32[]{:S(2)}, u32[]{:S(2)}) async-start(s32[32,1,32]{2,1,0:T(1,128)} %all_to_all.12), calls=%async_computation | async-start | bytes 32768 | tf_op jit(solution)/shard_map/all_to_all | solution.py:68
  21.6 4.8 scatter_custom_fusion.1
  28.5 5.3 all-to-all-start.1
  35.2 26.9 %all-to-all-done.1 = bf16[32,32,1024]{2,1,0:T(8,128)(2,1)S(1)} async-done(((bf16[32,32,1024]{2,1,0:T(8,128)(2,1)}), bf16[32,32,1024]{2,1,0:T(8,128)(2,1)S(1)}, u32[]{:S(2)}, u32[]{:S(2)}) %all-to-all-start.1) | async-done | bytes 2097184 | tf_op jit(solution)/shard_map/all_to_all | solution.py:61
  62.1 6.2 scatter_custom_fusion.2
  68.5 45.7 %all-gather.6.cloned.1.call-done = bf16[512,4096]{1,0:T(8,128)(2,1)} async-done(((bf16[512,1024]{1,0:T(8,128)(2,1)}), bf16[512,4096]{1,0:T(8,128)(2,1)}) %all-gather.6.cloned.1.call-update) | async-done | bytes 4194320 | tf_op jit(solution)/shard_map/all_gather | solution.py:78
  120.8 4.2 convolution_convert_fusion
  125.6 24.9 %all-gather.1 = s32[32,1,512]{2,1,0:T(1,128)S(1)} all-gather(s32[1,1,512]{2,1,0:T(1,128)S(1)} %bitcast.137), channel_id=1, replica_groups=mesh['dp'=32,'mp'=4] {'dp'}, dimensions={0}, use_global_device_ids=true | all-gather | bytes 67584 | tf_op jit(solution)/shard_map/all_gather | solution.py:134
  156.4 6.2 fusion.48
  166.8 4.1 all-gather.8.cloned.1.call-done
  170.9 48.1 %all-gather.10.cloned.1.call-done = bf16[16384,128]{1,0:T(8,128)(2,1)} async-done(((bf16[512,128]{1,0:T(8,128)(2,1)}), bf16[16384,128]{1,0:T(8,128)(2,1)}) %all-gather.10.cloned.1.call-update) | async-done | bytes 4194320 | tf_op jit(solution)/shard_map/all_gather | solution.py:133
  219.0 329.5 %conditional.1 = (f32[1,4,512]{2,1,0:T(4,128)}, f32[1,4,512,128]{2,3,1,0:T(8,128)S(1)}) conditional(s32[]{:T(128)} %bitcast.9, () %tuple.17, (bf16[16384,1,128]{0,2,1:T(8,128)(2,1)}, bf16[16384,1,128]{2,0,1:T(8,128)(2,1)}, s32[16384]{0:T(1024)S(1)}, s32[512]{0:T(512)S(1)}, s32[512]{0:T(512)S(1)}, ...), branch_computations={%region_7.8_spmd, %region_8.13_spmd} | conditional | flops 550023168 | bytes 48317764 | solution.py:158
  219.0 6.4 copy.23
  225.4 320.3 %while.14 = (s32[]{:T(128)}, f32[1,4,512]{2,1,0:T(4,128)S(1)}, f32[1,4,512]{2,1,0:T(4,128)}, f32[1,4,512,128]{3,2,1,0:T(8,128)S(1)}, s32[512]{0:T(512)S(1)}, /*i...) while((s32[]{:T(128)}, f32[1,4,512]{2,1,0:T(4,128)S(1)}, ...), condition=%wide.region_12.12_spmd.clone, body=%wide.region_9.11_spmd.clone.sunk | while | flops 549990400 | bytes 33440936 | solution.py:153
  248.8 3.8 fusion.72
  258.8 3.8 fusion.72
  268.8 3.8 fusion.72
  278.9 3.8 fusion.72
  288.9 3.8 fusion.72
  298.9 3.8 fusion.72
  309.0 3.8 fusion.72
  319.0 3.8 fusion.72
  329.0 3.8 fusion.72
  339.0 3.8 fusion.72
  349.1 3.8 fusion.72
  359.1 3.8 fusion.72
  369.1 3.8 fusion.72
  379.2 3.8 fusion.72
  389.2 3.8 fusion.72
  399.2 3.8 fusion.72
  409.3 3.8 fusion.72
  419.3 3.8 fusion.72
  429.3 3.8 fusion.72
  439.3 3.8 fusion.72
  449.4 3.8 fusion.72
  459.4 3.8 fusion.72
  469.4 3.8 fusion.72
  479.5 3.8 fusion.72
  489.5 3.8 fusion.72
  499.5 3.8 fusion.72
  519.6 3.8 fusion.72
  529.6 3.8 fusion.72
  539.6 3.8 fusion.72
  549.4 7.8 %fusion.55 = f32[512,4096]{1,0:T(8,128)} fusion(bf16[512,512]{0,1:T(8,128)(2,1)S(1)} %bitcast.130, bf16[512,4096]{1,0:T(8,128)(2,1)} %param.19), kind=kOutput, calls=%fused_computation.97 | convolution fusion | flops 2147483648 | bytes 13107200 | tf_op jit(solution)/shard_map/dot_general | solution.py:165
  557.2 79.5 %reduce-scatter.2.cloned.1.call-done = f32[512,1024]{1,0:T(8,128)} async-done(((f32[512,4096]{1,0:T(8,128)}), f32[512,1024]{1,0:T(8,128)}) %reduce-scatter.2.cloned.1.call-update) | async-done | bytes 2097168 | tf_op jit(solution)/shard_map/reduce_scatter | solution.py:166
  638.7 5.3 gather_fusion
  644.0 7.7 %all-to-all-start.2 = ((bf16[32,32,1024]{2,1,0:T(8,128)(2,1)}), bf16[32,32,1024]{2,1,0:T(8,128)(2,1)S(1)}, u32[]{:S(2)}, u32[]{:S(2)}) async-start(bf16[32,32,1024]{2,1,0:T(8,128)(2,1)} %bitcast.126), calls=%async_computation.3 | async-start | bytes 4194304 | tf_op jit(solution)/shard_map/all_to_all | solution.py:169
  651.7 28.3 %all-to-all-done.2 = bf16[32,32,1024]{2,1,0:T(8,128)(2,1)S(1)} async-done(((bf16[32,32,1024]{2,1,0:T(8,128)(2,1)}), bf16[32,32,1024]{2,1,0:T(8,128)(2,1)S(1)}, u32[]{:S(2)}, u32[]{:S(2)}) %all-to-all-start.2) | async-done | bytes 2097184 | tf_op jit(solution)/shard_map/all_to_all | solution.py:169
  (356 shorter events, 240.0 us)
Async XLA Ops:
  6.5 110.9 %copy-start = (bf16[4096,128]{1,0:T(8,128)(2,1)S(1)}, bf16[4096,128]{1,0:T(8,128)(2,1)}, u32[]{:S(2)}) copy-start(bf16[4096,128]{1,0:T(8,128)(2,1)} %param.17) | copy-start | bytes 3145732
  12.0 16.5 %all-to-all-start = ((s32[32,1,32]{2,1,0:T(1,128)}), s32[32,1,32]{2,1,0:T(1,128)S(1)}, u32[]{:S(2)}, u32[]{:S(2)}) async-start(s32[32,1,32]{2,1,0:T(1,128)} %all_to_all.12), calls=%async_computation | async-start | bytes 32768 | tf_op jit(solution)/shard_map/all_to_all | solution.py:68
  28.5 33.6 %all-to-all-start.1 = ((bf16[32,32,1024]{2,1,0:T(8,128)(2,1)}), bf16[32,32,1024]{2,1,0:T(8,128)(2,1)S(1)}, u32[]{:S(2)}, u32[]{:S(2)}) async-start(bf16[32,32,1024]{2,1,0:T(8,128)(2,1)} %bitcast.5), calls=%async_computation.1 | async-start | bytes 4194304 | tf_op jit(solution)/shard_map/all_to_all | solution.py:61
  33.9 83.6 %copy-start.7 = (f32[4096]{0:T(1024)S(1)}, f32[4096]{0:T(1024)}, u32[]{:S(2)}) copy-start(f32[4096]{0:T(1024)} %param.15) | copy-start | bytes 49156
  33.9 80.3 %all-gather.6.cloned.1.call-start = ((), (), s32[]{:S(2)}) async-start(), calls=%async_computation.4 | async-start | bytes 5242880 | tf_op jit(solution)/shard_map/all_gather | solution.py:78
  68.4 102.5 %all-gather.8.cloned.1.call-start = ((), (), s32[]{:S(2)}) async-start(), calls=%async_computation.5 | async-start | bytes 4325376 | tf_op jit(solution)/shard_map/all_gather | solution.py:132
  114.2 3.4 copy-start.3
  117.6 3.1 copy-start.6
  120.5 5.1 copy-start.5
  120.5 98.5 %all-gather.10.cloned.1.call-start = ((), (), s32[]{:S(2)}) async-start(), calls=%async_computation.7 | async-start | bytes 4325376 | tf_op jit(solution)/shard_map/all_gather | solution.py:133
  124.9 511.8 %reduce-scatter.2.cloned.1.call-start = ((), (), s32[]{:S(2)}) async-start(), calls=%async_computation.6 | async-start | bytes 10485760 | tf_op jit(solution)/shard_map/reduce_scatter | solution.py:166
  229.4 3.8 copy-start.1
  238.7 3.8 copy-start.1
  248.8 3.8 copy-start.1
  258.8 3.8 copy-start.1
  268.8 3.8 copy-start.1
  278.9 3.8 copy-start.1
  288.9 3.8 copy-start.1
  298.9 3.8 copy-start.1
  308.9 3.8 copy-start.1
  319.0 3.8 copy-start.1
  329.0 3.8 copy-start.1
  339.0 3.8 copy-start.1
  349.1 3.8 copy-start.1
  359.1 3.8 copy-start.1
  369.1 3.8 copy-start.1
  379.1 3.8 copy-start.1
  389.2 3.8 copy-start.1
  399.2 3.8 copy-start.1
  409.2 3.8 copy-start.1
  419.3 3.8 copy-start.1
  429.3 3.8 copy-start.1
  439.3 3.8 copy-start.1
  449.4 3.8 copy-start.1
  459.4 3.8 copy-start.1
  469.4 3.8 copy-start.1
  479.4 3.8 copy-start.1
  489.5 3.8 copy-start.1
  499.5 3.8 copy-start.1
  509.5 3.8 copy-start.1
  519.6 3.8 copy-start.1
  529.6 3.8 copy-start.1
  539.6 3.8 copy-start.1
  545.7 1.0 copy-start.4
  557.2 79.6 %copy-start.2 = (bf16[512,1024]{1,0:T(8,128)(2,1)S(1)}, bf16[512,1024]{1,0:T(8,128)(2,1)}, u32[]{:S(2)}) copy-start(bf16[512,1024]{1,0:T(8,128)(2,1)} %scatter_custom_fusion.2) | copy-start | bytes 3145732
  644.0 36.0 %all-to-all-start.2 = ((bf16[32,32,1024]{2,1,0:T(8,128)(2,1)}), bf16[32,32,1024]{2,1,0:T(8,128)(2,1)S(1)}, u32[]{:S(2)}, u32[]{:S(2)}) async-start(bf16[32,32,1024]{2,1,0:T(8,128)(2,1)} %bitcast.126), calls=%async_computation.3 | async-start | bytes 4194304 | tf_op jit(solution)/shard_map/all_to_all | solution.py:169
Sparse Core Ops, SparseCore 0:
  68.5 45.6 all-gather.5
  120.6 50.2 all-gather.7
  173.2 45.8 all-gather.9
  557.3 79.3 reduce-scatter.1
where the time goes:
time: 692 us; the launch traced here: 689 us
  matrix products  259 us (37%)
  waiting for transfers between devices  235 us (34%)
  other arithmetic  93.1 us (13%)
  local copies, waits for them, and re-layouts  37.1 us (5%)
  blocking collectives  24.9 us (4%)
  starting transfers between devices  22.9 us (3%)
  between operations  16.3 us (2%)
    dot_general x32, matrix products, attend_block(): jnp.einsum('grqk,kgd->grqd', exp_scores.astype(jnp.bfloat16), values_blk,...  122 us
    dot_general x32, matrix products, attend_block(): jnp.einsum('qgrd,kgd->grqk', queries, keys_blk, preferred_element_type=jn...  117 us
    reduce_scatter x1, waiting for transfers between devices, local(): lax.psum_scatter(partial_out, 'mp', scatter_dimension=1, tiled=True)  79.5 us
    all_gather x1, waiting for transfers between devices, local(): values_piece = lax.all_gather(values_own, 'dp', axis=0, tiled=True)  48.1 us
    all_gather x1, waiting for transfers between devices, local(): routed = lax.all_gather(routed_part, 'mp', axis=1, tiled=True)  45.7 us
    add x32, other arithmetic, attend_block(): row_total = row_total * rescale + jnp.sum(exp_scores, axis=-1)  41.2 us
    reduce_sum x32, other arithmetic, attend_block(): row_total = row_total * rescale + jnp.sum(exp_scores, axis=-1)  29.3 us
    all_to_all x1, waiting for transfers between devices, local(): lax.all_to_all(backward, 'dp', split_axis=0, concat_axis=0, tiled=True)  28.3 us
  transfers between devices with their start and end apart: 7, of which 7 were waited for; matrix products, arithmetic and copies ran while one was open for 4% of the time, Pallas kernels for 0%

commit v1 on v0

v1 whole, which is shorter than its diff:
```python
import functools
import math

import jax
import jax.numpy as jnp
from jax import lax
from jax.experimental import pallas as pl
from jax.experimental.pallas import tpu as pltpu
from jax.sharding import PartitionSpec as P

HD = 128
DOC_MAX = 8704

ROPE_BASE = 500000.0
NORM_EPS = 1e-05
NEG_START = -1e30
KEY_BLOCK = 512


def rope_angles(row_index):
    lane_index = jnp.arange(HD // 2, dtype=jnp.float32)
    frequency = jnp.power(jnp.float32(ROPE_BASE), -2.0 * lane_index / HD)
    return row_index.astype(jnp.float32)[:, None] * frequency[None, :]


def rotate(head_values, angles):
    half_width = head_values.shape[-1] // 2
    first_half = head_values[..., :half_width]
    second_half = head_values[..., half_width:]
    cosine = jnp.cos(angles)[:, None, :]
    sine_part = jnp.sin(angles)[:, None, :]
    return jnp.concatenate(
        [
            first_half * cosine - second_half * sine_part,
            second_half * cosine + first_half * sine_part,
        ],
        axis=-1,
    )


def normalize(routed, norm_gain):
    wide_rows = routed.astype(jnp.float32)
    inv_rms = lax.rsqrt(jnp.mean(wide_rows * wide_rows, axis=1, keepdims=True) + NORM_EPS)
    return (wide_rows * inv_rms * norm_gain[None, :]).astype(jnp.bfloat16)


def flash_kernel(span_ref, q_ref, k_ref, v_ref, start_ref, row_ref, o_ref, m_sc, l_sc, acc_sc):
    step = pl.program_id(0)
    heads = q_ref.shape[0]
    block = k_ref.shape[0]
    scale = HD ** (-0.5)

    @pl.when(step == 0)
    def _init():
        m_sc[...] = jnp.full(m_sc.shape, NEG_START, jnp.float32)
        l_sc[...] = jnp.zeros(l_sc.shape, jnp.float32)
        acc_sc[...] = jnp.zeros(acc_sc.shape, jnp.float32)

    @pl.when(step < span_ref[1])
    def _body():
        key_first = (span_ref[0] + step) * block
        key_rows = key_first + lax.broadcasted_iota(jnp.int32, (1, block), 1)
        allowed = (key_rows >= start_ref[...]) & (key_rows <= row_ref[...])
        keys = k_ref[...]
        values = v_ref[...]
        for h in range(heads):
            scores = lax.dot_general(
                q_ref[h], keys, (((1,), (1,)), ((), ())), preferred_element_type=jnp.float32
            ) * scale
            scores = jnp.where(allowed, scores, -jnp.inf)
            m_old = m_sc[h]
            m_new = jnp.maximum(m_old, jnp.max(scores, axis=-1, keepdims=True))
            rescale = jnp.exp(m_old - m_new)
            exp_scores = jnp.exp(scores - m_new)
            l_sc[h] = l_sc[h] * rescale + jnp.sum(exp_scores, axis=-1, keepdims=True)
            acc_sc[h] = acc_sc[h] * rescale + jnp.dot(
                exp_scores.astype(jnp.bfloat16), values, preferred_element_type=jnp.float32
            )
            m_sc[h] = m_new

    @pl.when(step == pl.num_programs(0) - 1)
    def _finish():
        for h in range(heads):
            o_ref[h] = (acc_sc[h] / l_sc[h]).astype(o_ref.dtype)


def flash_attention(span, queries, keys, values, row_start, row_index, max_blocks):
    heads, rows, _ = queries.shape
    block = KEY_BLOCK

    def kv_map(step, span_ref):
        return (span_ref[0] + jnp.minimum(step, span_ref[1] - 1), 0)

    grid_spec = pltpu.PrefetchScalarGridSpec(
        num_scalar_prefetch=1,
        grid=(max_blocks,),
        in_specs=[
            pl.BlockSpec((heads, rows, HD), lambda step, span_ref: (0, 0, 0)),
            pl.BlockSpec((block, HD), kv_map),
            pl.BlockSpec((block, HD), kv_map),
            pl.BlockSpec((rows, 1), lambda step, span_ref: (0, 0)),
            pl.BlockSpec((rows, 1), lambda step, span_ref: (0, 0)),
        ],
        out_specs=pl.BlockSpec((heads, rows, HD), lambda step, span_ref: (0, 0, 0)),
        scratch_shapes=[
            pltpu.VMEM((heads, rows, 1), jnp.float32),
            pltpu.VMEM((heads, rows, 1), jnp.float32),
            pltpu.VMEM((heads, rows, HD), jnp.float32),
        ],
    )
    flops = 4 * heads * rows * block * HD * max_blocks
    return pl.pallas_call(
        flash_kernel,
        grid_spec=grid_spec,
        out_shape=jax.ShapeDtypeStruct((heads, rows, HD), jnp.bfloat16),
        compiler_params=pltpu.CompilerParams(dimension_semantics=("arbitrary",)),
        cost_estimate=pl.CostEstimate(
            flops=flops,
            transcendentals=heads * rows * block * max_blocks,
            bytes_accessed=2 * block * HD * 2 * max_blocks + 2 * 2 * heads * rows * HD,
        ),
    )(span, queries, keys, values, row_start, row_index)


def local(hidden_rows, destination, doc_ids, norm_gain, w_query, w_key, w_value, w_out):
    owners = lax.axis_size("dp")
    my_index = lax.axis_index("dp")
    tok_dev, columns = hidden_rows.shape
    capacity = 2 * tok_dev // owners
    target = destination // tok_dev
    owner_ids = jnp.arange(owners, dtype=jnp.int32)
    one_hot = (target[:, None] == owner_ids[None, :]).astype(jnp.int32)
    slot_rank = jnp.sum((jnp.cumsum(one_hot, axis=0) - 1) * one_hot, axis=1)
    flat_slot = target * capacity + slot_rank
    outgoing = (
        jnp.zeros((owners * capacity, columns), hidden_rows.dtype).at[flat_slot].set(hidden_rows)
    )
    places = (
        jnp.full((owners * capacity,), tok_dev, jnp.int32).at[flat_slot].set(destination % tok_dev)
    )
    block_first = my_index * tok_dev
    first_id = doc_ids[0]
    last_id = doc_ids[tok_dev - 1]
    less_count = jnp.sum((doc_ids[None, :] < doc_ids[:, None]).astype(jnp.int32), axis=1)
    last_run_start = block_first + less_count[tok_dev - 1]
    info = jnp.broadcast_to(jnp.stack([last_id, last_run_start])[None, :], (owners, 2))
    places_info = jnp.concatenate([places.reshape(owners, capacity), info], axis=1)
    arrived = lax.all_to_all(
        outgoing.reshape(owners, capacity, columns), "dp", split_axis=0, concat_axis=0, tiled=True
    )
    arrived_info = lax.all_to_all(places_info, "dp", split_axis=0, concat_axis=0, tiled=True)
    arrived_rows = arrived_info[:, :capacity].reshape(-1)
    peer_last_id = arrived_info[:, capacity]
    peer_run_start = arrived_info[:, capacity + 1]
    earlier = (owner_ids < my_index) & (peer_last_id == first_id)
    doc_low = jnp.minimum(block_first, jnp.min(jnp.where(earlier, peer_run_start, block_first)))
    row_index = block_first + jnp.arange(tok_dev, dtype=jnp.int32)
    row_start = jnp.where(doc_ids == first_id, doc_low, block_first + less_count)

    routed_part = (
        jnp.zeros((tok_dev, columns), hidden_rows.dtype)
        .at[arrived_rows]
        .set(arrived.reshape(-1, columns), mode="drop")
    )
    routed = lax.all_gather(routed_part, "mp", axis=1, tiled=True)
    normed = normalize(routed, norm_gain)
    heads_dev = w_query.shape[1] // HD
    kv_dev = w_key.shape[1] // HD
    angles = rope_angles(row_index)
    queries = jnp.dot(normed, w_query, preferred_element_type=jnp.float32).reshape(
        tok_dev, heads_dev, HD
    )
    queries = rotate(queries, angles).astype(jnp.bfloat16)
    keys_own = jnp.dot(normed, w_key, preferred_element_type=jnp.float32).reshape(
        tok_dev, kv_dev, HD
    )
    keys_own = rotate(keys_own, angles).astype(jnp.bfloat16).reshape(tok_dev, kv_dev * HD)
    values_own = jnp.dot(normed, w_value, preferred_element_type=jnp.float32).astype(jnp.bfloat16)
    keys_all = lax.all_gather(keys_own, "dp", axis=0, tiled=True)
    values_all = lax.all_gather(values_own, "dp", axis=0, tiled=True)

    block = KEY_BLOCK
    last_block = (block_first + tok_dev - 1) // block
    first_block = doc_low // block
    max_blocks = min((tok_dev - 1) // block + -(-(DOC_MAX - 1) // block) + 1, owners * tok_dev // block)
    span = jnp.stack([first_block, last_block - first_block + 1]).astype(jnp.int32)
    context = flash_attention(
        span,
        jnp.transpose(queries, (1, 0, 2)),
        keys_all,
        values_all,
        row_start[:, None],
        row_index[:, None],
        max_blocks,
    )
    context = jnp.transpose(context, (1, 0, 2)).reshape(tok_dev, heads_dev * HD)
    context_all = lax.all_gather(context, "mp", axis=1, tiled=True)
    w_cols = lax.all_to_all(w_out, "mp", split_axis=1, concat_axis=0, tiled=True)
    summed = jnp.dot(context_all, w_cols, preferred_element_type=jnp.float32)
    attended = (routed_part.astype(jnp.float32) + summed).astype(jnp.bfloat16)
    backward = attended[jnp.minimum(arrived_rows, tok_dev - 1)].reshape(owners, capacity, columns)
    returned = lax.all_to_all(backward, "dp", split_axis=0, concat_axis=0, tiled=True)
    return returned.reshape(owners * capacity, columns)[flat_slot]


def solution(mesh):
    in_specs = (
        P("dp", "mp"),
        P("dp"),
        P("dp"),
        P(),
        P(None, "mp"),
        P(None, "mp"),
        P(None, "mp"),
        P("mp", None),
    )
    out_specs = P("dp", "mp")
    return jax.shard_map(local, mesh=mesh, in_specs=in_specs, out_specs=out_specs, check_vma=False)
```

time: 692 us -> 403 us (0.58)
  matrix products: 259 us -> 16.6 us
  other arithmetic: 93.1 us -> 16.9 us
  waiting for transfers between devices: 235 us -> 267 us
  blocking collectives: 24.9 us -> 0 us
  Pallas kernels: 0 us -> 14.3 us
    dot_general x65 -> x1, matrix products: 247 us -> 5.17 us  [local(): summed = jnp.dot(context_all, w_cols, preferred_element_type=jnp.float32)]
    all_gather x2 -> x3, waiting for transfers between devices: 52.2 us -> 163 us  [the longest x1 101 us: local(): context_all = lax.all_gather(context, 'mp', axis=1, tiled=True)]
    reduce_scatter x1 -> x0, waiting for transfers between devices: 79.5 us -> none  [local(): lax.psum_scatter(partial_out, 'mp', scatter_dimension=1, tiled=True)]
    add x33 -> x1, other arithmetic: 41.2 us -> 0.71 us  [local(): row_index = block_first + jnp.arange(tok_dev, dtype=jnp.int32)]
    reduce_sum x32 -> x1, other arithmetic: 29.3 us -> 1.03 us  [local(): jnp.sum((doc_ids[None, :] < doc_ids[:, None]).astype(jnp.int32), axis=1)]
    all_gather x1 -> x0, blocking collectives: 24.9 us -> none  [local(): ids_piece = lax.all_gather(doc_ids, 'dp', axis=0, tiled=True)]
    pallas_call x0 -> x1, Pallas kernels: none -> 14.3 us  [flash_attention(): pl.pallas_call(flash_kernel, grid_spec=grid_spec, out_shape=jax.ShapeDtyp...]
    and x32 -> x0, other arithmetic: 8.84 us -> none  [attend_block(): (doc_ids[:, None] == ids_blk[None, :]) & (key_rows[None, :] <= query_rows...]
  transfers between devices with their start and end apart: 7 -> 8, of which waited for: 7 -> 7; matrix products, arithmetic and copies ran while one was open for 4% -> 10% of each run, Pallas kernels for 0% -> 4%
where the time goes in v1:
time: 403 us; the launch traced here: 401 us
  waiting for transfers between devices  267 us (66%)
  local copies, waits for them, and re-layouts  42.9 us (11%)
  starting transfers between devices  28 us (7%)
  other arithmetic  16.9 us (4%)
  matrix products  16.6 us (4%)
  between operations  14.6 us (4%)
  Pallas kernels  14.3 us (4%)
    all_gather x1, waiting for transfers between devices, local(): context_all = lax.all_gather(context, 'mp', axis=1, tiled=True)  101 us
    all_gather x1, waiting for transfers between devices, local(): values_all = lax.all_gather(values_own, 'dp', axis=0, tiled=True)  48 us
    all_gather x1, waiting for transfers between devices, local(): routed = lax.all_gather(routed_part, 'mp', axis=1, tiled=True)  45.7 us
    all_to_all x1, waiting for transfers between devices, local(): lax.all_to_all(backward, 'dp', split_axis=0, concat_axis=0, tiled=True)  28.3 us
    all_to_all x1, waiting for transfers between devices, local(): lax.all_to_all(outgoing.reshape(owners, capacity, columns), 'dp', split_a...  28.1 us
    pallas_call x1, Pallas kernels, flash_attention(): pl.pallas_call(flash_kernel, grid_spec=grid_spec, out_shape=jax.ShapeDtyp...  14.3 us
    all_gather x1, waiting for transfers between devices, local(): keys_all = lax.all_gather(keys_own, 'dp', axis=0, tiled=True)  13.7 us
    all_to_all x1, starting transfers between devices, local(): lax.all_to_all(places_info, 'dp', split_axis=0, concat_axis=0, tiled=True)  9.6 us
  transfers between devices with their start and end apart: 8, of which 7 were waited for; matrix products, arithmetic and copies ran while one was open for 10% of the time, Pallas kernels for 4%

profile of v1, /device:TPU:1, one launch (start us, length us, event | category | flops | bytes accessed | tf_op | source)
XLA Modules:
  0.0 400.6 jit_solution(13557334669274854657)
XLA Ops:
  6.5 1.0 convert_reduce_fusion
  7.6 1.3 fusion.30
  8.9 0.7 add_select_fusion
  9.6 1.2 reduce-window.6
  10.8 0.2 slice_reduce_fusion
  11.2 2.4 scatter_custom_fusion
  13.7 0.6 slice.39
  14.9 0.6 pad_add_fusion.1
  15.6 0.6 pad_add_fusion
  16.2 9.6 %all-to-all-start = ((s32[32,1,34]{2,1,0:T(1,128)}), s32[32,1,34]{2,1,0:T(1,128)S(1)}, u32[]{:S(2)}, u32[]{:S(2)}) async-start(s32[32,1,34]{2,1,0:T(1,128)} %bitcast.5), calls=%async_computation | async-start | bytes 32768 | tf_op jit(solution)/shard_map/all_to_all | solution.py:151
  25.9 4.8 %scatter_custom_fusion.1 = bf16[1024,1024]{1,0:T(8,128)(2,1)} fusion(s32[512]{0:T(512)S(1)} %compare_select_fusion.2, bf16[512,1024]{1,0:T(8,128)(2,1)} %param.8, bf16[]{:T(256)} %constant.70.clone.1), kind=kCustom, calls=%fused_computation.15 | custom fusion | bytes 2097664 | tf_op jit(solution)/shard_map/scatter | solution.py:136
  30.7 2.0 all-to-all-done
  32.7 5.3 %all-to-all-start.1 = ((bf16[32,32,1024]{2,1,0:T(8,128)(2,1)}), bf16[32,32,1024]{2,1,0:T(8,128)(2,1)S(1)}, u32[]{:S(2)}, u32[]{:S(2)}) async-start(bf16[32,32,1024]{2,1,0:T(8,128)(2,1)} %bitcast.8), calls=%async_computation.1 | async-start | bytes 4194304 | tf_op jit(solution)/shard_map/all_to_all | solution.py:148
  38.2 28.1 %all-to-all-done.1 = bf16[32,32,1024]{2,1,0:T(8,128)(2,1)S(1)} async-done(((bf16[32,32,1024]{2,1,0:T(8,128)(2,1)}), bf16[32,32,1024]{2,1,0:T(8,128)(2,1)S(1)}, u32[]{:S(2)}, u32[]{:S(2)}) %all-to-all-start.1) | async-done | bytes 2097184 | tf_op jit(solution)/shard_map/all_to_all | solution.py:148
  66.4 6.2 %scatter_custom_fusion.2 = bf16[512,1024]{1,0:T(8,128)(2,1)} fusion(s32[1024]{0:T(1024)S(1)} %bitcast.66, bf16[1024,1024]{1,0:T(8,128)(2,1)S(1)} %bitcast.56, bf16[]{:T(256)} %constant.70.clone.1), kind=kCustom, calls=%fused_computation.19 | custom fusion | bytes 1048578 | tf_op jit(solution)/shard_map/scatter | solution.py:163
  72.7 45.7 %all-gather.5.cloned.1.call-done = bf16[512,4096]{1,0:T(8,128)(2,1)} async-done(((bf16[512,1024]{1,0:T(8,128)(2,1)}), bf16[512,4096]{1,0:T(8,128)(2,1)}) %all-gather.5.cloned.1.call-update) | async-done | bytes 4194320 | tf_op jit(solution)/shard_map/all_gather | solution.py:165
  118.4 3.2 fusion
  121.9 1.3 convolution_bitcast_fusion
  123.2 1.2 fusion.16
  124.4 0.8 pad_maximum_fusion
  125.2 4.2 %convolution_convert_fusion = bf16[512,128]{1,0:T(8,128)(2,1)} fusion(bf16[4096,128]{1,0:T(8,128)(2,1)S(1)} %copy-done.4, bf16[512,4096]{1,0:T(8,128)(2,1)} %all-gather.5.cloned.1.call-done, f32[4096]{0:T(1024)S(1)} %copy-done.5, f32[512]{0:T(512)S(1)} %add_rsqrt_fusion), kind=kOutput, calls=%fused_computation.12 | convolution fusion | flops 545325056 | bytes 5392384 | tf_op jit(solution)/shard_map/dot_general | solution.py:178
  129.4 6.5 %copy.40 = bf16[512,4096]{0,1:T(8,128)(2,1)} copy(bf16[512,4096]{1,0:T(8,128)(2,1)} %param.15) | data formatting | bytes 8388608 | tf_op args[7]
  136.0 5.0 %all-to-all-start.2 = ((bf16[512,4,1024]{0,2,1:T(8,128)(2,1)}), bf16[512,4,1024]{0,2,1:T(8,128)(2,1)}, u32[]{:S(2)}, u32[]{:S(2)}) async-start(bf16[512,4,1024]{0,2,1:T(8,128)(2,1)} %bitcast.53), calls=%async_computation.2 | async-start | bytes 8388608 | tf_op jit(solution)/shard_map/all_to_all | solution.py:198
  141.0 0.2 all-gather.11.cloned.1.call-start
  141.2 0.7 iota_add_fusion.row_ref
  141.9 1.7 multiply_cosine_fusion.1
  143.9 0.8 fusion.20
  144.6 0.7 fusion.24
  145.9 0.6 add_select_fusion.2
  146.5 0.9 copy.38.start_ref
  147.4 0.6 pad_add_fusion.2.span_ref
  148.0 5.9 %fusion.27 = f32[512,512]{0,1:T(8,128)S(1)} fusion(bf16[4096,512]{1,0:T(8,128)(2,1)} %param.12, bf16[512,4096]{1,0:T(8,128)(2,1)} %all-gather.5.cloned.1.call-done, f32[4096]{0:T(1024)S(1)} %copy-done.5, f32[512]{0:T(512)S(1)} %add_rsqrt_fusion), kind=kOutput, calls=%fused_computation.72 | convolution fusion | flops 2155872256 | bytes 9455616 | tf_op jit(solution)/shard_map/dot_general | solution.py:170
  153.9 0.9 fusion.29
  154.8 0.3 copy.44
  155.1 1.4 copy.43
  156.5 1.2 subtract_convert_fusion
  157.8 1.1 maximum_bitcast_fusion.q_ref
  158.8 13.7 %all-gather.7.cloned.1.call-done.k_ref = bf16[16384,128]{1,0:T(8,128)(2,1)} async-done(((bf16[512,128]{1,0:T(8,128)(2,1)}), bf16[16384,128]{1,0:T(8,128)(2,1)}) %all-gather.7.cloned.1.call-update) | async-done | bytes 4194320 | tf_op jit(solution)/shard_map/all_gather | solution.py:179
  172.6 48.0 %all-gather.9.cloned.1.call-done.v_ref = bf16[16384,128]{1,0:T(8,128)(2,1)} async-done(((bf16[512,128]{1,0:T(8,128)(2,1)}), bf16[16384,128]{1,0:T(8,128)(2,1)}) %all-gather.9.cloned.1.call-update) | async-done | bytes 4194320 | tf_op jit(solution)/shard_map/all_gather | solution.py:180
  220.6 14.3 %shard_map.82 = bf16[4,512,128]{2,1,0:T(8,128)(2,1)} custom-call(s32[2]{0:T(128)} %pad_add_fusion.2.span_ref, bf16[4,512,128]{2,1,0:T(8,128)(2,1)} %maximum_bitcast_fusion.q_ref, bf16[16384,128]{1,0:T(8,128)(2,1)} %all-gather.7.cloned.1.call-done.k_ref, bf16[16384,128]{1,0:T(8,128)(2,1)} %all-gather.9.cloned.1.call-done.v_ref, s32[512,1]{1,0:T(8,128)} %copy.38.start_ref, ...), custom_call_target="tpu_custom_call" | custom-call | flops 9663676416 | bytes 5767168 | tf_op jit(solution)/shard_map/pallas_call | solution.py:112
  234.9 2.1 copy.39
  237.0 6.4 %copy.41 = bf16[4,512,1024]{2,1,0:T(8,128)(2,1)} copy(bf16[4,512,1024]{1,2,0:T(8,128)(2,1)} %bitcast.22) | data formatting | bytes 8388608 | tf_op jit(solution)/shard_map/all_to_all | solution.py:198
  243.4 101.3 %all-gather.11.cloned.1.call-done = bf16[512,2048]{0,1:T(8,128)(2,1)} async-done(((bf16[512,512]{0,1:T(8,128)(2,1)}), bf16[512,2048]{0,1:T(8,128)(2,1)}) %all-gather.11.cloned.1.call-update) | async-done | bytes 2097168 | tf_op jit(solution)/shard_map/all_gather | solution.py:197
  344.8 5.2 %add_convert_fusion = bf16[512,1024]{1,0:T(8,128)(2,1)S(1)} fusion(bf16[512,1024]{1,0:T(8,128)(2,1)S(1)} %copy-done.2, bf16[512,2048]{0,1:T(8,128)(2,1)} %all-gather.11.cloned.1.call-done, bf16[2048,1024]{1,0:T(8,128)(2,1)} %bitcast.55), kind=kOutput, calls=%fused_computation.10 | convolution fusion | flops 2149056512 | bytes 8388608 | tf_op jit(solution)/shard_map/dot_general | solution.py:199
  349.9 5.4 %gather_fusion = bf16[1024,1024]{1,0:T(8,128)(2,1)} fusion(bf16[512,1024]{1,0:T(8,128)(2,1)S(1)} %add_convert_fusion, s32[1024]{0:T(1024)S(1)} %broadcast_clamp_fusion), kind=kCustom, calls=%fused_computation | custom fusion | bytes 4198400 | tf_op jit(solution)/shard_map/gather | solution.py:201
  355.3 7.7 %all-to-all-start.3 = ((bf16[32,32,1024]{2,1,0:T(8,128)(2,1)}), bf16[32,32,1024]{2,1,0:T(8,128)(2,1)S(1)}, u32[]{:S(2)}, u32[]{:S(2)}) async-start(bf16[32,32,1024]{2,1,0:T(8,128)(2,1)} %bitcast.54), calls=%async_computation.3 | async-start | bytes 4194304 | tf_op jit(solution)/shard_map/all_to_all | solution.py:202
  363.0 28.3 %all-to-all-done.3 = bf16[32,32,1024]{2,1,0:T(8,128)(2,1)S(1)} async-done(((bf16[32,32,1024]{2,1,0:T(8,128)(2,1)}), bf16[32,32,1024]{2,1,0:T(8,128)(2,1)S(1)}, u32[]{:S(2)}, u32[]{:S(2)}) %all-to-all-start.3) | async-done | bytes 2097184 | tf_op jit(solution)/shard_map/all_to_all | solution.py:202
  391.3 2.8 gather_fusion.1
  (35 shorter events, 1.0 us)
Async XLA Ops:
  6.5 115.1 %copy-start = (bf16[4096,128]{1,0:T(8,128)(2,1)S(1)}, bf16[4096,128]{1,0:T(8,128)(2,1)}, u32[]{:S(2)}) copy-start(bf16[4096,128]{1,0:T(8,128)(2,1)} %param.13) | copy-start | bytes 3145732
  16.2 16.5 %all-to-all-start = ((s32[32,1,34]{2,1,0:T(1,128)}), s32[32,1,34]{2,1,0:T(1,128)S(1)}, u32[]{:S(2)}, u32[]{:S(2)}) async-start(s32[32,1,34]{2,1,0:T(1,128)} %bitcast.5), calls=%async_computation | async-start | bytes 32768 | tf_op jit(solution)/shard_map/all_to_all | solution.py:151
  32.7 33.6 %all-to-all-start.1 = ((bf16[32,32,1024]{2,1,0:T(8,128)(2,1)}), bf16[32,32,1024]{2,1,0:T(8,128)(2,1)S(1)}, u32[]{:S(2)}, u32[]{:S(2)}) async-start(bf16[32,32,1024]{2,1,0:T(8,128)(2,1)} %bitcast.8), calls=%async_computation.1 | async-start | bytes 4194304 | tf_op jit(solution)/shard_map/all_to_all | solution.py:148
  38.1 83.6 %copy-start.5 = (f32[4096]{0:T(1024)S(1)}, f32[4096]{0:T(1024)}, u32[]{:S(2)}) copy-start(f32[4096]{0:T(1024)} %param.11) | copy-start | bytes 49156
  38.1 80.3 %all-gather.5.cloned.1.call-start = ((), (), s32[]{:S(2)}) async-start(), calls=%async_computation.4 | async-start | bytes 5242880 | tf_op jit(solution)/shard_map/all_gather | solution.py:165
  72.6 100.0 %all-gather.7.cloned.1.call-start = ((), (), s32[]{:S(2)}) async-start(), calls=%async_computation.5 | async-start | bytes 4325376 | tf_op jit(solution)/shard_map/all_gather | solution.py:179
  118.4 3.4 copy-start.1
  121.9 3.4 copy-start.4
  125.2 95.4 %all-gather.9.cloned.1.call-start = ((), (), s32[]{:S(2)}) async-start(), calls=%async_computation.6 | async-start | bytes 4325376 | tf_op jit(solution)/shard_map/all_gather | solution.py:180
  136.0 9.9 %copy-start.3 = (s32[512]{0:T(512)S(1)}, s32[512]{0:T(512)}, u32[]{:S(2)}) copy-start(s32[512]{0:T(512)} %param.10) | copy-start | bytes 6148
  136.0 101.0 %all-to-all-start.2 = ((bf16[512,4,1024]{0,2,1:T(8,128)(2,1)}), bf16[512,4,1024]{0,2,1:T(8,128)(2,1)}, u32[]{:S(2)}, u32[]{:S(2)}) async-start(bf16[512,4,1024]{0,2,1:T(8,128)(2,1)} %bitcast.53), calls=%async_computation.2 | async-start | bytes 8388608 | tf_op jit(solution)/shard_map/all_to_all | solution.py:198
  141.0 203.8 %all-gather.11.cloned.1.call-start = ((), (), s32[]{:S(2)}) async-start(), calls=%async_computation.7 | async-start | bytes 2621440 | tf_op jit(solution)/shard_map/all_gather | solution.py:197
  237.0 107.8 %copy-start.2 = (bf16[512,1024]{1,0:T(8,128)(2,1)S(1)}, bf16[512,1024]{1,0:T(8,128)(2,1)}, u32[]{:S(2)}) copy-start(bf16[512,1024]{1,0:T(8,128)(2,1)} %scatter_custom_fusion.2) | copy-start | bytes 3145732
  355.3 36.0 %all-to-all-start.3 = ((bf16[32,32,1024]{2,1,0:T(8,128)(2,1)}), bf16[32,32,1024]{2,1,0:T(8,128)(2,1)S(1)}, u32[]{:S(2)}, u32[]{:S(2)}) async-start(bf16[32,32,1024]{2,1,0:T(8,128)(2,1)} %bitcast.54), calls=%async_computation.3 | async-start | bytes 4194304 | tf_op jit(solution)/shard_map/all_to_all | solution.py:202
Sparse Core Ops, SparseCore 0:
  72.7 45.6 all-gather.4
  125.3 47.2 all-gather.6
  174.8 45.6 all-gather.8
  237.1 107.6 all-gather.10

commit v2 on v1

--- a/solution.py
+++ b/solution.py
@@ -46,7 +46,7 @@
 
 def flash_kernel(span_ref, q_ref, k_ref, v_ref, start_ref, row_ref, o_ref, m_sc, l_sc, acc_sc):
     step = pl.program_id(0)
-    heads = q_ref.shape[0]
+    heads = m_sc.shape[0]
     block = k_ref.shape[0]
     scale = HD ** (-0.5)
 
@@ -56,18 +56,23 @@
         l_sc[...] = jnp.zeros(l_sc.shape, jnp.float32)
         acc_sc[...] = jnp.zeros(acc_sc.shape, jnp.float32)
 
-    @pl.when(step < span_ref[1])
-    def _body():
-        key_first = (span_ref[0] + step) * block
-        key_rows = key_first + lax.broadcasted_iota(jnp.int32, (1, block), 1)
-        allowed = (key_rows >= start_ref[...]) & (key_rows <= row_ref[...])
+    key_first = (span_ref[0] + step) * block
+    active = step < span_ref[1]
+    whole = (key_first >= span_ref[2]) & (key_first + block - 1 <= span_ref[3])
+
+    def accumulate(masked):
         keys = k_ref[...]
         values = v_ref[...]
+        if masked:
+            key_rows = key_first + lax.broadcasted_iota(jnp.int32, (1, block), 1)
+            allowed = (key_rows >= start_ref[...]) & (key_rows <= row_ref[...])
         for h in range(heads):
             scores = lax.dot_general(
-                q_ref[h], keys, (((1,), (1,)), ((), ())), preferred_element_type=jnp.float32
+                q_ref[:, h * HD:(h + 1) * HD], keys, (((1,), (1,)), ((), ())),
+                preferred_element_type=jnp.float32,
             ) * scale
-            scores = jnp.where(allowed, scores, -jnp.inf)
+            if masked:
+                scores = jnp.where(allowed, scores, -jnp.inf)
             m_old = m_sc[h]
             m_new = jnp.maximum(m_old, jnp.max(scores, axis=-1, keepdims=True))
             rescale = jnp.exp(m_old - m_new)
@@ -78,30 +83,43 @@
             )
             m_sc[h] = m_new
 
+    @pl.when(active & whole)
+    def _whole():
+        accumulate(False)
+
+    @pl.when(active & jnp.logical_not(whole))
+    def _masked():
+        accumulate(True)
+
     @pl.when(step == pl.num_programs(0) - 1)
     def _finish():
         for h in range(heads):
-            o_ref[h] = (acc_sc[h] / l_sc[h]).astype(o_ref.dtype)
-
-
-def flash_attention(span, queries, keys, values, row_start, row_index, max_blocks):
-    heads, rows, _ = queries.shape
+            o_ref[:, h * HD:(h + 1) * HD] = (acc_sc[h] / l_sc[h]).astype(o_ref.dtype)
+
+
+def flash_attention(span, queries, kv_all, row_start, row_index, max_blocks):
+    rows, width = queries.shape
+    heads = width // HD
     block = KEY_BLOCK
-
-    def kv_map(step, span_ref):
-        return (span_ref[0] + jnp.minimum(step, span_ref[1] - 1), 0)
+    halves = kv_all.shape[0]
+
+    def kv_map(column):
+        def index_map(step, span_ref):
+            key_block = span_ref[0] + jnp.minimum(step, span_ref[1] - 1)
+            return (key_block % halves, key_block // halves, 0, column)
+        return index_map
 
     grid_spec = pltpu.PrefetchScalarGridSpec(
         num_scalar_prefetch=1,
         grid=(max_blocks,),
         in_specs=[
-            pl.BlockSpec((heads, rows, HD), lambda step, span_ref: (0, 0, 0)),
-            pl.BlockSpec((block, HD), kv_map),
-            pl.BlockSpec((block, HD), kv_map),
+            pl.BlockSpec((rows, width), lambda step, span_ref: (0, 0)),
+            pl.BlockSpec((None, None, block, HD), kv_map(0)),
+            pl.BlockSpec((None, None, block, HD), kv_map(1)),
             pl.BlockSpec((rows, 1), lambda step, span_ref: (0, 0)),
             pl.BlockSpec((rows, 1), lambda step, span_ref: (0, 0)),
         ],
-        out_specs=pl.BlockSpec((heads, rows, HD), lambda step, span_ref: (0, 0, 0)),
+        out_specs=pl.BlockSpec((rows, width), lambda step, span_ref: (0, 0)),
         scratch_shapes=[
             pltpu.VMEM((heads, rows, 1), jnp.float32),
             pltpu.VMEM((heads, rows, 1), jnp.float32),
@@ -112,19 +130,19 @@
     return pl.pallas_call(
         flash_kernel,
         grid_spec=grid_spec,
-        out_shape=jax.ShapeDtypeStruct((heads, rows, HD), jnp.bfloat16),
+        out_shape=jax.ShapeDtypeStruct((rows, width), jnp.bfloat16),
         compiler_params=pltpu.CompilerParams(dimension_semantics=("arbitrary",)),
         cost_estimate=pl.CostEstimate(
             flops=flops,
             transcendentals=heads * rows * block * max_blocks,
-            bytes_accessed=2 * block * HD * 2 * max_blocks + 2 * 2 * heads * rows * HD,
+            bytes_accessed=2 * block * HD * 2 * max_blocks + 2 * 2 * rows * width,
         ),
-    )(span, queries, keys, values, row_start, row_index)
+    )(span, queries, kv_all, kv_all, row_start, row_index)
 
 
 def local(hidden_rows, destination, doc_ids, norm_gain, w_query, w_key, w_value, w_out):
-    owners = lax.axis_size("dp")
-    my_index = lax.axis_index("dp")
+    owners = lax.axis_size(("chip", "core"))
+    my_index = lax.axis_index(("chip", "core"))
     tok_dev, columns = hidden_rows.shape
     capacity = 2 * tok_dev // owners
     target = destination // tok_dev
@@ -146,9 +164,9 @@
     info = jnp.broadcast_to(jnp.stack([last_id, last_run_start])[None, :], (owners, 2))
     places_info = jnp.concatenate([places.reshape(owners, capacity), info], axis=1)
     arrived = lax.all_to_all(
-        outgoing.reshape(owners, capacity, columns), "dp", split_axis=0, concat_axis=0, tiled=True
-    )
-    arrived_info = lax.all_to_all(places_info, "dp", split_axis=0, concat_axis=0, tiled=True)
+        outgoing.reshape(owners, capacity, columns), ("chip", "core"), split_axis=0, concat_axis=0, tiled=True
+    )
+    arrived_info = lax.all_to_all(places_info, ("chip", "core"), split_axis=0, concat_axis=0, tiled=True)
     arrived_rows = arrived_info[:, :capacity].reshape(-1)
     peer_last_id = arrived_info[:, capacity]
     peer_run_start = arrived_info[:, capacity + 1]
@@ -170,49 +188,56 @@
     queries = jnp.dot(normed, w_query, preferred_element_type=jnp.float32).reshape(
         tok_dev, heads_dev, HD
     )
-    queries = rotate(queries, angles).astype(jnp.bfloat16)
+    queries = rotate(queries, angles).astype(jnp.bfloat16).reshape(tok_dev, heads_dev * HD)
     keys_own = jnp.dot(normed, w_key, preferred_element_type=jnp.float32).reshape(
         tok_dev, kv_dev, HD
     )
     keys_own = rotate(keys_own, angles).astype(jnp.bfloat16).reshape(tok_dev, kv_dev * HD)
     values_own = jnp.dot(normed, w_value, preferred_element_type=jnp.float32).astype(jnp.bfloat16)
-    keys_all = lax.all_gather(keys_own, "dp", axis=0, tiled=True)
-    values_all = lax.all_gather(values_own, "dp", axis=0, tiled=True)
+    kv_own = jnp.concatenate([keys_own, values_own], axis=1)
+    kv_chips = lax.all_gather(kv_own, "chip", axis=0, tiled=False)
+    kv_all = lax.all_gather(kv_chips, "core", axis=0, tiled=False)
 
     block = KEY_BLOCK
     last_block = (block_first + tok_dev - 1) // block
     first_block = doc_low // block
     max_blocks = min((tok_dev - 1) // block + -(-(DOC_MAX - 1) // block) + 1, owners * tok_dev // block)
-    span = jnp.stack([first_block, last_block - first_block + 1]).astype(jnp.int32)
+    span = jnp.stack(
+        [first_block, last_block - first_block + 1, jnp.max(row_start), block_first]
+    ).astype(jnp.int32)
     context = flash_attention(
-        span,
-        jnp.transpose(queries, (1, 0, 2)),
-        keys_all,
-        values_all,
-        row_start[:, None],
-        row_index[:, None],
-        max_blocks,
-    )
-    context = jnp.transpose(context, (1, 0, 2)).reshape(tok_dev, heads_dev * HD)
+        span, queries, kv_all, row_start[:, None], row_index[:, None], max_blocks
+    )
     context_all = lax.all_gather(context, "mp", axis=1, tiled=True)
-    w_cols = lax.all_to_all(w_out, "mp", split_axis=1, concat_axis=0, tiled=True)
-    summed = jnp.dot(context_all, w_cols, preferred_element_type=jnp.float32)
+    mp_size = lax.axis_size("mp")
+    w_split = jnp.transpose(w_out.reshape(w_out.shape[0], mp_size, -1), (1, 0, 2))
+    w_cols = lax.all_to_all(w_split, "mp", split_axis=0, concat_axis=0, tiled=True)
+    summed = jnp.dot(
+        context_all, w_cols.reshape(-1, w_cols.shape[2]), preferred_element_type=jnp.float32
+    )
     attended = (routed_part.astype(jnp.float32) + summed).astype(jnp.bfloat16)
     backward = attended[jnp.minimum(arrived_rows, tok_dev - 1)].reshape(owners, capacity, columns)
-    returned = lax.all_to_all(backward, "dp", split_axis=0, concat_axis=0, tiled=True)
+    returned = lax.all_to_all(backward, ("chip", "core"), split_axis=0, concat_axis=0, tiled=True)
     return returned.reshape(owners * capacity, columns)[flat_slot]
 
 
 def solution(mesh):
+    dp_size, mp_size = mesh.devices.shape
+    split_mesh = jax.sharding.Mesh(
+        mesh.devices.reshape(dp_size // 2, 2, mp_size), ("chip", "core", "mp")
+    )
+    rows = ("chip", "core")
     in_specs = (
-        P("dp", "mp"),
-        P("dp"),
-        P("dp"),
+        P(rows, "mp"),
+        P(rows),
+        P(rows),
         P(),
         P(None, "mp"),
         P(None, "mp"),
         P(None, "mp"),
         P("mp", None),
     )
-    out_specs = P("dp", "mp")
-    return jax.shard_map(local, mesh=mesh, in_specs=in_specs, out_specs=out_specs, check_vma=False)
+    out_specs = P(rows, "mp")
+    return jax.shard_map(
+        local, mesh=split_mesh, in_specs=in_specs, out_specs=out_specs, check_vma=False
+    )

time: 403 us -> 401 us (level)
    all_to_all x4, waiting for transfers between devices: 58.5 us -> 74.5 us  [the longest x1 28.3 us: local(): lax.all_to_all(backward, ('chip', 'core'), split_axis=0, concat_axis=0, t...]
    all_gather x1, waiting for transfers between devices: 101 us -> 87.1 us  [local(): context_all = lax.all_gather(context, 'mp', axis=1, tiled=True)]
    all_gather x0 -> x1, local copies, waits for them, and re-layouts: none -> 6.37 us  [local(): kv_chips = lax.all_gather(kv_own, 'chip', axis=0, tiled=False)]
    all_gather x2, waiting for transfers between devices: 61.7 us -> 57.4 us  [the longest x1 57.4 us: local(): kv_chips = lax.all_gather(kv_own, 'chip', axis=0, tiled=False)]
    unnamed x15 -> x18, local copies, waits for them, and re-layouts: 8.46 us -> 8.38 us
  transfers between devices with their start and end apart: 8 -> 8, of which waited for: 7 -> 7; matrix products, arithmetic and copies ran while one was open for 10% -> 8% of each run, Pallas kernels for 4% -> 4%
where the time goes in v2:
time: 401 us; the launch traced here: 399 us
  waiting for transfers between devices  265 us (66%)
  local copies, waits for them, and re-layouts  46.2 us (12%)
  starting transfers between devices  28.2 us (7%)
  other arithmetic  15.6 us (4%)
  Pallas kernels  15 us (4%)
  between operations  14.7 us (4%)
  matrix products  14.3 us (4%)
    all_gather x1, waiting for transfers between devices, local(): context_all = lax.all_gather(context, 'mp', axis=1, tiled=True)  87.1 us
    all_gather x1, waiting for transfers between devices, local(): kv_chips = lax.all_gather(kv_own, 'chip', axis=0, tiled=False)  57.4 us
    all_gather x1, waiting for transfers between devices, local(): routed = lax.all_gather(routed_part, 'mp', axis=1, tiled=True)  45.5 us
    all_to_all x1, waiting for transfers between devices, local(): lax.all_to_all(backward, ('chip', 'core'), split_axis=0, concat_axis=0, t...  28.3 us
    all_to_all x1, waiting for transfers between devices, local(): lax.all_to_all(outgoing.reshape(owners, capacity, columns), ('chip', 'cor...  28.1 us
    all_to_all x1, waiting for transfers between devices, local(): lax.all_to_all(w_split, 'mp', split_axis=0, concat_axis=0, tiled=True)  16.1 us
    pallas_call x1, Pallas kernels, flash_attention(): pl.pallas_call(flash_kernel, grid_spec=grid_spec, out_shape=jax.ShapeDtyp...  15 us
    all_to_all x1, starting transfers between devices, local(): lax.all_to_all(places_info, ('chip', 'core'), split_axis=0, concat_axis=0...  9.6 us
  transfers between devices with their start and end apart: 8, of which 7 were waited for; matrix products, arithmetic and copies ran while one was open for 8% of the time, Pallas kernels for 4%

profile of v2, /device:TPU:1, one launch (start us, length us, event | category | flops | bytes accessed | tf_op | source)
XLA Modules:
  0.0 398.6 jit_solution(17969276018416160695)
XLA Ops:
  6.5 1.0 convert_reduce_fusion
  7.6 1.4 fusion.31
  8.9 0.7 add_select_fusion
  9.6 1.2 reduce-window.6
  10.8 0.2 slice_reduce_fusion
  11.2 2.4 scatter_custom_fusion
  13.7 0.6 slice.39
  15.0 0.7 pad_add_fusion.1
  15.7 0.6 pad_add_fusion
  16.4 9.6 %all-to-all-start = ((s32[32,1,34]{2,1,0:T(1,128)}), s32[32,1,34]{2,1,0:T(1,128)S(1)}, u32[]{:S(2)}, u32[]{:S(2)}) async-start(s32[32,1,34]{2,1,0:T(1,128)} %bitcast.5), calls=%async_computation | async-start | bytes 32768 | tf_op jit(solution)/shard_map/all_to_all | solution.py:169
  26.0 4.8 %scatter_custom_fusion.1 = bf16[1024,1024]{1,0:T(8,128)(2,1)} fusion(s32[512]{0:T(512)S(1)} %compare_select_fusion.2, bf16[512,1024]{1,0:T(8,128)(2,1)} %param.8, bf16[]{:T(256)} %constant.76.clone.1), kind=kCustom, calls=%fused_computation.15 | custom fusion | bytes 2097664 | tf_op jit(solution)/shard_map/scatter | solution.py:154
  30.8 2.0 all-to-all-done
  32.8 5.3 %all-to-all-start.1 = ((bf16[32,32,1024]{2,1,0:T(8,128)(2,1)}), bf16[32,32,1024]{2,1,0:T(8,128)(2,1)S(1)}, u32[]{:S(2)}, u32[]{:S(2)}) async-start(bf16[32,32,1024]{2,1,0:T(8,128)(2,1)} %bitcast.8), calls=%async_computation.1 | async-start | bytes 4194304 | tf_op jit(solution)/shard_map/all_to_all | solution.py:166
  38.3 28.1 %all-to-all-done.1 = bf16[32,32,1024]{2,1,0:T(8,128)(2,1)S(1)} async-done(((bf16[32,32,1024]{2,1,0:T(8,128)(2,1)}), bf16[32,32,1024]{2,1,0:T(8,128)(2,1)S(1)}, u32[]{:S(2)}, u32[]{:S(2)}) %all-to-all-start.1) | async-done | bytes 2097184 | tf_op jit(solution)/shard_map/all_to_all | solution.py:166
  66.5 6.2 %scatter_custom_fusion.2 = bf16[512,1024]{1,0:T(8,128)(2,1)} fusion(s32[1024]{0:T(1024)S(1)} %bitcast.72, bf16[1024,1024]{1,0:T(8,128)(2,1)S(1)} %bitcast.63, bf16[]{:T(256)} %constant.76.clone.1), kind=kCustom, calls=%fused_computation.20 | custom fusion | bytes 1048578 | tf_op jit(solution)/shard_map/scatter | solution.py:181
  72.7 0.2 all-gather.11.cloned.1.call-start
  73.0 45.5 %all-gather.7.cloned.1.call-done = bf16[512,4096]{1,0:T(8,128)(2,1)} async-done(((bf16[512,1024]{1,0:T(8,128)(2,1)}), bf16[512,4096]{1,0:T(8,128)(2,1)}) %all-gather.7.cloned.1.call-update) | async-done | bytes 4194320 | tf_op jit(solution)/shard_map/all_gather | solution.py:183
  118.5 3.2 fusion
  122.0 1.6 convolution_bitcast_fusion
  123.6 0.6 fusion.18
  124.2 1.6 convolution_convert_fusion
  125.8 0.7 pad_maximum_fusion.1
  126.6 57.4 %all-gather.11.cloned.1.call-done = bf16[8192,256]{0,1:T(8,128)(2,1)} async-done(((bf16[512,256]{0,1:T(8,128)(2,1)}), bf16[8192,256]{0,1:T(8,128)(2,1)}) %all-gather.11.cloned.1.call-update) | async-done | bytes 4194320 | tf_op jit(solution)/shard_map/all_gather | solution.py:198
  183.9 6.4 %copy.40 = bf16[8192,256]{1,0:T(8,128)(2,1)} copy(bf16[8192,256]{0,1:T(8,128)(2,1)} %all-gather.11.cloned.1.call-done) | data formatting | bytes 8388608 | tf_op jit(solution)/shard_map/all_gather | solution.py:198
  190.3 6.5 %copy.38 = bf16[512,4096]{0,1:T(8,128)(2,1)} copy(bf16[512,4096]{1,0:T(8,128)(2,1)} %param.15) | data formatting | bytes 8388608 | tf_op args[7]
  196.8 5.2 %all-to-all-start.2 = ((bf16[4,512,1024]{1,2,0:T(8,128)(2,1)}), bf16[4,512,1024]{1,2,0:T(8,128)(2,1)}, u32[]{:S(2)}, u32[]{:S(2)}) async-start(bf16[4,512,1024]{1,2,0:T(8,128)(2,1)} %bitcast.58), calls=%async_computation.2 | async-start | bytes 8388608 | tf_op jit(solution)/shard_map/all_to_all | solution.py:214
  202.1 0.7 iota_add_fusion.row_ref
  202.9 1.0 multiply_cosine_fusion
  204.0 0.8 fusion.20
  204.8 0.7 fusion.24
  206.1 1.2 fusion.29
  207.3 0.9 copy.37.start_ref
  208.2 1.2 pad_add_fusion.2.span_ref
  209.3 5.9 %fusion.27 = f32[512,512]{0,1:T(8,128)S(1)} fusion(bf16[4096,512]{1,0:T(8,128)(2,1)} %param.12, bf16[512,4096]{1,0:T(8,128)(2,1)} %all-gather.7.cloned.1.call-done, f32[4096]{0:T(1024)S(1)} %copy-done.6, f32[512]{0:T(512)S(1)} %add_rsqrt_fusion), kind=kOutput, calls=%fused_computation.73 | convolution fusion | flops 2155872256 | bytes 9455616 | tf_op jit(solution)/shard_map/dot_general | solution.py:188
  215.4 0.4 copy.42
  215.8 0.4 copy.41
  216.2 0.5 subtract_convert_fusion
  216.7 0.7 pad_maximum_fusion
  217.4 0.9 copy.47
  218.3 15.0 %shard_map.82 = bf16[512,512]{1,0:T(8,128)(2,1)} custom-call(s32[4]{0:T(128)} %pad_add_fusion.2.span_ref, bf16[512,512]{1,0:T(8,128)(2,1)} %bitcast.65, bf16[2,16,512,256]{3,2,1,0:T(8,128)(2,1)} %bitcast.73, bf16[2,16,512,256]{3,2,1,0:T(8,128)(2,1)} %bitcast.74, s32[512,1]{1,0:T(8,128)} %copy.37.start_ref, s32[512,1]{1,0:T(8,128)} %iota_add_fusion.row_ref), custom_call_target="tpu_custom_call" | custom-call | flops 9663676416 | bytes 5767168 | tf_op jit(solution)/shard_map/pallas_call | solution.py:130
  233.4 16.1 %all-to-all-done.2 = bf16[4,512,1024]{1,2,0:T(8,128)(2,1)} async-done(((bf16[4,512,1024]{1,2,0:T(8,128)(2,1)}), bf16[4,512,1024]{1,2,0:T(8,128)(2,1)}, u32[]{:S(2)}, u32[]{:S(2)}) %all-to-all-start.2) | async-done | bytes 4194336 | tf_op jit(solution)/shard_map/all_to_all | solution.py:214
  249.4 6.3 %copy.39 = bf16[4,512,1024]{2,1,0:T(8,128)(2,1)} copy(bf16[4,512,1024]{1,2,0:T(8,128)(2,1)} %all-to-all-done.2) | data formatting | bytes 8388608 | tf_op jit(solution)/shard_map/all_to_all | solution.py:214
  255.7 87.1 %all-gather.9.cloned.1.call-done = bf16[512,2048]{1,0:T(8,128)(2,1)} async-done(((bf16[512,512]{1,0:T(8,128)(2,1)}), bf16[512,2048]{1,0:T(8,128)(2,1)}) %all-gather.9.cloned.1.call-update) | async-done | bytes 2097168 | tf_op jit(solution)/shard_map/all_gather | solution.py:211
  342.8 5.2 %add_convert_fusion = bf16[512,1024]{1,0:T(8,128)(2,1)S(1)} fusion(bf16[512,1024]{1,0:T(8,128)(2,1)S(1)} %copy-done.3, bf16[512,2048]{1,0:T(8,128)(2,1)} %all-gather.9.cloned.1.call-done, bf16[2048,1024]{1,0:T(8,128)(2,1)} %bitcast.61), kind=kOutput, calls=%fused_computation.10 | convolution fusion | flops 2149056512 | bytes 8388608 | tf_op jit(solution)/shard_map/dot_general | solution.py:215
  348.0 5.4 %gather_fusion = bf16[1024,1024]{1,0:T(8,128)(2,1)} fusion(bf16[512,1024]{1,0:T(8,128)(2,1)S(1)} %add_convert_fusion, s32[1024]{0:T(1024)S(1)} %broadcast_clamp_fusion), kind=kCustom, calls=%fused_computation | custom fusion | bytes 4198400 | tf_op jit(solution)/shard_map/gather | solution.py:219
  353.3 7.7 %all-to-all-start.3 = ((bf16[32,32,1024]{2,1,0:T(8,128)(2,1)}), bf16[32,32,1024]{2,1,0:T(8,128)(2,1)S(1)}, u32[]{:S(2)}, u32[]{:S(2)}) async-start(bf16[32,32,1024]{2,1,0:T(8,128)(2,1)} %bitcast.60), calls=%async_computation.3 | async-start | bytes 4194304 | tf_op jit(solution)/shard_map/all_to_all | solution.py:220
  361.0 28.3 %all-to-all-done.3 = bf16[32,32,1024]{2,1,0:T(8,128)(2,1)S(1)} async-done(((bf16[32,32,1024]{2,1,0:T(8,128)(2,1)}), bf16[32,32,1024]{2,1,0:T(8,128)(2,1)S(1)}, u32[]{:S(2)}, u32[]{:S(2)}) %all-to-all-start.3) | async-done | bytes 2097184 | tf_op jit(solution)/shard_map/all_to_all | solution.py:220
  389.3 2.8 gather_fusion.1
  (38 shorter events, 1.1 us)
Async XLA Ops:
  6.5 115.2 %copy-start = (bf16[4096,128]{1,0:T(8,128)(2,1)S(1)}, bf16[4096,128]{1,0:T(8,128)(2,1)}, u32[]{:S(2)}) copy-start(bf16[4096,128]{1,0:T(8,128)(2,1)} %param.13) | copy-start | bytes 3145732
  16.4 16.5 %all-to-all-start = ((s32[32,1,34]{2,1,0:T(1,128)}), s32[32,1,34]{2,1,0:T(1,128)S(1)}, u32[]{:S(2)}, u32[]{:S(2)}) async-start(s32[32,1,34]{2,1,0:T(1,128)} %bitcast.5), calls=%async_computation | async-start | bytes 32768 | tf_op jit(solution)/shard_map/all_to_all | solution.py:169
  32.8 33.6 %all-to-all-start.1 = ((bf16[32,32,1024]{2,1,0:T(8,128)(2,1)}), bf16[32,32,1024]{2,1,0:T(8,128)(2,1)S(1)}, u32[]{:S(2)}, u32[]{:S(2)}) async-start(bf16[32,32,1024]{2,1,0:T(8,128)(2,1)} %bitcast.8), calls=%async_computation.1 | async-start | bytes 4194304 | tf_op jit(solution)/shard_map/all_to_all | solution.py:166
  38.2 83.6 %copy-start.6 = (f32[4096]{0:T(1024)S(1)}, f32[4096]{0:T(1024)}, u32[]{:S(2)}) copy-start(f32[4096]{0:T(1024)} %param.11) | copy-start | bytes 49156
  38.2 80.3 %all-gather.7.cloned.1.call-start = ((), (), s32[]{:S(2)}) async-start(), calls=%async_computation.4 | async-start | bytes 5242880 | tf_op jit(solution)/shard_map/all_gather | solution.py:183
  72.7 111.2 %all-gather.11.cloned.1.call-start = ((), (), s32[]{:S(2)}) async-start(), calls=%async_computation.6 | async-start | bytes 4456448 | tf_op jit(solution)/shard_map/all_gather | solution.py:198
  118.5 3.4 copy-start.2
  122.0 2.2 copy-start.5
  126.5 91.8 %all-gather.13.cloned.1.call-start = ((), (), s32[]{:S(2)}) async-start(), calls=%async_computation.7 | async-start | bytes 12582912 | tf_op jit(solution)/shard_map/all_gather | solution.py:199
  196.8 9.3 %copy-start.4 = (s32[512]{0:T(512)S(1)}, s32[512]{0:T(512)}, u32[]{:S(2)}) copy-start(s32[512]{0:T(512)} %param.10) | copy-start | bytes 6148
  196.8 52.6 %all-to-all-start.2 = ((bf16[4,512,1024]{1,2,0:T(8,128)(2,1)}), bf16[4,512,1024]{1,2,0:T(8,128)(2,1)}, u32[]{:S(2)}, u32[]{:S(2)}) async-start(bf16[4,512,1024]{1,2,0:T(8,128)(2,1)} %bitcast.58), calls=%async_computation.2 | async-start | bytes 8388608 | tf_op jit(solution)/shard_map/all_to_all | solution.py:214
  202.1 140.7 %all-gather.9.cloned.1.call-start = ((), (), s32[]{:S(2)}) async-start(), calls=%async_computation.5 | async-start | bytes 2621440 | tf_op jit(solution)/shard_map/all_gather | solution.py:211
  233.3 109.4 %copy-start.3 = (bf16[512,1024]{1,0:T(8,128)(2,1)S(1)}, bf16[512,1024]{1,0:T(8,128)(2,1)}, u32[]{:S(2)}) copy-start(bf16[512,1024]{1,0:T(8,128)(2,1)} %scatter_custom_fusion.2) | copy-start | bytes 3145732
  353.3 36.0 %all-to-all-start.3 = ((bf16[32,32,1024]{2,1,0:T(8,128)(2,1)}), bf16[32,32,1024]{2,1,0:T(8,128)(2,1)S(1)}, u32[]{:S(2)}, u32[]{:S(2)}) async-start(bf16[32,32,1024]{2,1,0:T(8,128)(2,1)} %bitcast.60), calls=%async_computation.3 | async-start | bytes 4194304 | tf_op jit(solution)/shard_map/all_to_all | solution.py:220
  389.3 2.8 copy-start.1
Sparse Core Ops, SparseCore 0:
  72.8 45.6 all-gather.6
  126.7 57.2 all-gather.10
  190.5 23.0 all-gather.12
  233.5 109.2 all-gather.8

commit v3 on v2

--- a/solution.py
+++ b/solution.py
@@ -101,12 +101,10 @@
     rows, width = queries.shape
     heads = width // HD
     block = KEY_BLOCK
-    halves = kv_all.shape[0]
 
     def kv_map(column):
         def index_map(step, span_ref):
-            key_block = span_ref[0] + jnp.minimum(step, span_ref[1] - 1)
-            return (key_block % halves, key_block // halves, 0, column)
+            return (span_ref[4] + jnp.minimum(step, span_ref[1] - 1), 0, column)
         return index_map
 
     grid_spec = pltpu.PrefetchScalarGridSpec(
@@ -114,8 +112,8 @@
         grid=(max_blocks,),
         in_specs=[
             pl.BlockSpec((rows, width), lambda step, span_ref: (0, 0)),
-            pl.BlockSpec((None, None, block, HD), kv_map(0)),
-            pl.BlockSpec((None, None, block, HD), kv_map(1)),
+            pl.BlockSpec((None, block, HD), kv_map(0)),
+            pl.BlockSpec((None, block, HD), kv_map(1)),
             pl.BlockSpec((rows, 1), lambda step, span_ref: (0, 0)),
             pl.BlockSpec((rows, 1), lambda step, span_ref: (0, 0)),
         ],
@@ -195,26 +193,52 @@
     keys_own = rotate(keys_own, angles).astype(jnp.bfloat16).reshape(tok_dev, kv_dev * HD)
     values_own = jnp.dot(normed, w_value, preferred_element_type=jnp.float32).astype(jnp.bfloat16)
     kv_own = jnp.concatenate([keys_own, values_own], axis=1)
-    kv_chips = lax.all_gather(kv_own, "chip", axis=0, tiled=False)
-    kv_all = lax.all_gather(kv_chips, "core", axis=0, tiled=False)
 
     block = KEY_BLOCK
     last_block = (block_first + tok_dev - 1) // block
     first_block = doc_low // block
     max_blocks = min((tok_dev - 1) // block + -(-(DOC_MAX - 1) // block) + 1, owners * tok_dev // block)
+    back = max_blocks - 1
+    pieces = []
+    for shift in range(back, 0, -1):
+        pairs = [(source, (source + shift) % owners) for source in range(owners)]
+        pieces.append(lax.ppermute(kv_own, ("chip", "core"), pairs))
+    pieces.append(kv_own)
+    kv_window = jnp.stack(pieces)
     span = jnp.stack(
-        [first_block, last_block - first_block + 1, jnp.max(row_start), block_first]
+        [
+            first_block,
+            last_block - first_block + 1,
+            jnp.max(row_start),
+            block_first,
+            first_block - (last_block - back),
+        ]
     ).astype(jnp.int32)
     context = flash_attention(
-        span, queries, kv_all, row_start[:, None], row_index[:, None], max_blocks
+        span, queries, kv_window, row_start[:, None], row_index[:, None], max_blocks
     )
     context_all = lax.all_gather(context, "mp", axis=1, tiled=True)
     mp_size = lax.axis_size("mp")
-    w_split = jnp.transpose(w_out.reshape(w_out.shape[0], mp_size, -1), (1, 0, 2))
-    w_cols = lax.all_to_all(w_split, "mp", split_axis=0, concat_axis=0, tiled=True)
+    mp_index = lax.axis_index("mp")
+    col_width = w_out.shape[1] // mp_size
+    head_rows = w_out.shape[0]
     summed = jnp.dot(
-        context_all, w_cols.reshape(-1, w_cols.shape[2]), preferred_element_type=jnp.float32
-    )
+        lax.dynamic_slice_in_dim(context_all, mp_index * head_rows, head_rows, 1),
+        lax.dynamic_slice_in_dim(w_out, mp_index * col_width, col_width, 1),
+        preferred_element_type=jnp.float32,
+    )
+    for shift in range(1, mp_size):
+        to_send = lax.dynamic_slice_in_dim(
+            w_out, ((mp_index + shift) % mp_size) * col_width, col_width, 1
+        )
+        pairs = [(source, (source + shift) % mp_size) for source in range(mp_size)]
+        received = lax.ppermute(to_send, "mp", pairs)
+        owner = (mp_index - shift) % mp_size
+        summed = summed + jnp.dot(
+            lax.dynamic_slice_in_dim(context_all, owner * head_rows, head_rows, 1),
+            received,
+            preferred_element_type=jnp.float32,
+        )
     attended = (routed_part.astype(jnp.float32) + summed).astype(jnp.bfloat16)
     backward = attended[jnp.minimum(arrived_rows, tok_dev - 1)].reshape(owners, capacity, columns)
     returned = lax.all_to_all(backward, ("chip", "core"), split_axis=0, concat_axis=0, tiled=True)

time: 401 us -> 442 us (1.10); the launches traced: 399 us -> 433 us
  starting transfers between devices: 28.2 us -> 119 us
  waiting for transfers between devices: 265 us -> 201 us
  local copies, waits for them, and re-layouts: 46.2 us -> 52.1 us
    ppermute x0 -> x20, starting transfers between devices: none -> 60.7 us  [the longest x17 56.1 us: local(): pieces.append(lax.ppermute(kv_own, ('chip', 'core'), pairs))]
    all_gather x2 -> x0, waiting for transfers between devices: 57.4 us -> none  [the longest x1 57.4 us: local(): kv_chips = lax.all_gather(kv_own, 'chip', axis=0, tiled=False)]
    all_to_all x1, starting transfers between devices: 7.71 us -> 31.5 us  [local(): lax.all_to_all(backward, ('chip', 'core'), split_axis=0, concat_axis=0, t...]
    all_gather x1, waiting for transfers between devices: 45.5 us -> 26.3 us  [local(): routed = lax.all_gather(routed_part, 'mp', axis=1, tiled=True)]
    ppermute x0 -> x20, waiting for transfers between devices: none -> 19.1 us  [the longest x17 19.1 us: local(): pieces.append(lax.ppermute(kv_own, ('chip', 'core'), pairs))]
    all_to_all x1 -> x0, waiting for transfers between devices: 16.1 us -> none  [local(): lax.all_to_all(w_split, 'mp', split_axis=0, concat_axis=0, tiled=True)]
    unnamed x18 -> x36, local copies, waits for them, and re-layouts: 8.38 us -> 19.8 us
    all_gather x1, starting transfers between devices: 0.04 us -> 11.4 us  [local(): context_all = lax.all_gather(context, 'mp', axis=1, tiled=True)]
  transfers between devices with their start and end apart: 8 -> 25, of which waited for: 7 -> 10; matrix products, arithmetic and copies ran while one was open for 8% -> 11% of each run, Pallas kernels for 4% -> 0%
where the time goes in v3:
time: 442 us; the launch traced here: 433 us
  waiting for transfers between devices  201 us (45%)
  starting transfers between devices  119 us (27%)
  local copies, waits for them, and re-layouts  52.1 us (12%)
  other arithmetic  16.8 us (4%)
  between operations  15.5 us (4%)
  matrix products  14.7 us (3%)
  Pallas kernels  14.5 us (3%)
    all_gather x1, waiting for transfers between devices, local(): context_all = lax.all_gather(context, 'mp', axis=1, tiled=True)  97 us
    ppermute x17, starting transfers between devices, local(): pieces.append(lax.ppermute(kv_own, ('chip', 'core'), pairs))  56.1 us
    all_to_all x1, starting transfers between devices, local(): lax.all_to_all(backward, ('chip', 'core'), split_axis=0, concat_axis=0, t...  31.5 us
    all_to_all x1, waiting for transfers between devices, local(): lax.all_to_all(backward, ('chip', 'core'), split_axis=0, concat_axis=0, t...  28.3 us
    all_to_all x1, waiting for transfers between devices, local(): lax.all_to_all(outgoing.reshape(owners, capacity, columns), ('chip', 'cor...  28.1 us
    all_gather x1, waiting for transfers between devices, local(): routed = lax.all_gather(routed_part, 'mp', axis=1, tiled=True)  26.3 us
    unnamed x36, local copies, waits for them, and re-layouts  19.8 us
    ppermute x17, waiting for transfers between devices, local(): pieces.append(lax.ppermute(kv_own, ('chip', 'core'), pairs))  19.1 us
  transfers between devices with their start and end apart: 25, of which 10 were waited for; matrix products, arithmetic and copies ran while one was open for 11% of the time, Pallas kernels for 0%

profile of v3, /device:TPU:1, one launch (start us, length us, event | category | flops | bytes accessed | tf_op | source)
XLA Modules:
  0.0 433.1 jit_solution(3545353792433675904)
XLA Ops:
  11.2 2.4 scatter_custom_fusion
  16.3 9.6 %all-to-all-start = ((s32[32,1,34]{2,1,0:T(1,128)}), s32[32,1,34]{2,1,0:T(1,128)S(1)}, u32[]{:S(2)}, u32[]{:S(2)}) async-start(s32[32,1,34]{2,1,0:T(1,128)} %bitcast.5), calls=%async_computation | async-start | bytes 32768 | tf_op jit(solution)/shard_map/all_to_all | solution.py:167
  25.9 4.8 %scatter_custom_fusion.1 = bf16[1024,1024]{1,0:T(8,128)(2,1)} fusion(s32[512]{0:T(512)S(1)} %compare_select_fusion.2, bf16[512,1024]{1,0:T(8,128)(2,1)} %param.8, bf16[]{:T(256)} %constant.117.clone.1), kind=kCustom, calls=%fused_computation.17 | custom fusion | bytes 2097664 | tf_op jit(solution)/shard_map/scatter | solution.py:152
  30.7 2.1 all-to-all-done
  32.8 5.3 %all-to-all-start.1 = ((bf16[32,32,1024]{2,1,0:T(8,128)(2,1)}), bf16[32,32,1024]{2,1,0:T(8,128)(2,1)S(1)}, u32[]{:S(2)}, u32[]{:S(2)}) async-start(bf16[32,32,1024]{2,1,0:T(8,128)(2,1)} %bitcast.8), calls=%async_computation.1 | async-start | bytes 4194304 | tf_op jit(solution)/shard_map/all_to_all | solution.py:164
  38.2 28.1 %all-to-all-done.1 = bf16[32,32,1024]{2,1,0:T(8,128)(2,1)S(1)} async-done(((bf16[32,32,1024]{2,1,0:T(8,128)(2,1)}), bf16[32,32,1024]{2,1,0:T(8,128)(2,1)S(1)}, u32[]{:S(2)}, u32[]{:S(2)}) %all-to-all-start.1) | async-done | bytes 2097184 | tf_op jit(solution)/shard_map/all_to_all | solution.py:164
  66.4 6.2 %scatter_custom_fusion.2 = bf16[512,1024]{1,0:T(8,128)(2,1)} fusion(s32[1024]{0:T(1024)S(1)} %bitcast.101, bf16[1024,1024]{1,0:T(8,128)(2,1)S(1)} %bitcast.92, bf16[]{:T(256)} %constant.117.clone.1), kind=kCustom, calls=%fused_computation.29 | custom fusion | bytes 1048578 | tf_op jit(solution)/shard_map/scatter | solution.py:179
  72.6 11.4 %all-gather.5.cloned.1.call-start = ((), (), s32[]{:S(2)}) async-start(), calls=%async_computation.4 | async-start | bytes 2621440 | tf_op jit(solution)/shard_map/all_gather | solution.py:220
  84.8 1.7 multiply_cosine_fusion.1
  92.2 26.3 %all-gather.3.cloned.1.call-done = bf16[512,4096]{1,0:T(8,128)(2,1)} async-done(((bf16[512,1024]{1,0:T(8,128)(2,1)}), bf16[512,4096]{1,0:T(8,128)(2,1)}) %all-gather.3.cloned.1.call-update) | async-done | bytes 4194320 | tf_op jit(solution)/shard_map/all_gather | solution.py:181
  118.5 3.1 fusion
  121.6 3.6 convolution_bitcast_fusion
  128.6 4.3 collective-permute-start
  133.2 1.7 collective-permute-start.2
  134.9 2.7 collective-permute-start.3
  137.6 2.8 collective-permute-start.4
  140.4 2.6 fusion.42
  144.3 1.4 copy.41
  145.8 1.5 subtract_convert_fusion
  148.9 2.0 collective-permute-start.5
  150.8 1.7 bitcast_dynamic-update-slice_fusion.17
  152.5 23.0 %collective-permute-start.6 = (bf16[512,256]{1,0:T(8,128)(2,1)}, bf16[512,256]{1,0:T(8,128)(2,1)S(1)}, u32[]{:S(2)}, u32[]{:S(2)}) collective-permute-start(bf16[512,256]{1,0:T(8,128)(2,1)} %pad_maximum_fusion.1), channel_id=1, source_target_pairs={{0,44},{4,48},{8,52},{12,56},{16,60},{20,64},{24,68},{28,72},{32,7... | collective-permute-start | bytes 786440 | tf_op jit(solution)/shard_map/ppermute | solution.py:205
  175.5 1.7 bitcast_dynamic-update-slice_fusion.16
  177.2 1.7 bitcast_dynamic-update-slice_fusion.15
  178.9 1.7 bitcast_dynamic-update-slice_fusion.14
  180.6 1.7 bitcast_dynamic-update-slice_fusion.13
  183.0 5.3 %collective-permute-start.11 = (bf16[512,256]{1,0:T(8,128)(2,1)}, bf16[512,256]{1,0:T(8,128)(2,1)S(1)}, u32[]{:S(2)}, u32[]{:S(2)}) collective-permute-start(bf16[512,256]{1,0:T(8,128)(2,1)} %pad_maximum_fusion.1), channel_id=1, source_target_pairs={{0,24},{4,28},{8,32},{12,36},{16,40},{20,44},{24,48},{28,52},{32,5... | collective-permute-start | bytes 786440 | tf_op jit(solution)/shard_map/ppermute | solution.py:205
  190.0 2.7 collective-permute-start.13
  193.4 1.8 collective-permute-start.14
  195.9 3.5 collective-permute-done.10
  199.4 2.4 collective-permute-start.15
  202.5 6.9 %collective-permute-start.16 = (bf16[512,256]{1,0:T(8,128)(2,1)}, bf16[512,256]{1,0:T(8,128)(2,1)S(1)}, u32[]{:S(2)}, u32[]{:S(2)}) collective-permute-start(bf16[512,256]{1,0:T(8,128)(2,1)} %pad_maximum_fusion.1), channel_id=1, source_target_pairs={{0,4},{4,8},{8,12},{12,16},{16,20},{20,24},{24,28},{28,32},{32,36}... | collective-permute-start | bytes 786440 | tf_op jit(solution)/shard_map/ppermute | solution.py:205
  212.0 4.7 %collective-permute-done.13 = bf16[512,256]{1,0:T(8,128)(2,1)S(1)} collective-permute-done((bf16[512,256]{1,0:T(8,128)(2,1)}, bf16[512,256]{1,0:T(8,128)(2,1)S(1)}, u32[]{:S(2)}, u32[]{:S(2)}) %collective-permute-start.13) | collective-permute-done | bytes 262176 | tf_op jit(solution)/shard_map/ppermute | solution.py:205
  217.4 5.4 %collective-permute-done.14 = bf16[512,256]{1,0:T(8,128)(2,1)S(1)} collective-permute-done((bf16[512,256]{1,0:T(8,128)(2,1)}, bf16[512,256]{1,0:T(8,128)(2,1)S(1)}, u32[]{:S(2)}, u32[]{:S(2)}) %collective-permute-start.14) | collective-permute-done | bytes 262176 | tf_op jit(solution)/shard_map/ppermute | solution.py:205
  223.6 4.3 %collective-permute-done.15 = bf16[512,256]{1,0:T(8,128)(2,1)S(1)} collective-permute-done((bf16[512,256]{1,0:T(8,128)(2,1)}, bf16[512,256]{1,0:T(8,128)(2,1)S(1)}, u32[]{:S(2)}, u32[]{:S(2)}) %collective-permute-start.15) | collective-permute-done | bytes 262176 | tf_op jit(solution)/shard_map/ppermute | solution.py:205
  229.3 1.7 bitcast_dynamic-update-slice_fusion.k_ref.v_ref
  231.0 14.5 %shard_map.82 = bf16[512,512]{1,0:T(8,128)(2,1)} custom-call(s32[5]{0:T(128)} %stack.88.span_ref, bf16[512,512]{1,0:T(8,128)(2,1)} %bitcast.94, bf16[18,512,256]{2,1,0:T(8,128)(2,1)} %bitcast_dynamic-update-slice_fusion.k_ref.v_ref, bf16[18,512,256]{2,1,0:T(8,128)(2,1)} %bitcast_dynamic-update-slice_fusion.k_ref.v_ref, s32[512,1]{1,0:T(8,128)} %copy.38.start_ref, ...), custom_call_target="tpu_custom_call" | custom-call | flops 9663676416 | bytes 5767168 | tf_op jit(solution)/shard_map/pallas_call | solution.py:128
  245.5 3.5 constant_dynamic-slice_fusion
  249.0 1.7 collective-permute-start.18
  250.8 2.9 collective-permute-start.19
  253.7 97.0 %all-gather.5.cloned.1.call-done = bf16[512,2048]{1,0:T(8,128)(2,1)} async-done(((bf16[512,512]{1,0:T(8,128)(2,1)}), bf16[512,2048]{1,0:T(8,128)(2,1)}) %all-gather.5.cloned.1.call-update) | async-done | bytes 2097168 | tf_op jit(solution)/shard_map/all_gather | solution.py:220
  350.6 2.2 fusion.3
  352.9 2.0 fusion.11
  355.0 1.9 fusion.13
  357.9 5.4 %gather_fusion = bf16[1024,1024]{1,0:T(8,128)(2,1)} fusion(bf16[512,1024]{1,0:T(8,128)(2,1)S(1)} %add_convert_fusion, s32[1024]{0:T(1024)S(1)} %broadcast_clamp_fusion), kind=kCustom, calls=%fused_computation | custom fusion | bytes 4198400 | tf_op jit(solution)/shard_map/gather | solution.py:243
  363.2 31.5 %all-to-all-start.2 = ((bf16[32,32,1024]{2,1,0:T(8,128)(2,1)}), bf16[32,32,1024]{2,1,0:T(8,128)(2,1)S(1)}, u32[]{:S(2)}, u32[]{:S(2)}) async-start(bf16[32,32,1024]{2,1,0:T(8,128)(2,1)} %bitcast.90), calls=%async_computation.2 | async-start | bytes 4194304 | tf_op jit(solution)/shard_map/all_to_all | solution.py:244
  394.7 28.3 %all-to-all-done.2 = bf16[32,32,1024]{2,1,0:T(8,128)(2,1)S(1)} async-done(((bf16[32,32,1024]{2,1,0:T(8,128)(2,1)}), bf16[32,32,1024]{2,1,0:T(8,128)(2,1)S(1)}, u32[]{:S(2)}, u32[]{:S(2)}) %all-to-all-start.2) | async-done | bytes 2097184 | tf_op jit(solution)/shard_map/all_to_all | solution.py:244
  423.0 2.8 gather_fusion.1
  (91 shorter events, 30.1 us)
Async XLA Ops:
  6.5 115.0 %copy-start = (bf16[4096,128]{1,0:T(8,128)(2,1)S(1)}, bf16[4096,128]{1,0:T(8,128)(2,1)}, u32[]{:S(2)}) copy-start(bf16[4096,128]{1,0:T(8,128)(2,1)} %param.13) | copy-start | bytes 3145732
  13.6 75.2 %copy-start.4 = (s32[512]{0:T(512)S(1)}, s32[512]{0:T(512)}, u32[]{:S(2)}) copy-start(s32[512]{0:T(512)} %param.10) | copy-start | bytes 6148
  16.3 16.5 %all-to-all-start = ((s32[32,1,34]{2,1,0:T(1,128)}), s32[32,1,34]{2,1,0:T(1,128)S(1)}, u32[]{:S(2)}, u32[]{:S(2)}) async-start(s32[32,1,34]{2,1,0:T(1,128)} %bitcast.5), calls=%async_computation | async-start | bytes 32768 | tf_op jit(solution)/shard_map/all_to_all | solution.py:167
  32.8 33.6 %all-to-all-start.1 = ((bf16[32,32,1024]{2,1,0:T(8,128)(2,1)}), bf16[32,32,1024]{2,1,0:T(8,128)(2,1)S(1)}, u32[]{:S(2)}, u32[]{:S(2)}) async-start(bf16[32,32,1024]{2,1,0:T(8,128)(2,1)} %bitcast.8), calls=%async_computation.1 | async-start | bytes 4194304 | tf_op jit(solution)/shard_map/all_to_all | solution.py:164
  38.1 83.5 %copy-start.7 = (f32[4096]{0:T(1024)S(1)}, f32[4096]{0:T(1024)}, u32[]{:S(2)}) copy-start(f32[4096]{0:T(1024)} %param.11) | copy-start | bytes 49156
  38.1 80.4 %all-gather.3.cloned.1.call-start = ((), (), s32[]{:S(2)}) async-start(), calls=%async_computation.3 | async-start | bytes 5242880 | tf_op jit(solution)/shard_map/all_gather | solution.py:181
  72.6 278.0 %all-gather.5.cloned.1.call-start = ((), (), s32[]{:S(2)}) async-start(), calls=%async_computation.4 | async-start | bytes 2621440 | tf_op jit(solution)/shard_map/all_gather | solution.py:220
  121.6 4.9 %copy-start.2 = (bf16[512,4096]{1,0:T(8,128)(2,1)S(1)}, bf16[512,4096]{1,0:T(8,128)(2,1)}, u32[]{:S(2)}) copy-start(bf16[512,4096]{1,0:T(8,128)(2,1)} %all-gather.3.cloned.1.call-done) | copy-start | bytes 12582916
  121.6 4.9 %copy-start.6 = (bf16[4096,128]{1,0:T(8,128)(2,1)S(1)}, bf16[4096,128]{1,0:T(8,128)(2,1)}, u32[]{:S(2)}) copy-start(bf16[4096,128]{1,0:T(8,128)(2,1)} %param.14) | copy-start | bytes 3145732
  126.5 14.0 %copy-start.5 = (bf16[4096,512]{1,0:T(8,128)(2,1)S(1)}, bf16[4096,512]{1,0:T(8,128)(2,1)}, u32[]{:S(2)}) copy-start(bf16[4096,512]{1,0:T(8,128)(2,1)} %param.12) | copy-start | bytes 12582916
  128.6 20.2 %collective-permute-start = (bf16[512,256]{1,0:T(8,128)(2,1)}, bf16[512,256]{1,0:T(8,128)(2,1)}, u32[]{:S(2)}, u32[]{:S(2)}) collective-permute-start(bf16[512,256]{1,0:T(8,128)(2,1)} %pad_maximum_fusion.1), channel_id=1, source_target_pairs={{0,68},{4,72},{8,76},{12,80},{16,84},{20,88},{24,92},{28,96},{32,1... | collective-permute-start | bytes 786440 | tf_op jit(solution)/shard_map/ppermute | solution.py:205
  133.0 19.5 %collective-permute-start.1 = (bf16[512,256]{1,0:T(8,128)(2,1)}, bf16[512,256]{1,0:T(8,128)(2,1)}, u32[]{:S(2)}, u32[]{:S(2)}) collective-permute-start(bf16[512,256]{1,0:T(8,128)(2,1)} %pad_maximum_fusion.1), channel_id=1, source_target_pairs={{0,64},{4,68},{8,72},{12,76},{16,80},{20,84},{24,88},{28,92},{32,9... | collective-permute-start | bytes 786440 | tf_op jit(solution)/shard_map/ppermute | solution.py:205
  133.2 44.0 %collective-permute-start.2 = (bf16[512,256]{1,0:T(8,128)(2,1)}, bf16[512,256]{1,0:T(8,128)(2,1)}, u32[]{:S(2)}, u32[]{:S(2)}) collective-permute-start(bf16[512,256]{1,0:T(8,128)(2,1)} %pad_maximum_fusion.1), channel_id=1, source_target_pairs={{0,60},{4,64},{8,68},{12,72},{16,76},{20,80},{24,84},{28,88},{32,9... | collective-permute-start | bytes 786440 | tf_op jit(solution)/shard_map/ppermute | solution.py:205
  134.9 44.0 %collective-permute-start.3 = (bf16[512,256]{1,0:T(8,128)(2,1)}, bf16[512,256]{1,0:T(8,128)(2,1)}, u32[]{:S(2)}, u32[]{:S(2)}) collective-permute-start(bf16[512,256]{1,0:T(8,128)(2,1)} %pad_maximum_fusion.1), channel_id=1, source_target_pairs={{0,56},{4,60},{8,64},{12,68},{16,72},{20,76},{24,80},{28,84},{32,8... | collective-permute-start | bytes 786440 | tf_op jit(solution)/shard_map/ppermute | solution.py:205
  137.6 42.9 %collective-permute-start.4 = (bf16[512,256]{1,0:T(8,128)(2,1)}, bf16[512,256]{1,0:T(8,128)(2,1)}, u32[]{:S(2)}, u32[]{:S(2)}) collective-permute-start(bf16[512,256]{1,0:T(8,128)(2,1)} %pad_maximum_fusion.1), channel_id=1, source_target_pairs={{0,52},{4,56},{8,60},{12,64},{16,68},{20,72},{24,76},{28,80},{32,8... | collective-permute-start | bytes 786440 | tf_op jit(solution)/shard_map/ppermute | solution.py:205
  148.9 33.4 %collective-permute-start.5 = (bf16[512,256]{1,0:T(8,128)(2,1)}, bf16[512,256]{1,0:T(8,128)(2,1)S(1)}, u32[]{:S(2)}, u32[]{:S(2)}) collective-permute-start(bf16[512,256]{1,0:T(8,128)(2,1)} %pad_maximum_fusion.1), channel_id=1, source_target_pairs={{0,48},{4,52},{8,56},{12,60},{16,64},{20,68},{24,72},{28,76},{32,8... | collective-permute-start | bytes 786440 | tf_op jit(solution)/shard_map/ppermute | solution.py:205
  152.5 30.5 %collective-permute-start.6 = (bf16[512,256]{1,0:T(8,128)(2,1)}, bf16[512,256]{1,0:T(8,128)(2,1)S(1)}, u32[]{:S(2)}, u32[]{:S(2)}) collective-permute-start(bf16[512,256]{1,0:T(8,128)(2,1)} %pad_maximum_fusion.1), channel_id=1, source_target_pairs={{0,44},{4,48},{8,52},{12,56},{16,60},{20,64},{24,68},{28,72},{32,7... | collective-permute-start | bytes 786440 | tf_op jit(solution)/shard_map/ppermute | solution.py:205
  177.2 11.8 %collective-permute-start.7 = (bf16[512,256]{1,0:T(8,128)(2,1)}, bf16[512,256]{1,0:T(8,128)(2,1)S(1)}, u32[]{:S(2)}, u32[]{:S(2)}) collective-permute-start(bf16[512,256]{1,0:T(8,128)(2,1)} %pad_maximum_fusion.1), channel_id=1, source_target_pairs={{0,40},{4,44},{8,48},{12,52},{16,56},{20,60},{24,64},{28,68},{32,7... | collective-permute-start | bytes 786440 | tf_op jit(solution)/shard_map/ppermute | solution.py:205
  178.9 11.2 %collective-permute-start.8 = (bf16[512,256]{1,0:T(8,128)(2,1)}, bf16[512,256]{1,0:T(8,128)(2,1)S(1)}, u32[]{:S(2)}, u32[]{:S(2)}) collective-permute-start(bf16[512,256]{1,0:T(8,128)(2,1)} %pad_maximum_fusion.1), channel_id=1, source_target_pairs={{0,36},{4,40},{8,44},{12,48},{16,52},{20,56},{24,60},{28,64},{32,6... | collective-permute-start | bytes 786440 | tf_op jit(solution)/shard_map/ppermute | solution.py:205
  180.6 12.9 %collective-permute-start.9 = (bf16[512,256]{1,0:T(8,128)(2,1)}, bf16[512,256]{1,0:T(8,128)(2,1)S(1)}, u32[]{:S(2)}, u32[]{:S(2)}) collective-permute-start(bf16[512,256]{1,0:T(8,128)(2,1)} %pad_maximum_fusion.1), channel_id=1, source_target_pairs={{0,32},{4,36},{8,40},{12,44},{16,48},{20,52},{24,56},{28,60},{32,6... | collective-permute-start | bytes 786440 | tf_op jit(solution)/shard_map/ppermute | solution.py:205
  182.3 17.2 %collective-permute-start.10 = (bf16[512,256]{1,0:T(8,128)(2,1)}, bf16[512,256]{1,0:T(8,128)(2,1)S(1)}, u32[]{:S(2)}, u32[]{:S(2)}) collective-permute-start(bf16[512,256]{1,0:T(8,128)(2,1)} %pad_maximum_fusion.1), channel_id=1, source_target_pairs={{0,28},{4,32},{8,36},{12,40},{16,44},{20,48},{24,52},{28,56},{32,6... | collective-permute-start | bytes 786440 | tf_op jit(solution)/shard_map/ppermute | solution.py:205
  183.0 19.6 %collective-permute-start.11 = (bf16[512,256]{1,0:T(8,128)(2,1)}, bf16[512,256]{1,0:T(8,128)(2,1)S(1)}, u32[]{:S(2)}, u32[]{:S(2)}) collective-permute-start(bf16[512,256]{1,0:T(8,128)(2,1)} %pad_maximum_fusion.1), channel_id=1, source_target_pairs={{0,24},{4,28},{8,32},{12,36},{16,40},{20,44},{24,48},{28,52},{32,5... | collective-permute-start | bytes 786440 | tf_op jit(solution)/shard_map/ppermute | solution.py:205
  189.0 22.3 %collective-permute-start.12 = (bf16[512,256]{1,0:T(8,128)(2,1)}, bf16[512,256]{1,0:T(8,128)(2,1)S(1)}, u32[]{:S(2)}, u32[]{:S(2)}) collective-permute-start(bf16[512,256]{1,0:T(8,128)(2,1)} %pad_maximum_fusion.1), channel_id=1, source_target_pairs={{0,20},{4,24},{8,28},{12,32},{16,36},{20,40},{24,44},{28,48},{32,5... | collective-permute-start | bytes 786440 | tf_op jit(solution)/shard_map/ppermute | solution.py:205
  190.0 26.7 %collective-permute-start.13 = (bf16[512,256]{1,0:T(8,128)(2,1)}, bf16[512,256]{1,0:T(8,128)(2,1)S(1)}, u32[]{:S(2)}, u32[]{:S(2)}) collective-permute-start(bf16[512,256]{1,0:T(8,128)(2,1)} %pad_maximum_fusion.1), channel_id=1, source_target_pairs={{0,16},{4,20},{8,24},{12,28},{16,32},{20,36},{24,40},{28,44},{32,4... | collective-permute-start | bytes 786440 | tf_op jit(solution)/shard_map/ppermute | solution.py:205
  193.4 29.4 %collective-permute-start.14 = (bf16[512,256]{1,0:T(8,128)(2,1)}, bf16[512,256]{1,0:T(8,128)(2,1)S(1)}, u32[]{:S(2)}, u32[]{:S(2)}) collective-permute-start(bf16[512,256]{1,0:T(8,128)(2,1)} %pad_maximum_fusion.1), channel_id=1, source_target_pairs={{0,12},{4,16},{8,20},{12,24},{16,28},{20,32},{24,36},{28,40},{32,4... | collective-permute-start | bytes 786440 | tf_op jit(solution)/shard_map/ppermute | solution.py:205
  199.4 28.5 %collective-permute-start.15 = (bf16[512,256]{1,0:T(8,128)(2,1)}, bf16[512,256]{1,0:T(8,128)(2,1)S(1)}, u32[]{:S(2)}, u32[]{:S(2)}) collective-permute-start(bf16[512,256]{1,0:T(8,128)(2,1)} %pad_maximum_fusion.1), channel_id=1, source_target_pairs={{0,8},{4,12},{8,16},{12,20},{16,24},{20,28},{24,32},{28,36},{32,40... | collective-permute-start | bytes 786440 | tf_op jit(solution)/shard_map/ppermute | solution.py:205
  202.5 26.1 %collective-permute-start.16 = (bf16[512,256]{1,0:T(8,128)(2,1)}, bf16[512,256]{1,0:T(8,128)(2,1)S(1)}, u32[]{:S(2)}, u32[]{:S(2)}) collective-permute-start(bf16[512,256]{1,0:T(8,128)(2,1)} %pad_maximum_fusion.1), channel_id=1, source_target_pairs={{0,4},{4,8},{8,12},{12,16},{16,20},{20,24},{24,28},{28,32},{32,36}... | collective-permute-start | bytes 786440 | tf_op jit(solution)/shard_map/ppermute | solution.py:205
  249.0 103.9 %collective-permute-start.18 = (bf16[512,1024]{1,0:T(8,128)(2,1)}, bf16[512,1024]{1,0:T(8,128)(2,1)}, u32[]{:S(2)}, u32[]{:S(2)}) collective-permute-start(bf16[512,1024]{1,0:T(8,128)(2,1)} %get-tuple-element.9), channel_id=1, source_target_pairs={{0,2},{1,3},{2,0},{3,1},{4,6},{5,7},{6,4},{7,5},{8,10},{9,11},{10,... | collective-permute-start | bytes 3145736 | tf_op jit(solution)/shard_map/ppermute | solution.py:235
  250.8 104.2 %collective-permute-start.17 = (bf16[512,1024]{1,0:T(8,128)(2,1)}, bf16[512,1024]{1,0:T(8,128)(2,1)}, u32[]{:S(2)}, u32[]{:S(2)}) collective-permute-start(bf16[512,1024]{1,0:T(8,128)(2,1)} %get-tuple-element.8), channel_id=1, source_target_pairs={{0,1},{1,2},{2,3},{3,0},{4,5},{5,6},{6,7},{7,4},{8,9},{9,10},{10,1... | collective-permute-start | bytes 3145736 | tf_op jit(solution)/shard_map/ppermute | solution.py:235
  250.8 106.2 %collective-permute-start.19 = (bf16[512,1024]{1,0:T(8,128)(2,1)S(1)}, bf16[512,1024]{1,0:T(8,128)(2,1)S(1)}, u32[]{:S(2)}, u32[]{:S(2)}) collective-permute-start(bf16[512,1024]{1,0:T(8,128)(2,1)S(1)} %get-tuple-element.7), channel_id=1, source_target_pairs={{0,3},{1,0},{2,1},{3,2},{4,7},{5,4},{6,5},{7,6},{8,11},{9,8},{10,9... | collective-permute-start | bytes 3145736 | tf_op jit(solution)/shard_map/ppermute | solution.py:235
  350.6 2.3 copy-start.3
  352.9 4.1 copy-start.1
  363.2 59.8 %all-to-all-start.2 = ((bf16[32,32,1024]{2,1,0:T(8,128)(2,1)}), bf16[32,32,1024]{2,1,0:T(8,128)(2,1)S(1)}, u32[]{:S(2)}, u32[]{:S(2)}) async-start(bf16[32,32,1024]{2,1,0:T(8,128)(2,1)} %bitcast.90), calls=%async_computation.2 | async-start | bytes 4194304 | tf_op jit(solution)/shard_map/all_to_all | solution.py:244
Sparse Core Ops, SparseCore 0:
  72.8 45.6 all-gather.2
  245.6 104.9 all-gather.4

commit v4 on v2

--- a/solution.py
+++ b/solution.py
@@ -44,7 +44,11 @@
     return (wide_rows * inv_rms * norm_gain[None, :]).astype(jnp.bfloat16)
 
 
-def flash_kernel(span_ref, q_ref, k_ref, v_ref, start_ref, row_ref, o_ref, m_sc, l_sc, acc_sc):
+def flash_kernel(final, span_ref, *refs):
+    if final:
+        q_ref, k_ref, v_ref, start_ref, row_ref, m_in, l_in, acc_in, o_ref, m_sc, l_sc, acc_sc = refs
+    else:
+        q_ref, k_ref, v_ref, start_ref, row_ref, m_sc, l_sc, acc_sc = refs
     step = pl.program_id(0)
     heads = m_sc.shape[0]
     block = k_ref.shape[0]
@@ -52,11 +56,16 @@
 
     @pl.when(step == 0)
     def _init():
-        m_sc[...] = jnp.full(m_sc.shape, NEG_START, jnp.float32)
-        l_sc[...] = jnp.zeros(l_sc.shape, jnp.float32)
-        acc_sc[...] = jnp.zeros(acc_sc.shape, jnp.float32)
-
-    key_first = (span_ref[0] + step) * block
+        if final:
+            m_sc[...] = m_in[...]
+            l_sc[...] = l_in[...]
+            acc_sc[...] = acc_in[...]
+        else:
+            m_sc[...] = jnp.full(m_sc.shape, NEG_START, jnp.float32)
+            l_sc[...] = jnp.zeros(l_sc.shape, jnp.float32)
+            acc_sc[...] = jnp.zeros(acc_sc.shape, jnp.float32)
+
+    key_first = (span_ref[0] + step) * span_ref[4] + span_ref[5]
     active = step < span_ref[1]
     whole = (key_first >= span_ref[2]) & (key_first + block - 1 <= span_ref[3])
 
@@ -91,53 +100,69 @@
     def _masked():
         accumulate(True)
 
-    @pl.when(step == pl.num_programs(0) - 1)
-    def _finish():
-        for h in range(heads):
-            o_ref[:, h * HD:(h + 1) * HD] = (acc_sc[h] / l_sc[h]).astype(o_ref.dtype)
-
-
-def flash_attention(span, queries, kv_all, row_start, row_index, max_blocks):
+    if final:
+        @pl.when(step == pl.num_programs(0) - 1)
+        def _finish():
+            for h in range(heads):
+                o_ref[:, h * HD:(h + 1) * HD] = (acc_sc[h] / l_sc[h]).astype(o_ref.dtype)
+
+
+def flash_pass(span, queries, kv_part, row_start, row_index, max_blocks, state):
     rows, width = queries.shape
     heads = width // HD
-    block = KEY_BLOCK
-    halves = kv_all.shape[0]
+    block = row_start.shape[0] // 2
+    final = state is not None
 
     def kv_map(column):
         def index_map(step, span_ref):
-            key_block = span_ref[0] + jnp.minimum(step, span_ref[1] - 1)
-            return (key_block % halves, key_block // halves, 0, column)
+            return (span_ref[0] + jnp.minimum(step, span_ref[1] - 1), column)
         return index_map
 
+    fixed2 = lambda step, span_ref: (0, 0)
+    fixed3 = lambda step, span_ref: (0, 0, 0)
+    in_specs = [
+        pl.BlockSpec((rows, width), fixed2),
+        pl.BlockSpec((block, HD), kv_map(0)),
+        pl.BlockSpec((block, HD), kv_map(1)),
+        pl.BlockSpec((rows, 1), fixed2),
+        pl.BlockSpec((rows, 1), fixed2),
+    ]
+    state_shapes = [
+        jax.ShapeDtypeStruct((heads, rows, 1), jnp.float32),
+        jax.ShapeDtypeStruct((heads, rows, 1), jnp.float32),
+        jax.ShapeDtypeStruct((heads, rows, HD), jnp.float32),
+    ]
+    state_specs = [pl.BlockSpec(x.shape, fixed3) for x in state_shapes]
+    if final:
+        in_specs = in_specs + state_specs
+        out_specs = pl.BlockSpec((rows, width), fixed2)
+        out_shape = jax.ShapeDtypeStruct((rows, width), jnp.bfloat16)
+        scratch = [pltpu.VMEM(x.shape, jnp.float32) for x in state_shapes]
+        operands = (span, queries, kv_part, kv_part, row_start, row_index) + tuple(state)
+    else:
+        out_specs = state_specs
+        out_shape = state_shapes
+        scratch = []
+        operands = (span, queries, kv_part, kv_part, row_start, row_index)
     grid_spec = pltpu.PrefetchScalarGridSpec(
         num_scalar_prefetch=1,
         grid=(max_blocks,),
-        in_specs=[
-            pl.BlockSpec((rows, width), lambda step, span_ref: (0, 0)),
-            pl.BlockSpec((None, None, block, HD), kv_map(0)),
-            pl.BlockSpec((None, None, block, HD), kv_map(1)),
-            pl.BlockSpec((rows, 1), lambda step, span_ref: (0, 0)),
-            pl.BlockSpec((rows, 1), lambda step, span_ref: (0, 0)),
-        ],
-        out_specs=pl.BlockSpec((rows, width), lambda step, span_ref: (0, 0)),
-        scratch_shapes=[
-            pltpu.VMEM((heads, rows, 1), jnp.float32),
-            pltpu.VMEM((heads, rows, 1), jnp.float32),
-            pltpu.VMEM((heads, rows, HD), jnp.float32),
-        ],
+        in_specs=in_specs,
+        out_specs=out_specs,
+        scratch_shapes=scratch,
     )
     flops = 4 * heads * rows * block * HD * max_blocks
     return pl.pallas_call(
-        flash_kernel,
+        functools.partial(flash_kernel, final),
         grid_spec=grid_spec,
-        out_shape=jax.ShapeDtypeStruct((rows, width), jnp.bfloat16),
+        out_shape=out_shape,
         compiler_params=pltpu.CompilerParams(dimension_semantics=("arbitrary",)),
         cost_estimate=pl.CostEstimate(
             flops=flops,
             transcendentals=heads * rows * block * max_blocks,
             bytes_accessed=2 * block * HD * 2 * max_blocks + 2 * 2 * rows * width,
         ),
-    )(span, queries, kv_all, kv_all, row_start, row_index)
+    )(*operands)
 
 
 def local(hidden_rows, destination, doc_ids, norm_gain, w_query, w_key, w_value, w_out):
@@ -195,18 +220,26 @@
     keys_own = rotate(keys_own, angles).astype(jnp.bfloat16).reshape(tok_dev, kv_dev * HD)
     values_own = jnp.dot(normed, w_value, preferred_element_type=jnp.float32).astype(jnp.bfloat16)
     kv_own = jnp.concatenate([keys_own, values_own], axis=1)
-    kv_chips = lax.all_gather(kv_own, "chip", axis=0, tiled=False)
-    kv_all = lax.all_gather(kv_chips, "core", axis=0, tiled=False)
+    half = tok_dev // 2
+    kv_low = lax.all_gather(kv_own[:half], ("chip", "core"), axis=0, tiled=True)
+    kv_high = lax.all_gather(kv_own[half:], ("chip", "core"), axis=0, tiled=True)
 
     block = KEY_BLOCK
     last_block = (block_first + tok_dev - 1) // block
     first_block = doc_low // block
     max_blocks = min((tok_dev - 1) // block + -(-(DOC_MAX - 1) // block) + 1, owners * tok_dev // block)
-    span = jnp.stack(
-        [first_block, last_block - first_block + 1, jnp.max(row_start), block_first]
-    ).astype(jnp.int32)
-    context = flash_attention(
-        span, queries, kv_all, row_start[:, None], row_index[:, None], max_blocks
+    max_start = jnp.max(row_start)
+
+    def span_for(offset):
+        return jnp.stack(
+            [first_block, last_block - first_block + 1, max_start, block_first, block, offset]
+        ).astype(jnp.int32)
+
+    state = flash_pass(
+        span_for(0), queries, kv_low, row_start[:, None], row_index[:, None], max_blocks, None
+    )
+    context = flash_pass(
+        span_for(half), queries, kv_high, row_start[:, None], row_index[:, None], max_blocks, state
     )
     context_all = lax.all_gather(context, "mp", axis=1, tiled=True)
     mp_size = lax.axis_size("mp")

time: 401 us -> 359 us (0.90)
  waiting for transfers between devices: 265 us -> 219 us
  Pallas kernels: 15 us -> 20 us
    all_gather x1, waiting for transfers between devices: 87.1 us -> 62.1 us  [local(): context_all = lax.all_gather(context, 'mp', axis=1, tiled=True)]
    all_to_all x1, waiting for transfers between devices: 16.1 us -> 0.01 us  [local(): lax.all_to_all(w_split, 'mp', split_axis=0, concat_axis=0, tiled=True)]
    all_gather x1 -> x0, local copies, waits for them, and re-layouts: 6.37 us -> none  [local(): kv_chips = lax.all_gather(kv_own, 'chip', axis=0, tiled=False)]
    pallas_call x1 -> x2, Pallas kernels: 15 us -> 20 us  [flash_pass(): pl.pallas_call(functools.partial(flash_kernel, final), grid_spec=grid_spe...]
    all_gather x2, waiting for transfers between devices: 57.4 us -> 52.6 us  [the longest x1 38.9 us: local(): lax.all_gather(kv_own[half:], ('chip', 'core'), axis=0, tiled=True)]
    unnamed x18 -> x16, local copies, waits for them, and re-layouts: 8.38 us -> 9.45 us
  transfers between devices with their start and end apart: 8 -> 8, of which waited for: 7 -> 7; matrix products, arithmetic and copies ran while one was open for 8% -> 11% of each run, Pallas kernels for 4% -> 6%
where the time goes in v4:
time: 359 us; the launch traced here: 357 us
  waiting for transfers between devices  219 us (61%)
  local copies, waits for them, and re-layouts  45 us (13%)
  starting transfers between devices  28 us (8%)
  Pallas kernels  20 us (6%)
  other arithmetic  16.4 us (5%)
  between operations  14.7 us (4%)
  matrix products  13.7 us (4%)
    all_gather x1, waiting for transfers between devices, local(): context_all = lax.all_gather(context, 'mp', axis=1, tiled=True)  62.1 us
    all_gather x1, waiting for transfers between devices, local(): routed = lax.all_gather(routed_part, 'mp', axis=1, tiled=True)  45.5 us
    all_gather x1, waiting for transfers between devices, local(): lax.all_gather(kv_own[half:], ('chip', 'core'), axis=0, tiled=True)  38.9 us
    all_to_all x1, waiting for transfers between devices, local(): lax.all_to_all(backward, ('chip', 'core'), split_axis=0, concat_axis=0, t...  28.3 us
    all_to_all x1, waiting for transfers between devices, local(): lax.all_to_all(outgoing.reshape(owners, capacity, columns), ('chip', 'cor...  28.1 us
    pallas_call x2, Pallas kernels, flash_pass(): pl.pallas_call(functools.partial(flash_kernel, final), grid_spec=grid_spe...  20 us
    all_gather x1, waiting for transfers between devices, local(): kv_low = lax.all_gather(kv_own[:half], ('chip', 'core'), axis=0, tiled=True)  13.7 us
    all_to_all x1, starting transfers between devices, local(): lax.all_to_all(places_info, ('chip', 'core'), split_axis=0, concat_axis=0...  9.6 us
  transfers between devices with their start and end apart: 8, of which 7 were waited for; matrix products, arithmetic and copies ran while one was open for 11% of the time, Pallas kernels for 6%

profile of v4, /device:TPU:1, one launch (start us, length us, event | category | flops | bytes accessed | tf_op | source)
XLA Modules:
  0.0 357.2 jit_solution(4686164512516688617)
XLA Ops:
  6.5 1.0 convert_reduce_fusion
  7.6 1.4 fusion.32
  8.9 0.7 add_select_fusion
  9.6 1.2 reduce-window.6
  11.2 2.4 scatter_custom_fusion
  13.7 0.6 slice.45
  14.9 0.7 pad_add_fusion.1
  15.7 0.6 pad_add_fusion
  16.3 9.6 %all-to-all-start = ((s32[32,1,34]{2,1,0:T(1,128)}), s32[32,1,34]{2,1,0:T(1,128)S(1)}, u32[]{:S(2)}, u32[]{:S(2)}) async-start(s32[32,1,34]{2,1,0:T(1,128)} %bitcast.5), calls=%async_computation | async-start | bytes 32768 | tf_op jit(solution)/shard_map/all_to_all | solution.py:194
  25.9 4.8 %scatter_custom_fusion.1 = bf16[1024,1024]{1,0:T(8,128)(2,1)} fusion(s32[512]{0:T(512)S(1)} %compare_select_fusion.2, bf16[512,1024]{1,0:T(8,128)(2,1)} %param.8, bf16[]{:T(256)} %constant.79.clone.1), kind=kCustom, calls=%fused_computation.15 | custom fusion | bytes 2097664 | tf_op jit(solution)/shard_map/scatter | solution.py:179
  30.8 2.0 all-to-all-done
  32.8 5.3 %all-to-all-start.1 = ((bf16[32,32,1024]{2,1,0:T(8,128)(2,1)}), bf16[32,32,1024]{2,1,0:T(8,128)(2,1)S(1)}, u32[]{:S(2)}, u32[]{:S(2)}) async-start(bf16[32,32,1024]{2,1,0:T(8,128)(2,1)} %bitcast.8), calls=%async_computation.1 | async-start | bytes 4194304 | tf_op jit(solution)/shard_map/all_to_all | solution.py:191
  38.3 28.1 %all-to-all-done.1 = bf16[32,32,1024]{2,1,0:T(8,128)(2,1)S(1)} async-done(((bf16[32,32,1024]{2,1,0:T(8,128)(2,1)}), bf16[32,32,1024]{2,1,0:T(8,128)(2,1)S(1)}, u32[]{:S(2)}, u32[]{:S(2)}) %all-to-all-start.1) | async-done | bytes 2097184 | tf_op jit(solution)/shard_map/all_to_all | solution.py:191
  66.5 6.2 %scatter_custom_fusion.2 = bf16[512,1024]{1,0:T(8,128)(2,1)} fusion(s32[1024]{0:T(1024)S(1)} %bitcast.70, bf16[1024,1024]{1,0:T(8,128)(2,1)S(1)} %bitcast.60, bf16[]{:T(256)} %constant.79.clone.1), kind=kCustom, calls=%fused_computation.20 | custom fusion | bytes 1048578 | tf_op jit(solution)/shard_map/scatter | solution.py:206
  72.9 45.5 %all-gather.5.cloned.1.call-done = bf16[512,4096]{1,0:T(8,128)(2,1)} async-done(((bf16[512,1024]{1,0:T(8,128)(2,1)}), bf16[512,4096]{1,0:T(8,128)(2,1)}) %all-gather.5.cloned.1.call-update) | async-done | bytes 4194320 | tf_op jit(solution)/shard_map/all_gather | solution.py:208
  118.5 3.2 fusion
  121.9 1.3 convolution_bitcast_fusion
  123.2 1.2 fusion.16
  124.5 1.3 convolution_convert_fusion
  126.0 0.7 fusion.31
  126.8 0.7 all-gather.7.cloned.1.call-update
  127.5 6.5 %copy.47 = bf16[512,4096]{0,1:T(8,128)(2,1)} copy(bf16[512,4096]{1,0:T(8,128)(2,1)} %param.15) | data formatting | bytes 8388608 | tf_op args[7]
  134.0 5.0 %all-to-all-start.2 = ((bf16[4,512,1024]{1,2,0:T(8,128)(2,1)}), bf16[4,512,1024]{1,2,0:T(8,128)(2,1)}, u32[]{:S(2)}, u32[]{:S(2)}) async-start(bf16[4,512,1024]{1,2,0:T(8,128)(2,1)} %bitcast.56), calls=%async_computation.2 | async-start | bytes 8388608 | tf_op jit(solution)/shard_map/all_to_all | solution.py:247
  139.1 0.7 iota_add_fusion.refs_4_
  139.8 1.7 multiply_cosine_fusion.1
  141.7 0.8 fusion.20
  142.5 0.7 fusion.24
  143.8 1.2 fusion.29
  145.0 0.9 copy.46.refs_3_
  145.9 1.3 stack.35.span_ref
  147.2 1.2 stack.34.span_ref
  148.4 5.9 %fusion.27 = f32[512,512]{0,1:T(8,128)S(1)} fusion(bf16[4096,512]{1,0:T(8,128)(2,1)} %param.12, bf16[512,4096]{1,0:T(8,128)(2,1)} %all-gather.5.cloned.1.call-done, f32[4096]{0:T(1024)S(1)} %copy-done.5, f32[512]{0:T(512)S(1)} %add_rsqrt_fusion), kind=kOutput, calls=%fused_computation.72 | convolution fusion | flops 2155872256 | bytes 9455616 | tf_op jit(solution)/shard_map/dot_general | solution.py:213
  154.3 0.9 fusion.30
  155.6 1.4 copy.52
  157.0 1.6 subtract_convert_fusion
  158.6 0.7 pad_maximum_fusion
  159.3 0.9 copy.57
  160.2 13.7 %all-gather.9.cloned.1.call-done.refs_1_.refs_2_ = bf16[8192,256]{1,0:T(8,128)(2,1)} async-done(((bf16[256,256]{1,0:T(8,128)(2,1)}), bf16[8192,256]{1,0:T(8,128)(2,1)}) %all-gather.9.cloned.1.call-update) | async-done | bytes 4194320 | tf_op jit(solution)/shard_map/all_gather | solution.py:224
  173.9 9.4 %shard_map.82 = (f32[4,512,1]{2,1,0:T(8,128)}, f32[4,512,1]{2,1,0:T(8,128)}, f32[4,512,128]{2,1,0:T(8,128)}) custom-call(s32[6]{0:T(128)} %stack.35.span_ref, bf16[512,512]{1,0:T(8,128)(2,1)} %bitcast.62, bf16[8192,256]{1,0:T(8,128)(2,1)} %all-gather.9.cloned.1.call-done.refs_1_.refs_2_, bf16[8192,256]{1,0:T(8,128)(2,1)} %all-gather.9.cloned.1.call-done.refs_1_.refs_2_, ...), custom_call_target="tpu_custom_call" | custom-call | flops 4831838208 | bytes 3407872 | tf_op jit(solution)/shard_map/pallas_call | solution.py:155
  183.3 38.9 %all-gather.7.cloned.1.call-done.refs_1_.refs_2_ = bf16[8192,256]{1,0:T(8,128)(2,1)} async-done(((bf16[256,256]{1,0:T(8,128)(2,1)}), bf16[8192,256]{1,0:T(8,128)(2,1)}) %all-gather.7.cloned.1.call-update) | async-done | bytes 4194320 | tf_op jit(solution)/shard_map/all_gather | solution.py:225
  222.1 10.6 %shard_map.83 = bf16[512,512]{1,0:T(8,128)(2,1)} custom-call(s32[6]{0:T(128)} %stack.34.span_ref, bf16[512,512]{1,0:T(8,128)(2,1)} %bitcast.63, bf16[8192,256]{1,0:T(8,128)(2,1)} %all-gather.7.cloned.1.call-done.refs_1_.refs_2_, bf16[8192,256]{1,0:T(8,128)(2,1)} %all-gather.7.cloned.1.call-done.refs_1_.refs_2_, s32[512,1]{1,0:T(8,128)} %copy.46.refs_3_, ...), custom_call_target="tpu_custom_call" | custom-call | flops 4831838208 | bytes 3407872 | tf_op jit(solution)/shard_map/pallas_call | solution.py:155
  232.8 6.4 %copy.48 = bf16[4,512,1024]{2,1,0:T(8,128)(2,1)} copy(bf16[4,512,1024]{1,2,0:T(8,128)(2,1)} %all-to-all-done.2) | data formatting | bytes 8388608 | tf_op jit(solution)/shard_map/all_to_all | solution.py:247
  239.2 62.1 %all-gather.11.cloned.1.call-done = bf16[512,2048]{1,0:T(8,128)(2,1)} async-done(((bf16[512,512]{1,0:T(8,128)(2,1)}), bf16[512,2048]{1,0:T(8,128)(2,1)}) %all-gather.11.cloned.1.call-update) | async-done | bytes 2097168 | tf_op jit(solution)/shard_map/all_gather | solution.py:244
  301.3 5.2 %add_convert_fusion = bf16[512,1024]{1,0:T(8,128)(2,1)S(1)} fusion(bf16[512,1024]{1,0:T(8,128)(2,1)S(1)} %copy-done.2, bf16[512,2048]{1,0:T(8,128)(2,1)} %all-gather.11.cloned.1.call-done, bf16[2048,1024]{1,0:T(8,128)(2,1)} %bitcast.58), kind=kOutput, calls=%fused_computation.10 | convolution fusion | flops 2149056512 | bytes 8388608 | tf_op jit(solution)/shard_map/dot_general | solution.py:248
  306.5 5.4 %gather_fusion = bf16[1024,1024]{1,0:T(8,128)(2,1)} fusion(bf16[512,1024]{1,0:T(8,128)(2,1)S(1)} %add_convert_fusion, s32[1024]{0:T(1024)S(1)} %broadcast_clamp_fusion), kind=kCustom, calls=%fused_computation | custom fusion | bytes 4198400 | tf_op jit(solution)/shard_map/gather | solution.py:252
  311.9 7.7 %all-to-all-start.3 = ((bf16[32,32,1024]{2,1,0:T(8,128)(2,1)}), bf16[32,32,1024]{2,1,0:T(8,128)(2,1)S(1)}, u32[]{:S(2)}, u32[]{:S(2)}) async-start(bf16[32,32,1024]{2,1,0:T(8,128)(2,1)} %bitcast.57), calls=%async_computation.3 | async-start | bytes 4194304 | tf_op jit(solution)/shard_map/all_to_all | solution.py:253
  319.6 28.3 %all-to-all-done.3 = bf16[32,32,1024]{2,1,0:T(8,128)(2,1)S(1)} async-done(((bf16[32,32,1024]{2,1,0:T(8,128)(2,1)}), bf16[32,32,1024]{2,1,0:T(8,128)(2,1)S(1)}, u32[]{:S(2)}, u32[]{:S(2)}) %all-to-all-start.3) | async-done | bytes 2097184 | tf_op jit(solution)/shard_map/all_to_all | solution.py:253
  347.9 2.8 gather_fusion.1
  (38 shorter events, 2.0 us)
Async XLA Ops:
  6.5 115.2 %copy-start = (bf16[4096,128]{1,0:T(8,128)(2,1)S(1)}, bf16[4096,128]{1,0:T(8,128)(2,1)}, u32[]{:S(2)}) copy-start(bf16[4096,128]{1,0:T(8,128)(2,1)} %param.13) | copy-start | bytes 3145732
  16.3 16.5 %all-to-all-start = ((s32[32,1,34]{2,1,0:T(1,128)}), s32[32,1,34]{2,1,0:T(1,128)S(1)}, u32[]{:S(2)}, u32[]{:S(2)}) async-start(s32[32,1,34]{2,1,0:T(1,128)} %bitcast.5), calls=%async_computation | async-start | bytes 32768 | tf_op jit(solution)/shard_map/all_to_all | solution.py:194
  32.8 33.6 %all-to-all-start.1 = ((bf16[32,32,1024]{2,1,0:T(8,128)(2,1)}), bf16[32,32,1024]{2,1,0:T(8,128)(2,1)S(1)}, u32[]{:S(2)}, u32[]{:S(2)}) async-start(bf16[32,32,1024]{2,1,0:T(8,128)(2,1)} %bitcast.8), calls=%async_computation.1 | async-start | bytes 4194304 | tf_op jit(solution)/shard_map/all_to_all | solution.py:191
  38.2 83.6 %copy-start.5 = (f32[4096]{0:T(1024)S(1)}, f32[4096]{0:T(1024)}, u32[]{:S(2)}) copy-start(f32[4096]{0:T(1024)} %param.11) | copy-start | bytes 49156
  38.2 80.3 %all-gather.5.cloned.1.call-start = ((), (), s32[]{:S(2)}) async-start(), calls=%async_computation.4 | async-start | bytes 5242880 | tf_op jit(solution)/shard_map/all_gather | solution.py:208
  72.7 101.2 %all-gather.9.cloned.1.call-start = ((), (), s32[]{:S(2)}) async-start(), calls=%async_computation.6 | async-start | bytes 4325376 | tf_op jit(solution)/shard_map/all_gather | solution.py:224
  118.5 3.4 copy-start.1
  121.9 2.5 copy-start.4
  126.7 95.4 %all-gather.7.cloned.1.call-start = ((), (), s32[]{:S(2)}) async-start(), calls=%async_computation.5 | async-start | bytes 4325376 | tf_op jit(solution)/shard_map/all_gather | solution.py:225
  134.0 9.8 %copy-start.3 = (s32[512]{0:T(512)S(1)}, s32[512]{0:T(512)}, u32[]{:S(2)}) copy-start(s32[512]{0:T(512)} %param.10) | copy-start | bytes 6148
  134.0 98.8 %all-to-all-start.2 = ((bf16[4,512,1024]{1,2,0:T(8,128)(2,1)}), bf16[4,512,1024]{1,2,0:T(8,128)(2,1)}, u32[]{:S(2)}, u32[]{:S(2)}) async-start(bf16[4,512,1024]{1,2,0:T(8,128)(2,1)} %bitcast.56), calls=%async_computation.2 | async-start | bytes 8388608 | tf_op jit(solution)/shard_map/all_to_all | solution.py:247
  139.0 162.3 %all-gather.11.cloned.1.call-start = ((), (), s32[]{:S(2)}) async-start(), calls=%async_computation.7 | async-start | bytes 2621440 | tf_op jit(solution)/shard_map/all_gather | solution.py:244
  232.8 68.6 %copy-start.2 = (bf16[512,1024]{1,0:T(8,128)(2,1)S(1)}, bf16[512,1024]{1,0:T(8,128)(2,1)}, u32[]{:S(2)}) copy-start(bf16[512,1024]{1,0:T(8,128)(2,1)} %scatter_custom_fusion.2) | copy-start | bytes 3145732
  311.9 36.0 %all-to-all-start.3 = ((bf16[32,32,1024]{2,1,0:T(8,128)(2,1)}), bf16[32,32,1024]{2,1,0:T(8,128)(2,1)S(1)}, u32[]{:S(2)}, u32[]{:S(2)}) async-start(bf16[32,32,1024]{2,1,0:T(8,128)(2,1)} %bitcast.57), calls=%async_computation.3 | async-start | bytes 4194304 | tf_op jit(solution)/shard_map/all_to_all | solution.py:253
Sparse Core Ops, SparseCore 0:
  72.8 45.6 all-gather.4
  126.8 47.0 all-gather.8
  176.2 45.8 all-gather.6
  232.9 68.4 all-gather.10

commit v5 on v4

--- a/solution.py
+++ b/solution.py
@@ -15,6 +15,7 @@
 NORM_EPS = 1e-05
 NEG_START = -1e30
 KEY_BLOCK = 512
+CHUNK = 128
 
 
 def rope_angles(row_index):
@@ -66,39 +67,57 @@
             acc_sc[...] = jnp.zeros(acc_sc.shape, jnp.float32)
 
     key_first = (span_ref[0] + step) * span_ref[4] + span_ref[5]
+    key_last = key_first + block - 1
     active = step < span_ref[1]
-    whole = (key_first >= span_ref[2]) & (key_first + block - 1 <= span_ref[3])
-
-    def accumulate(masked):
+    chunk = CHUNK
+    chunks = q_ref.shape[0] // chunk
+
+    def accumulate(c, masked):
+        r0 = pl.multiple_of(c * chunk, chunk)
         keys = k_ref[...]
         values = v_ref[...]
         if masked:
             key_rows = key_first + lax.broadcasted_iota(jnp.int32, (1, block), 1)
-            allowed = (key_rows >= start_ref[...]) & (key_rows <= row_ref[...])
+            allowed = (key_rows >= start_ref[pl.ds(r0, chunk), :]) & (
+                key_rows <= row_ref[pl.ds(r0, chunk), :]
+            )
         for h in range(heads):
             scores = lax.dot_general(
-                q_ref[:, h * HD:(h + 1) * HD], keys, (((1,), (1,)), ((), ())),
+                q_ref[pl.ds(r0, chunk), h * HD:(h + 1) * HD], keys, (((1,), (1,)), ((), ())),
                 preferred_element_type=jnp.float32,
             ) * scale
             if masked:
                 scores = jnp.where(allowed, scores, -jnp.inf)
-            m_old = m_sc[h]
+            m_old = m_sc[h, pl.ds(r0, chunk), :]
             m_new = jnp.maximum(m_old, jnp.max(scores, axis=-1, keepdims=True))
             rescale = jnp.exp(m_old - m_new)
             exp_scores = jnp.exp(scores - m_new)
-            l_sc[h] = l_sc[h] * rescale + jnp.sum(exp_scores, axis=-1, keepdims=True)
-            acc_sc[h] = acc_sc[h] * rescale + jnp.dot(
+            l_sc[h, pl.ds(r0, chunk), :] = l_sc[h, pl.ds(r0, chunk), :] * rescale + jnp.sum(
+                exp_scores, axis=-1, keepdims=True
+            )
+            acc_sc[h, pl.ds(r0, chunk), :] = acc_sc[h, pl.ds(r0, chunk), :] * rescale + jnp.dot(
                 exp_scores.astype(jnp.bfloat16), values, preferred_element_type=jnp.float32
             )
-            m_sc[h] = m_new
-
-    @pl.when(active & whole)
-    def _whole():
-        accumulate(False)
-
-    @pl.when(active & jnp.logical_not(whole))
-    def _masked():
-        accumulate(True)
+            m_sc[h, pl.ds(r0, chunk), :] = m_new
+
+    @pl.when(active)
+    def _visit():
+        @pl.loop(0, chunks)
+        def _chunk(c):
+            row_first = span_ref[3] + c * chunk
+            row_last = row_first + chunk - 1
+            least_start = span_ref[6 + c]
+            most_start = span_ref[6 + chunks + c]
+            needed = (least_start <= key_last) & (row_last >= key_first)
+            whole = (most_start <= key_first) & (key_last <= row_first)
+
+            @pl.when(needed & whole)
+            def _whole():
+                accumulate(c, False)
+
+            @pl.when(needed & jnp.logical_not(whole))
+            def _masked():
+                accumulate(c, True)
 
     if final:
         @pl.when(step == pl.num_programs(0) - 1)
@@ -228,23 +247,25 @@
     last_block = (block_first + tok_dev - 1) // block
     first_block = doc_low // block
     max_blocks = min((tok_dev - 1) // block + -(-(DOC_MAX - 1) // block) + 1, owners * tok_dev // block)
-    max_start = jnp.max(row_start)
+    chunk_starts = row_start.reshape(-1, CHUNK)
+    least_starts = jnp.min(chunk_starts, axis=1)
+    most_starts = jnp.max(chunk_starts, axis=1)
 
     def span_for(offset):
-        return jnp.stack(
-            [first_block, last_block - first_block + 1, max_start, block_first, block, offset]
-        ).astype(jnp.int32)
+        head = jnp.stack([first_block, last_block - first_block + 1, 0, block_first, block, offset])
+        return jnp.concatenate([head, least_starts, most_starts]).astype(jnp.int32)
 
     state = flash_pass(
         span_for(0), queries, kv_low, row_start[:, None], row_index[:, None], max_blocks, None
     )
-    context = flash_pass(
-        span_for(half), queries, kv_high, row_start[:, None], row_index[:, None], max_blocks, state
-    )
-    context_all = lax.all_gather(context, "mp", axis=1, tiled=True)
     mp_size = lax.axis_size("mp")
     w_split = jnp.transpose(w_out.reshape(w_out.shape[0], mp_size, -1), (1, 0, 2))
     w_cols = lax.all_to_all(w_split, "mp", split_axis=0, concat_axis=0, tiled=True)
+    state, w_cols = lax.optimization_barrier((state, w_cols))
+    context = flash_pass(
+        span_for(half), queries, kv_high, row_start[:, None], row_index[:, None], max_blocks, state
+    )
+    context_all = lax.all_gather(context, "mp", axis=1, tiled=True)
     summed = jnp.dot(
         context_all, w_cols.reshape(-1, w_cols.shape[2]), preferred_element_type=jnp.float32
     )

time: 359 us -> 425 us (1.18)
  waiting for transfers between devices: 219 us -> 285 us
  Pallas kernels: 20 us -> 26.1 us
    all_gather x1, waiting for transfers between devices: 62.1 us -> 130 us  [local(): context_all = lax.all_gather(context, 'mp', axis=1, tiled=True)]
    all_to_all x1 -> x0, local copies, waits for them, and re-layouts: 6.43 us -> none  [local(): lax.all_to_all(w_split, 'mp', split_axis=0, concat_axis=0, tiled=True)]
    optimization_barrier x0 -> x1, local copies, waits for them, and re-layouts: none -> 6.41 us  [local(): state, w_cols = lax.optimization_barrier((state, w_cols))]
    pallas_call x2, Pallas kernels: 20 us -> 26.1 us  [flash_pass(): pl.pallas_call(functools.partial(flash_kernel, final), grid_spec=grid_spe...]
    all_gather x1, waiting for transfers between devices: 38.9 us -> 34.2 us  [local(): lax.all_gather(kv_own[half:], ('chip', 'core'), axis=0, tiled=True)]
  transfers between devices with their start and end apart: 8 -> 8, of which waited for: 7 -> 7; matrix products, arithmetic and copies ran while one was open for 11% -> 9% of each run, Pallas kernels for 6% -> 3%
where the time goes in v5:
time: 425 us; the launch traced here: 427 us
  waiting for transfers between devices  285 us (67%)
  local copies, waits for them, and re-layouts  43.7 us (10%)
  starting transfers between devices  28 us (7%)
  Pallas kernels  26.1 us (6%)
  other arithmetic  16 us (4%)
  between operations  14.6 us (3%)
  matrix products  13.7 us (3%)
    all_gather x1, waiting for transfers between devices, local(): context_all = lax.all_gather(context, 'mp', axis=1, tiled=True)  130 us
    all_gather x1, waiting for transfers between devices, local(): routed = lax.all_gather(routed_part, 'mp', axis=1, tiled=True)  45.5 us
    all_gather x1, waiting for transfers between devices, local(): lax.all_gather(kv_own[half:], ('chip', 'core'), axis=0, tiled=True)  34.2 us
    all_to_all x1, waiting for transfers between devices, local(): lax.all_to_all(backward, ('chip', 'core'), split_axis=0, concat_axis=0, t...  28.3 us
    all_to_all x1, waiting for transfers between devices, local(): lax.all_to_all(outgoing.reshape(owners, capacity, columns), ('chip', 'cor...  28.1 us
    pallas_call x2, Pallas kernels, flash_pass(): pl.pallas_call(functools.partial(flash_kernel, final), grid_spec=grid_spe...  26.1 us
    all_gather x1, waiting for transfers between devices, local(): kv_low = lax.all_gather(kv_own[:half], ('chip', 'core'), axis=0, tiled=True)  15.8 us
    all_to_all x1, starting transfers between devices, local(): lax.all_to_all(places_info, ('chip', 'core'), split_axis=0, concat_axis=0...  9.6 us
  transfers between devices with their start and end apart: 8, of which 7 were waited for; matrix products, arithmetic and copies ran while one was open for 9% of the time, Pallas kernels for 3%

profile of v5, /device:TPU:1, one launch (start us, length us, event | category | flops | bytes accessed | tf_op | source)
XLA Modules:
  0.0 426.7 jit_solution(3310679642205270548)
XLA Ops:
  6.5 1.0 convert_reduce_fusion
  7.6 1.4 fusion.31
  8.9 0.7 add_select_fusion
  9.6 1.2 reduce-window.6
  11.2 2.4 scatter_custom_fusion
  13.7 0.6 slice.45
  14.9 0.6 pad_add_fusion.1
  15.7 0.6 pad_add_fusion
  16.3 9.6 %all-to-all-start = ((s32[32,1,34]{2,1,0:T(1,128)}), s32[32,1,34]{2,1,0:T(1,128)S(1)}, u32[]{:S(2)}, u32[]{:S(2)}) async-start(s32[32,1,34]{2,1,0:T(1,128)} %bitcast.5), calls=%async_computation | async-start | bytes 32768 | tf_op jit(solution)/shard_map/all_to_all | solution.py:213
  25.9 4.8 %scatter_custom_fusion.1 = bf16[1024,1024]{1,0:T(8,128)(2,1)} fusion(s32[512]{0:T(512)S(1)} %compare_select_fusion.2, bf16[512,1024]{1,0:T(8,128)(2,1)} %param.8, bf16[]{:T(256)} %constant.79.clone.1), kind=kCustom, calls=%fused_computation.15 | custom fusion | bytes 2097664 | tf_op jit(solution)/shard_map/scatter | solution.py:198
  30.7 2.0 all-to-all-done
  32.8 5.3 %all-to-all-start.1 = ((bf16[32,32,1024]{2,1,0:T(8,128)(2,1)}), bf16[32,32,1024]{2,1,0:T(8,128)(2,1)S(1)}, u32[]{:S(2)}, u32[]{:S(2)}) async-start(bf16[32,32,1024]{2,1,0:T(8,128)(2,1)} %bitcast.8), calls=%async_computation.1 | async-start | bytes 4194304 | tf_op jit(solution)/shard_map/all_to_all | solution.py:210
  38.3 28.1 %all-to-all-done.1 = bf16[32,32,1024]{2,1,0:T(8,128)(2,1)S(1)} async-done(((bf16[32,32,1024]{2,1,0:T(8,128)(2,1)}), bf16[32,32,1024]{2,1,0:T(8,128)(2,1)S(1)}, u32[]{:S(2)}, u32[]{:S(2)}) %all-to-all-start.1) | async-done | bytes 2097184 | tf_op jit(solution)/shard_map/all_to_all | solution.py:210
  66.4 6.2 %scatter_custom_fusion.2 = bf16[512,1024]{1,0:T(8,128)(2,1)} fusion(s32[1024]{0:T(1024)S(1)} %bitcast.72, bf16[1024,1024]{1,0:T(8,128)(2,1)S(1)} %bitcast.62, bf16[]{:T(256)} %constant.79.clone.1), kind=kCustom, calls=%fused_computation.20 | custom fusion | bytes 1048578 | tf_op jit(solution)/shard_map/scatter | solution.py:225
  72.9 45.5 %all-gather.5.cloned.1.call-done = bf16[512,4096]{1,0:T(8,128)(2,1)} async-done(((bf16[512,1024]{1,0:T(8,128)(2,1)}), bf16[512,4096]{1,0:T(8,128)(2,1)}) %all-gather.5.cloned.1.call-update) | async-done | bytes 4194320 | tf_op jit(solution)/shard_map/all_gather | solution.py:227
  118.5 3.2 fusion
  121.9 1.3 convolution_bitcast_fusion
  123.2 1.2 fusion.16
  124.4 1.3 convolution_convert_fusion
  125.9 0.7 fusion.30
  126.7 0.7 all-gather.7.cloned.1.call-update
  127.4 6.5 %copy.46 = bf16[512,4096]{0,1:T(8,128)(2,1)} copy(bf16[512,4096]{1,0:T(8,128)(2,1)} %param.15) | data formatting | bytes 8388608 | tf_op args[7]
  133.9 5.0 %all-to-all-start.2 = ((bf16[4,512,1024]{1,2,0:T(8,128)(2,1)}), bf16[4,512,1024]{1,2,0:T(8,128)(2,1)}, u32[]{:S(2)}, u32[]{:S(2)}) async-start(bf16[4,512,1024]{1,2,0:T(8,128)(2,1)} %bitcast.58), calls=%async_computation.2 | async-start | bytes 8388608 | tf_op jit(solution)/shard_map/all_to_all | solution.py:263
  139.0 0.7 iota_add_fusion.refs_4_
  139.7 1.7 multiply_cosine_fusion.1
  141.6 0.9 fusion.20
  142.5 0.7 fusion.24
  143.8 0.8 bitcast_reduce_fusion
  144.6 0.9 copy.47.refs_3_
  145.4 0.6 concatenate.32.span_ref
  146.0 0.6 concatenate.27.span_ref
  146.7 5.9 %fusion.27 = f32[512,512]{0,1:T(8,128)S(1)} fusion(bf16[4096,512]{1,0:T(8,128)(2,1)} %param.12, bf16[512,4096]{1,0:T(8,128)(2,1)} %all-gather.5.cloned.1.call-done, f32[4096]{0:T(1024)S(1)} %copy-done.5, f32[512]{0:T(512)S(1)} %add_rsqrt_fusion), kind=kOutput, calls=%fused_computation.74 | convolution fusion | flops 2155872256 | bytes 9455616 | tf_op jit(solution)/shard_map/dot_general | solution.py:232
  152.6 0.9 fusion.29
  153.9 1.4 copy.52
  155.3 1.5 subtract_convert_fusion
  156.8 0.7 pad_maximum_fusion
  157.6 0.9 copy.57
  158.4 15.8 %all-gather.9.cloned.1.call-done.refs_1_.refs_2_ = bf16[8192,256]{1,0:T(8,128)(2,1)} async-done(((bf16[256,256]{1,0:T(8,128)(2,1)}), bf16[8192,256]{1,0:T(8,128)(2,1)}) %all-gather.9.cloned.1.call-update) | async-done | bytes 4194320 | tf_op jit(solution)/shard_map/all_gather | solution.py:243
  174.2 13.9 %shard_map.82 = (f32[4,512,1]{2,1,0:T(8,128)}, f32[4,512,1]{2,1,0:T(8,128)}, f32[4,512,128]{2,1,0:T(8,128)}) custom-call(s32[14]{0:T(128)} %concatenate.32.span_ref, bf16[512,512]{1,0:T(8,128)(2,1)} %bitcast.64, bf16[8192,256]{1,0:T(8,128)(2,1)} %all-gather.9.cloned.1.call-done.refs_1_.refs_2_, ...), custom_call_target="tpu_custom_call" | custom-call | flops 4831838208 | bytes 3407872 | tf_op jit(solution)/shard_map/pallas_call | solution.py:174
  188.1 34.2 %all-gather.7.cloned.1.call-done.refs_1_.refs_2_ = bf16[8192,256]{1,0:T(8,128)(2,1)} async-done(((bf16[256,256]{1,0:T(8,128)(2,1)}), bf16[8192,256]{1,0:T(8,128)(2,1)}) %all-gather.7.cloned.1.call-update) | async-done | bytes 4194320 | tf_op jit(solution)/shard_map/all_gather | solution.py:244
  222.2 12.3 %shard_map.83 = bf16[512,512]{1,0:T(8,128)(2,1)} custom-call(s32[14]{0:T(128)} %concatenate.27.span_ref, bf16[512,512]{1,0:T(8,128)(2,1)} %bitcast.65, bf16[8192,256]{1,0:T(8,128)(2,1)} %all-gather.7.cloned.1.call-done.refs_1_.refs_2_, bf16[8192,256]{1,0:T(8,128)(2,1)} %all-gather.7.cloned.1.call-done.refs_1_.refs_2_, s32[512,1]{1,0:T(8,128)} %copy.47.refs_3_, ...), custom_call_target="tpu_custom_call" | custom-call | flops 4831838208 | bytes 3407872 | tf_op jit(solution)/shard_map/pallas_call | solution.py:174
  234.5 6.4 %copy.48 = bf16[4,512,1024]{2,1,0:T(8,128)(2,1)} copy(bf16[4,512,1024]{1,2,0:T(8,128)(2,1)} %all-to-all-done.2) | data formatting | bytes 8388608 | tf_op jit(solution)/shard_map/optimization_barrier | solution.py:264
  240.9 130.0 %all-gather.11.cloned.1.call-done = bf16[512,2048]{1,0:T(8,128)(2,1)} async-done(((bf16[512,512]{1,0:T(8,128)(2,1)}), bf16[512,2048]{1,0:T(8,128)(2,1)}) %all-gather.11.cloned.1.call-update) | async-done | bytes 2097168 | tf_op jit(solution)/shard_map/all_gather | solution.py:268
  370.9 5.2 %add_convert_fusion = bf16[512,1024]{1,0:T(8,128)(2,1)S(1)} fusion(bf16[512,1024]{1,0:T(8,128)(2,1)S(1)} %copy-done.2, bf16[512,2048]{1,0:T(8,128)(2,1)} %all-gather.11.cloned.1.call-done, bf16[2048,1024]{1,0:T(8,128)(2,1)} %bitcast.60), kind=kOutput, calls=%fused_computation.10 | convolution fusion | flops 2149056512 | bytes 8388608 | tf_op jit(solution)/shard_map/dot_general | solution.py:269
  376.1 5.4 %gather_fusion = bf16[1024,1024]{1,0:T(8,128)(2,1)} fusion(bf16[512,1024]{1,0:T(8,128)(2,1)S(1)} %add_convert_fusion, s32[1024]{0:T(1024)S(1)} %broadcast_clamp_fusion), kind=kCustom, calls=%fused_computation | custom fusion | bytes 4198400 | tf_op jit(solution)/shard_map/gather | solution.py:273
  381.4 7.7 %all-to-all-start.3 = ((bf16[32,32,1024]{2,1,0:T(8,128)(2,1)}), bf16[32,32,1024]{2,1,0:T(8,128)(2,1)S(1)}, u32[]{:S(2)}, u32[]{:S(2)}) async-start(bf16[32,32,1024]{2,1,0:T(8,128)(2,1)} %bitcast.59), calls=%async_computation.3 | async-start | bytes 4194304 | tf_op jit(solution)/shard_map/all_to_all | solution.py:274
  389.2 28.3 %all-to-all-done.3 = bf16[32,32,1024]{2,1,0:T(8,128)(2,1)S(1)} async-done(((bf16[32,32,1024]{2,1,0:T(8,128)(2,1)}), bf16[32,32,1024]{2,1,0:T(8,128)(2,1)S(1)}, u32[]{:S(2)}, u32[]{:S(2)}) %all-to-all-start.3) | async-done | bytes 2097184 | tf_op jit(solution)/shard_map/all_to_all | solution.py:274
  417.4 2.8 gather_fusion.1
  (38 shorter events, 2.0 us)
Async XLA Ops:
  6.5 115.2 %copy-start = (bf16[4096,128]{1,0:T(8,128)(2,1)S(1)}, bf16[4096,128]{1,0:T(8,128)(2,1)}, u32[]{:S(2)}) copy-start(bf16[4096,128]{1,0:T(8,128)(2,1)} %param.13) | copy-start | bytes 3145732
  16.3 16.5 %all-to-all-start = ((s32[32,1,34]{2,1,0:T(1,128)}), s32[32,1,34]{2,1,0:T(1,128)S(1)}, u32[]{:S(2)}, u32[]{:S(2)}) async-start(s32[32,1,34]{2,1,0:T(1,128)} %bitcast.5), calls=%async_computation | async-start | bytes 32768 | tf_op jit(solution)/shard_map/all_to_all | solution.py:213
  32.8 33.6 %all-to-all-start.1 = ((bf16[32,32,1024]{2,1,0:T(8,128)(2,1)}), bf16[32,32,1024]{2,1,0:T(8,128)(2,1)S(1)}, u32[]{:S(2)}, u32[]{:S(2)}) async-start(bf16[32,32,1024]{2,1,0:T(8,128)(2,1)} %bitcast.8), calls=%async_computation.1 | async-start | bytes 4194304 | tf_op jit(solution)/shard_map/all_to_all | solution.py:210
  38.1 83.6 %copy-start.5 = (f32[4096]{0:T(1024)S(1)}, f32[4096]{0:T(1024)}, u32[]{:S(2)}) copy-start(f32[4096]{0:T(1024)} %param.11) | copy-start | bytes 49156
  38.1 80.3 %all-gather.5.cloned.1.call-start = ((), (), s32[]{:S(2)}) async-start(), calls=%async_computation.4 | async-start | bytes 5242880 | tf_op jit(solution)/shard_map/all_gather | solution.py:227
  72.6 101.6 %all-gather.9.cloned.1.call-start = ((), (), s32[]{:S(2)}) async-start(), calls=%async_computation.6 | async-start | bytes 4325376 | tf_op jit(solution)/shard_map/all_gather | solution.py:243
  118.5 3.4 copy-start.1
  121.9 2.5 copy-start.4
  126.7 95.5 %all-gather.7.cloned.1.call-start = ((), (), s32[]{:S(2)}) async-start(), calls=%async_computation.5 | async-start | bytes 4325376 | tf_op jit(solution)/shard_map/all_gather | solution.py:244
  133.9 9.8 %copy-start.3 = (s32[512]{0:T(512)S(1)}, s32[512]{0:T(512)}, u32[]{:S(2)}) copy-start(s32[512]{0:T(512)} %param.10) | copy-start | bytes 6148
  133.9 54.2 %all-to-all-start.2 = ((bf16[4,512,1024]{1,2,0:T(8,128)(2,1)}), bf16[4,512,1024]{1,2,0:T(8,128)(2,1)}, u32[]{:S(2)}, u32[]{:S(2)}) async-start(bf16[4,512,1024]{1,2,0:T(8,128)(2,1)} %bitcast.58), calls=%async_computation.2 | async-start | bytes 8388608 | tf_op jit(solution)/shard_map/all_to_all | solution.py:263
  138.9 232.0 %all-gather.11.cloned.1.call-start = ((), (), s32[]{:S(2)}) async-start(), calls=%async_computation.7 | async-start | bytes 2621440 | tf_op jit(solution)/shard_map/all_gather | solution.py:268
  234.5 136.4 %copy-start.2 = (bf16[512,1024]{1,0:T(8,128)(2,1)S(1)}, bf16[512,1024]{1,0:T(8,128)(2,1)}, u32[]{:S(2)}) copy-start(bf16[512,1024]{1,0:T(8,128)(2,1)} %scatter_custom_fusion.2) | copy-start | bytes 3145732
  381.4 36.0 %all-to-all-start.3 = ((bf16[32,32,1024]{2,1,0:T(8,128)(2,1)}), bf16[32,32,1024]{2,1,0:T(8,128)(2,1)S(1)}, u32[]{:S(2)}, u32[]{:S(2)}) async-start(bf16[32,32,1024]{2,1,0:T(8,128)(2,1)} %bitcast.59), calls=%async_computation.3 | async-start | bytes 4194304 | tf_op jit(solution)/shard_map/all_to_all | solution.py:274
Sparse Core Ops, SparseCore 0:
  72.8 45.6 all-gather.4
  126.8 47.3 all-gather.8
  176.5 45.7 all-gather.6
  234.6 136.2 all-gather.10

commit v6 on v4

--- a/solution.py
+++ b/solution.py
@@ -205,24 +205,34 @@
         .at[arrived_rows]
         .set(arrived.reshape(-1, columns), mode="drop")
     )
-    routed = lax.all_gather(routed_part, "mp", axis=1, tiled=True)
-    normed = normalize(routed, norm_gain)
+    half = tok_dev // 2
+    mp_size = lax.axis_size("mp")
+    routed_low = lax.all_gather(routed_part[:half], "mp", axis=1, tiled=True)
+    copies = jnp.broadcast_to(routed_part[half:][None], (mp_size, half, columns))
+    pieces = lax.all_to_all(copies, "mp", split_axis=0, concat_axis=0, tiled=True)
+    routed_high = jnp.transpose(pieces, (1, 0, 2)).reshape(half, mp_size * columns)
     heads_dev = w_query.shape[1] // HD
     kv_dev = w_key.shape[1] // HD
-    angles = rope_angles(row_index)
-    queries = jnp.dot(normed, w_query, preferred_element_type=jnp.float32).reshape(
-        tok_dev, heads_dev, HD
-    )
-    queries = rotate(queries, angles).astype(jnp.bfloat16).reshape(tok_dev, heads_dev * HD)
-    keys_own = jnp.dot(normed, w_key, preferred_element_type=jnp.float32).reshape(
-        tok_dev, kv_dev, HD
-    )
-    keys_own = rotate(keys_own, angles).astype(jnp.bfloat16).reshape(tok_dev, kv_dev * HD)
-    values_own = jnp.dot(normed, w_value, preferred_element_type=jnp.float32).astype(jnp.bfloat16)
-    kv_own = jnp.concatenate([keys_own, values_own], axis=1)
-    half = tok_dev // 2
-    kv_low = lax.all_gather(kv_own[:half], ("chip", "core"), axis=0, tiled=True)
-    kv_high = lax.all_gather(kv_own[half:], ("chip", "core"), axis=0, tiled=True)
+
+    def project(routed_rows, rows):
+        normed = normalize(routed_rows, norm_gain)
+        angles = rope_angles(rows)
+        queries = jnp.dot(normed, w_query, preferred_element_type=jnp.float32).reshape(
+            rows.shape[0], heads_dev, HD
+        )
+        queries = rotate(queries, angles).astype(jnp.bfloat16).reshape(rows.shape[0], heads_dev * HD)
+        keys = jnp.dot(normed, w_key, preferred_element_type=jnp.float32).reshape(
+            rows.shape[0], kv_dev, HD
+        )
+        keys = rotate(keys, angles).astype(jnp.bfloat16).reshape(rows.shape[0], kv_dev * HD)
+        values = jnp.dot(normed, w_value, preferred_element_type=jnp.float32).astype(jnp.bfloat16)
+        return queries, jnp.concatenate([keys, values], axis=1)
+
+    queries_low, kv_a = project(routed_low, row_index[:half])
+    kv_low = lax.all_gather(kv_a, ("chip", "core"), axis=0, tiled=True)
+    queries_high, kv_b = project(routed_high, row_index[half:])
+    kv_high = lax.all_gather(kv_b, ("chip", "core"), axis=0, tiled=True)
+    queries = jnp.concatenate([queries_low, queries_high], axis=0)
 
     block = KEY_BLOCK
     last_block = (block_first + tok_dev - 1) // block
@@ -242,7 +252,6 @@
         span_for(half), queries, kv_high, row_start[:, None], row_index[:, None], max_blocks, state
     )
     context_all = lax.all_gather(context, "mp", axis=1, tiled=True)
-    mp_size = lax.axis_size("mp")
     w_split = jnp.transpose(w_out.reshape(w_out.shape[0], mp_size, -1), (1, 0, 2))
     w_cols = lax.all_to_all(w_split, "mp", split_axis=0, concat_axis=0, tiled=True)
     summed = jnp.dot(

time: 359 us -> 371 us (1.033)
  local copies, waits for them, and re-layouts: 45 us -> 64 us
  waiting for transfers between devices: 219 us -> 200 us
  other arithmetic: 16.4 us -> 23.8 us
  starting transfers between devices: 28 us -> 32.8 us
    all_gather x3, waiting for transfers between devices: 98.1 us -> 46.3 us  [the longest x1 38.6 us: local(): kv_high = lax.all_gather(kv_b, ('chip', 'core'), axis=0, tiled=True)]
    all_to_all x0 -> x1, waiting for transfers between devices: none -> 31 us  [local(): lax.all_to_all(copies, 'mp', split_axis=0, concat_axis=0, tiled=True)]
    dot_general x0 -> x1, local copies, waits for them, and re-layouts: none -> 6.47 us  [project(): jnp.dot(normed, w_query, preferred_element_type=jnp.float32)]
    convert_element_type x0 -> x2, local copies, waits for them, and re-layouts: none -> 5.8 us  [the longest x1 5.65 us: normalize(): wide_rows = routed.astype(jnp.float32)]
    convert_element_type x0 -> x2, other arithmetic: none -> 5.1 us  [the longest x1 2.77 us: normalize(): return (wide_rows * inv_rms * norm_gain[None, :]).astype(jnp.bfloat16)]
    all_to_all x0 -> x1, starting transfers between devices: none -> 4.57 us  [local(): lax.all_to_all(copies, 'mp', split_axis=0, concat_axis=0, tiled=True)]
    unnamed x16 -> x42, local copies, waits for them, and re-layouts: 9.45 us -> 11.3 us
    dot_general x3 -> x6, matrix products: 8.55 us -> 9.38 us  [the longest x2 4.72 us: project(): jnp.dot(normed, w_query, preferred_element_type=jnp.float32)]
  transfers between devices with their start and end apart: 8 -> 9, of which waited for: 7 -> 7; matrix products, arithmetic and copies ran while one was open for 11% -> 16% of each run, Pallas kernels for 6% -> 5%
where the time goes in v6:
time: 371 us; the launch traced here: 369 us
  waiting for transfers between devices  200 us (54%)
  local copies, waits for them, and re-layouts  64 us (17%)
  starting transfers between devices  32.8 us (9%)
  other arithmetic  23.8 us (6%)
  Pallas kernels  19.7 us (5%)
  between operations  14.8 us (4%)
  matrix products  14.5 us (4%)
    all_gather x1, waiting for transfers between devices, local(): context_all = lax.all_gather(context, 'mp', axis=1, tiled=True)  63.8 us
    all_gather x1, waiting for transfers between devices, local(): kv_high = lax.all_gather(kv_b, ('chip', 'core'), axis=0, tiled=True)  38.6 us
    all_to_all x1, waiting for transfers between devices, local(): lax.all_to_all(copies, 'mp', split_axis=0, concat_axis=0, tiled=True)  31 us
    all_to_all x1, waiting for transfers between devices, local(): lax.all_to_all(backward, ('chip', 'core'), split_axis=0, concat_axis=0, t...  28.3 us
    all_to_all x1, waiting for transfers between devices, local(): lax.all_to_all(outgoing.reshape(owners, capacity, columns), ('chip', 'cor...  27.6 us
    pallas_call x2, Pallas kernels, flash_pass(): pl.pallas_call(functools.partial(flash_kernel, final), grid_spec=grid_spe...  19.7 us
    unnamed x42, local copies, waits for them, and re-layouts  11.3 us
    all_to_all x1, starting transfers between devices, local(): lax.all_to_all(places_info, ('chip', 'core'), split_axis=0, concat_axis=0...  9.6 us
  transfers between devices with their start and end apart: 9, of which 7 were waited for; matrix products, arithmetic and copies ran while one was open for 16% of the time, Pallas kernels for 5%

profile of v6, /device:TPU:1, one launch (start us, length us, event | category | flops | bytes accessed | tf_op | source)
XLA Modules:
  0.0 369.5 jit_solution(13747807421572333025)
XLA Ops:
  6.5 1.0 convert_reduce_fusion
  7.6 1.4 fusion.41
  9.7 1.2 reduce-window.6
  11.2 2.4 scatter_custom_fusion
  16.4 9.6 %all-to-all-start = ((s32[32,1,34]{2,1,0:T(1,128)}), s32[32,1,34]{2,1,0:T(1,128)S(1)}, u32[]{:S(2)}, u32[]{:S(2)}) async-start(s32[32,1,34]{2,1,0:T(1,128)} %bitcast.5), calls=%async_computation | async-start | bytes 32768 | tf_op jit(solution)/shard_map/all_to_all | solution.py:194
  26.0 4.8 %scatter_custom_fusion.1 = bf16[1024,1024]{1,0:T(8,128)(2,1)} fusion(s32[512]{0:T(512)S(1)} %compare_select_fusion.2, bf16[512,1024]{1,0:T(8,128)(2,1)} %param.8, bf16[]{:T(256)} %constant.80.clone.1), kind=kCustom, calls=%fused_computation.18 | custom fusion | bytes 2097664 | tf_op jit(solution)/shard_map/scatter | solution.py:179
  30.8 2.1 all-to-all-done
  32.8 5.3 %all-to-all-start.1 = ((bf16[32,32,1024]{2,1,0:T(8,128)(2,1)}), bf16[32,32,1024]{2,1,0:T(8,128)(2,1)S(1)}, u32[]{:S(2)}, u32[]{:S(2)}) async-start(bf16[32,32,1024]{2,1,0:T(8,128)(2,1)} %bitcast.8), calls=%async_computation.1 | async-start | bytes 4194304 | tf_op jit(solution)/shard_map/all_to_all | solution.py:191
  38.9 27.6 %all-to-all-done.1 = bf16[32,32,1024]{2,1,0:T(8,128)(2,1)S(1)} async-done(((bf16[32,32,1024]{2,1,0:T(8,128)(2,1)}), bf16[32,32,1024]{2,1,0:T(8,128)(2,1)S(1)}, u32[]{:S(2)}, u32[]{:S(2)}) %all-to-all-start.1) | async-done | bytes 2097184 | tf_op jit(solution)/shard_map/all_to_all | solution.py:191
  66.5 1.3 copy-done.8
  67.8 6.2 %scatter_custom_fusion.2 = bf16[512,1024]{1,0:T(8,128)(2,1)S(1)} fusion(s32[1024]{0:T(1024)S(1)} %bitcast.95, bf16[1024,1024]{1,0:T(8,128)(2,1)} %bitcast.85, bf16[]{:T(256)} %constant.80.clone.1), kind=kCustom, calls=%fused_computation.24 | custom fusion | bytes 1049088 | tf_op jit(solution)/shard_map/scatter | solution.py:206
  74.0 0.9 fusion.40
  74.9 1.6 broadcast_in_dim.26
  76.5 4.6 %all-to-all-start.2 = ((bf16[4,256,1024]{2,1,0:T(8,128)(2,1)}), bf16[4,256,1024]{2,1,0:T(8,128)(2,1)}, u32[]{:S(2)}, u32[]{:S(2)}) async-start(bf16[4,256,1024]{2,1,0:T(8,128)(2,1)} %broadcast_in_dim.26), calls=%async_computation.2 | async-start | bytes 4194304 | tf_op jit(solution)/shard_map/all_to_all | solution.py:212
  82.3 0.9 fusion.30
  84.5 2.0 fusion.39
  86.5 31.0 %all-to-all-done.2 = bf16[4,256,1024]{2,1,0:T(8,128)(2,1)} async-done(((bf16[4,256,1024]{2,1,0:T(8,128)(2,1)}), bf16[4,256,1024]{2,1,0:T(8,128)(2,1)}, u32[]{:S(2)}, u32[]{:S(2)}) %all-to-all-start.2) | async-done | bytes 2097184 | tf_op jit(solution)/shard_map/all_to_all | solution.py:212
  117.5 2.8 copy.75
  120.4 2.3 convert_element_type.77
  122.7 5.7 %copy.96 = f32[256,4096]{1,0:T(8,128)} copy(f32[256,4096]{0,1:T(8,128)} %bitcast.79) | data formatting | bytes 8388608 | tf_op jit(solution)/shard_map/convert_element_type | solution.py:42
  129.1 2.8 multiply_convert_fusion
  131.9 1.3 copy-done.2
  133.9 2.2 fusion
  137.0 1.2 fusion.28
  138.3 0.8 convolution_convert_fusion
  140.0 2.3 convolution_convert_fusion.1
  143.1 6.5 %copy.86 = bf16[512,4096]{0,1:T(8,128)(2,1)} copy(bf16[512,4096]{1,0:T(8,128)(2,1)} %param.15) | data formatting | bytes 8388608 | tf_op args[7]
  149.6 4.8 %all-to-all-start.3 = ((bf16[4,512,1024]{1,2,0:T(8,128)(2,1)}), bf16[4,512,1024]{1,2,0:T(8,128)(2,1)}, u32[]{:S(2)}, u32[]{:S(2)}) async-start(bf16[4,512,1024]{1,2,0:T(8,128)(2,1)} %bitcast.78), calls=%async_computation.3 | async-start | bytes 8388608 | tf_op jit(solution)/shard_map/all_to_all | solution.py:256
  154.8 6.5 %copy.94 = bf16[512,4096]{1,0:T(8,128)(2,1)} copy(bf16[512,4096]{0,1:T(8,128)(2,1)} %bitcast.81) | data formatting | bytes 8388608 | tf_op jit(solution)/shard_map/dot_general | solution.py:220
  163.4 0.9 copy.85.refs_3_
  164.2 1.3 stack.34.span_ref
  165.5 1.3 stack.35.span_ref
  167.4 1.8 copy-done.3
  169.3 1.2 fusion.42
  170.9 3.5 fusion.37
  174.5 1.4 subtract_convert_fusion
  176.3 0.8 pad_maximum_fusion.refs_0_
  177.2 7.7 %all-gather.9.cloned.1.call-done.refs_1_.refs_2_ = bf16[8192,256]{1,0:T(8,128)(2,1)} async-done(((bf16[256,256]{1,0:T(8,128)(2,1)}), bf16[8192,256]{1,0:T(8,128)(2,1)}) %all-gather.9.cloned.1.call-update) | async-done | bytes 4194320 | tf_op jit(solution)/shard_map/all_gather | solution.py:232
  184.9 9.4 %shard_map.82 = (f32[4,512,1]{2,1,0:T(8,128)}, f32[4,512,1]{2,1,0:T(8,128)}, f32[4,512,128]{2,1,0:T(8,128)}) custom-call(s32[6]{0:T(128)} %stack.35.span_ref, bf16[512,512]{1,0:T(8,128)(2,1)} %pad_maximum_fusion.refs_0_, bf16[8192,256]{1,0:T(8,128)(2,1)} %all-gather.9.cloned.1.call-done.refs_1_.refs_2_, ...), custom_call_target="tpu_custom_call" | custom-call | flops 4831838208 | bytes 3407872 | tf_op jit(solution)/shard_map/pallas_call | solution.py:155
  194.3 38.6 %all-gather.7.cloned.1.call-done.refs_1_.refs_2_ = bf16[8192,256]{1,0:T(8,128)(2,1)} async-done(((bf16[256,256]{1,0:T(8,128)(2,1)}), bf16[8192,256]{1,0:T(8,128)(2,1)}) %all-gather.7.cloned.1.call-update) | async-done | bytes 4194320 | tf_op jit(solution)/shard_map/all_gather | solution.py:234
  232.9 10.4 %shard_map.83 = bf16[512,512]{1,0:T(8,128)(2,1)} custom-call(s32[6]{0:T(128)} %stack.34.span_ref, bf16[512,512]{1,0:T(8,128)(2,1)} %pad_maximum_fusion.refs_0_, bf16[8192,256]{1,0:T(8,128)(2,1)} %all-gather.7.cloned.1.call-done.refs_1_.refs_2_, bf16[8192,256]{1,0:T(8,128)(2,1)} %all-gather.7.cloned.1.call-done.refs_1_.refs_2_, s32[512,1]{1,0:T(8,128)} %copy.85.refs_3_, ...), custom_call_target="tpu_custom_call" | custom-call | flops 4831838208 | bytes 3407872 | tf_op jit(solution)/shard_map/pallas_call | solution.py:155
  243.3 6.4 %copy.87 = bf16[4,512,1024]{2,1,0:T(8,128)(2,1)} copy(bf16[4,512,1024]{1,2,0:T(8,128)(2,1)} %all-to-all-done.3) | data formatting | bytes 8388608 | tf_op jit(solution)/shard_map/all_to_all | solution.py:256
  249.7 63.8 %all-gather.11.cloned.1.call-done = bf16[512,2048]{1,0:T(8,128)(2,1)} async-done(((bf16[512,512]{1,0:T(8,128)(2,1)}), bf16[512,2048]{1,0:T(8,128)(2,1)}) %all-gather.11.cloned.1.call-update) | async-done | bytes 2097168 | tf_op jit(solution)/shard_map/all_gather | solution.py:254
  313.5 5.2 %add_convert_fusion = bf16[512,1024]{1,0:T(8,128)(2,1)S(1)} fusion(bf16[512,1024]{1,0:T(8,128)(2,1)S(1)} %copy-done.5, bf16[512,2048]{1,0:T(8,128)(2,1)} %all-gather.11.cloned.1.call-done, bf16[2048,1024]{1,0:T(8,128)(2,1)} %bitcast.83), kind=kOutput, calls=%fused_computation.13 | convolution fusion | flops 2149056512 | bytes 8388608 | tf_op jit(solution)/shard_map/dot_general | solution.py:257
  318.6 5.4 %gather_fusion = bf16[1024,1024]{1,0:T(8,128)(2,1)} fusion(bf16[512,1024]{1,0:T(8,128)(2,1)S(1)} %add_convert_fusion, s32[1024]{0:T(1024)S(1)} %broadcast_clamp_fusion), kind=kCustom, calls=%fused_computation | custom fusion | bytes 4198400 | tf_op jit(solution)/shard_map/gather | solution.py:261
  324.0 7.8 %all-to-all-start.4 = ((bf16[32,32,1024]{2,1,0:T(8,128)(2,1)}), bf16[32,32,1024]{2,1,0:T(8,128)(2,1)S(1)}, u32[]{:S(2)}, u32[]{:S(2)}) async-start(bf16[32,32,1024]{2,1,0:T(8,128)(2,1)} %bitcast.80), calls=%async_computation.4 | async-start | bytes 4194304 | tf_op jit(solution)/shard_map/all_to_all | solution.py:262
  331.9 28.3 %all-to-all-done.4 = bf16[32,32,1024]{2,1,0:T(8,128)(2,1)S(1)} async-done(((bf16[32,32,1024]{2,1,0:T(8,128)(2,1)}), bf16[32,32,1024]{2,1,0:T(8,128)(2,1)S(1)}, u32[]{:S(2)}, u32[]{:S(2)}) %all-to-all-start.4) | async-done | bytes 2097184 | tf_op jit(solution)/shard_map/all_to_all | solution.py:262
  360.2 2.8 gather_fusion.1
  (86 shorter events, 13.6 us)
Async XLA Ops:
  6.5 126.7 %copy-start = (bf16[4096,128]{1,0:T(8,128)(2,1)S(1)}, bf16[4096,128]{1,0:T(8,128)(2,1)}, u32[]{:S(2)}) copy-start(bf16[4096,128]{1,0:T(8,128)(2,1)} %param.13) | copy-start | bytes 3145732
  11.2 21.6 %copy-start.17 = (s32[512]{0:T(512)}, s32[512]{0:T(512)S(1)}, u32[]{:S(2)}) copy-start(s32[512]{0:T(512)S(1)} %compare_select_fusion.2) | copy-start | bytes 6148
  16.4 16.5 %all-to-all-start = ((s32[32,1,34]{2,1,0:T(1,128)}), s32[32,1,34]{2,1,0:T(1,128)S(1)}, u32[]{:S(2)}, u32[]{:S(2)}) async-start(s32[32,1,34]{2,1,0:T(1,128)} %bitcast.5), calls=%async_computation | async-start | bytes 32768 | tf_op jit(solution)/shard_map/all_to_all | solution.py:194
  32.8 33.6 %all-to-all-start.1 = ((bf16[32,32,1024]{2,1,0:T(8,128)(2,1)}), bf16[32,32,1024]{2,1,0:T(8,128)(2,1)S(1)}, u32[]{:S(2)}, u32[]{:S(2)}) async-start(bf16[32,32,1024]{2,1,0:T(8,128)(2,1)} %bitcast.8), calls=%async_computation.1 | async-start | bytes 4194304 | tf_op jit(solution)/shard_map/all_to_all | solution.py:191
  66.5 1.3 copy-start.8
  74.0 2.6 copy-start.4
  76.5 7.9 %copy-start.12 = (s32[512]{0:T(512)S(1)}, s32[512]{0:T(512)}, u32[]{:S(2)}) copy-start(s32[512]{0:T(512)} %param.10) | copy-start | bytes 6148
  76.5 41.0 %all-to-all-start.2 = ((bf16[4,256,1024]{2,1,0:T(8,128)(2,1)}), bf16[4,256,1024]{2,1,0:T(8,128)(2,1)}, u32[]{:S(2)}, u32[]{:S(2)}) async-start(bf16[4,256,1024]{2,1,0:T(8,128)(2,1)} %broadcast_in_dim.26), calls=%async_computation.2 | async-start | bytes 4194304 | tf_op jit(solution)/shard_map/all_to_all | solution.py:212
  81.1 52.8 %all-gather.5.cloned.1.call-start = ((), (), s32[]{:S(2)}) async-start(), calls=%async_computation.5 | async-start | bytes 2621440 | tf_op jit(solution)/shard_map/all_gather | solution.py:210
  81.9 103.0 %all-gather.9.cloned.1.call-start = ((), (), s32[]{:S(2)}) async-start(), calls=%async_computation.7 | async-start | bytes 4325376 | tf_op jit(solution)/shard_map/all_gather | solution.py:232
  128.3 0.7 copy-start.11
  129.1 2.8 copy-start.14
  131.8 1.3 copy-start.2
  133.9 2.3 copy-start.6
  136.2 2.1 copy-start.19
  136.2 2.1 copy-start.9
  138.3 1.7 copy-start.10
  139.9 92.9 %all-gather.7.cloned.1.call-start = ((), (), s32[]{:S(2)}) async-start(), calls=%async_computation.6 | async-start | bytes 4325376 | tf_op jit(solution)/shard_map/all_gather | solution.py:234
  149.6 93.7 %all-to-all-start.3 = ((bf16[4,512,1024]{1,2,0:T(8,128)(2,1)}), bf16[4,512,1024]{1,2,0:T(8,128)(2,1)}, u32[]{:S(2)}, u32[]{:S(2)}) async-start(bf16[4,512,1024]{1,2,0:T(8,128)(2,1)} %bitcast.78), calls=%async_computation.3 | async-start | bytes 8388608 | tf_op jit(solution)/shard_map/all_to_all | solution.py:256
  154.5 159.0 %all-gather.11.cloned.1.call-start = ((), (), s32[]{:S(2)}) async-start(), calls=%async_computation.8 | async-start | bytes 2621440 | tf_op jit(solution)/shard_map/all_gather | solution.py:254
  154.7 8.6 %copy-start.16 = (s32[512]{0:T(512)S(1)}, s32[512]{0:T(512)}, u32[]{:S(2)}) copy-start(s32[512]{0:T(512)} %get-tuple-element.12) | copy-start | bytes 6148
  154.8 12.0 %copy-start.15 = (f32[256]{0:T(256)S(1)}, f32[256]{0:T(256)}, u32[]{:S(2)}) copy-start(f32[256]{0:T(256)} %copy-done.14) | copy-start | bytes 3076
  166.7 2.5 copy-start.3
  169.3 1.6 copy-start.7
  232.9 10.4 %copy-start.13 = (s32[1024,1]{0,1:T(1,128)S(1)}, s32[1024,1]{0,1:T(1,128)}, u32[]{:S(2)}) copy-start(s32[1024,1]{0,1:T(1,128)} %get-tuple-element.23) | copy-start | bytes 12292
  243.3 70.2 %copy-start.5 = (bf16[512,1024]{1,0:T(8,128)(2,1)S(1)}, bf16[512,1024]{1,0:T(8,128)(2,1)}, u32[]{:S(2)}) copy-start(bf16[512,1024]{1,0:T(8,128)(2,1)} %copy-done.4) | copy-start | bytes 3145732
  324.0 7.8 %copy-start.18 = (s32[512]{0:T(512)S(1)}, s32[512]{0:T(512)}, u32[]{:S(2)}) copy-start(s32[512]{0:T(512)} %copy-done.17) | copy-start | bytes 6148
  324.0 36.1 %all-to-all-start.4 = ((bf16[32,32,1024]{2,1,0:T(8,128)(2,1)}), bf16[32,32,1024]{2,1,0:T(8,128)(2,1)S(1)}, u32[]{:S(2)}, u32[]{:S(2)}) async-start(bf16[32,32,1024]{2,1,0:T(8,128)(2,1)} %bitcast.80), calls=%async_computation.4 | async-start | bytes 4194304 | tf_op jit(solution)/shard_map/all_to_all | solution.py:262
  360.2 2.8 copy-start.1
Sparse Core Ops, SparseCore 0:
  83.6 41.1 all-gather.4
  140.1 44.7 all-gather.8
  187.1 45.6 all-gather.6
  243.4 70.0 all-gather.10

commit v7 on v4

--- a/solution.py
+++ b/solution.py
@@ -73,22 +73,20 @@
         keys = k_ref[...]
         values = v_ref[...]
         if masked:
-            key_rows = key_first + lax.broadcasted_iota(jnp.int32, (1, block), 1)
+            key_rows = key_first + lax.broadcasted_iota(jnp.int32, (block, 1), 0)
             allowed = (key_rows >= start_ref[...]) & (key_rows <= row_ref[...])
         for h in range(heads):
-            scores = lax.dot_general(
-                q_ref[:, h * HD:(h + 1) * HD], keys, (((1,), (1,)), ((), ())),
-                preferred_element_type=jnp.float32,
-            ) * scale
+            scores = jnp.dot(keys, q_ref[h], preferred_element_type=jnp.float32) * scale
             if masked:
                 scores = jnp.where(allowed, scores, -jnp.inf)
             m_old = m_sc[h]
-            m_new = jnp.maximum(m_old, jnp.max(scores, axis=-1, keepdims=True))
+            m_new = jnp.maximum(m_old, jnp.max(scores, axis=0, keepdims=True))
             rescale = jnp.exp(m_old - m_new)
             exp_scores = jnp.exp(scores - m_new)
-            l_sc[h] = l_sc[h] * rescale + jnp.sum(exp_scores, axis=-1, keepdims=True)
-            acc_sc[h] = acc_sc[h] * rescale + jnp.dot(
-                exp_scores.astype(jnp.bfloat16), values, preferred_element_type=jnp.float32
+            l_sc[h] = l_sc[h] * rescale + jnp.sum(exp_scores, axis=0, keepdims=True)
+            acc_sc[h] = acc_sc[h] * rescale + lax.dot_general(
+                values, exp_scores.astype(jnp.bfloat16), (((0,), (0,)), ((), ())),
+                preferred_element_type=jnp.float32,
             )
             m_sc[h] = m_new
 
@@ -104,13 +102,11 @@
         @pl.when(step == pl.num_programs(0) - 1)
         def _finish():
             for h in range(heads):
-                o_ref[:, h * HD:(h + 1) * HD] = (acc_sc[h] / l_sc[h]).astype(o_ref.dtype)
-
-
-def flash_pass(span, queries, kv_part, row_start, row_index, max_blocks, state):
-    rows, width = queries.shape
-    heads = width // HD
-    block = row_start.shape[0] // 2
+                o_ref[h] = (acc_sc[h] / l_sc[h]).astype(o_ref.dtype)
+
+
+def flash_pass(span, queries_t, kv_part, row_start, row_index, block, max_blocks, state):
+    heads, _, rows = queries_t.shape
     final = state is not None
 
     def kv_map(column):
@@ -121,29 +117,29 @@
     fixed2 = lambda step, span_ref: (0, 0)
     fixed3 = lambda step, span_ref: (0, 0, 0)
     in_specs = [
-        pl.BlockSpec((rows, width), fixed2),
+        pl.BlockSpec((heads, HD, rows), fixed3),
         pl.BlockSpec((block, HD), kv_map(0)),
         pl.BlockSpec((block, HD), kv_map(1)),
-        pl.BlockSpec((rows, 1), fixed2),
-        pl.BlockSpec((rows, 1), fixed2),
+        pl.BlockSpec((1, rows), fixed2),
+        pl.BlockSpec((1, rows), fixed2),
     ]
     state_shapes = [
-        jax.ShapeDtypeStruct((heads, rows, 1), jnp.float32),
-        jax.ShapeDtypeStruct((heads, rows, 1), jnp.float32),
-        jax.ShapeDtypeStruct((heads, rows, HD), jnp.float32),
+        jax.ShapeDtypeStruct((heads, 1, rows), jnp.float32),
+        jax.ShapeDtypeStruct((heads, 1, rows), jnp.float32),
+        jax.ShapeDtypeStruct((heads, HD, rows), jnp.float32),
     ]
     state_specs = [pl.BlockSpec(x.shape, fixed3) for x in state_shapes]
     if final:
         in_specs = in_specs + state_specs
-        out_specs = pl.BlockSpec((rows, width), fixed2)
-        out_shape = jax.ShapeDtypeStruct((rows, width), jnp.bfloat16)
+        out_specs = pl.BlockSpec((heads, HD, rows), fixed3)
+        out_shape = jax.ShapeDtypeStruct((heads, HD, rows), jnp.bfloat16)
         scratch = [pltpu.VMEM(x.shape, jnp.float32) for x in state_shapes]
-        operands = (span, queries, kv_part, kv_part, row_start, row_index) + tuple(state)
+        operands = (span, queries_t, kv_part, kv_part, row_start, row_index) + tuple(state)
     else:
         out_specs = state_specs
         out_shape = state_shapes
         scratch = []
-        operands = (span, queries, kv_part, kv_part, row_start, row_index)
+        operands = (span, queries_t, kv_part, kv_part, row_start, row_index)
     grid_spec = pltpu.PrefetchScalarGridSpec(
         num_scalar_prefetch=1,
         grid=(max_blocks,),
@@ -160,7 +156,7 @@
         cost_estimate=pl.CostEstimate(
             flops=flops,
             transcendentals=heads * rows * block * max_blocks,
-            bytes_accessed=2 * block * HD * 2 * max_blocks + 2 * 2 * rows * width,
+            bytes_accessed=2 * block * HD * 2 * max_blocks + 2 * 2 * rows * heads * HD,
         ),
     )(*operands)
 
@@ -235,12 +231,15 @@
             [first_block, last_block - first_block + 1, max_start, block_first, block, offset]
         ).astype(jnp.int32)
 
+    queries_t = jnp.transpose(queries.reshape(tok_dev, heads_dev, HD), (1, 2, 0))
     state = flash_pass(
-        span_for(0), queries, kv_low, row_start[:, None], row_index[:, None], max_blocks, None
-    )
-    context = flash_pass(
-        span_for(half), queries, kv_high, row_start[:, None], row_index[:, None], max_blocks, state
-    )
+        span_for(0), queries_t, kv_low, row_start[None, :], row_index[None, :], half, max_blocks, None
+    )
+    context_t = flash_pass(
+        span_for(half), queries_t, kv_high, row_start[None, :], row_index[None, :], half, max_blocks,
+        state,
+    )
+    context = jnp.transpose(context_t, (2, 0, 1)).reshape(tok_dev, heads_dev * HD)
     context_all = lax.all_gather(context, "mp", axis=1, tiled=True)
     mp_size = lax.axis_size("mp")
     w_split = jnp.transpose(w_out.reshape(w_out.shape[0], mp_size, -1), (1, 0, 2))

time: 359 us -> 340 us (0.947)
  waiting for transfers between devices: 219 us -> 213 us
  Pallas kernels: 20 us -> 14.5 us
  local copies, waits for them, and re-layouts: 45 us -> 40.8 us
    all_gather x1, waiting for transfers between devices: 62.1 us -> 47.1 us  [local(): context_all = lax.all_gather(context, 'mp', axis=1, tiled=True)]
    all_gather x1, waiting for transfers between devices: 13.7 us -> 20.1 us  [local(): kv_low = lax.all_gather(kv_own[:half], ('chip', 'core'), axis=0, tiled=True)]
    pallas_call x2, Pallas kernels: 20 us -> 14.5 us  [flash_pass(): pl.pallas_call(functools.partial(flash_kernel, final), grid_spec=grid_spe...]
    unnamed x16 -> x13, local copies, waits for them, and re-layouts: 9.45 us -> 6.77 us
  transfers between devices with their start and end apart: 8 -> 8, of which waited for: 7 -> 7; matrix products, arithmetic and copies ran while one was open for 11% -> 10% of each run, Pallas kernels for 6% -> 4%
where the time goes in v7:
time: 340 us; the launch traced here: 339 us
  waiting for transfers between devices  213 us (63%)
  local copies, waits for them, and re-layouts  40.8 us (12%)
  starting transfers between devices  28 us (8%)
  other arithmetic  14.6 us (4%)
  between operations  14.6 us (4%)
  Pallas kernels  14.5 us (4%)
  matrix products  13.7 us (4%)
    all_gather x1, waiting for transfers between devices, local(): context_all = lax.all_gather(context, 'mp', axis=1, tiled=True)  47.1 us
    all_gather x1, waiting for transfers between devices, local(): routed = lax.all_gather(routed_part, 'mp', axis=1, tiled=True)  45.5 us
    all_gather x1, waiting for transfers between devices, local(): lax.all_gather(kv_own[half:], ('chip', 'core'), axis=0, tiled=True)  40.9 us
    all_to_all x1, waiting for transfers between devices, local(): lax.all_to_all(backward, ('chip', 'core'), split_axis=0, concat_axis=0, t...  28.3 us
    all_to_all x1, waiting for transfers between devices, local(): lax.all_to_all(outgoing.reshape(owners, capacity, columns), ('chip', 'cor...  28.1 us
    all_gather x1, waiting for transfers between devices, local(): kv_low = lax.all_gather(kv_own[:half], ('chip', 'core'), axis=0, tiled=True)  20.1 us
    pallas_call x2, Pallas kernels, flash_pass(): pl.pallas_call(functools.partial(flash_kernel, final), grid_spec=grid_spe...  14.5 us
    all_to_all x1, starting transfers between devices, local(): lax.all_to_all(places_info, ('chip', 'core'), split_axis=0, concat_axis=0...  9.6 us
  transfers between devices with their start and end apart: 8, of which 7 were waited for; matrix products, arithmetic and copies ran while one was open for 10% of the time, Pallas kernels for 4%

profile of v7, /device:TPU:1, one launch (start us, length us, event | category | flops | bytes accessed | tf_op | source)
XLA Modules:
  0.0 339.0 jit_solution(17698858269238778612)
XLA Ops:
  6.5 1.0 convert_reduce_fusion
  7.6 1.4 fusion.31
  9.0 0.7 add_select_fusion
  9.7 1.2 reduce-window.6
  10.9 0.2 slice_reduce_fusion
  11.2 2.4 scatter_custom_fusion
  13.8 0.6 slice.45
  15.0 0.8 pad_add_fusion.1
  15.8 0.6 pad_add_fusion
  16.5 9.6 %all-to-all-start = ((s32[32,1,34]{2,1,0:T(1,128)}), s32[32,1,34]{2,1,0:T(1,128)S(1)}, u32[]{:S(2)}, u32[]{:S(2)}) async-start(s32[32,1,34]{2,1,0:T(1,128)} %bitcast.5), calls=%async_computation | async-start | bytes 32768 | tf_op jit(solution)/shard_map/all_to_all | solution.py:190
  26.1 4.8 %scatter_custom_fusion.1 = bf16[1024,1024]{1,0:T(8,128)(2,1)} fusion(s32[512]{0:T(512)S(1)} %compare_select_fusion.2, bf16[512,1024]{1,0:T(8,128)(2,1)} %param.8, bf16[]{:T(256)} %constant.79.clone.1), kind=kCustom, calls=%fused_computation.13 | custom fusion | bytes 2097664 | tf_op jit(solution)/shard_map/scatter | solution.py:175
  30.9 2.0 all-to-all-done
  32.9 5.3 %all-to-all-start.1 = ((bf16[32,32,1024]{2,1,0:T(8,128)(2,1)}), bf16[32,32,1024]{2,1,0:T(8,128)(2,1)S(1)}, u32[]{:S(2)}, u32[]{:S(2)}) async-start(bf16[32,32,1024]{2,1,0:T(8,128)(2,1)} %bitcast.8), calls=%async_computation.1 | async-start | bytes 4194304 | tf_op jit(solution)/shard_map/all_to_all | solution.py:187
  38.5 28.1 %all-to-all-done.1 = bf16[32,32,1024]{2,1,0:T(8,128)(2,1)S(1)} async-done(((bf16[32,32,1024]{2,1,0:T(8,128)(2,1)}), bf16[32,32,1024]{2,1,0:T(8,128)(2,1)S(1)}, u32[]{:S(2)}, u32[]{:S(2)}) %all-to-all-start.1) | async-done | bytes 2097184 | tf_op jit(solution)/shard_map/all_to_all | solution.py:187
  66.6 6.2 %scatter_custom_fusion.2 = bf16[512,1024]{1,0:T(8,128)(2,1)} fusion(s32[1024]{0:T(1024)S(1)} %bitcast.68, bf16[1024,1024]{1,0:T(8,128)(2,1)S(1)} %bitcast.60, bf16[]{:T(256)} %constant.79.clone.1), kind=kCustom, calls=%fused_computation.19 | custom fusion | bytes 1048578 | tf_op jit(solution)/shard_map/scatter | solution.py:202
  72.8 0.2 all-gather.9.cloned.1.call-start
  73.1 45.5 %all-gather.5.cloned.1.call-done = bf16[512,4096]{1,0:T(8,128)(2,1)} async-done(((bf16[512,1024]{1,0:T(8,128)(2,1)}), bf16[512,4096]{1,0:T(8,128)(2,1)}) %all-gather.5.cloned.1.call-update) | async-done | bytes 4194320 | tf_op jit(solution)/shard_map/all_gather | solution.py:204
  118.6 3.2 fusion
  121.9 0.2 copy-done.1
  122.1 1.3 convolution_bitcast_fusion
  123.4 1.2 fusion.16
  124.6 1.3 convolution_convert_fusion
  126.1 0.7 fusion.30
  126.9 0.7 all-gather.7.cloned.1.call-update
  127.6 6.6 %copy.29 = bf16[512,4096]{0,1:T(8,128)(2,1)} copy(bf16[512,4096]{1,0:T(8,128)(2,1)} %param.15) | data formatting | bytes 8388608 | tf_op args[7]
  134.1 5.0 %all-to-all-start.2 = ((bf16[4,512,1024]{1,2,0:T(8,128)(2,1)}), bf16[4,512,1024]{1,2,0:T(8,128)(2,1)}, u32[]{:S(2)}, u32[]{:S(2)}) async-start(bf16[4,512,1024]{1,2,0:T(8,128)(2,1)} %bitcast.57), calls=%async_computation.2 | async-start | bytes 8388608 | tf_op jit(solution)/shard_map/all_to_all | solution.py:246
  139.2 0.6 iota_add_fusion.refs_4_
  139.8 0.5 multiply_cosine_fusion.1
  140.3 0.2 slice_reduce_fusion.1
  140.5 0.8 fusion.20
  141.3 0.6 fusion.24
  142.6 1.9 fusion.29
  144.5 1.3 stack.35.span_ref
  145.8 1.3 stack.34.span_ref
  147.1 5.9 %fusion.27 = f32[512,512]{0,1:T(8,128)S(1)} fusion(bf16[4096,512]{1,0:T(8,128)(2,1)} %param.12, bf16[512,4096]{1,0:T(8,128)(2,1)} %all-gather.5.cloned.1.call-done, f32[4096]{0:T(1024)S(1)} %copy-done.5, f32[512]{0:T(512)S(1)} %add_rsqrt_fusion), kind=kOutput, calls=%fused_computation.71 | convolution fusion | flops 2155872256 | bytes 9455616 | tf_op jit(solution)/shard_map/dot_general | solution.py:209
  153.1 0.2 subtract_convert_fusion
  153.3 0.9 maximum_bitcast_fusion.refs_0_
  154.1 20.1 %all-gather.9.cloned.1.call-done.refs_1_.refs_2_ = bf16[8192,256]{1,0:T(8,128)(2,1)} async-done(((bf16[256,256]{1,0:T(8,128)(2,1)}), bf16[8192,256]{1,0:T(8,128)(2,1)}) %all-gather.9.cloned.1.call-update) | async-done | bytes 4194320 | tf_op jit(solution)/shard_map/all_gather | solution.py:220
  174.2 7.1 %shard_map.82 = (f32[4,1,512]{2,1,0:T(1,128)}, f32[4,1,512]{2,1,0:T(1,128)}, f32[4,128,512]{2,1,0:T(8,128)}) custom-call(s32[6]{0:T(128)} %stack.35.span_ref, bf16[4,128,512]{2,1,0:T(8,128)(2,1)} %maximum_bitcast_fusion.refs_0_, bf16[8192,256]{1,0:T(8,128)(2,1)} %all-gather.9.cloned.1.call-done.refs_1_.refs_2_, ...), custom_call_target="tpu_custom_call" | custom-call | flops 4831838208 | bytes 3407872 | tf_op jit(solution)/shard_map/pallas_call | solution.py:151
  181.3 40.9 %all-gather.7.cloned.1.call-done.refs_1_.refs_2_ = bf16[8192,256]{1,0:T(8,128)(2,1)} async-done(((bf16[256,256]{1,0:T(8,128)(2,1)}), bf16[8192,256]{1,0:T(8,128)(2,1)}) %all-gather.7.cloned.1.call-update) | async-done | bytes 4194320 | tf_op jit(solution)/shard_map/all_gather | solution.py:221
  222.2 7.4 %shard_map.83 = bf16[4,128,512]{2,1,0:T(8,128)(2,1)} custom-call(s32[6]{0:T(128)} %stack.34.span_ref, bf16[4,128,512]{2,1,0:T(8,128)(2,1)} %maximum_bitcast_fusion.refs_0_, bf16[8192,256]{1,0:T(8,128)(2,1)} %all-gather.7.cloned.1.call-done.refs_1_.refs_2_, bf16[8192,256]{1,0:T(8,128)(2,1)} %all-gather.7.cloned.1.call-done.refs_1_.refs_2_, ...), custom_call_target="tpu_custom_call" | custom-call | flops 4831838208 | bytes 3407872 | tf_op jit(solution)/shard_map/pallas_call | solution.py:151
  229.7 6.4 %copy.30 = bf16[4,512,1024]{2,1,0:T(8,128)(2,1)} copy(bf16[4,512,1024]{1,2,0:T(8,128)(2,1)} %all-to-all-done.2) | data formatting | bytes 8388608 | tf_op jit(solution)/shard_map/all_to_all | solution.py:246
  236.1 47.1 %all-gather.11.cloned.1.call-done = bf16[512,2048]{0,1:T(8,128)(2,1)} async-done(((bf16[512,512]{0,1:T(8,128)(2,1)}), bf16[512,2048]{0,1:T(8,128)(2,1)}) %all-gather.11.cloned.1.call-update) | async-done | bytes 2097168 | tf_op jit(solution)/shard_map/all_gather | solution.py:243
  283.2 5.2 %add_convert_fusion = bf16[512,1024]{1,0:T(8,128)(2,1)S(1)} fusion(bf16[512,1024]{1,0:T(8,128)(2,1)S(1)} %copy-done.2, bf16[512,2048]{0,1:T(8,128)(2,1)} %all-gather.11.cloned.1.call-done, bf16[2048,1024]{1,0:T(8,128)(2,1)} %bitcast.59), kind=kOutput, calls=%fused_computation.10 | convolution fusion | flops 2149056512 | bytes 8388608 | tf_op jit(solution)/shard_map/dot_general | solution.py:247
  288.4 5.4 %gather_fusion = bf16[1024,1024]{1,0:T(8,128)(2,1)} fusion(bf16[512,1024]{1,0:T(8,128)(2,1)S(1)} %add_convert_fusion, s32[1024]{0:T(1024)S(1)} %broadcast_clamp_fusion), kind=kCustom, calls=%fused_computation | custom fusion | bytes 4198400 | tf_op jit(solution)/shard_map/gather | solution.py:251
  293.7 7.7 %all-to-all-start.3 = ((bf16[32,32,1024]{2,1,0:T(8,128)(2,1)}), bf16[32,32,1024]{2,1,0:T(8,128)(2,1)S(1)}, u32[]{:S(2)}, u32[]{:S(2)}) async-start(bf16[32,32,1024]{2,1,0:T(8,128)(2,1)} %bitcast.58), calls=%async_computation.3 | async-start | bytes 4194304 | tf_op jit(solution)/shard_map/all_to_all | solution.py:252
  301.4 28.3 %all-to-all-done.3 = bf16[32,32,1024]{2,1,0:T(8,128)(2,1)S(1)} async-done(((bf16[32,32,1024]{2,1,0:T(8,128)(2,1)}), bf16[32,32,1024]{2,1,0:T(8,128)(2,1)S(1)}, u32[]{:S(2)}, u32[]{:S(2)}) %all-to-all-start.3) | async-done | bytes 2097184 | tf_op jit(solution)/shard_map/all_to_all | solution.py:252
  329.7 2.8 gather_fusion.1
  (33 shorter events, 0.8 us)
Async XLA Ops:
  6.5 115.3 %copy-start = (bf16[4096,128]{1,0:T(8,128)(2,1)S(1)}, bf16[4096,128]{1,0:T(8,128)(2,1)}, u32[]{:S(2)}) copy-start(bf16[4096,128]{1,0:T(8,128)(2,1)} %param.13) | copy-start | bytes 3145732
  16.5 16.5 %all-to-all-start = ((s32[32,1,34]{2,1,0:T(1,128)}), s32[32,1,34]{2,1,0:T(1,128)S(1)}, u32[]{:S(2)}, u32[]{:S(2)}) async-start(s32[32,1,34]{2,1,0:T(1,128)} %bitcast.5), calls=%async_computation | async-start | bytes 32768 | tf_op jit(solution)/shard_map/all_to_all | solution.py:190
  32.9 33.6 %all-to-all-start.1 = ((bf16[32,32,1024]{2,1,0:T(8,128)(2,1)}), bf16[32,32,1024]{2,1,0:T(8,128)(2,1)S(1)}, u32[]{:S(2)}, u32[]{:S(2)}) async-start(bf16[32,32,1024]{2,1,0:T(8,128)(2,1)} %bitcast.8), calls=%async_computation.1 | async-start | bytes 4194304 | tf_op jit(solution)/shard_map/all_to_all | solution.py:187
  38.3 83.6 %copy-start.5 = (f32[4096]{0:T(1024)S(1)}, f32[4096]{0:T(1024)}, u32[]{:S(2)}) copy-start(f32[4096]{0:T(1024)} %param.11) | copy-start | bytes 49156
  38.3 80.3 %all-gather.5.cloned.1.call-start = ((), (), s32[]{:S(2)}) async-start(), calls=%async_computation.4 | async-start | bytes 5242880 | tf_op jit(solution)/shard_map/all_gather | solution.py:204
  72.8 101.4 %all-gather.9.cloned.1.call-start = ((), (), s32[]{:S(2)}) async-start(), calls=%async_computation.6 | async-start | bytes 4325376 | tf_op jit(solution)/shard_map/all_gather | solution.py:220
  118.6 3.4 %copy-start.1 = (bf16[512,4096]{1,0:T(8,128)(2,1)S(1)}, bf16[512,4096]{1,0:T(8,128)(2,1)}, u32[]{:S(2)}) copy-start(bf16[512,4096]{1,0:T(8,128)(2,1)} %all-gather.5.cloned.1.call-done) | copy-start | bytes 12582916
  122.1 2.5 copy-start.4
  126.8 95.4 %all-gather.7.cloned.1.call-start = ((), (), s32[]{:S(2)}) async-start(), calls=%async_computation.5 | async-start | bytes 4325376 | tf_op jit(solution)/shard_map/all_gather | solution.py:221
  134.1 8.5 %copy-start.3 = (s32[512]{0:T(512)S(1)}, s32[512]{0:T(512)}, u32[]{:S(2)}) copy-start(s32[512]{0:T(512)} %param.10) | copy-start | bytes 6148
  134.1 95.6 %all-to-all-start.2 = ((bf16[4,512,1024]{1,2,0:T(8,128)(2,1)}), bf16[4,512,1024]{1,2,0:T(8,128)(2,1)}, u32[]{:S(2)}, u32[]{:S(2)}) async-start(bf16[4,512,1024]{1,2,0:T(8,128)(2,1)} %bitcast.57), calls=%async_computation.2 | async-start | bytes 8388608 | tf_op jit(solution)/shard_map/all_to_all | solution.py:246
  139.1 144.0 %all-gather.11.cloned.1.call-start = ((), (), s32[]{:S(2)}) async-start(), calls=%async_computation.7 | async-start | bytes 2621440 | tf_op jit(solution)/shard_map/all_gather | solution.py:243
  229.7 53.5 %copy-start.2 = (bf16[512,1024]{1,0:T(8,128)(2,1)S(1)}, bf16[512,1024]{1,0:T(8,128)(2,1)}, u32[]{:S(2)}) copy-start(bf16[512,1024]{1,0:T(8,128)(2,1)} %scatter_custom_fusion.2) | copy-start | bytes 3145732
  293.7 36.0 %all-to-all-start.3 = ((bf16[32,32,1024]{2,1,0:T(8,128)(2,1)}), bf16[32,32,1024]{2,1,0:T(8,128)(2,1)S(1)}, u32[]{:S(2)}, u32[]{:S(2)}) async-start(bf16[32,32,1024]{2,1,0:T(8,128)(2,1)} %bitcast.58), calls=%async_computation.3 | async-start | bytes 4194304 | tf_op jit(solution)/shard_map/all_to_all | solution.py:252
Sparse Core Ops, SparseCore 0:
  73.0 45.6 all-gather.4
  126.9 47.2 all-gather.8
  176.5 45.6 all-gather.6
  229.8 53.3 all-gather.10

commit v8 on v7

--- a/solution.py
+++ b/solution.py
@@ -218,7 +218,10 @@
     kv_own = jnp.concatenate([keys_own, values_own], axis=1)
     half = tok_dev // 2
     kv_low = lax.all_gather(kv_own[:half], ("chip", "core"), axis=0, tiled=True)
-    kv_high = lax.all_gather(kv_own[half:], ("chip", "core"), axis=0, tiled=True)
+    kv_copies = jnp.broadcast_to(kv_own[half:][None], (owners, half, kv_own.shape[1]))
+    kv_high = lax.all_to_all(
+        kv_copies, ("chip", "core"), split_axis=0, concat_axis=0, tiled=True
+    ).reshape(owners * half, kv_own.shape[1])
 
     block = KEY_BLOCK
     last_block = (block_first + tok_dev - 1) // block
@@ -244,8 +247,11 @@
     mp_size = lax.axis_size("mp")
     w_split = jnp.transpose(w_out.reshape(w_out.shape[0], mp_size, -1), (1, 0, 2))
     w_cols = lax.all_to_all(w_split, "mp", split_axis=0, concat_axis=0, tiled=True)
-    summed = jnp.dot(
-        context_all, w_cols.reshape(-1, w_cols.shape[2]), preferred_element_type=jnp.float32
+    summed = jnp.einsum(
+        "tsr,src->tc",
+        context_all.reshape(tok_dev, mp_size, -1),
+        w_cols,
+        preferred_element_type=jnp.float32,
     )
     attended = (routed_part.astype(jnp.float32) + summed).astype(jnp.bfloat16)
     backward = attended[jnp.minimum(arrived_rows, tok_dev - 1)].reshape(owners, capacity, columns)

time: 340 us -> 357 us (1.050)
  starting transfers between devices: 28 us -> 36.8 us
  waiting for transfers between devices: 213 us -> 220 us
    all_gather x1 -> x0, waiting for transfers between devices: 40.9 us -> none  [local(): lax.all_gather(kv_own[half:], ('chip', 'core'), axis=0, tiled=True)]
    all_to_all x1, waiting for transfers between devices: 0.01 us -> 40.4 us  [local(): lax.all_to_all(w_split, 'mp', split_axis=0, concat_axis=0, tiled=True)]
    all_gather x1, waiting for transfers between devices: 20.1 us -> 38 us  [local(): kv_low = lax.all_gather(kv_own[:half], ('chip', 'core'), axis=0, tiled=True)]
    all_gather x1, waiting for transfers between devices: 47.1 us -> 37.2 us  [local(): context_all = lax.all_gather(context, 'mp', axis=1, tiled=True)]
    all_to_all x0 -> x1, starting transfers between devices: none -> 7.8 us  [local(): lax.all_to_all(kv_copies, ('chip', 'core'), split_axis=0, concat_axis=0,...]
    all_to_all x1 -> x0, local copies, waits for them, and re-layouts: 6.41 us -> none  [local(): lax.all_to_all(w_split, 'mp', split_axis=0, concat_axis=0, tiled=True)]
    reshape x0 -> x1, local copies, waits for them, and re-layouts: none -> 6.32 us  [local(): w_out.reshape(w_out.shape[0], mp_size, -1)]
where the time goes in v8:
time: 357 us
  waiting for transfers between devices  220 us (62%)
  local copies, waits for them, and re-layouts  42.9 us (12%)
  starting transfers between devices  36.8 us (10%)
  Pallas kernels  14.7 us (4%)
  other arithmetic  14.6 us (4%)
  between operations  14.6 us (4%)
  matrix products  13.7 us (4%)
    all_gather x1, waiting for transfers between devices, local(): routed = lax.all_gather(routed_part, 'mp', axis=1, tiled=True)  45.5 us
    all_to_all x1, waiting for transfers between devices, local(): lax.all_to_all(w_split, 'mp', split_axis=0, concat_axis=0, tiled=True)  40.4 us
    all_gather x1, waiting for transfers between devices, local(): kv_low = lax.all_gather(kv_own[:half], ('chip', 'core'), axis=0, tiled=True)  38 us
    all_gather x1, waiting for transfers between devices, local(): context_all = lax.all_gather(context, 'mp', axis=1, tiled=True)  37.2 us
    all_to_all x1, waiting for transfers between devices, local(): lax.all_to_all(backward, ('chip', 'core'), split_axis=0, concat_axis=0, t...  28.3 us
    all_to_all x1, waiting for transfers between devices, local(): lax.all_to_all(outgoing.reshape(owners, capacity, columns), ('chip', 'cor...  28.1 us
    pallas_call x2, Pallas kernels, flash_pass(): pl.pallas_call(functools.partial(flash_kernel, final), grid_spec=grid_spe...  14.7 us
    all_to_all x1, starting transfers between devices, local(): lax.all_to_all(places_info, ('chip', 'core'), split_axis=0, concat_axis=0...  9.6 us
  transfers between devices with their start and end apart: 8, of which 7 were waited for; matrix products, arithmetic and copies ran while one was open for 10% of the time, Pallas kernels for 4%

profile of v8, /device:TPU:1, one launch (start us, length us, event | category | flops | bytes accessed | tf_op | source)
XLA Modules:
  0.0 357.0 jit_solution(10786399810266413293)
XLA Ops:
  6.5 1.0 convert_reduce_fusion
  7.6 1.4 fusion.32
  9.0 0.7 add_select_fusion
  9.7 1.2 reduce-window.6
  10.9 0.2 slice_reduce_fusion
  11.2 2.4 scatter_custom_fusion
  13.8 0.6 slice.45
  15.0 0.8 pad_add_fusion.1
  15.8 0.6 pad_add_fusion
  16.5 9.6 %all-to-all-start = ((s32[32,1,34]{2,1,0:T(1,128)}), s32[32,1,34]{2,1,0:T(1,128)S(1)}, u32[]{:S(2)}, u32[]{:S(2)}) async-start(s32[32,1,34]{2,1,0:T(1,128)} %bitcast.5), calls=%async_computation | async-start | bytes 32768 | tf_op jit(solution)/shard_map/all_to_all | solution.py:190
  26.1 4.8 %scatter_custom_fusion.1 = bf16[1024,1024]{1,0:T(8,128)(2,1)} fusion(s32[512]{0:T(512)S(1)} %compare_select_fusion.2, bf16[512,1024]{1,0:T(8,128)(2,1)} %param.8, bf16[]{:T(256)} %constant.79.clone.1), kind=kCustom, calls=%fused_computation.14 | custom fusion | bytes 2097664 | tf_op jit(solution)/shard_map/scatter | solution.py:175
  30.9 2.0 all-to-all-done
  32.9 5.3 %all-to-all-start.1 = ((bf16[32,32,1024]{2,1,0:T(8,128)(2,1)}), bf16[32,32,1024]{2,1,0:T(8,128)(2,1)S(1)}, u32[]{:S(2)}, u32[]{:S(2)}) async-start(bf16[32,32,1024]{2,1,0:T(8,128)(2,1)} %bitcast.8), calls=%async_computation.1 | async-start | bytes 4194304 | tf_op jit(solution)/shard_map/all_to_all | solution.py:187
  38.5 28.1 %all-to-all-done.1 = bf16[32,32,1024]{2,1,0:T(8,128)(2,1)S(1)} async-done(((bf16[32,32,1024]{2,1,0:T(8,128)(2,1)}), bf16[32,32,1024]{2,1,0:T(8,128)(2,1)S(1)}, u32[]{:S(2)}, u32[]{:S(2)}) %all-to-all-start.1) | async-done | bytes 2097184 | tf_op jit(solution)/shard_map/all_to_all | solution.py:187
  66.6 6.2 %scatter_custom_fusion.2 = bf16[512,1024]{1,0:T(8,128)(2,1)} fusion(s32[1024]{0:T(1024)S(1)} %bitcast.72, bf16[1024,1024]{1,0:T(8,128)(2,1)S(1)} %bitcast.64, bf16[]{:T(256)} %constant.79.clone.1), kind=kCustom, calls=%fused_computation.20 | custom fusion | bytes 1048578 | tf_op jit(solution)/shard_map/scatter | solution.py:202
  72.8 0.2 all-gather.6.cloned.1.call-start
  73.1 45.5 %all-gather.4.cloned.1.call-done = bf16[512,4096]{1,0:T(8,128)(2,1)} async-done(((bf16[512,1024]{1,0:T(8,128)(2,1)}), bf16[512,4096]{1,0:T(8,128)(2,1)}) %all-gather.4.cloned.1.call-update) | async-done | bytes 4194320 | tf_op jit(solution)/shard_map/all_gather | solution.py:204
  118.6 3.2 fusion
  121.9 0.2 copy-done.1
  122.1 1.3 convolution_bitcast_fusion
  123.4 1.2 fusion.17
  124.6 1.3 convolution_convert_fusion
  126.1 0.7 fusion.31
  126.8 2.4 broadcast_in_dim.26
  129.2 7.8 %all-to-all-start.2 = ((bf16[32,256,256]{2,1,0:T(8,128)(2,1)}), bf16[32,256,256]{2,1,0:T(8,128)(2,1)}, u32[]{:S(2)}, u32[]{:S(2)}) async-start(bf16[32,256,256]{2,1,0:T(8,128)(2,1)} %broadcast_in_dim.26), calls=%async_computation.2 | async-start | bytes 8388608 | tf_op jit(solution)/shard_map/all_to_all | solution.py:222
  137.0 6.5 %copy.34 = bf16[512,4096]{0,1:T(8,128)(2,1)} copy(bf16[512,4096]{1,0:T(8,128)(2,1)} %param.15) | data formatting | bytes 8388608 | tf_op args[7]
  143.5 6.3 %copy.35 = bf16[512,4,1024]{2,0,1:T(8,128)(2,1)} copy(bf16[512,4,1024]{0,2,1:T(8,128)(2,1)} %bitcast.62) | data formatting | bytes 8388608 | tf_op jit(solution)/shard_map/reshape | solution.py:248
  149.9 0.6 iota_add_fusion.refs_4_
  150.4 0.5 multiply_cosine_fusion.1
  151.2 0.9 fusion.21
  152.0 0.7 fusion.25
  153.3 1.9 fusion.30
  155.2 1.3 stack.35.span_ref
  156.5 1.2 stack.34.span_ref
  157.7 5.9 %fusion.28 = f32[512,512]{0,1:T(8,128)S(1)} fusion(bf16[4096,512]{1,0:T(8,128)(2,1)} %param.12, bf16[512,4096]{1,0:T(8,128)(2,1)} %all-gather.4.cloned.1.call-done, f32[4096]{0:T(1024)S(1)} %copy-done.5, f32[512]{0:T(512)S(1)} %add_rsqrt_fusion), kind=kOutput, calls=%fused_computation.72 | convolution fusion | flops 2155872256 | bytes 9455616 | tf_op jit(solution)/shard_map/dot_general | solution.py:209
  163.9 0.9 maximum_bitcast_fusion.refs_0_
  164.7 38.0 %all-gather.6.cloned.1.call-done.refs_1_.refs_2_ = bf16[8192,256]{1,0:T(8,128)(2,1)} async-done(((bf16[256,256]{1,0:T(8,128)(2,1)}), bf16[8192,256]{1,0:T(8,128)(2,1)}) %all-gather.6.cloned.1.call-update) | async-done | bytes 4194320 | tf_op jit(solution)/shard_map/all_gather | solution.py:220
  202.8 7.1 %shard_map.82 = (f32[4,1,512]{2,1,0:T(1,128)}, f32[4,1,512]{2,1,0:T(1,128)}, f32[4,128,512]{2,1,0:T(8,128)}) custom-call(s32[6]{0:T(128)} %stack.35.span_ref, bf16[4,128,512]{2,1,0:T(8,128)(2,1)} %maximum_bitcast_fusion.refs_0_, bf16[8192,256]{1,0:T(8,128)(2,1)} %all-gather.6.cloned.1.call-done.refs_1_.refs_2_, ...), custom_call_target="tpu_custom_call" | custom-call | flops 4831838208 | bytes 3407872 | tf_op jit(solution)/shard_map/pallas_call | solution.py:151
  209.9 4.9 %all-to-all-start.3 = ((bf16[4,512,1024]{2,1,0:T(8,128)(2,1)}), bf16[4,512,1024]{2,1,0:T(8,128)(2,1)}, u32[]{:S(2)}, u32[]{:S(2)}) async-start(bf16[4,512,1024]{2,1,0:T(8,128)(2,1)} %bitcast.61), calls=%async_computation.3 | async-start | bytes 8388608 | tf_op jit(solution)/shard_map/all_to_all | solution.py:249
  214.8 0.3 all-gather.8.cloned.1.call-start
  215.1 7.6 %shard_map.83 = bf16[4,128,512]{2,1,0:T(8,128)(2,1)} custom-call(s32[6]{0:T(128)} %stack.34.span_ref, bf16[4,128,512]{2,1,0:T(8,128)(2,1)} %maximum_bitcast_fusion.refs_0_, bf16[8192,256]{1,0:T(8,128)(2,1)} %bitcast.20.refs_1_.refs_2_, bf16[8192,256]{1,0:T(8,128)(2,1)} %bitcast.20.refs_1_.refs_2_, s32[1,512]{1,0:T(1,128)} %bitcast.74, ...), custom_call_target="tpu_custom_call" | custom-call | flops 4831838208 | bytes 3407872 | tf_op jit(solution)/shard_map/pallas_call | solution.py:151
  222.7 40.4 %all-to-all-done.3 = bf16[4,512,1024]{2,1,0:T(8,128)(2,1)} async-done(((bf16[4,512,1024]{2,1,0:T(8,128)(2,1)}), bf16[4,512,1024]{2,1,0:T(8,128)(2,1)}, u32[]{:S(2)}, u32[]{:S(2)}) %all-to-all-start.3) | async-done | bytes 4194336 | tf_op jit(solution)/shard_map/all_to_all | solution.py:249
  263.1 37.2 %all-gather.8.cloned.1.call-done = bf16[512,2048]{0,1:T(8,128)(2,1)} async-done(((bf16[512,512]{0,1:T(8,128)(2,1)}), bf16[512,2048]{0,1:T(8,128)(2,1)}) %all-gather.8.cloned.1.call-update) | async-done | bytes 2097168 | tf_op jit(solution)/shard_map/all_gather | solution.py:246
  300.3 5.2 %fusion.3 = bf16[512,1024]{1,0:T(8,128)(2,1)S(1)} fusion(bf16[512,1024]{1,0:T(8,128)(2,1)S(1)} %copy-done.2, bf16[512,4,512]{0,2,1:T(8,128)(2,1)} %bitcast.75, bf16[4,512,1024]{2,1,0:T(8,128)(2,1)} %all-to-all-done.3), kind=kOutput, calls=%fused_computation.11 | convolution fusion | flops 2149056512 | bytes 8388608 | tf_op jit(solution)/shard_map/tsr,src->tc/dot_general | solution.py:250
  305.5 5.4 %gather_fusion = bf16[1024,1024]{1,0:T(8,128)(2,1)} fusion(bf16[512,1024]{1,0:T(8,128)(2,1)S(1)} %fusion.3, s32[1024]{0:T(1024)S(1)} %broadcast_clamp_fusion), kind=kCustom, calls=%fused_computation | custom fusion | bytes 4198400 | tf_op jit(solution)/shard_map/gather | solution.py:257
  310.9 8.6 %all-to-all-start.4 = ((bf16[32,32,1024]{2,1,0:T(8,128)(2,1)}), bf16[32,32,1024]{2,1,0:T(8,128)(2,1)S(1)}, u32[]{:S(2)}, u32[]{:S(2)}) async-start(bf16[32,32,1024]{2,1,0:T(8,128)(2,1)} %bitcast.63), calls=%async_computation.4 | async-start | bytes 4194304 | tf_op jit(solution)/shard_map/all_to_all | solution.py:258
  319.4 28.3 %all-to-all-done.4 = bf16[32,32,1024]{2,1,0:T(8,128)(2,1)S(1)} async-done(((bf16[32,32,1024]{2,1,0:T(8,128)(2,1)}), bf16[32,32,1024]{2,1,0:T(8,128)(2,1)S(1)}, u32[]{:S(2)}, u32[]{:S(2)}) %all-to-all-start.4) | async-done | bytes 2097184 | tf_op jit(solution)/shard_map/all_to_all | solution.py:258
  347.7 2.8 gather_fusion.1
  (33 shorter events, 1.1 us)
Async XLA Ops:
  6.5 115.3 %copy-start = (bf16[4096,128]{1,0:T(8,128)(2,1)S(1)}, bf16[4096,128]{1,0:T(8,128)(2,1)}, u32[]{:S(2)}) copy-start(bf16[4096,128]{1,0:T(8,128)(2,1)} %param.13) | copy-start | bytes 3145732
  16.5 16.5 %all-to-all-start = ((s32[32,1,34]{2,1,0:T(1,128)}), s32[32,1,34]{2,1,0:T(1,128)S(1)}, u32[]{:S(2)}, u32[]{:S(2)}) async-start(s32[32,1,34]{2,1,0:T(1,128)} %bitcast.5), calls=%async_computation | async-start | bytes 32768 | tf_op jit(solution)/shard_map/all_to_all | solution.py:190
  32.9 33.6 %all-to-all-start.1 = ((bf16[32,32,1024]{2,1,0:T(8,128)(2,1)}), bf16[32,32,1024]{2,1,0:T(8,128)(2,1)S(1)}, u32[]{:S(2)}, u32[]{:S(2)}) async-start(bf16[32,32,1024]{2,1,0:T(8,128)(2,1)} %bitcast.8), calls=%async_computation.1 | async-start | bytes 4194304 | tf_op jit(solution)/shard_map/all_to_all | solution.py:187
  38.3 83.6 %copy-start.5 = (f32[4096]{0:T(1024)S(1)}, f32[4096]{0:T(1024)}, u32[]{:S(2)}) copy-start(f32[4096]{0:T(1024)} %param.11) | copy-start | bytes 49156
  38.3 80.3 %all-gather.4.cloned.1.call-start = ((), (), s32[]{:S(2)}) async-start(), calls=%async_computation.5 | async-start | bytes 5242880 | tf_op jit(solution)/shard_map/all_gather | solution.py:204
  72.8 129.9 %all-gather.6.cloned.1.call-start = ((), (), s32[]{:S(2)}) async-start(), calls=%async_computation.6 | async-start | bytes 4325376 | tf_op jit(solution)/shard_map/all_gather | solution.py:220
  118.6 3.4 copy-start.1
  122.1 2.5 copy-start.4
  129.2 80.6 %all-to-all-start.2 = ((bf16[32,256,256]{2,1,0:T(8,128)(2,1)}), bf16[32,256,256]{2,1,0:T(8,128)(2,1)}, u32[]{:S(2)}, u32[]{:S(2)}) async-start(bf16[32,256,256]{2,1,0:T(8,128)(2,1)} %broadcast_in_dim.26), calls=%async_computation.2 | async-start | bytes 8388608 | tf_op jit(solution)/shard_map/all_to_all | solution.py:222
  143.5 9.8 %copy-start.3 = (s32[512]{0:T(512)S(1)}, s32[512]{0:T(512)}, u32[]{:S(2)}) copy-start(s32[512]{0:T(512)} %param.10) | copy-start | bytes 6148
  209.9 53.2 %all-to-all-start.3 = ((bf16[4,512,1024]{2,1,0:T(8,128)(2,1)}), bf16[4,512,1024]{2,1,0:T(8,128)(2,1)}, u32[]{:S(2)}, u32[]{:S(2)}) async-start(bf16[4,512,1024]{2,1,0:T(8,128)(2,1)} %bitcast.61), calls=%async_computation.3 | async-start | bytes 8388608 | tf_op jit(solution)/shard_map/all_to_all | solution.py:249
  214.8 85.5 %all-gather.8.cloned.1.call-start = ((), (), s32[]{:S(2)}) async-start(), calls=%async_computation.7 | async-start | bytes 2621440 | tf_op jit(solution)/shard_map/all_gather | solution.py:246
  215.1 85.3 %copy-start.2 = (bf16[512,1024]{1,0:T(8,128)(2,1)S(1)}, bf16[512,1024]{1,0:T(8,128)(2,1)}, u32[]{:S(2)}) copy-start(bf16[512,1024]{1,0:T(8,128)(2,1)} %scatter_custom_fusion.2) | copy-start | bytes 3145732
  310.9 36.9 %all-to-all-start.4 = ((bf16[32,32,1024]{2,1,0:T(8,128)(2,1)}), bf16[32,32,1024]{2,1,0:T(8,128)(2,1)S(1)}, u32[]{:S(2)}, u32[]{:S(2)}) async-start(bf16[32,32,1024]{2,1,0:T(8,128)(2,1)} %bitcast.63), calls=%async_computation.4 | async-start | bytes 4194304 | tf_op jit(solution)/shard_map/all_to_all | solution.py:258
Sparse Core Ops, SparseCore 0:
  73.0 45.6 all-gather.3
  126.9 75.7 all-gather.5
  222.8 77.4 all-gather.7

commit v9 on v8

--- a/solution.py
+++ b/solution.py
@@ -218,10 +218,7 @@
     kv_own = jnp.concatenate([keys_own, values_own], axis=1)
     half = tok_dev // 2
     kv_low = lax.all_gather(kv_own[:half], ("chip", "core"), axis=0, tiled=True)
-    kv_copies = jnp.broadcast_to(kv_own[half:][None], (owners, half, kv_own.shape[1]))
-    kv_high = lax.all_to_all(
-        kv_copies, ("chip", "core"), split_axis=0, concat_axis=0, tiled=True
-    ).reshape(owners * half, kv_own.shape[1])
+    kv_high = lax.all_gather(kv_own[half:], ("chip", "core"), axis=0, tiled=True)
 
     block = KEY_BLOCK
     last_block = (block_first + tok_dev - 1) // block

time: 357 us -> 340 us (0.952)
  starting transfers between devices: 36.8 us -> 28 us
  waiting for transfers between devices: 220 us -> 214 us
    all_gather x0 -> x1, waiting for transfers between devices: none -> 40.9 us  [local(): lax.all_gather(kv_own[half:], ('chip', 'core'), axis=0, tiled=True)]
    all_to_all x1, waiting for transfers between devices: 40.4 us -> 0.01 us  [local(): lax.all_to_all(w_split, 'mp', split_axis=0, concat_axis=0, tiled=True)]
    all_gather x1, waiting for transfers between devices: 38 us -> 13.8 us  [local(): kv_low = lax.all_gather(kv_own[:half], ('chip', 'core'), axis=0, tiled=True)]
    all_gather x1, waiting for transfers between devices: 37.2 us -> 54.1 us  [local(): context_all = lax.all_gather(context, 'mp', axis=1, tiled=True)]
    all_to_all x1 -> x0, starting transfers between devices: 7.8 us -> none  [local(): lax.all_to_all(kv_copies, ('chip', 'core'), split_axis=0, concat_axis=0,...]
  transfers between devices with their start and end apart: 8 -> 8, of which waited for: 7 -> 7; matrix products, arithmetic and copies ran while one was open for 10% -> 9% of each run, Pallas kernels for 4% -> 4%
where the time goes in v9:
time: 340 us
  waiting for transfers between devices  214 us (63%)
  local copies, waits for them, and re-layouts  40.6 us (12%)
  starting transfers between devices  28 us (8%)
  Pallas kernels  14.7 us (4%)
  other arithmetic  14.6 us (4%)
  between operations  14.6 us (4%)
  matrix products  13.7 us (4%)
    all_gather x1, waiting for transfers between devices, local(): context_all = lax.all_gather(context, 'mp', axis=1, tiled=True)  54.1 us
    all_gather x1, waiting for transfers between devices, local(): routed = lax.all_gather(routed_part, 'mp', axis=1, tiled=True)  45.5 us
    all_gather x1, waiting for transfers between devices, local(): lax.all_gather(kv_own[half:], ('chip', 'core'), axis=0, tiled=True)  40.9 us
    all_to_all x1, waiting for transfers between devices, local(): lax.all_to_all(backward, ('chip', 'core'), split_axis=0, concat_axis=0, t...  28.3 us
    all_to_all x1, waiting for transfers between devices, local(): lax.all_to_all(outgoing.reshape(owners, capacity, columns), ('chip', 'cor...  28.1 us
    pallas_call x2, Pallas kernels, flash_pass(): pl.pallas_call(functools.partial(flash_kernel, final), grid_spec=grid_spe...  14.7 us
    all_gather x1, waiting for transfers between devices, local(): kv_low = lax.all_gather(kv_own[:half], ('chip', 'core'), axis=0, tiled=True)  13.8 us
    all_to_all x1, starting transfers between devices, local(): lax.all_to_all(places_info, ('chip', 'core'), split_axis=0, concat_axis=0...  9.6 us
  transfers between devices with their start and end apart: 8, of which 7 were waited for; matrix products, arithmetic and copies ran while one was open for 9% of the time, Pallas kernels for 4%

profile of v9, /device:TPU:1, one launch (start us, length us, event | category | flops | bytes accessed | tf_op | source)
XLA Modules:
  0.0 339.8 jit_solution(3246464196854708454)
XLA Ops:
  6.5 1.0 convert_reduce_fusion
  7.6 1.4 fusion.32
  9.0 0.7 add_select_fusion
  9.7 1.2 reduce-window.6
  10.9 0.2 slice_reduce_fusion
  11.2 2.4 scatter_custom_fusion
  13.8 0.6 slice.45
  15.0 0.8 pad_add_fusion.1
  15.8 0.6 pad_add_fusion
  16.5 9.6 %all-to-all-start = ((s32[32,1,34]{2,1,0:T(1,128)}), s32[32,1,34]{2,1,0:T(1,128)S(1)}, u32[]{:S(2)}, u32[]{:S(2)}) async-start(s32[32,1,34]{2,1,0:T(1,128)} %bitcast.5), calls=%async_computation | async-start | bytes 32768 | tf_op jit(solution)/shard_map/all_to_all | solution.py:190
  26.1 4.8 %scatter_custom_fusion.1 = bf16[1024,1024]{1,0:T(8,128)(2,1)} fusion(s32[512]{0:T(512)S(1)} %compare_select_fusion.2, bf16[512,1024]{1,0:T(8,128)(2,1)} %param.8, bf16[]{:T(256)} %constant.79.clone.1), kind=kCustom, calls=%fused_computation.14 | custom fusion | bytes 2097664 | tf_op jit(solution)/shard_map/scatter | solution.py:175
  30.9 2.0 all-to-all-done
  32.9 5.3 %all-to-all-start.1 = ((bf16[32,32,1024]{2,1,0:T(8,128)(2,1)}), bf16[32,32,1024]{2,1,0:T(8,128)(2,1)S(1)}, u32[]{:S(2)}, u32[]{:S(2)}) async-start(bf16[32,32,1024]{2,1,0:T(8,128)(2,1)} %bitcast.8), calls=%async_computation.1 | async-start | bytes 4194304 | tf_op jit(solution)/shard_map/all_to_all | solution.py:187
  38.5 28.1 %all-to-all-done.1 = bf16[32,32,1024]{2,1,0:T(8,128)(2,1)S(1)} async-done(((bf16[32,32,1024]{2,1,0:T(8,128)(2,1)}), bf16[32,32,1024]{2,1,0:T(8,128)(2,1)S(1)}, u32[]{:S(2)}, u32[]{:S(2)}) %all-to-all-start.1) | async-done | bytes 2097184 | tf_op jit(solution)/shard_map/all_to_all | solution.py:187
  66.6 6.2 %scatter_custom_fusion.2 = bf16[512,1024]{1,0:T(8,128)(2,1)} fusion(s32[1024]{0:T(1024)S(1)} %bitcast.71, bf16[1024,1024]{1,0:T(8,128)(2,1)S(1)} %bitcast.63, bf16[]{:T(256)} %constant.79.clone.1), kind=kCustom, calls=%fused_computation.20 | custom fusion | bytes 1048578 | tf_op jit(solution)/shard_map/scatter | solution.py:202
  72.8 0.2 all-gather.9.cloned.1.call-start
  73.1 45.5 %all-gather.5.cloned.1.call-done = bf16[512,4096]{1,0:T(8,128)(2,1)} async-done(((bf16[512,1024]{1,0:T(8,128)(2,1)}), bf16[512,4096]{1,0:T(8,128)(2,1)}) %all-gather.5.cloned.1.call-update) | async-done | bytes 4194320 | tf_op jit(solution)/shard_map/all_gather | solution.py:204
  118.6 3.2 fusion
  121.9 0.2 copy-done.1
  122.1 1.3 convolution_bitcast_fusion
  123.4 1.2 fusion.17
  124.6 1.3 convolution_convert_fusion
  126.1 0.7 fusion.31
  126.9 0.7 all-gather.7.cloned.1.call-update
  127.6 6.5 %copy.34 = bf16[512,4096]{0,1:T(8,128)(2,1)} copy(bf16[512,4096]{1,0:T(8,128)(2,1)} %param.15) | data formatting | bytes 8388608 | tf_op args[7]
  134.0 6.3 %copy.35 = bf16[512,4,1024]{2,0,1:T(8,128)(2,1)} copy(bf16[512,4,1024]{0,2,1:T(8,128)(2,1)} %bitcast.61) | data formatting | bytes 8388608 | tf_op jit(solution)/shard_map/reshape | solution.py:245
  140.4 5.0 %all-to-all-start.2 = ((bf16[4,512,1024]{2,1,0:T(8,128)(2,1)}), bf16[4,512,1024]{2,1,0:T(8,128)(2,1)}, u32[]{:S(2)}, u32[]{:S(2)}) async-start(bf16[4,512,1024]{2,1,0:T(8,128)(2,1)} %bitcast.60), calls=%async_computation.2 | async-start | bytes 8388608 | tf_op jit(solution)/shard_map/all_to_all | solution.py:246
  145.4 0.6 iota_add_fusion.refs_4_
  146.0 0.5 multiply_cosine_fusion.1
  146.6 0.2 slice_reduce_fusion.1
  146.7 0.8 fusion.21
  147.6 0.6 fusion.25
  148.8 1.9 fusion.30
  150.7 1.3 stack.35.span_ref
  152.1 1.3 stack.34.span_ref
  153.4 5.9 %fusion.28 = f32[512,512]{0,1:T(8,128)S(1)} fusion(bf16[4096,512]{1,0:T(8,128)(2,1)} %param.12, bf16[512,4096]{1,0:T(8,128)(2,1)} %all-gather.5.cloned.1.call-done, f32[4096]{0:T(1024)S(1)} %copy-done.5, f32[512]{0:T(512)S(1)} %add_rsqrt_fusion), kind=kOutput, calls=%fused_computation.72 | convolution fusion | flops 2155872256 | bytes 9455616 | tf_op jit(solution)/shard_map/dot_general | solution.py:209
  159.3 0.2 subtract_convert_fusion
  159.5 0.9 maximum_bitcast_fusion.refs_0_
  160.4 13.8 %all-gather.9.cloned.1.call-done.refs_1_.refs_2_ = bf16[8192,256]{1,0:T(8,128)(2,1)} async-done(((bf16[256,256]{1,0:T(8,128)(2,1)}), bf16[8192,256]{1,0:T(8,128)(2,1)}) %all-gather.9.cloned.1.call-update) | async-done | bytes 4194320 | tf_op jit(solution)/shard_map/all_gather | solution.py:220
  174.2 7.1 %shard_map.82 = (f32[4,1,512]{2,1,0:T(1,128)}, f32[4,1,512]{2,1,0:T(1,128)}, f32[4,128,512]{2,1,0:T(8,128)}) custom-call(s32[6]{0:T(128)} %stack.35.span_ref, bf16[4,128,512]{2,1,0:T(8,128)(2,1)} %maximum_bitcast_fusion.refs_0_, bf16[8192,256]{1,0:T(8,128)(2,1)} %all-gather.9.cloned.1.call-done.refs_1_.refs_2_, ...), custom_call_target="tpu_custom_call" | custom-call | flops 4831838208 | bytes 3407872 | tf_op jit(solution)/shard_map/pallas_call | solution.py:151
  181.3 40.9 %all-gather.7.cloned.1.call-done.refs_1_.refs_2_ = bf16[8192,256]{1,0:T(8,128)(2,1)} async-done(((bf16[256,256]{1,0:T(8,128)(2,1)}), bf16[8192,256]{1,0:T(8,128)(2,1)}) %all-gather.7.cloned.1.call-update) | async-done | bytes 4194320 | tf_op jit(solution)/shard_map/all_gather | solution.py:221
  222.2 7.6 %shard_map.83 = bf16[4,128,512]{2,1,0:T(8,128)(2,1)} custom-call(s32[6]{0:T(128)} %stack.34.span_ref, bf16[4,128,512]{2,1,0:T(8,128)(2,1)} %maximum_bitcast_fusion.refs_0_, bf16[8192,256]{1,0:T(8,128)(2,1)} %all-gather.7.cloned.1.call-done.refs_1_.refs_2_, bf16[8192,256]{1,0:T(8,128)(2,1)} %all-gather.7.cloned.1.call-done.refs_1_.refs_2_, ...), custom_call_target="tpu_custom_call" | custom-call | flops 4831838208 | bytes 3407872 | tf_op jit(solution)/shard_map/pallas_call | solution.py:151
  229.9 54.1 %all-gather.11.cloned.1.call-done = bf16[512,2048]{0,1:T(8,128)(2,1)} async-done(((bf16[512,512]{0,1:T(8,128)(2,1)}), bf16[512,2048]{0,1:T(8,128)(2,1)}) %all-gather.11.cloned.1.call-update) | async-done | bytes 2097168 | tf_op jit(solution)/shard_map/all_gather | solution.py:243
  284.0 5.2 %fusion.3 = bf16[512,1024]{1,0:T(8,128)(2,1)S(1)} fusion(bf16[512,1024]{1,0:T(8,128)(2,1)S(1)} %copy-done.2, bf16[512,4,512]{0,2,1:T(8,128)(2,1)} %bitcast.74, bf16[4,512,1024]{2,1,0:T(8,128)(2,1)} %all-to-all-done.2), kind=kOutput, calls=%fused_computation.11 | convolution fusion | flops 2149056512 | bytes 8388608 | tf_op jit(solution)/shard_map/tsr,src->tc/dot_general | solution.py:247
  289.1 5.4 %gather_fusion = bf16[1024,1024]{1,0:T(8,128)(2,1)} fusion(bf16[512,1024]{1,0:T(8,128)(2,1)S(1)} %fusion.3, s32[1024]{0:T(1024)S(1)} %broadcast_clamp_fusion), kind=kCustom, calls=%fused_computation | custom fusion | bytes 4198400 | tf_op jit(solution)/shard_map/gather | solution.py:254
  294.5 7.7 %all-to-all-start.3 = ((bf16[32,32,1024]{2,1,0:T(8,128)(2,1)}), bf16[32,32,1024]{2,1,0:T(8,128)(2,1)S(1)}, u32[]{:S(2)}, u32[]{:S(2)}) async-start(bf16[32,32,1024]{2,1,0:T(8,128)(2,1)} %bitcast.62), calls=%async_computation.3 | async-start | bytes 4194304 | tf_op jit(solution)/shard_map/all_to_all | solution.py:255
  302.2 28.3 %all-to-all-done.3 = bf16[32,32,1024]{2,1,0:T(8,128)(2,1)S(1)} async-done(((bf16[32,32,1024]{2,1,0:T(8,128)(2,1)}), bf16[32,32,1024]{2,1,0:T(8,128)(2,1)S(1)}, u32[]{:S(2)}, u32[]{:S(2)}) %all-to-all-start.3) | async-done | bytes 2097184 | tf_op jit(solution)/shard_map/all_to_all | solution.py:255
  330.5 2.8 gather_fusion.1
  (33 shorter events, 0.8 us)
Async XLA Ops:
  6.5 115.3 %copy-start = (bf16[4096,128]{1,0:T(8,128)(2,1)S(1)}, bf16[4096,128]{1,0:T(8,128)(2,1)}, u32[]{:S(2)}) copy-start(bf16[4096,128]{1,0:T(8,128)(2,1)} %param.13) | copy-start | bytes 3145732
  16.5 16.5 %all-to-all-start = ((s32[32,1,34]{2,1,0:T(1,128)}), s32[32,1,34]{2,1,0:T(1,128)S(1)}, u32[]{:S(2)}, u32[]{:S(2)}) async-start(s32[32,1,34]{2,1,0:T(1,128)} %bitcast.5), calls=%async_computation | async-start | bytes 32768 | tf_op jit(solution)/shard_map/all_to_all | solution.py:190
  32.9 33.6 %all-to-all-start.1 = ((bf16[32,32,1024]{2,1,0:T(8,128)(2,1)}), bf16[32,32,1024]{2,1,0:T(8,128)(2,1)S(1)}, u32[]{:S(2)}, u32[]{:S(2)}) async-start(bf16[32,32,1024]{2,1,0:T(8,128)(2,1)} %bitcast.8), calls=%async_computation.1 | async-start | bytes 4194304 | tf_op jit(solution)/shard_map/all_to_all | solution.py:187
  38.3 83.6 %copy-start.5 = (f32[4096]{0:T(1024)S(1)}, f32[4096]{0:T(1024)}, u32[]{:S(2)}) copy-start(f32[4096]{0:T(1024)} %param.11) | copy-start | bytes 49156
  38.3 80.3 %all-gather.5.cloned.1.call-start = ((), (), s32[]{:S(2)}) async-start(), calls=%async_computation.4 | async-start | bytes 5242880 | tf_op jit(solution)/shard_map/all_gather | solution.py:204
  72.8 101.4 %all-gather.9.cloned.1.call-start = ((), (), s32[]{:S(2)}) async-start(), calls=%async_computation.6 | async-start | bytes 4325376 | tf_op jit(solution)/shard_map/all_gather | solution.py:220
  118.6 3.4 %copy-start.1 = (bf16[512,4096]{1,0:T(8,128)(2,1)S(1)}, bf16[512,4096]{1,0:T(8,128)(2,1)}, u32[]{:S(2)}) copy-start(bf16[512,4096]{1,0:T(8,128)(2,1)} %all-gather.5.cloned.1.call-done) | copy-start | bytes 12582916
  122.1 2.5 copy-start.4
  126.8 95.4 %all-gather.7.cloned.1.call-start = ((), (), s32[]{:S(2)}) async-start(), calls=%async_computation.5 | async-start | bytes 4325376 | tf_op jit(solution)/shard_map/all_gather | solution.py:221
  140.4 8.4 %copy-start.3 = (s32[512]{0:T(512)S(1)}, s32[512]{0:T(512)}, u32[]{:S(2)}) copy-start(s32[512]{0:T(512)} %param.10) | copy-start | bytes 6148
  140.4 89.5 %all-to-all-start.2 = ((bf16[4,512,1024]{2,1,0:T(8,128)(2,1)}), bf16[4,512,1024]{2,1,0:T(8,128)(2,1)}, u32[]{:S(2)}, u32[]{:S(2)}) async-start(bf16[4,512,1024]{2,1,0:T(8,128)(2,1)} %bitcast.60), calls=%async_computation.2 | async-start | bytes 8388608 | tf_op jit(solution)/shard_map/all_to_all | solution.py:246
  145.4 138.6 %all-gather.11.cloned.1.call-start = ((), (), s32[]{:S(2)}) async-start(), calls=%async_computation.7 | async-start | bytes 2621440 | tf_op jit(solution)/shard_map/all_gather | solution.py:243
  222.2 61.7 %copy-start.2 = (bf16[512,1024]{1,0:T(8,128)(2,1)S(1)}, bf16[512,1024]{1,0:T(8,128)(2,1)}, u32[]{:S(2)}) copy-start(bf16[512,1024]{1,0:T(8,128)(2,1)} %scatter_custom_fusion.2) | copy-start | bytes 3145732
  294.5 36.0 %all-to-all-start.3 = ((bf16[32,32,1024]{2,1,0:T(8,128)(2,1)}), bf16[32,32,1024]{2,1,0:T(8,128)(2,1)S(1)}, u32[]{:S(2)}, u32[]{:S(2)}) async-start(bf16[32,32,1024]{2,1,0:T(8,128)(2,1)} %bitcast.62), calls=%async_computation.3 | async-start | bytes 4194304 | tf_op jit(solution)/shard_map/all_to_all | solution.py:255
Sparse Core Ops, SparseCore 0:
  73.0 45.6 all-gather.4
  126.9 47.2 all-gather.8
  176.5 45.7 all-gather.6
  230.0 53.9 all-gather.10

commit v10 on v9

--- a/solution.py
+++ b/solution.py
@@ -44,9 +44,11 @@
     return (wide_rows * inv_rms * norm_gain[None, :]).astype(jnp.bfloat16)
 
 
-def flash_kernel(final, span_ref, *refs):
-    if final:
+def flash_kernel(carried, final, span_ref, *refs):
+    if carried and final:
         q_ref, k_ref, v_ref, start_ref, row_ref, m_in, l_in, acc_in, o_ref, m_sc, l_sc, acc_sc = refs
+    elif carried:
+        q_ref, k_ref, v_ref, start_ref, row_ref, m_in, l_in, acc_in, m_sc, l_sc, acc_sc = refs
     else:
         q_ref, k_ref, v_ref, start_ref, row_ref, m_sc, l_sc, acc_sc = refs
     step = pl.program_id(0)
@@ -56,7 +58,7 @@
 
     @pl.when(step == 0)
     def _init():
-        if final:
+        if carried:
             m_sc[...] = m_in[...]
             l_sc[...] = l_in[...]
             acc_sc[...] = acc_in[...]
@@ -105,9 +107,9 @@
                 o_ref[h] = (acc_sc[h] / l_sc[h]).astype(o_ref.dtype)
 
 
-def flash_pass(span, queries_t, kv_part, row_start, row_index, block, max_blocks, state):
+def flash_pass(span, queries_t, kv_part, row_start, row_index, block, max_blocks, state, final):
     heads, _, rows = queries_t.shape
-    final = state is not None
+    carried = state is not None
 
     def kv_map(column):
         def index_map(step, span_ref):
@@ -129,17 +131,18 @@
         jax.ShapeDtypeStruct((heads, HD, rows), jnp.float32),
     ]
     state_specs = [pl.BlockSpec(x.shape, fixed3) for x in state_shapes]
+    operands = (span, queries_t, kv_part, kv_part, row_start, row_index)
+    if carried:
+        in_specs = in_specs + state_specs
+        operands = operands + tuple(state)
     if final:
-        in_specs = in_specs + state_specs
         out_specs = pl.BlockSpec((heads, HD, rows), fixed3)
         out_shape = jax.ShapeDtypeStruct((heads, HD, rows), jnp.bfloat16)
         scratch = [pltpu.VMEM(x.shape, jnp.float32) for x in state_shapes]
-        operands = (span, queries_t, kv_part, kv_part, row_start, row_index) + tuple(state)
     else:
         out_specs = state_specs
         out_shape = state_shapes
         scratch = []
-        operands = (span, queries_t, kv_part, kv_part, row_start, row_index)
     grid_spec = pltpu.PrefetchScalarGridSpec(
         num_scalar_prefetch=1,
         grid=(max_blocks,),
@@ -149,7 +152,7 @@
     )
     flops = 4 * heads * rows * block * HD * max_blocks
     return pl.pallas_call(
-        functools.partial(flash_kernel, final),
+        functools.partial(flash_kernel, carried, final),
         grid_spec=grid_spec,
         out_shape=out_shape,
         compiler_params=pltpu.CompilerParams(dimension_semantics=("arbitrary",)),
@@ -216,10 +219,11 @@
     keys_own = rotate(keys_own, angles).astype(jnp.bfloat16).reshape(tok_dev, kv_dev * HD)
     values_own = jnp.dot(normed, w_value, preferred_element_type=jnp.float32).astype(jnp.bfloat16)
     kv_own = jnp.concatenate([keys_own, values_own], axis=1)
-    half = tok_dev // 2
-    kv_low = lax.all_gather(kv_own[:half], ("chip", "core"), axis=0, tiled=True)
-    kv_high = lax.all_gather(kv_own[half:], ("chip", "core"), axis=0, tiled=True)
-
+    parts = [(0, tok_dev // 2), (tok_dev // 2, tok_dev // 4), (3 * tok_dev // 4, tok_dev // 4)]
+    kv_parts = [
+        lax.all_gather(kv_own[first:first + size], ("chip", "core"), axis=0, tiled=True)
+        for first, size in parts
+    ]
     block = KEY_BLOCK
     last_block = (block_first + tok_dev - 1) // block
     first_block = doc_low // block
@@ -232,13 +236,13 @@
         ).astype(jnp.int32)
 
     queries_t = jnp.transpose(queries.reshape(tok_dev, heads_dev, HD), (1, 2, 0))
-    state = flash_pass(
-        span_for(0), queries_t, kv_low, row_start[None, :], row_index[None, :], half, max_blocks, None
-    )
-    context_t = flash_pass(
-        span_for(half), queries_t, kv_high, row_start[None, :], row_index[None, :], half, max_blocks,
-        state,
-    )
+    state = None
+    for number, ((first, size), kv_part) in enumerate(zip(parts, kv_parts)):
+        state = flash_pass(
+            span_for(first), queries_t, kv_part, row_start[None, :], row_index[None, :], size,
+            max_blocks, state, number == len(parts) - 1,
+        )
+    context_t = state
     context = jnp.transpose(context_t, (2, 0, 1)).reshape(tok_dev, heads_dev * HD)
     context_all = lax.all_gather(context, "mp", axis=1, tiled=True)
     mp_size = lax.axis_size("mp")

time: 340 us -> 376 us (1.11)
  waiting for transfers between devices: 214 us -> 241 us
  Pallas kernels: 14.7 us -> 20.8 us
    all_gather x2 -> x3, waiting for transfers between devices: 54.8 us -> 89.1 us  [local(): lax.all_gather(kv_own[first:first + size], ('chip', 'core'), axis=0, tile...]
    all_gather x1, waiting for transfers between devices: 54.1 us -> 47.6 us  [local(): context_all = lax.all_gather(context, 'mp', axis=1, tiled=True)]
    pallas_call x2 -> x3, Pallas kernels: 14.7 us -> 20.8 us  [flash_pass(): pl.pallas_call(functools.partial(flash_kernel, carried, final), grid_spec...]
  transfers between devices with their start and end apart: 8 -> 9, of which waited for: 7 -> 8; matrix products, arithmetic and copies ran while one was open for 9% -> 9% of each run, Pallas kernels for 4% -> 6%
where the time goes in v10:
time: 376 us; the launch traced here: 375 us
  waiting for transfers between devices  241 us (64%)
  local copies, waits for them, and re-layouts  40.9 us (11%)
  starting transfers between devices  28 us (7%)
  Pallas kernels  20.8 us (6%)
  other arithmetic  15.6 us (4%)
  between operations  14.6 us (4%)
  matrix products  14 us (4%)
    all_gather x3, waiting for transfers between devices, local(): lax.all_gather(kv_own[first:first + size], ('chip', 'core'), axis=0, tile...  89.1 us
    all_gather x1, waiting for transfers between devices, local(): context_all = lax.all_gather(context, 'mp', axis=1, tiled=True)  47.6 us
    all_gather x1, waiting for transfers between devices, local(): routed = lax.all_gather(routed_part, 'mp', axis=1, tiled=True)  45.5 us
    all_to_all x1, waiting for transfers between devices, local(): lax.all_to_all(backward, ('chip', 'core'), split_axis=0, concat_axis=0, t...  28.3 us
    all_to_all x1, waiting for transfers between devices, local(): lax.all_to_all(outgoing.reshape(owners, capacity, columns), ('chip', 'cor...  28.1 us
    pallas_call x3, Pallas kernels, flash_pass(): pl.pallas_call(functools.partial(flash_kernel, carried, final), grid_spec...  20.8 us
    all_to_all x1, starting transfers between devices, local(): lax.all_to_all(places_info, ('chip', 'core'), split_axis=0, concat_axis=0...  9.6 us
    all_to_all x1, starting transfers between devices, local(): lax.all_to_all(backward, ('chip', 'core'), split_axis=0, concat_axis=0, t...  7.71 us
  transfers between devices with their start and end apart: 9, of which 8 were waited for; matrix products, arithmetic and copies ran while one was open for 9% of the time, Pallas kernels for 6%

profile of v10, /device:TPU:1, one launch (start us, length us, event | category | flops | bytes accessed | tf_op | source)
XLA Modules:
  0.0 375.3 jit_solution(17539001837535285429)
XLA Ops:
  6.5 1.0 convert_reduce_fusion
  7.6 1.4 fusion.31
  8.9 0.7 add_select_fusion
  9.6 1.2 reduce-window.6
  11.2 2.4 scatter_custom_fusion
  13.7 0.6 slice.48
  15.0 0.7 pad_add_fusion.1
  15.7 0.6 pad_add_fusion
  16.3 9.6 %all-to-all-start = ((s32[32,1,34]{2,1,0:T(1,128)}), s32[32,1,34]{2,1,0:T(1,128)S(1)}, u32[]{:S(2)}, u32[]{:S(2)}) async-start(s32[32,1,34]{2,1,0:T(1,128)} %bitcast.5), calls=%async_computation | async-start | bytes 32768 | tf_op jit(solution)/shard_map/all_to_all | solution.py:193
  25.9 4.8 %scatter_custom_fusion.1 = bf16[1024,1024]{1,0:T(8,128)(2,1)} fusion(s32[512]{0:T(512)S(1)} %compare_select_fusion.2, bf16[512,1024]{1,0:T(8,128)(2,1)} %param.8, bf16[]{:T(256)} %constant.80.clone.1), kind=kCustom, calls=%fused_computation.14 | custom fusion | bytes 2097664 | tf_op jit(solution)/shard_map/scatter | solution.py:178
  30.7 2.1 all-to-all-done
  32.8 5.3 %all-to-all-start.1 = ((bf16[32,32,1024]{2,1,0:T(8,128)(2,1)}), bf16[32,32,1024]{2,1,0:T(8,128)(2,1)S(1)}, u32[]{:S(2)}, u32[]{:S(2)}) async-start(bf16[32,32,1024]{2,1,0:T(8,128)(2,1)} %bitcast.8), calls=%async_computation.1 | async-start | bytes 4194304 | tf_op jit(solution)/shard_map/all_to_all | solution.py:190
  38.3 28.1 %all-to-all-done.1 = bf16[32,32,1024]{2,1,0:T(8,128)(2,1)S(1)} async-done(((bf16[32,32,1024]{2,1,0:T(8,128)(2,1)}), bf16[32,32,1024]{2,1,0:T(8,128)(2,1)S(1)}, u32[]{:S(2)}, u32[]{:S(2)}) %all-to-all-start.1) | async-done | bytes 2097184 | tf_op jit(solution)/shard_map/all_to_all | solution.py:190
  66.4 6.2 %scatter_custom_fusion.2 = bf16[512,1024]{1,0:T(8,128)(2,1)} fusion(s32[1024]{0:T(1024)S(1)} %bitcast.71, bf16[1024,1024]{1,0:T(8,128)(2,1)S(1)} %bitcast.63, bf16[]{:T(256)} %constant.80.clone.1), kind=kCustom, calls=%fused_computation.20 | custom fusion | bytes 1048578 | tf_op jit(solution)/shard_map/scatter | solution.py:205
  72.7 0.2 all-gather.12.cloned.1.call-start
  72.9 45.5 %all-gather.6.cloned.1.call-done = bf16[512,4096]{1,0:T(8,128)(2,1)} async-done(((bf16[512,1024]{1,0:T(8,128)(2,1)}), bf16[512,4096]{1,0:T(8,128)(2,1)}) %all-gather.6.cloned.1.call-update) | async-done | bytes 4194320 | tf_op jit(solution)/shard_map/all_gather | solution.py:207
  118.5 3.2 fusion
  121.9 1.3 convolution_bitcast_fusion
  123.2 1.2 fusion.17
  124.5 1.3 convolution_convert_fusion
  125.8 0.7 pad_maximum_fusion
  126.6 0.8 pad_maximum_fusion.2
  127.4 0.5 all-gather.8.cloned.1.call-update
  128.0 6.5 %copy.34 = bf16[512,4096]{0,1:T(8,128)(2,1)} copy(bf16[512,4096]{1,0:T(8,128)(2,1)} %param.15) | data formatting | bytes 8388608 | tf_op args[7]
  134.5 6.3 %copy.35 = bf16[512,4,1024]{2,0,1:T(8,128)(2,1)} copy(bf16[512,4,1024]{0,2,1:T(8,128)(2,1)} %bitcast.61) | data formatting | bytes 8388608 | tf_op jit(solution)/shard_map/reshape | solution.py:249
  140.8 5.0 %all-to-all-start.2 = ((bf16[4,512,1024]{2,1,0:T(8,128)(2,1)}), bf16[4,512,1024]{2,1,0:T(8,128)(2,1)}, u32[]{:S(2)}, u32[]{:S(2)}) async-start(bf16[4,512,1024]{2,1,0:T(8,128)(2,1)} %bitcast.60), calls=%async_computation.2 | async-start | bytes 8388608 | tf_op jit(solution)/shard_map/all_to_all | solution.py:250
  145.8 0.6 iota_add_fusion.refs_4_
  146.4 0.5 multiply_cosine_fusion.1
  147.2 0.7 fusion.21
  147.9 0.7 fusion.25
  149.2 1.8 fusion.30
  151.0 1.2 stack.43.span_ref
  152.2 1.3 stack.42.span_ref
  153.5 1.2 stack.41.span_ref
  154.6 6.3 %fusion.28 = f32[512,512]{0,1:T(8,128)S(1)} fusion(bf16[4096,512]{1,0:T(8,128)(2,1)} %param.12, bf16[512,4096]{1,0:T(8,128)(2,1)} %all-gather.6.cloned.1.call-done, f32[4096]{0:T(1024)S(1)} %copy-done.5, f32[512]{0:T(512)S(1)} %add_rsqrt_fusion), kind=kOutput, calls=%fused_computation.75 | convolution fusion | flops 2155872256 | bytes 9455616 | tf_op jit(solution)/shard_map/dot_general | solution.py:212
  161.1 0.8 maximum_bitcast_fusion.refs_0_
  161.9 12.1 %all-gather.12.cloned.1.call-done.refs_1_.refs_2_ = bf16[8192,256]{1,0:T(8,128)(2,1)} async-done(((bf16[256,256]{1,0:T(8,128)(2,1)}), bf16[8192,256]{1,0:T(8,128)(2,1)}) %all-gather.12.cloned.1.call-update) | async-done | bytes 4194320 | tf_op jit(solution)/shard_map/all_gather | solution.py:224
  174.0 7.1 %shard_map.82 = (f32[4,1,512]{2,1,0:T(1,128)}, f32[4,1,512]{2,1,0:T(1,128)}, f32[4,128,512]{2,1,0:T(8,128)}) custom-call(s32[6]{0:T(128)} %stack.43.span_ref, bf16[4,128,512]{2,1,0:T(8,128)(2,1)} %maximum_bitcast_fusion.refs_0_, bf16[8192,256]{1,0:T(8,128)(2,1)} %all-gather.12.cloned.1.call-done.refs_1_.refs_2_, ...), custom_call_target="tpu_custom_call" | custom-call | flops 4831838208 | bytes 3407872 | tf_op jit(solution)/shard_map/pallas_call | solution.py:154
  181.2 38.5 %all-gather.10.cloned.1.call-done.refs_1_.refs_2_ = bf16[4096,256]{1,0:T(8,128)(2,1)} async-done(((bf16[128,256]{1,0:T(8,128)(2,1)}), bf16[4096,256]{1,0:T(8,128)(2,1)}) %all-gather.10.cloned.1.call-update) | async-done | bytes 2097168 | tf_op jit(solution)/shard_map/all_gather | solution.py:224
  219.6 6.9 %shard_map.83 = (f32[4,1,512]{2,1,0:T(1,128)}, f32[4,1,512]{2,1,0:T(1,128)}, f32[4,128,512]{2,1,0:T(8,128)}) custom-call(s32[6]{0:T(128)} %stack.42.span_ref, bf16[4,128,512]{2,1,0:T(8,128)(2,1)} %maximum_bitcast_fusion.refs_0_, bf16[4096,256]{1,0:T(8,128)(2,1)} %all-gather.10.cloned.1.call-done.refs_1_.refs_2_, ...), custom_call_target="tpu_custom_call" | custom-call | flops 2415919104 | bytes 2228224 | tf_op jit(solution)/shard_map/pallas_call | solution.py:154
  226.5 38.5 %all-gather.8.cloned.1.call-done.refs_1_.refs_2_ = bf16[4096,256]{1,0:T(8,128)(2,1)} async-done(((bf16[128,256]{1,0:T(8,128)(2,1)}), bf16[4096,256]{1,0:T(8,128)(2,1)}) %all-gather.8.cloned.1.call-update) | async-done | bytes 2097168 | tf_op jit(solution)/shard_map/all_gather | solution.py:224
  265.0 6.8 %shard_map.84 = bf16[4,128,512]{2,1,0:T(8,128)(2,1)} custom-call(s32[6]{0:T(128)} %stack.41.span_ref, bf16[4,128,512]{2,1,0:T(8,128)(2,1)} %maximum_bitcast_fusion.refs_0_, bf16[4096,256]{1,0:T(8,128)(2,1)} %all-gather.8.cloned.1.call-done.refs_1_.refs_2_, bf16[4096,256]{1,0:T(8,128)(2,1)} %all-gather.8.cloned.1.call-done.refs_1_.refs_2_, ...), custom_call_target="tpu_custom_call" | custom-call | flops 2415919104 | bytes 2228224 | tf_op jit(solution)/shard_map/pallas_call | solution.py:154
  271.9 47.6 %all-gather.14.cloned.1.call-done = bf16[512,2048]{0,1:T(8,128)(2,1)} async-done(((bf16[512,512]{0,1:T(8,128)(2,1)}), bf16[512,2048]{0,1:T(8,128)(2,1)}) %all-gather.14.cloned.1.call-update) | async-done | bytes 2097168 | tf_op jit(solution)/shard_map/all_gather | solution.py:247
  319.4 5.2 %fusion.3 = bf16[512,1024]{1,0:T(8,128)(2,1)S(1)} fusion(bf16[512,1024]{1,0:T(8,128)(2,1)S(1)} %copy-done.2, bf16[512,4,512]{0,2,1:T(8,128)(2,1)} %bitcast.75, bf16[4,512,1024]{2,1,0:T(8,128)(2,1)} %all-to-all-done.2), kind=kOutput, calls=%fused_computation.11 | convolution fusion | flops 2149056512 | bytes 8388608 | tf_op jit(solution)/shard_map/tsr,src->tc/dot_general | solution.py:251
  324.6 5.3 %gather_fusion = bf16[1024,1024]{1,0:T(8,128)(2,1)} fusion(bf16[512,1024]{1,0:T(8,128)(2,1)S(1)} %fusion.3, s32[1024]{0:T(1024)S(1)} %broadcast_clamp_fusion), kind=kCustom, calls=%fused_computation | custom fusion | bytes 4198400 | tf_op jit(solution)/shard_map/gather | solution.py:258
  329.9 7.7 %all-to-all-start.3 = ((bf16[32,32,1024]{2,1,0:T(8,128)(2,1)}), bf16[32,32,1024]{2,1,0:T(8,128)(2,1)S(1)}, u32[]{:S(2)}, u32[]{:S(2)}) async-start(bf16[32,32,1024]{2,1,0:T(8,128)(2,1)} %bitcast.62), calls=%async_computation.3 | async-start | bytes 4194304 | tf_op jit(solution)/shard_map/all_to_all | solution.py:259
  337.7 28.3 %all-to-all-done.3 = bf16[32,32,1024]{2,1,0:T(8,128)(2,1)S(1)} async-done(((bf16[32,32,1024]{2,1,0:T(8,128)(2,1)}), bf16[32,32,1024]{2,1,0:T(8,128)(2,1)S(1)}, u32[]{:S(2)}, u32[]{:S(2)}) %all-to-all-start.3) | async-done | bytes 2097184 | tf_op jit(solution)/shard_map/all_to_all | solution.py:259
  366.0 2.8 gather_fusion.1
  (38 shorter events, 1.5 us)
Async XLA Ops:
  6.5 115.2 %copy-start = (bf16[4096,128]{1,0:T(8,128)(2,1)S(1)}, bf16[4096,128]{1,0:T(8,128)(2,1)}, u32[]{:S(2)}) copy-start(bf16[4096,128]{1,0:T(8,128)(2,1)} %param.13) | copy-start | bytes 3145732
  16.3 16.5 %all-to-all-start = ((s32[32,1,34]{2,1,0:T(1,128)}), s32[32,1,34]{2,1,0:T(1,128)S(1)}, u32[]{:S(2)}, u32[]{:S(2)}) async-start(s32[32,1,34]{2,1,0:T(1,128)} %bitcast.5), calls=%async_computation | async-start | bytes 32768 | tf_op jit(solution)/shard_map/all_to_all | solution.py:193
  32.8 33.6 %all-to-all-start.1 = ((bf16[32,32,1024]{2,1,0:T(8,128)(2,1)}), bf16[32,32,1024]{2,1,0:T(8,128)(2,1)S(1)}, u32[]{:S(2)}, u32[]{:S(2)}) async-start(bf16[32,32,1024]{2,1,0:T(8,128)(2,1)} %bitcast.8), calls=%async_computation.1 | async-start | bytes 4194304 | tf_op jit(solution)/shard_map/all_to_all | solution.py:190
  38.1 83.6 %copy-start.5 = (f32[4096]{0:T(1024)S(1)}, f32[4096]{0:T(1024)}, u32[]{:S(2)}) copy-start(f32[4096]{0:T(1024)} %param.11) | copy-start | bytes 49156
  38.2 80.3 %all-gather.6.cloned.1.call-start = ((), (), s32[]{:S(2)}) async-start(), calls=%async_computation.4 | async-start | bytes 5242880 | tf_op jit(solution)/shard_map/all_gather | solution.py:207
  72.7 101.4 %all-gather.12.cloned.1.call-start = ((), (), s32[]{:S(2)}) async-start(), calls=%async_computation.7 | async-start | bytes 4325376 | tf_op jit(solution)/shard_map/all_gather | solution.py:224
  118.5 3.4 copy-start.1
  121.9 2.5 copy-start.4
  126.6 93.1 %all-gather.10.cloned.1.call-start = ((), (), s32[]{:S(2)}) async-start(), calls=%async_computation.6 | async-start | bytes 2162688 | tf_op jit(solution)/shard_map/all_gather | solution.py:224
  127.4 137.6 %all-gather.8.cloned.1.call-start = ((), (), s32[]{:S(2)}) async-start(), calls=%async_computation.5 | async-start | bytes 2162688 | tf_op jit(solution)/shard_map/all_gather | solution.py:224
  140.8 8.4 %copy-start.3 = (s32[512]{0:T(512)S(1)}, s32[512]{0:T(512)}, u32[]{:S(2)}) copy-start(s32[512]{0:T(512)} %param.10) | copy-start | bytes 6148
  140.8 131.0 %all-to-all-start.2 = ((bf16[4,512,1024]{2,1,0:T(8,128)(2,1)}), bf16[4,512,1024]{2,1,0:T(8,128)(2,1)}, u32[]{:S(2)}, u32[]{:S(2)}) async-start(bf16[4,512,1024]{2,1,0:T(8,128)(2,1)} %bitcast.60), calls=%async_computation.2 | async-start | bytes 8388608 | tf_op jit(solution)/shard_map/all_to_all | solution.py:250
  145.8 173.6 %all-gather.14.cloned.1.call-start = ((), (), s32[]{:S(2)}) async-start(), calls=%async_computation.8 | async-start | bytes 2621440 | tf_op jit(solution)/shard_map/all_gather | solution.py:247
  265.0 54.4 %copy-start.2 = (bf16[512,1024]{1,0:T(8,128)(2,1)S(1)}, bf16[512,1024]{1,0:T(8,128)(2,1)}, u32[]{:S(2)}) copy-start(bf16[512,1024]{1,0:T(8,128)(2,1)} %scatter_custom_fusion.2) | copy-start | bytes 3145732
  329.9 36.0 %all-to-all-start.3 = ((bf16[32,32,1024]{2,1,0:T(8,128)(2,1)}), bf16[32,32,1024]{2,1,0:T(8,128)(2,1)S(1)}, u32[]{:S(2)}, u32[]{:S(2)}) async-start(bf16[32,32,1024]{2,1,0:T(8,128)(2,1)} %bitcast.62), calls=%async_computation.3 | async-start | bytes 4194304 | tf_op jit(solution)/shard_map/all_to_all | solution.py:259
Sparse Core Ops, SparseCore 0:
  72.8 45.6 all-gather.5
  126.7 47.3 all-gather.11
  176.3 43.2 all-gather.9
  221.8 43.2 all-gather.7
  272.0 47.4 all-gather.13

commit v11 on v9

--- a/solution.py
+++ b/solution.py
@@ -182,15 +182,30 @@
     last_id = doc_ids[tok_dev - 1]
     less_count = jnp.sum((doc_ids[None, :] < doc_ids[:, None]).astype(jnp.int32), axis=1)
     last_run_start = block_first + less_count[tok_dev - 1]
-    info = jnp.broadcast_to(jnp.stack([last_id, last_run_start])[None, :], (owners, 2))
-    places_info = jnp.concatenate([places.reshape(owners, capacity), info], axis=1)
-    arrived = lax.all_to_all(
-        outgoing.reshape(owners, capacity, columns), ("chip", "core"), split_axis=0, concat_axis=0, tiled=True
-    )
-    arrived_info = lax.all_to_all(places_info, ("chip", "core"), split_axis=0, concat_axis=0, tiled=True)
-    arrived_rows = arrived_info[:, :capacity].reshape(-1)
-    peer_last_id = arrived_info[:, capacity]
-    peer_run_start = arrived_info[:, capacity + 1]
+    digit = 64
+    slot_count = owners * capacity
+    meta = jnp.stack(
+        [
+            places // digit,
+            places % digit,
+            jnp.broadcast_to(last_id, (slot_count,)),
+            jnp.broadcast_to(last_run_start // digit, (slot_count,)),
+            jnp.broadcast_to(last_run_start % digit, (slot_count,)),
+        ],
+        axis=1,
+    )
+    meta_width = 128
+    meta = jnp.pad(meta, ((0, 0), (0, meta_width - meta.shape[1]))).astype(hidden_rows.dtype)
+    wide = jnp.concatenate([outgoing, meta], axis=1)
+    arrived_wide = lax.all_to_all(
+        wide.reshape(owners, capacity, columns + meta_width), ("chip", "core"),
+        split_axis=0, concat_axis=0, tiled=True,
+    )
+    arrived = arrived_wide[:, :, :columns]
+    arrived_meta = arrived_wide[:, :, columns:columns + 5].astype(jnp.int32)
+    arrived_rows = (arrived_meta[:, :, 0] * digit + arrived_meta[:, :, 1]).reshape(-1)
+    peer_last_id = arrived_meta[:, 0, 2]
+    peer_run_start = arrived_meta[:, 0, 3] * digit + arrived_meta[:, 0, 4]
     earlier = (owner_ids < my_index) & (peer_last_id == first_id)
     doc_low = jnp.minimum(block_first, jnp.min(jnp.where(earlier, peer_run_start, block_first)))
     row_index = block_first + jnp.arange(tok_dev, dtype=jnp.int32)

time: 340 us -> 338 us (level)
  blocking collectives: 0 us -> 40.9 us
  waiting for transfers between devices: 214 us -> 179 us
  starting transfers between devices: 28 us -> 13 us
    all_to_all x0 -> x1, blocking collectives: none -> 40.9 us  [local(): lax.all_to_all(wide.reshape(owners, capacity, columns + meta_width), ('ch...]
    all_to_all x2 -> x0, waiting for transfers between devices: 30.2 us -> none  [the longest x1 28.1 us: local(): lax.all_to_all(outgoing.reshape(owners, capacity, columns), ('chip', 'cor...]
    all_to_all x2 -> x0, starting transfers between devices: 14.9 us -> none  [the longest x1 9.6 us: local(): lax.all_to_all(places_info, ('chip', 'core'), split_axis=0, concat_axis=0...]
    unnamed x13 -> x15, local copies, waits for them, and re-layouts: 6.68 us -> 7.47 us
  transfers between devices with their start and end apart: 8 -> 6, of which waited for: 7 -> 5; matrix products, arithmetic and copies ran while one was open for 9% -> 9% of each run, Pallas kernels for 4% -> 4%
where the time goes in v11:
time: 338 us; the launch traced here: 337 us
  waiting for transfers between devices  179 us (53%)
  local copies, waits for them, and re-layouts  42.4 us (13%)
  blocking collectives  40.9 us (12%)
  other arithmetic  17.3 us (5%)
  between operations  15.3 us (5%)
  Pallas kernels  14.7 us (4%)
  matrix products  14.1 us (4%)
  starting transfers between devices  13 us (4%)
    all_gather x1, waiting for transfers between devices, local(): context_all = lax.all_gather(context, 'mp', axis=1, tiled=True)  52.9 us
    all_gather x1, waiting for transfers between devices, local(): routed = lax.all_gather(routed_part, 'mp', axis=1, tiled=True)  45.4 us
    all_gather x1, waiting for transfers between devices, local(): lax.all_gather(kv_own[half:], ('chip', 'core'), axis=0, tiled=True)  40.9 us
    all_to_all x1, blocking collectives, local(): lax.all_to_all(wide.reshape(owners, capacity, columns + meta_width), ('ch...  40.9 us
    all_to_all x1, waiting for transfers between devices, local(): lax.all_to_all(backward, ('chip', 'core'), split_axis=0, concat_axis=0, t...  28.3 us
    pallas_call x2, Pallas kernels, flash_pass(): pl.pallas_call(functools.partial(flash_kernel, final), grid_spec=grid_spe...  14.7 us
    all_gather x1, waiting for transfers between devices, local(): kv_low = lax.all_gather(kv_own[:half], ('chip', 'core'), axis=0, tiled=True)  11 us
    all_to_all x1, starting transfers between devices, local(): lax.all_to_all(backward, ('chip', 'core'), split_axis=0, concat_axis=0, t...  7.7 us
  transfers between devices with their start and end apart: 6, of which 5 were waited for; matrix products, arithmetic and copies ran while one was open for 9% of the time, Pallas kernels for 4%

profile of v11, /device:TPU:1, one launch (start us, length us, event | category | flops | bytes accessed | tf_op | source)
XLA Modules:
  0.0 336.7 jit_solution(6773545087789432390)
XLA Ops:
  6.5 1.0 convert_reduce_fusion
  7.6 0.6 slice.57
  8.8 1.3 fusion.39
  10.2 0.7 add_select_fusion.2
  10.9 1.2 reduce-window.6
  12.0 0.2 slice_reduce_fusion
  12.4 2.4 scatter_custom_fusion.1
  15.7 0.2 copy.36
  15.9 3.9 %scatter_custom_fusion = bf16[1024,1024]{1,0:T(8,128)(2,1)S(1)} fusion(s32[512]{0:T(512)S(1)} %compare_select_fusion.2, bf16[512,1024]{1,0:T(8,128)(2,1)} %param.8, bf16[]{:T(256)} %constant.117.clone.1), kind=kCustom, calls=%fused_computation.18 | custom fusion | bytes 2097664 | tf_op jit(solution)/shard_map/scatter | solution.py:175
  19.8 0.2 fusion.4
  20.0 40.9 %all_to_all.15 = bf16[32,32,1152]{2,1,0:T(8,128)(2,1)S(1)} all-to-all(bf16[32,32,1152]{2,1,0:T(8,128)(2,1)S(1)} %bitcast.57), channel_id=1, replica_groups=mesh['chip'=16,'core'=2,'mp'=4] {'chip','core'}, dimensions={0} | all-to-all | bytes 4718592 | tf_op jit(solution)/shard_map/all_to_all | solution.py:200
  60.9 0.8 copy-done.1
  61.7 0.8 fusion.8
  62.6 1.7 slice.80
  64.3 6.9 %scatter_custom_fusion.2 = bf16[512,1024]{1,0:T(8,128)(2,1)} fusion(s32[1024]{0:T(1024)S(1)} %bitcast.64, bf16[1024,1024]{1,0:T(8,128)(2,1)} %bitcast.59, bf16[]{:T(256)} %constant.117.clone.1), kind=kCustom, calls=%fused_computation.26 | custom fusion | bytes 1049088 | tf_op jit(solution)/shard_map/scatter | solution.py:217
  71.2 0.2 all-gather.9.cloned.1.call-start
  71.4 45.4 %all-gather.5.cloned.1.call-done = bf16[512,4096]{1,0:T(8,128)(2,1)} async-done(((bf16[512,1024]{1,0:T(8,128)(2,1)}), bf16[512,4096]{1,0:T(8,128)(2,1)}) %all-gather.5.cloned.1.call-update) | async-done | bytes 4194320 | tf_op jit(solution)/shard_map/all_gather | solution.py:219
  116.8 3.2 fusion
  120.0 0.2 copy-done.2
  120.2 1.3 convolution_bitcast_fusion
  121.5 1.2 fusion.20
  122.8 1.3 convolution_convert_fusion
  124.2 0.7 fusion.38
  125.0 0.7 all-gather.7.cloned.1.call-update
  125.7 6.5 %copy.39 = bf16[512,4096]{0,1:T(8,128)(2,1)} copy(bf16[512,4096]{1,0:T(8,128)(2,1)} %param.15) | data formatting | bytes 8388608 | tf_op args[7]
  132.2 6.3 %copy.40 = bf16[512,4,1024]{2,0,1:T(8,128)(2,1)} copy(bf16[512,4,1024]{0,2,1:T(8,128)(2,1)} %bitcast.56) | data formatting | bytes 8388608 | tf_op jit(solution)/shard_map/reshape | solution.py:260
  138.5 5.0 %all-to-all-start.1 = ((bf16[4,512,1024]{2,1,0:T(8,128)(2,1)}), bf16[4,512,1024]{2,1,0:T(8,128)(2,1)}, u32[]{:S(2)}, u32[]{:S(2)}) async-start(bf16[4,512,1024]{2,1,0:T(8,128)(2,1)} %bitcast.55), calls=%async_computation.1 | async-start | bytes 8388608 | tf_op jit(solution)/shard_map/all_to_all | solution.py:261
  143.6 0.6 iota_add_fusion.refs_4_
  144.2 0.5 multiply_cosine_fusion.1
  144.7 2.2 compare_reduce_fusion
  146.9 1.7 fusion.24
  148.7 0.7 fusion.32
  150.0 1.7 fusion.37
  151.7 1.2 stack.42.span_ref
  152.9 1.2 stack.41.span_ref
  154.1 6.3 %fusion.35 = f32[512,512]{0,1:T(8,128)S(1)} fusion(bf16[4096,512]{1,0:T(8,128)(2,1)} %param.12, bf16[512,4096]{1,0:T(8,128)(2,1)} %all-gather.5.cloned.1.call-done, f32[4096]{0:T(1024)S(1)} %copy-done.6, f32[512]{0:T(512)S(1)} %add_rsqrt_fusion), kind=kOutput, calls=%fused_computation.88 | convolution fusion | flops 2155872256 | bytes 9455616 | tf_op jit(solution)/shard_map/dot_general | solution.py:224
  160.3 0.2 subtract_convert_fusion
  160.5 0.9 maximum_bitcast_fusion.refs_0_
  161.4 11.0 %all-gather.9.cloned.1.call-done.refs_1_.refs_2_ = bf16[8192,256]{1,0:T(8,128)(2,1)} async-done(((bf16[256,256]{1,0:T(8,128)(2,1)}), bf16[8192,256]{1,0:T(8,128)(2,1)}) %all-gather.9.cloned.1.call-update) | async-done | bytes 4194320 | tf_op jit(solution)/shard_map/all_gather | solution.py:235
  172.4 7.1 %shard_map.82 = (f32[4,1,512]{2,1,0:T(1,128)}, f32[4,1,512]{2,1,0:T(1,128)}, f32[4,128,512]{2,1,0:T(8,128)}) custom-call(s32[6]{0:T(128)} %stack.42.span_ref, bf16[4,128,512]{2,1,0:T(8,128)(2,1)} %maximum_bitcast_fusion.refs_0_, bf16[8192,256]{1,0:T(8,128)(2,1)} %all-gather.9.cloned.1.call-done.refs_1_.refs_2_, ...), custom_call_target="tpu_custom_call" | custom-call | flops 4831838208 | bytes 3407872 | tf_op jit(solution)/shard_map/pallas_call | solution.py:151
  179.5 40.9 %all-gather.7.cloned.1.call-done.refs_1_.refs_2_ = bf16[8192,256]{1,0:T(8,128)(2,1)} async-done(((bf16[256,256]{1,0:T(8,128)(2,1)}), bf16[8192,256]{1,0:T(8,128)(2,1)}) %all-gather.7.cloned.1.call-update) | async-done | bytes 4194320 | tf_op jit(solution)/shard_map/all_gather | solution.py:236
  220.4 7.6 %shard_map.83 = bf16[4,128,512]{2,1,0:T(8,128)(2,1)} custom-call(s32[6]{0:T(128)} %stack.41.span_ref, bf16[4,128,512]{2,1,0:T(8,128)(2,1)} %maximum_bitcast_fusion.refs_0_, bf16[8192,256]{1,0:T(8,128)(2,1)} %all-gather.7.cloned.1.call-done.refs_1_.refs_2_, bf16[8192,256]{1,0:T(8,128)(2,1)} %all-gather.7.cloned.1.call-done.refs_1_.refs_2_, ...), custom_call_target="tpu_custom_call" | custom-call | flops 4831838208 | bytes 3407872 | tf_op jit(solution)/shard_map/pallas_call | solution.py:151
  228.0 52.9 %all-gather.11.cloned.1.call-done = bf16[512,2048]{0,1:T(8,128)(2,1)} async-done(((bf16[512,512]{0,1:T(8,128)(2,1)}), bf16[512,2048]{0,1:T(8,128)(2,1)}) %all-gather.11.cloned.1.call-update) | async-done | bytes 2097168 | tf_op jit(solution)/shard_map/all_gather | solution.py:258
  280.9 5.2 %fusion.5 = bf16[512,1024]{1,0:T(8,128)(2,1)S(1)} fusion(bf16[512,1024]{1,0:T(8,128)(2,1)S(1)} %copy-done.3, bf16[512,4,512]{0,2,1:T(8,128)(2,1)} %bitcast.67, bf16[4,512,1024]{2,1,0:T(8,128)(2,1)} %all-to-all-done.1), kind=kOutput, calls=%fused_computation.14 | convolution fusion | flops 2149056512 | bytes 8388608 | tf_op jit(solution)/shard_map/tsr,src->tc/dot_general | solution.py:262
  286.0 5.4 %gather_fusion = bf16[1024,1024]{1,0:T(8,128)(2,1)} fusion(bf16[512,1024]{1,0:T(8,128)(2,1)S(1)} %fusion.5, s32[1024]{0:T(1024)S(1)} %broadcast_clamp_fusion), kind=kCustom, calls=%fused_computation | custom fusion | bytes 4198400 | tf_op jit(solution)/shard_map/gather | solution.py:269
  291.4 7.7 %all-to-all-start.2 = ((bf16[32,32,1024]{2,1,0:T(8,128)(2,1)}), bf16[32,32,1024]{2,1,0:T(8,128)(2,1)S(1)}, u32[]{:S(2)}, u32[]{:S(2)}) async-start(bf16[32,32,1024]{2,1,0:T(8,128)(2,1)} %bitcast.58), calls=%async_computation.2 | async-start | bytes 4194304 | tf_op jit(solution)/shard_map/all_to_all | solution.py:270
  299.1 28.3 %all-to-all-done.2 = bf16[32,32,1024]{2,1,0:T(8,128)(2,1)S(1)} async-done(((bf16[32,32,1024]{2,1,0:T(8,128)(2,1)}), bf16[32,32,1024]{2,1,0:T(8,128)(2,1)S(1)}, u32[]{:S(2)}, u32[]{:S(2)}) %all-to-all-start.2) | async-done | bytes 2097184 | tf_op jit(solution)/shard_map/all_to_all | solution.py:270
  327.4 2.8 gather_fusion.1
  (40 shorter events, 0.7 us)
Async XLA Ops:
  6.5 113.5 %copy-start = (bf16[4096,128]{1,0:T(8,128)(2,1)S(1)}, bf16[4096,128]{1,0:T(8,128)(2,1)}, u32[]{:S(2)}) copy-start(bf16[4096,128]{1,0:T(8,128)(2,1)} %param.13) | copy-start | bytes 3145732
  6.5 110.3 %all-gather.5.cloned.1.call-start = ((), (), s32[]{:S(2)}) async-start(), calls=%async_computation.3 | async-start | bytes 5242880 | tf_op jit(solution)/shard_map/all_gather | solution.py:219
  60.9 0.8 copy-start.1
  64.2 55.8 %copy-start.6 = (f32[4096]{0:T(1024)S(1)}, f32[4096]{0:T(1024)}, u32[]{:S(2)}) copy-start(f32[4096]{0:T(1024)} %param.11) | copy-start | bytes 49156
  71.2 101.2 %all-gather.9.cloned.1.call-start = ((), (), s32[]{:S(2)}) async-start(), calls=%async_computation.5 | async-start | bytes 4325376 | tf_op jit(solution)/shard_map/all_gather | solution.py:235
  116.8 3.4 %copy-start.2 = (bf16[512,4096]{1,0:T(8,128)(2,1)S(1)}, bf16[512,4096]{1,0:T(8,128)(2,1)}, u32[]{:S(2)}) copy-start(bf16[512,4096]{1,0:T(8,128)(2,1)} %all-gather.5.cloned.1.call-done) | copy-start | bytes 12582916
  120.2 2.5 copy-start.5
  125.0 95.4 %all-gather.7.cloned.1.call-start = ((), (), s32[]{:S(2)}) async-start(), calls=%async_computation.4 | async-start | bytes 4325376 | tf_op jit(solution)/shard_map/all_gather | solution.py:236
  138.5 11.4 %copy-start.4 = (s32[512]{0:T(512)S(1)}, s32[512]{0:T(512)}, u32[]{:S(2)}) copy-start(s32[512]{0:T(512)} %param.10) | copy-start | bytes 6148
  138.5 89.5 %all-to-all-start.1 = ((bf16[4,512,1024]{2,1,0:T(8,128)(2,1)}), bf16[4,512,1024]{2,1,0:T(8,128)(2,1)}, u32[]{:S(2)}, u32[]{:S(2)}) async-start(bf16[4,512,1024]{2,1,0:T(8,128)(2,1)} %bitcast.55), calls=%async_computation.1 | async-start | bytes 8388608 | tf_op jit(solution)/shard_map/all_to_all | solution.py:261
  143.5 137.3 %all-gather.11.cloned.1.call-start = ((), (), s32[]{:S(2)}) async-start(), calls=%async_computation.6 | async-start | bytes 2621440 | tf_op jit(solution)/shard_map/all_gather | solution.py:258
  220.4 60.5 %copy-start.3 = (bf16[512,1024]{1,0:T(8,128)(2,1)S(1)}, bf16[512,1024]{1,0:T(8,128)(2,1)}, u32[]{:S(2)}) copy-start(bf16[512,1024]{1,0:T(8,128)(2,1)} %scatter_custom_fusion.2) | copy-start | bytes 3145732
  291.4 36.0 %all-to-all-start.2 = ((bf16[32,32,1024]{2,1,0:T(8,128)(2,1)}), bf16[32,32,1024]{2,1,0:T(8,128)(2,1)S(1)}, u32[]{:S(2)}, u32[]{:S(2)}) async-start(bf16[32,32,1024]{2,1,0:T(8,128)(2,1)} %bitcast.58), calls=%async_computation.2 | async-start | bytes 4194304 | tf_op jit(solution)/shard_map/all_to_all | solution.py:270
Sparse Core Ops, SparseCore 0:
  71.3 45.4 all-gather.4
  125.1 47.2 all-gather.8
  174.6 45.6 all-gather.6
  228.1 52.7 all-gather.10

commit v12 on v11

--- a/solution.py
+++ b/solution.py
@@ -250,21 +250,32 @@
     state = flash_pass(
         span_for(0), queries_t, kv_low, row_start[None, :], row_index[None, :], half, max_blocks, None
     )
-    context_t = flash_pass(
-        span_for(half), queries_t, kv_high, row_start[None, :], row_index[None, :], half, max_blocks,
-        state,
-    )
-    context = jnp.transpose(context_t, (2, 0, 1)).reshape(tok_dev, heads_dev * HD)
-    context_all = lax.all_gather(context, "mp", axis=1, tiled=True)
+    head_groups = 2
+    group = heads_dev // head_groups
     mp_size = lax.axis_size("mp")
     w_split = jnp.transpose(w_out.reshape(w_out.shape[0], mp_size, -1), (1, 0, 2))
     w_cols = lax.all_to_all(w_split, "mp", split_axis=0, concat_axis=0, tiled=True)
-    summed = jnp.einsum(
-        "tsr,src->tc",
-        context_all.reshape(tok_dev, mp_size, -1),
-        w_cols,
-        preferred_element_type=jnp.float32,
-    )
+    w_groups = [
+        w_cols.reshape(mp_size, head_groups, group * HD, w_cols.shape[2])[:, g]
+        for g in range(head_groups)
+    ]
+    w_groups, state = lax.optimization_barrier((w_groups, state))
+    summed = None
+    for g in range(head_groups):
+        heads_g = slice(g * group, (g + 1) * group)
+        context_t = flash_pass(
+            span_for(half), queries_t[heads_g], kv_high, row_start[None, :], row_index[None, :], half,
+            max_blocks, tuple(x[heads_g] for x in state),
+        )
+        context = jnp.transpose(context_t, (2, 0, 1)).reshape(tok_dev, group * HD)
+        context_all = lax.all_gather(context, "mp", axis=1, tiled=True)
+        part = jnp.einsum(
+            "tsr,src->tc",
+            context_all.reshape(tok_dev, mp_size, -1),
+            w_groups[g],
+            preferred_element_type=jnp.float32,
+        )
+        summed = part if summed is None else summed + part
     attended = (routed_part.astype(jnp.float32) + summed).astype(jnp.bfloat16)
     backward = attended[jnp.minimum(arrived_rows, tok_dev - 1)].reshape(owners, capacity, columns)
     returned = lax.all_to_all(backward, ("chip", "core"), split_axis=0, concat_axis=0, tiled=True)

time: 338 us -> 362 us (1.071)
  local copies, waits for them, and re-layouts: 42.4 us -> 52.8 us
  waiting for transfers between devices: 179 us -> 189 us
    all_to_all x1, waiting for transfers between devices: 0.01 us -> 37.3 us  [local(): lax.all_to_all(w_split, 'mp', split_axis=0, concat_axis=0, tiled=True)]
    all_gather x1, waiting for transfers between devices: 40.9 us -> 8.46 us  [local(): lax.all_gather(kv_own[half:], ('chip', 'core'), axis=0, tiled=True)]
    all_gather x1 -> x2, waiting for transfers between devices: 52.9 us -> 69.2 us  [local(): context_all = lax.all_gather(context, 'mp', axis=1, tiled=True)]
    all_gather x1, waiting for transfers between devices: 11 us -> 0.01 us  [local(): kv_low = lax.all_gather(kv_own[:half], ('chip', 'core'), axis=0, tiled=True)]
    all_to_all x0 -> x1, local copies, waits for them, and re-layouts: none -> 6.35 us  [local(): lax.all_to_all(w_split, 'mp', split_axis=0, concat_axis=0, tiled=True)]
    reshape x1 -> x0, local copies, waits for them, and re-layouts: 6.33 us -> none  [local(): w_out.reshape(w_out.shape[0], mp_size, -1)]
    slice x1 -> x4, local copies, waits for them, and re-layouts: 0.22 us -> 4.72 us  [the longest x2 3.63 us: local(): x[heads_g]]
    squeeze x0 -> x1, local copies, waits for them, and re-layouts: none -> 4.36 us  [local(): w_cols.reshape(mp_size, head_groups, group * HD, w_cols.shape[2])[:, g]]
  transfers between devices with their start and end apart: 6 -> 7, of which waited for: 5 -> 6; matrix products, arithmetic and copies ran while one was open for 9% -> 11% of each run, Pallas kernels for 4% -> 4%
where the time goes in v12:
time: 362 us; the launch traced here: 361 us
  waiting for transfers between devices  189 us (52%)
  local copies, waits for them, and re-layouts  52.8 us (15%)
  blocking collectives  40.9 us (11%)
  Pallas kernels  18.3 us (5%)
  other arithmetic  16.6 us (5%)
  between operations  15.3 us (4%)
  starting transfers between devices  14.2 us (4%)
  matrix products  13.1 us (4%)
    all_gather x2, waiting for transfers between devices, local(): context_all = lax.all_gather(context, 'mp', axis=1, tiled=True)  69.2 us
    all_gather x1, waiting for transfers between devices, local(): routed = lax.all_gather(routed_part, 'mp', axis=1, tiled=True)  45.4 us
    all_to_all x1, blocking collectives, local(): lax.all_to_all(wide.reshape(owners, capacity, columns + meta_width), ('ch...  40.9 us
    all_to_all x1, waiting for transfers between devices, local(): lax.all_to_all(w_split, 'mp', split_axis=0, concat_axis=0, tiled=True)  37.3 us
    all_to_all x1, waiting for transfers between devices, local(): lax.all_to_all(backward, ('chip', 'core'), split_axis=0, concat_axis=0, t...  28.3 us
    pallas_call x3, Pallas kernels, flash_pass(): pl.pallas_call(functools.partial(flash_kernel, final), grid_spec=grid_spe...  18.3 us
    unnamed x21, local copies, waits for them, and re-layouts  8.76 us
    all_to_all x1, starting transfers between devices, local(): lax.all_to_all(backward, ('chip', 'core'), split_axis=0, concat_axis=0, t...  8.61 us
  transfers between devices with their start and end apart: 7, of which 6 were waited for; matrix products, arithmetic and copies ran while one was open for 11% of the time, Pallas kernels for 4%

profile of v12, /device:TPU:1, one launch (start us, length us, event | category | flops | bytes accessed | tf_op | source)
XLA Modules:
  0.0 360.6 jit_solution(10185884817910657724)
XLA Ops:
  6.5 1.0 convert_reduce_fusion
  7.6 0.6 slice.87
  8.8 1.3 fusion.44
  10.2 0.7 add_select_fusion.2
  10.9 1.2 reduce-window.6
  12.4 2.4 scatter_custom_fusion.1
  15.9 3.9 %scatter_custom_fusion = bf16[1024,1024]{1,0:T(8,128)(2,1)S(1)} fusion(s32[512]{0:T(512)S(1)} %compare_select_fusion.2, bf16[512,1024]{1,0:T(8,128)(2,1)} %param.8, bf16[]{:T(256)} %constant.117.clone.1), kind=kCustom, calls=%fused_computation.21 | custom fusion | bytes 2097664 | tf_op jit(solution)/shard_map/scatter | solution.py:175
  20.0 40.9 %all_to_all.15 = bf16[32,32,1152]{2,1,0:T(8,128)(2,1)S(1)} all-to-all(bf16[32,32,1152]{2,1,0:T(8,128)(2,1)S(1)} %bitcast.73), channel_id=1, replica_groups=mesh['chip'=16,'core'=2,'mp'=4] {'chip','core'}, dimensions={0} | all-to-all | bytes 4718592 | tf_op jit(solution)/shard_map/all_to_all | solution.py:200
  60.9 0.8 copy-done.2
  61.7 0.8 fusion.9
  62.6 1.6 slice.120
  64.2 6.9 %scatter_custom_fusion.2 = bf16[512,1024]{1,0:T(8,128)(2,1)} fusion(s32[1024]{0:T(1024)S(1)} %bitcast.85, bf16[1024,1024]{1,0:T(8,128)(2,1)} %bitcast.75, bf16[]{:T(256)} %constant.117.clone.1), kind=kCustom, calls=%fused_computation.29 | custom fusion | bytes 1049088 | tf_op jit(solution)/shard_map/scatter | solution.py:217
  71.4 45.4 %all-gather.6.cloned.1.call-done = bf16[512,4096]{1,0:T(8,128)(2,1)} async-done(((bf16[512,1024]{1,0:T(8,128)(2,1)}), bf16[512,4096]{1,0:T(8,128)(2,1)}) %all-gather.6.cloned.1.call-update) | async-done | bytes 4194320 | tf_op jit(solution)/shard_map/all_gather | solution.py:219
  116.8 3.2 fusion
  120.2 1.3 convolution_bitcast_fusion
  121.5 1.2 fusion.21
  122.8 1.3 convolution_convert_fusion
  124.2 0.7 fusion.41
  125.0 0.7 all-gather.8.cloned.1.call-update
  125.7 6.5 %copy.40 = bf16[512,4096]{0,1:T(8,128)(2,1)} copy(bf16[512,4096]{1,0:T(8,128)(2,1)} %param.15) | data formatting | bytes 8388608 | tf_op args[7]
  132.3 5.1 %all-to-all-start.1 = ((bf16[4,512,1024]{1,2,0:T(8,128)(2,1)}), bf16[4,512,1024]{1,2,0:T(8,128)(2,1)}, u32[]{:S(2)}, u32[]{:S(2)}) async-start(bf16[4,512,1024]{1,2,0:T(8,128)(2,1)} %bitcast.71), calls=%async_computation.1 | async-start | bytes 8388608 | tf_op jit(solution)/shard_map/all_to_all | solution.py:257
  137.4 0.6 iota_add_fusion.refs_4_
  138.5 2.3 compare_reduce_fusion
  140.8 1.7 fusion.25
  142.5 0.6 fusion.33
  143.7 1.9 fusion.38
  145.6 1.3 stack.47.span_ref
  146.9 1.3 stack.46.span_ref
  148.2 37.3 %all-to-all-done.1 = bf16[4,512,1024]{1,2,0:T(8,128)(2,1)} async-done(((bf16[4,512,1024]{1,2,0:T(8,128)(2,1)}), bf16[4,512,1024]{1,2,0:T(8,128)(2,1)}, u32[]{:S(2)}, u32[]{:S(2)}) %all-to-all-start.1) | async-done | bytes 4194336 | tf_op jit(solution)/shard_map/all_to_all | solution.py:257
  185.5 6.3 %copy.41 = bf16[4,512,1024]{2,1,0:T(8,128)(2,1)} copy(bf16[4,512,1024]{1,2,0:T(8,128)(2,1)} %all-to-all-done.1) | data formatting | bytes 8388608 | tf_op jit(solution)/shard_map/all_to_all | solution.py:257
  191.9 4.4 %slice_bitcast_fusion = (bf16[4,256,1024]{2,1,0:T(8,128)(2,1)}, bf16[4,256,1024]{2,1,0:T(8,128)(2,1)S(1)}) fusion(bf16[4,2,256,1024]{3,2,1,0:T(8,128)(2,1)} %bitcast.72), kind=kLoop, calls=%fused_computation.13 | loop fusion | bytes 8388608 | tf_op jit(solution)/shard_map/squeeze | solution.py:259
  196.2 1.1 copy-done.7
  197.4 2.6 fusion.36
  200.2 0.9 fusion.40
  201.2 7.2 %shard_map.82 = (f32[4,1,512]{2,1,0:T(1,128)}, f32[4,1,512]{2,1,0:T(1,128)}, f32[4,128,512]{2,1,0:T(8,128)}) custom-call(s32[6]{0:T(128)} %stack.47.span_ref, bf16[4,128,512]{2,1,0:T(8,128)(2,1)} %copy-done.5, bf16[8192,256]{1,0:T(8,128)(2,1)} %all-gather.10.cloned.1.call-done.refs_1_.refs_2_, ...), custom_call_target="tpu_custom_call" | custom-call | flops 4831838208 | bytes 3407872 | tf_op jit(solution)/shard_map/pallas_call | solution.py:151
  208.3 1.3 fusion.42
  209.7 2.3 fusion.39
  212.0 8.5 %all-gather.8.cloned.1.call-done.refs_1_.refs_2_ = bf16[8192,256]{1,0:T(8,128)(2,1)} async-done(((bf16[256,256]{1,0:T(8,128)(2,1)}), bf16[8192,256]{1,0:T(8,128)(2,1)}) %all-gather.8.cloned.1.call-update) | async-done | bytes 4194320 | tf_op jit(solution)/shard_map/all_gather | solution.py:236
  220.4 5.6 %shard_map.83 = bf16[2,128,512]{2,1,0:T(8,128)(2,1)} custom-call(s32[6]{0:T(128)} %stack.46.span_ref, bf16[2,128,512]{2,1,0:T(8,128)(2,1)} %get-tuple-element.30.refs_0_, bf16[8192,256]{1,0:T(8,128)(2,1)} %all-gather.8.cloned.1.call-done.refs_1_.refs_2_, bf16[8192,256]{1,0:T(8,128)(2,1)} %all-gather.8.cloned.1.call-done.refs_1_.refs_2_, s32[1,512]{1,0:T(1,128)} %bitcast.82, ...), custom_call_target="tpu_custom_call" | custom-call | flops 2415919104 | bytes 2883584 | tf_op jit(solution)/shard_map/pallas_call | solution.py:151
  226.3 5.6 %shard_map.84 = bf16[2,128,512]{2,1,0:T(8,128)(2,1)} custom-call(s32[6]{0:T(128)} %stack.46.span_ref, bf16[2,128,512]{2,1,0:T(8,128)(2,1)} %get-tuple-element.29.refs_0_, bf16[8192,256]{1,0:T(8,128)(2,1)} %all-gather.8.cloned.1.call-done.refs_1_.refs_2_, bf16[8192,256]{1,0:T(8,128)(2,1)} %all-gather.8.cloned.1.call-done.refs_1_.refs_2_, s32[1,512]{1,0:T(1,128)} %bitcast.83, ...), custom_call_target="tpu_custom_call" | custom-call | flops 2415919104 | bytes 2883584 | tf_op jit(solution)/shard_map/pallas_call | solution.py:151
  231.9 47.2 %all-gather.12.cloned.1.call-done = bf16[512,1024]{0,1:T(8,128)(2,1)} async-done(((bf16[512,256]{0,1:T(8,128)(2,1)}), bf16[512,1024]{0,1:T(8,128)(2,1)}) %all-gather.12.cloned.1.call-update) | async-done | bytes 1048592 | tf_op jit(solution)/shard_map/all_gather | solution.py:271
  279.1 3.8 %fusion.45 = f32[512,1024,1]{1,0,2:T(8,128)} fusion(bf16[512,4,256]{0,2,1:T(8,128)(2,1)} %bitcast.76, bf16[4,256,1024]{2,1,0:T(8,128)(2,1)S(1)} %get-tuple-element.19), kind=kOutput, calls=%fused_computation.99 | convolution fusion | flops 1073741824 | bytes 5242880 | tf_op jit(solution)/shard_map/tsr,src->tc/dot_general | solution.py:272
  282.9 22.0 %all-gather.14.cloned.1.call-done = bf16[512,1024]{0,1:T(8,128)(2,1)} async-done(((bf16[512,256]{0,1:T(8,128)(2,1)}), bf16[512,1024]{0,1:T(8,128)(2,1)}) %all-gather.14.cloned.1.call-update) | async-done | bytes 1048592 | tf_op jit(solution)/shard_map/all_gather | solution.py:271
  304.9 4.1 %fusion.6 = bf16[512,1024]{1,0:T(8,128)(2,1)S(1)} fusion(f32[512,1024,1]{1,0,2:T(8,128)} %fusion.45, bf16[512,1024]{1,0:T(8,128)(2,1)} %scatter_custom_fusion.2, bf16[512,4,256]{0,2,1:T(8,128)(2,1)} %bitcast.86, bf16[4,256,1024]{2,1,0:T(8,128)(2,1)} %get-tuple-element.20), kind=kOutput, calls=%fused_computation.17 | convolution fusion | flops 1075838976 | bytes 7340032 | tf_op jit(solution)/shard_map/tsr,src->tc/dot_general | solution.py:272
  309.0 5.3 %gather_fusion = bf16[1024,1024]{1,0:T(8,128)(2,1)} fusion(bf16[512,1024]{1,0:T(8,128)(2,1)S(1)} %fusion.6, s32[1024]{0:T(1024)S(1)} %broadcast_clamp_fusion), kind=kCustom, calls=%fused_computation | custom fusion | bytes 4198400 | tf_op jit(solution)/shard_map/gather | solution.py:280
  314.3 8.6 %all-to-all-start.2 = ((bf16[32,32,1024]{2,1,0:T(8,128)(2,1)}), bf16[32,32,1024]{2,1,0:T(8,128)(2,1)S(1)}, u32[]{:S(2)}, u32[]{:S(2)}) async-start(bf16[32,32,1024]{2,1,0:T(8,128)(2,1)} %bitcast.74), calls=%async_computation.2 | async-start | bytes 4194304 | tf_op jit(solution)/shard_map/all_to_all | solution.py:281
  323.0 28.3 %all-to-all-done.2 = bf16[32,32,1024]{2,1,0:T(8,128)(2,1)S(1)} async-done(((bf16[32,32,1024]{2,1,0:T(8,128)(2,1)}), bf16[32,32,1024]{2,1,0:T(8,128)(2,1)S(1)}, u32[]{:S(2)}, u32[]{:S(2)}) %all-to-all-start.2) | async-done | bytes 2097184 | tf_op jit(solution)/shard_map/all_to_all | solution.py:281
  351.3 2.8 gather_fusion.1
  (55 shorter events, 2.9 us)
Async XLA Ops:
  6.5 113.5 %copy-start = (bf16[4096,128]{1,0:T(8,128)(2,1)S(1)}, bf16[4096,128]{1,0:T(8,128)(2,1)}, u32[]{:S(2)}) copy-start(bf16[4096,128]{1,0:T(8,128)(2,1)} %param.13) | copy-start | bytes 3145732
  6.5 110.2 %all-gather.6.cloned.1.call-start = ((), (), s32[]{:S(2)}) async-start(), calls=%async_computation.3 | async-start | bytes 5242880 | tf_op jit(solution)/shard_map/all_gather | solution.py:219
  60.9 0.8 copy-start.2
  64.2 55.8 %copy-start.9 = (f32[4096]{0:T(1024)S(1)}, f32[4096]{0:T(1024)}, u32[]{:S(2)}) copy-start(f32[4096]{0:T(1024)} %param.11) | copy-start | bytes 49156
  71.2 130.0 %all-gather.10.cloned.1.call-start = ((), (), s32[]{:S(2)}) async-start(), calls=%async_computation.5 | async-start | bytes 4325376 | tf_op jit(solution)/shard_map/all_gather | solution.py:235
  116.8 3.4 copy-start.3
  120.2 2.5 copy-start.8
  125.0 95.4 %all-gather.8.cloned.1.call-start = ((), (), s32[]{:S(2)}) async-start(), calls=%async_computation.4 | async-start | bytes 4325376 | tf_op jit(solution)/shard_map/all_gather | solution.py:236
  132.3 11.5 %copy-start.6 = (s32[512]{0:T(512)S(1)}, s32[512]{0:T(512)}, u32[]{:S(2)}) copy-start(s32[512]{0:T(512)} %param.10) | copy-start | bytes 6148
  132.3 53.3 %all-to-all-start.1 = ((bf16[4,512,1024]{1,2,0:T(8,128)(2,1)}), bf16[4,512,1024]{1,2,0:T(8,128)(2,1)}, u32[]{:S(2)}, u32[]{:S(2)}) async-start(bf16[4,512,1024]{1,2,0:T(8,128)(2,1)} %bitcast.71), calls=%async_computation.1 | async-start | bytes 8388608 | tf_op jit(solution)/shard_map/all_to_all | solution.py:257
  137.3 141.8 %all-gather.12.cloned.1.call-start = ((), (), s32[]{:S(2)}) async-start(), calls=%async_computation.6 | async-start | bytes 1310720 | tf_op jit(solution)/shard_map/all_gather | solution.py:271
  191.9 4.4 %copy-start.4 = (bf16[512,4096]{1,0:T(8,128)(2,1)S(1)}, bf16[512,4096]{1,0:T(8,128)(2,1)}, u32[]{:S(2)}) copy-start(bf16[512,4096]{1,0:T(8,128)(2,1)} %all-gather.6.cloned.1.call-done) | copy-start | bytes 12582916
  191.9 5.5 %copy-start.7 = (bf16[4096,512]{1,0:T(8,128)(2,1)S(1)}, bf16[4096,512]{1,0:T(8,128)(2,1)}, u32[]{:S(2)}) copy-start(bf16[4096,512]{1,0:T(8,128)(2,1)} %param.12) | copy-start | bytes 12582916
  200.2 1.0 copy-start.5
  226.0 78.9 %all-gather.14.cloned.1.call-start = ((), (), s32[]{:S(2)}) async-start(), calls=%async_computation.7 | async-start | bytes 1310720 | tf_op jit(solution)/shard_map/all_gather | solution.py:271
  314.3 36.9 %all-to-all-start.2 = ((bf16[32,32,1024]{2,1,0:T(8,128)(2,1)}), bf16[32,32,1024]{2,1,0:T(8,128)(2,1)S(1)}, u32[]{:S(2)}, u32[]{:S(2)}) async-start(bf16[32,32,1024]{2,1,0:T(8,128)(2,1)} %bitcast.74), calls=%async_computation.2 | async-start | bytes 4194304 | tf_op jit(solution)/shard_map/all_to_all | solution.py:281
  351.3 2.8 copy-start.1
Sparse Core Ops, SparseCore 0:
  71.3 45.4 all-gather.5
  125.1 47.2 all-gather.9
  174.7 45.7 all-gather.7
  226.1 52.9 all-gather.11
  280.6 24.2 all-gather.13

commit v13 on v11

--- a/solution.py
+++ b/solution.py
@@ -65,15 +65,19 @@
             l_sc[...] = jnp.zeros(l_sc.shape, jnp.float32)
             acc_sc[...] = jnp.zeros(acc_sc.shape, jnp.float32)
 
-    key_first = (span_ref[0] + step) * span_ref[4] + span_ref[5]
+    part = block // 2
+    pair = span_ref[0] // 2 + step
+    key_first = 2 * pair * span_ref[4] + span_ref[5]
+    key_last = (2 * pair + 1) * span_ref[4] + span_ref[5] + part - 1
     active = step < span_ref[1]
-    whole = (key_first >= span_ref[2]) & (key_first + block - 1 <= span_ref[3])
+    whole = (key_first >= span_ref[2]) & (key_last <= span_ref[3])
 
     def accumulate(masked):
         keys = k_ref[...]
         values = v_ref[...]
         if masked:
-            key_rows = key_first + lax.broadcasted_iota(jnp.int32, (block, 1), 0)
+            sub = lax.broadcasted_iota(jnp.int32, (block, 1), 0)
+            key_rows = key_first + (sub // part) * span_ref[4] + sub % part
             allowed = (key_rows >= start_ref[...]) & (key_rows <= row_ref[...])
         for h in range(heads):
             scores = jnp.dot(keys, q_ref[h], preferred_element_type=jnp.float32) * scale
@@ -111,15 +115,15 @@
 
     def kv_map(column):
         def index_map(step, span_ref):
-            return (span_ref[0] + jnp.minimum(step, span_ref[1] - 1), column)
+            return (span_ref[0] // 2 + jnp.minimum(step, span_ref[1] - 1), column)
         return index_map
 
     fixed2 = lambda step, span_ref: (0, 0)
     fixed3 = lambda step, span_ref: (0, 0, 0)
     in_specs = [
         pl.BlockSpec((heads, HD, rows), fixed3),
-        pl.BlockSpec((block, HD), kv_map(0)),
-        pl.BlockSpec((block, HD), kv_map(1)),
+        pl.BlockSpec((2 * block, HD), kv_map(0)),
+        pl.BlockSpec((2 * block, HD), kv_map(1)),
         pl.BlockSpec((1, rows), fixed2),
         pl.BlockSpec((1, rows), fixed2),
     ]
@@ -147,7 +151,7 @@
         out_specs=out_specs,
         scratch_shapes=scratch,
     )
-    flops = 4 * heads * rows * block * HD * max_blocks
+    flops = 8 * heads * rows * block * HD * max_blocks
     return pl.pallas_call(
         functools.partial(flash_kernel, final),
         grid_spec=grid_spec,
@@ -155,8 +159,8 @@
         compiler_params=pltpu.CompilerParams(dimension_semantics=("arbitrary",)),
         cost_estimate=pl.CostEstimate(
             flops=flops,
-            transcendentals=heads * rows * block * max_blocks,
-            bytes_accessed=2 * block * HD * 2 * max_blocks + 2 * 2 * rows * heads * HD,
+            transcendentals=2 * heads * rows * block * max_blocks,
+            bytes_accessed=4 * block * HD * 2 * max_blocks + 2 * 2 * rows * heads * HD,
         ),
     )(*operands)
 
@@ -239,19 +243,20 @@
     last_block = (block_first + tok_dev - 1) // block
     first_block = doc_low // block
     max_blocks = min((tok_dev - 1) // block + -(-(DOC_MAX - 1) // block) + 1, owners * tok_dev // block)
+    max_pairs = min(max_blocks // 2 + 1, owners * tok_dev // block // 2)
     max_start = jnp.max(row_start)
 
     def span_for(offset):
         return jnp.stack(
-            [first_block, last_block - first_block + 1, max_start, block_first, block, offset]
+            [first_block, last_block // 2 - first_block // 2 + 1, max_start, block_first, block, offset]
         ).astype(jnp.int32)
 
     queries_t = jnp.transpose(queries.reshape(tok_dev, heads_dev, HD), (1, 2, 0))
     state = flash_pass(
-        span_for(0), queries_t, kv_low, row_start[None, :], row_index[None, :], half, max_blocks, None
+        span_for(0), queries_t, kv_low, row_start[None, :], row_index[None, :], half, max_pairs, None
     )
     context_t = flash_pass(
-        span_for(half), queries_t, kv_high, row_start[None, :], row_index[None, :], half, max_blocks,
+        span_for(half), queries_t, kv_high, row_start[None, :], row_index[None, :], half, max_pairs,
         state,
     )
     context = jnp.transpose(context_t, (2, 0, 1)).reshape(tok_dev, heads_dev * HD)

time: 338 us -> 333 us (0.985)
    all_gather x1, waiting for transfers between devices: 52.9 us -> 48.7 us  [local(): context_all = lax.all_gather(context, 'mp', axis=1, tiled=True)]
where the time goes in v13:
time: 333 us; the launch traced here: 331 us
  waiting for transfers between devices  176 us (53%)
  local copies, waits for them, and re-layouts  42.4 us (13%)
  blocking collectives  40.9 us (12%)
  other arithmetic  17.3 us (5%)
  between operations  15.4 us (5%)
  matrix products  14.1 us (4%)
  starting transfers between devices  13 us (4%)
  Pallas kernels  12.8 us (4%)
    all_gather x1, waiting for transfers between devices, local(): context_all = lax.all_gather(context, 'mp', axis=1, tiled=True)  48.7 us
    all_gather x1, waiting for transfers between devices, local(): routed = lax.all_gather(routed_part, 'mp', axis=1, tiled=True)  45.4 us
    all_gather x1, waiting for transfers between devices, local(): lax.all_gather(kv_own[half:], ('chip', 'core'), axis=0, tiled=True)  41.7 us
    all_to_all x1, blocking collectives, local(): lax.all_to_all(wide.reshape(owners, capacity, columns + meta_width), ('ch...  40.9 us
    all_to_all x1, waiting for transfers between devices, local(): lax.all_to_all(backward, ('chip', 'core'), split_axis=0, concat_axis=0, t...  28.3 us
    pallas_call x2, Pallas kernels, flash_pass(): pl.pallas_call(functools.partial(flash_kernel, final), grid_spec=grid_spe...  12.8 us
    all_gather x1, waiting for transfers between devices, local(): kv_low = lax.all_gather(kv_own[:half], ('chip', 'core'), axis=0, tiled=True)  11 us
    all_to_all x1, starting transfers between devices, local(): lax.all_to_all(backward, ('chip', 'core'), split_axis=0, concat_axis=0, t...  7.7 us
  transfers between devices with their start and end apart: 6, of which 5 were waited for; matrix products, arithmetic and copies ran while one was open for 9% of the time, Pallas kernels for 4%

profile of v13, /device:TPU:1, one launch (start us, length us, event | category | flops | bytes accessed | tf_op | source)
XLA Modules:
  0.0 331.4 jit_solution(5943465675069533444)
XLA Ops:
  6.5 1.0 convert_reduce_fusion
  7.6 0.6 slice.57
  8.8 1.3 fusion.39
  10.2 0.7 add_select_fusion.2
  10.9 1.2 reduce-window.6
  12.0 0.2 slice_reduce_fusion
  12.4 2.4 scatter_custom_fusion.1
  15.7 0.2 copy.36
  15.9 3.9 %scatter_custom_fusion = bf16[1024,1024]{1,0:T(8,128)(2,1)S(1)} fusion(s32[512]{0:T(512)S(1)} %compare_select_fusion.2, bf16[512,1024]{1,0:T(8,128)(2,1)} %param.8, bf16[]{:T(256)} %constant.136.clone.1), kind=kCustom, calls=%fused_computation.18 | custom fusion | bytes 2097664 | tf_op jit(solution)/shard_map/scatter | solution.py:179
  19.8 0.2 fusion.4
  20.0 40.9 %all_to_all.15 = bf16[32,32,1152]{2,1,0:T(8,128)(2,1)S(1)} all-to-all(bf16[32,32,1152]{2,1,0:T(8,128)(2,1)S(1)} %bitcast.57), channel_id=1, replica_groups=mesh['chip'=16,'core'=2,'mp'=4] {'chip','core'}, dimensions={0} | all-to-all | bytes 4718592 | tf_op jit(solution)/shard_map/all_to_all | solution.py:204
  60.9 0.8 copy-done.1
  61.7 0.8 fusion.8
  62.6 1.7 slice.80
  64.3 6.9 %scatter_custom_fusion.2 = bf16[512,1024]{1,0:T(8,128)(2,1)} fusion(s32[1024]{0:T(1024)S(1)} %bitcast.64, bf16[1024,1024]{1,0:T(8,128)(2,1)} %bitcast.59, bf16[]{:T(256)} %constant.136.clone.1), kind=kCustom, calls=%fused_computation.26 | custom fusion | bytes 1049088 | tf_op jit(solution)/shard_map/scatter | solution.py:221
  71.2 0.2 all-gather.9.cloned.1.call-start
  71.4 45.4 %all-gather.5.cloned.1.call-done = bf16[512,4096]{1,0:T(8,128)(2,1)} async-done(((bf16[512,1024]{1,0:T(8,128)(2,1)}), bf16[512,4096]{1,0:T(8,128)(2,1)}) %all-gather.5.cloned.1.call-update) | async-done | bytes 4194320 | tf_op jit(solution)/shard_map/all_gather | solution.py:223
  116.8 3.2 fusion
  120.0 0.2 copy-done.2
  120.2 1.3 convolution_bitcast_fusion
  121.5 1.2 fusion.20
  122.8 1.3 convolution_convert_fusion
  124.2 0.7 fusion.38
  125.0 0.7 all-gather.7.cloned.1.call-update
  125.7 6.5 %copy.39 = bf16[512,4096]{0,1:T(8,128)(2,1)} copy(bf16[512,4096]{1,0:T(8,128)(2,1)} %param.15) | data formatting | bytes 8388608 | tf_op args[7]
  132.2 6.3 %copy.40 = bf16[512,4,1024]{2,0,1:T(8,128)(2,1)} copy(bf16[512,4,1024]{0,2,1:T(8,128)(2,1)} %bitcast.56) | data formatting | bytes 8388608 | tf_op jit(solution)/shard_map/reshape | solution.py:265
  138.5 5.0 %all-to-all-start.1 = ((bf16[4,512,1024]{2,1,0:T(8,128)(2,1)}), bf16[4,512,1024]{2,1,0:T(8,128)(2,1)}, u32[]{:S(2)}, u32[]{:S(2)}) async-start(bf16[4,512,1024]{2,1,0:T(8,128)(2,1)} %bitcast.55), calls=%async_computation.1 | async-start | bytes 8388608 | tf_op jit(solution)/shard_map/all_to_all | solution.py:266
  143.6 0.6 iota_add_fusion.refs_4_
  144.2 0.5 multiply_cosine_fusion.1
  144.7 2.2 compare_reduce_fusion
  146.9 1.7 fusion.24
  148.7 0.7 fusion.32
  150.0 1.7 fusion.37
  151.8 1.2 stack.42.span_ref
  152.9 1.2 stack.41.span_ref
  154.1 6.3 %fusion.35 = f32[512,512]{0,1:T(8,128)S(1)} fusion(bf16[4096,512]{1,0:T(8,128)(2,1)} %param.12, bf16[512,4096]{1,0:T(8,128)(2,1)} %all-gather.5.cloned.1.call-done, f32[4096]{0:T(1024)S(1)} %copy-done.6, f32[512]{0:T(512)S(1)} %add_rsqrt_fusion), kind=kOutput, calls=%fused_computation.88 | convolution fusion | flops 2155872256 | bytes 9455616 | tf_op jit(solution)/shard_map/dot_general | solution.py:228
  160.4 0.2 subtract_convert_fusion
  160.6 0.9 maximum_bitcast_fusion.refs_0_
  161.4 11.0 %all-gather.9.cloned.1.call-done.refs_1_.refs_2_ = bf16[8192,256]{1,0:T(8,128)(2,1)} async-done(((bf16[256,256]{1,0:T(8,128)(2,1)}), bf16[8192,256]{1,0:T(8,128)(2,1)}) %all-gather.9.cloned.1.call-update) | async-done | bytes 4194320 | tf_op jit(solution)/shard_map/all_gather | solution.py:239
  172.4 6.3 %shard_map.82 = (f32[4,1,512]{2,1,0:T(1,128)}, f32[4,1,512]{2,1,0:T(1,128)}, f32[4,128,512]{2,1,0:T(8,128)}) custom-call(s32[6]{0:T(128)} %stack.42.span_ref, bf16[4,128,512]{2,1,0:T(8,128)(2,1)} %maximum_bitcast_fusion.refs_0_, bf16[8192,256]{1,0:T(8,128)(2,1)} %all-gather.9.cloned.1.call-done.refs_1_.refs_2_, ...), custom_call_target="tpu_custom_call" | custom-call | flops 5368709120 | bytes 3670016 | tf_op jit(solution)/shard_map/pallas_call | solution.py:155
  178.7 41.7 %all-gather.7.cloned.1.call-done.refs_1_.refs_2_ = bf16[8192,256]{1,0:T(8,128)(2,1)} async-done(((bf16[256,256]{1,0:T(8,128)(2,1)}), bf16[8192,256]{1,0:T(8,128)(2,1)}) %all-gather.7.cloned.1.call-update) | async-done | bytes 4194320 | tf_op jit(solution)/shard_map/all_gather | solution.py:240
  220.4 6.5 %shard_map.83 = bf16[4,128,512]{2,1,0:T(8,128)(2,1)} custom-call(s32[6]{0:T(128)} %stack.41.span_ref, bf16[4,128,512]{2,1,0:T(8,128)(2,1)} %maximum_bitcast_fusion.refs_0_, bf16[8192,256]{1,0:T(8,128)(2,1)} %all-gather.7.cloned.1.call-done.refs_1_.refs_2_, bf16[8192,256]{1,0:T(8,128)(2,1)} %all-gather.7.cloned.1.call-done.refs_1_.refs_2_, ...), custom_call_target="tpu_custom_call" | custom-call | flops 5368709120 | bytes 3670016 | tf_op jit(solution)/shard_map/pallas_call | solution.py:155
  226.9 48.7 %all-gather.11.cloned.1.call-done = bf16[512,2048]{0,1:T(8,128)(2,1)} async-done(((bf16[512,512]{0,1:T(8,128)(2,1)}), bf16[512,2048]{0,1:T(8,128)(2,1)}) %all-gather.11.cloned.1.call-update) | async-done | bytes 2097168 | tf_op jit(solution)/shard_map/all_gather | solution.py:263
  275.6 5.2 %fusion.5 = bf16[512,1024]{1,0:T(8,128)(2,1)S(1)} fusion(bf16[512,1024]{1,0:T(8,128)(2,1)S(1)} %copy-done.3, bf16[512,4,512]{0,2,1:T(8,128)(2,1)} %bitcast.67, bf16[4,512,1024]{2,1,0:T(8,128)(2,1)} %all-to-all-done.1), kind=kOutput, calls=%fused_computation.14 | convolution fusion | flops 2149056512 | bytes 8388608 | tf_op jit(solution)/shard_map/tsr,src->tc/dot_general | solution.py:267
  280.8 5.4 %gather_fusion = bf16[1024,1024]{1,0:T(8,128)(2,1)} fusion(bf16[512,1024]{1,0:T(8,128)(2,1)S(1)} %fusion.5, s32[1024]{0:T(1024)S(1)} %broadcast_clamp_fusion), kind=kCustom, calls=%fused_computation | custom fusion | bytes 4198400 | tf_op jit(solution)/shard_map/gather | solution.py:274
  286.1 7.7 %all-to-all-start.2 = ((bf16[32,32,1024]{2,1,0:T(8,128)(2,1)}), bf16[32,32,1024]{2,1,0:T(8,128)(2,1)S(1)}, u32[]{:S(2)}, u32[]{:S(2)}) async-start(bf16[32,32,1024]{2,1,0:T(8,128)(2,1)} %bitcast.58), calls=%async_computation.2 | async-start | bytes 4194304 | tf_op jit(solution)/shard_map/all_to_all | solution.py:275
  293.9 28.3 %all-to-all-done.2 = bf16[32,32,1024]{2,1,0:T(8,128)(2,1)S(1)} async-done(((bf16[32,32,1024]{2,1,0:T(8,128)(2,1)}), bf16[32,32,1024]{2,1,0:T(8,128)(2,1)S(1)}, u32[]{:S(2)}, u32[]{:S(2)}) %all-to-all-start.2) | async-done | bytes 2097184 | tf_op jit(solution)/shard_map/all_to_all | solution.py:275
  322.1 2.8 gather_fusion.1
  (40 shorter events, 0.7 us)
Async XLA Ops:
  6.5 113.5 %copy-start = (bf16[4096,128]{1,0:T(8,128)(2,1)S(1)}, bf16[4096,128]{1,0:T(8,128)(2,1)}, u32[]{:S(2)}) copy-start(bf16[4096,128]{1,0:T(8,128)(2,1)} %param.13) | copy-start | bytes 3145732
  6.5 110.3 %all-gather.5.cloned.1.call-start = ((), (), s32[]{:S(2)}) async-start(), calls=%async_computation.3 | async-start | bytes 5242880 | tf_op jit(solution)/shard_map/all_gather | solution.py:223
  60.9 0.8 copy-start.1
  64.2 55.8 %copy-start.6 = (f32[4096]{0:T(1024)S(1)}, f32[4096]{0:T(1024)}, u32[]{:S(2)}) copy-start(f32[4096]{0:T(1024)} %param.11) | copy-start | bytes 49156
  71.2 101.2 %all-gather.9.cloned.1.call-start = ((), (), s32[]{:S(2)}) async-start(), calls=%async_computation.5 | async-start | bytes 4325376 | tf_op jit(solution)/shard_map/all_gather | solution.py:239
  116.8 3.4 %copy-start.2 = (bf16[512,4096]{1,0:T(8,128)(2,1)S(1)}, bf16[512,4096]{1,0:T(8,128)(2,1)}, u32[]{:S(2)}) copy-start(bf16[512,4096]{1,0:T(8,128)(2,1)} %all-gather.5.cloned.1.call-done) | copy-start | bytes 12582916
  120.2 2.5 copy-start.5
  125.0 95.4 %all-gather.7.cloned.1.call-start = ((), (), s32[]{:S(2)}) async-start(), calls=%async_computation.4 | async-start | bytes 4325376 | tf_op jit(solution)/shard_map/all_gather | solution.py:240
  138.5 11.5 %copy-start.4 = (s32[512]{0:T(512)S(1)}, s32[512]{0:T(512)}, u32[]{:S(2)}) copy-start(s32[512]{0:T(512)} %param.10) | copy-start | bytes 6148
  138.5 88.4 %all-to-all-start.1 = ((bf16[4,512,1024]{2,1,0:T(8,128)(2,1)}), bf16[4,512,1024]{2,1,0:T(8,128)(2,1)}, u32[]{:S(2)}, u32[]{:S(2)}) async-start(bf16[4,512,1024]{2,1,0:T(8,128)(2,1)} %bitcast.55), calls=%async_computation.1 | async-start | bytes 8388608 | tf_op jit(solution)/shard_map/all_to_all | solution.py:266
  143.5 132.1 %all-gather.11.cloned.1.call-start = ((), (), s32[]{:S(2)}) async-start(), calls=%async_computation.6 | async-start | bytes 2621440 | tf_op jit(solution)/shard_map/all_gather | solution.py:263
  220.4 55.2 %copy-start.3 = (bf16[512,1024]{1,0:T(8,128)(2,1)S(1)}, bf16[512,1024]{1,0:T(8,128)(2,1)}, u32[]{:S(2)}) copy-start(bf16[512,1024]{1,0:T(8,128)(2,1)} %scatter_custom_fusion.2) | copy-start | bytes 3145732
  286.1 36.0 %all-to-all-start.2 = ((bf16[32,32,1024]{2,1,0:T(8,128)(2,1)}), bf16[32,32,1024]{2,1,0:T(8,128)(2,1)S(1)}, u32[]{:S(2)}, u32[]{:S(2)}) async-start(bf16[32,32,1024]{2,1,0:T(8,128)(2,1)} %bitcast.58), calls=%async_computation.2 | async-start | bytes 4194304 | tf_op jit(solution)/shard_map/all_to_all | solution.py:275
Sparse Core Ops, SparseCore 0:
  71.3 45.4 all-gather.4
  125.1 47.2 all-gather.8
  174.6 45.6 all-gather.6
  227.0 48.5 all-gather.10

commit v14 on v13

--- a/solution.py
+++ b/solution.py
@@ -15,6 +15,7 @@
 NORM_EPS = 1e-05
 NEG_START = -1e30
 KEY_BLOCK = 512
+GROUP = 4
 
 
 def rope_angles(row_index):
@@ -65,10 +66,10 @@
             l_sc[...] = jnp.zeros(l_sc.shape, jnp.float32)
             acc_sc[...] = jnp.zeros(acc_sc.shape, jnp.float32)
 
-    part = block // 2
-    pair = span_ref[0] // 2 + step
-    key_first = 2 * pair * span_ref[4] + span_ref[5]
-    key_last = (2 * pair + 1) * span_ref[4] + span_ref[5] + part - 1
+    part = block // GROUP
+    pair = span_ref[0] // GROUP + step
+    key_first = GROUP * pair * span_ref[4] + span_ref[5]
+    key_last = (GROUP * pair + GROUP - 1) * span_ref[4] + span_ref[5] + part - 1
     active = step < span_ref[1]
     whole = (key_first >= span_ref[2]) & (key_last <= span_ref[3])
 
@@ -115,15 +116,15 @@
 
     def kv_map(column):
         def index_map(step, span_ref):
-            return (span_ref[0] // 2 + jnp.minimum(step, span_ref[1] - 1), column)
+            return (span_ref[0] // GROUP + jnp.minimum(step, span_ref[1] - 1), column)
         return index_map
 
     fixed2 = lambda step, span_ref: (0, 0)
     fixed3 = lambda step, span_ref: (0, 0, 0)
     in_specs = [
         pl.BlockSpec((heads, HD, rows), fixed3),
-        pl.BlockSpec((2 * block, HD), kv_map(0)),
-        pl.BlockSpec((2 * block, HD), kv_map(1)),
+        pl.BlockSpec((GROUP * block, HD), kv_map(0)),
+        pl.BlockSpec((GROUP * block, HD), kv_map(1)),
         pl.BlockSpec((1, rows), fixed2),
         pl.BlockSpec((1, rows), fixed2),
     ]
@@ -151,7 +152,7 @@
         out_specs=out_specs,
         scratch_shapes=scratch,
     )
-    flops = 8 * heads * rows * block * HD * max_blocks
+    flops = 4 * GROUP * heads * rows * block * HD * max_blocks
     return pl.pallas_call(
         functools.partial(flash_kernel, final),
         grid_spec=grid_spec,
@@ -159,8 +160,8 @@
         compiler_params=pltpu.CompilerParams(dimension_semantics=("arbitrary",)),
         cost_estimate=pl.CostEstimate(
             flops=flops,
-            transcendentals=2 * heads * rows * block * max_blocks,
-            bytes_accessed=4 * block * HD * 2 * max_blocks + 2 * 2 * rows * heads * HD,
+            transcendentals=GROUP * heads * rows * block * max_blocks,
+            bytes_accessed=2 * GROUP * block * HD * 2 * max_blocks + 2 * 2 * rows * heads * HD,
         ),
     )(*operands)
 
@@ -243,12 +244,12 @@
     last_block = (block_first + tok_dev - 1) // block
     first_block = doc_low // block
     max_blocks = min((tok_dev - 1) // block + -(-(DOC_MAX - 1) // block) + 1, owners * tok_dev // block)
-    max_pairs = min(max_blocks // 2 + 1, owners * tok_dev // block // 2)
+    max_pairs = min((max_blocks - 1) // GROUP + 2, owners * tok_dev // block // GROUP)
     max_start = jnp.max(row_start)
 
     def span_for(offset):
         return jnp.stack(
-            [first_block, last_block // 2 - first_block // 2 + 1, max_start, block_first, block, offset]
+            [first_block, last_block // GROUP - first_block // GROUP + 1, max_start, block_first, block, offset]
         ).astype(jnp.int32)
 
     queries_t = jnp.transpose(queries.reshape(tok_dev, heads_dev, HD), (1, 2, 0))

time: 333 us -> 341 us (1.024)
  Pallas kernels: 12.8 us -> 23 us
  waiting for transfers between devices: 176 us -> 171 us
    pallas_call x2, Pallas kernels: 12.8 us -> 23 us  [flash_pass(): pl.pallas_call(functools.partial(flash_kernel, final), grid_spec=grid_spe...]
    all_gather x1, waiting for transfers between devices: 48.7 us -> 45.2 us  [local(): context_all = lax.all_gather(context, 'mp', axis=1, tiled=True)]
  transfers between devices with their start and end apart: 6 -> 6, of which waited for: 5 -> 5; matrix products, arithmetic and copies ran while one was open for 9% -> 9% of each run, Pallas kernels for 4% -> 7%
where the time goes in v14:
time: 341 us; the launch traced here: 337 us
  waiting for transfers between devices  171 us (50%)
  local copies, waits for them, and re-layouts  42.4 us (12%)
  blocking collectives  40.9 us (12%)
  Pallas kernels  23 us (7%)
  other arithmetic  17.3 us (5%)
  between operations  15.6 us (5%)
  matrix products  14 us (4%)
  starting transfers between devices  13.1 us (4%)
    all_gather x1, waiting for transfers between devices, local(): routed = lax.all_gather(routed_part, 'mp', axis=1, tiled=True)  45.3 us
    all_gather x1, waiting for transfers between devices, local(): context_all = lax.all_gather(context, 'mp', axis=1, tiled=True)  45.2 us
    all_to_all x1, blocking collectives, local(): lax.all_to_all(wide.reshape(owners, capacity, columns + meta_width), ('ch...  40.9 us
    all_gather x1, waiting for transfers between devices, local(): lax.all_gather(kv_own[half:], ('chip', 'core'), axis=0, tiled=True)  40.7 us
    all_to_all x1, waiting for transfers between devices, local(): lax.all_to_all(backward, ('chip', 'core'), split_axis=0, concat_axis=0, t...  28.3 us
    pallas_call x2, Pallas kernels, flash_pass(): pl.pallas_call(functools.partial(flash_kernel, final), grid_spec=grid_spe...  23 us
    all_gather x1, waiting for transfers between devices, local(): kv_low = lax.all_gather(kv_own[:half], ('chip', 'core'), axis=0, tiled=True)  11 us
    all_to_all x1, starting transfers between devices, local(): lax.all_to_all(backward, ('chip', 'core'), split_axis=0, concat_axis=0, t...  7.7 us
  transfers between devices with their start and end apart: 6, of which 5 were waited for; matrix products, arithmetic and copies ran while one was open for 9% of the time, Pallas kernels for 7%

profile of v14, /device:TPU:1, one launch (start us, length us, event | category | flops | bytes accessed | tf_op | source)
XLA Modules:
  0.0 337.4 jit_solution(15176030016689119314)
XLA Ops:
  6.5 1.0 convert_reduce_fusion
  7.6 0.6 slice.57
  8.8 1.3 fusion.39
  10.2 0.7 add_select_fusion.2
  10.9 1.2 reduce-window.6
  12.0 0.2 slice_reduce_fusion
  12.4 2.4 scatter_custom_fusion.1
  15.7 0.2 copy.36
  15.9 3.9 %scatter_custom_fusion = bf16[1024,1024]{1,0:T(8,128)(2,1)S(1)} fusion(s32[512]{0:T(512)S(1)} %compare_select_fusion.2, bf16[512,1024]{1,0:T(8,128)(2,1)} %param.8, bf16[]{:T(256)} %constant.137.clone.1), kind=kCustom, calls=%fused_computation.18 | custom fusion | bytes 2097664 | tf_op jit(solution)/shard_map/scatter | solution.py:180
  19.8 0.2 fusion.4
  20.0 40.9 %all_to_all.15 = bf16[32,32,1152]{2,1,0:T(8,128)(2,1)S(1)} all-to-all(bf16[32,32,1152]{2,1,0:T(8,128)(2,1)S(1)} %bitcast.57), channel_id=1, replica_groups=mesh['chip'=16,'core'=2,'mp'=4] {'chip','core'}, dimensions={0} | all-to-all | bytes 4718592 | tf_op jit(solution)/shard_map/all_to_all | solution.py:205
  60.9 0.8 copy-done.1
  61.7 0.8 fusion.8
  62.6 1.7 slice.80
  64.3 6.9 %scatter_custom_fusion.2 = bf16[512,1024]{1,0:T(8,128)(2,1)} fusion(s32[1024]{0:T(1024)S(1)} %bitcast.64, bf16[1024,1024]{1,0:T(8,128)(2,1)} %bitcast.59, bf16[]{:T(256)} %constant.137.clone.1), kind=kCustom, calls=%fused_computation.26 | custom fusion | bytes 1049088 | tf_op jit(solution)/shard_map/scatter | solution.py:222
  71.2 0.3 all-gather.9.cloned.1.call-start
  71.5 45.3 %all-gather.5.cloned.1.call-done = bf16[512,4096]{1,0:T(8,128)(2,1)} async-done(((bf16[512,1024]{1,0:T(8,128)(2,1)}), bf16[512,4096]{1,0:T(8,128)(2,1)}) %all-gather.5.cloned.1.call-update) | async-done | bytes 4194320 | tf_op jit(solution)/shard_map/all_gather | solution.py:224
  116.8 3.2 fusion
  120.0 0.2 copy-done.2
  120.2 1.3 convolution_bitcast_fusion
  121.5 1.2 fusion.20
  122.8 1.3 convolution_convert_fusion
  124.2 0.7 fusion.38
  125.0 0.7 all-gather.7.cloned.1.call-update
  125.7 6.5 %copy.39 = bf16[512,4096]{0,1:T(8,128)(2,1)} copy(bf16[512,4096]{1,0:T(8,128)(2,1)} %param.15) | data formatting | bytes 8388608 | tf_op args[7]
  132.2 6.3 %copy.40 = bf16[512,4,1024]{2,0,1:T(8,128)(2,1)} copy(bf16[512,4,1024]{0,2,1:T(8,128)(2,1)} %bitcast.56) | data formatting | bytes 8388608 | tf_op jit(solution)/shard_map/reshape | solution.py:266
  138.5 5.0 %all-to-all-start.1 = ((bf16[4,512,1024]{2,1,0:T(8,128)(2,1)}), bf16[4,512,1024]{2,1,0:T(8,128)(2,1)}, u32[]{:S(2)}, u32[]{:S(2)}) async-start(bf16[4,512,1024]{2,1,0:T(8,128)(2,1)} %bitcast.55), calls=%async_computation.1 | async-start | bytes 8388608 | tf_op jit(solution)/shard_map/all_to_all | solution.py:267
  143.6 0.6 iota_add_fusion.refs_4_
  144.2 0.5 multiply_cosine_fusion.1
  144.7 2.2 compare_reduce_fusion
  146.9 1.7 fusion.24
  148.7 0.7 fusion.32
  150.0 1.7 fusion.37
  151.8 1.2 stack.42.span_ref
  152.9 1.2 stack.41.span_ref
  154.1 6.3 %fusion.35 = f32[512,512]{0,1:T(8,128)S(1)} fusion(bf16[4096,512]{1,0:T(8,128)(2,1)} %param.12, bf16[512,4096]{1,0:T(8,128)(2,1)} %all-gather.5.cloned.1.call-done, f32[4096]{0:T(1024)S(1)} %copy-done.6, f32[512]{0:T(512)S(1)} %add_rsqrt_fusion), kind=kOutput, calls=%fused_computation.88 | convolution fusion | flops 2155872256 | bytes 9455616 | tf_op jit(solution)/shard_map/dot_general | solution.py:229
  160.4 0.2 subtract_convert_fusion
  160.6 0.9 maximum_bitcast_fusion.refs_0_
  161.4 11.0 %all-gather.9.cloned.1.call-done.refs_1_.refs_2_ = bf16[8192,256]{1,0:T(8,128)(2,1)} async-done(((bf16[256,256]{1,0:T(8,128)(2,1)}), bf16[8192,256]{1,0:T(8,128)(2,1)}) %all-gather.9.cloned.1.call-update) | async-done | bytes 4194320 | tf_op jit(solution)/shard_map/all_gather | solution.py:240
  172.4 7.3 %shard_map.82 = (f32[4,1,512]{2,1,0:T(1,128)}, f32[4,1,512]{2,1,0:T(1,128)}, f32[4,128,512]{2,1,0:T(8,128)}) custom-call(s32[6]{0:T(128)} %stack.42.span_ref, bf16[4,128,512]{2,1,0:T(8,128)(2,1)} %maximum_bitcast_fusion.refs_0_, bf16[8192,256]{1,0:T(8,128)(2,1)} %all-gather.9.cloned.1.call-done.refs_1_.refs_2_, ...), custom_call_target="tpu_custom_call" | custom-call | flops 6442450944 | bytes 4194304 | tf_op jit(solution)/shard_map/pallas_call | solution.py:156
  179.7 40.7 %all-gather.7.cloned.1.call-done.refs_1_.refs_2_ = bf16[8192,256]{1,0:T(8,128)(2,1)} async-done(((bf16[256,256]{1,0:T(8,128)(2,1)}), bf16[8192,256]{1,0:T(8,128)(2,1)}) %all-gather.7.cloned.1.call-update) | async-done | bytes 4194320 | tf_op jit(solution)/shard_map/all_gather | solution.py:241
  220.4 15.7 %shard_map.83 = bf16[4,128,512]{2,1,0:T(8,128)(2,1)} custom-call(s32[6]{0:T(128)} %stack.41.span_ref, bf16[4,128,512]{2,1,0:T(8,128)(2,1)} %maximum_bitcast_fusion.refs_0_, bf16[8192,256]{1,0:T(8,128)(2,1)} %all-gather.7.cloned.1.call-done.refs_1_.refs_2_, bf16[8192,256]{1,0:T(8,128)(2,1)} %all-gather.7.cloned.1.call-done.refs_1_.refs_2_, ...), custom_call_target="tpu_custom_call" | custom-call | flops 6442450944 | bytes 4194304 | tf_op jit(solution)/shard_map/pallas_call | solution.py:156
  236.1 45.2 %all-gather.11.cloned.1.call-done = bf16[512,2048]{0,1:T(8,128)(2,1)} async-done(((bf16[512,512]{0,1:T(8,128)(2,1)}), bf16[512,2048]{0,1:T(8,128)(2,1)}) %all-gather.11.cloned.1.call-update) | async-done | bytes 2097168 | tf_op jit(solution)/shard_map/all_gather | solution.py:264
  281.3 5.2 %fusion.5 = bf16[512,1024]{1,0:T(8,128)(2,1)S(1)} fusion(bf16[512,1024]{1,0:T(8,128)(2,1)S(1)} %copy-done.3, bf16[512,4,512]{0,2,1:T(8,128)(2,1)} %bitcast.67, bf16[4,512,1024]{2,1,0:T(8,128)(2,1)} %all-to-all-done.1), kind=kOutput, calls=%fused_computation.14 | convolution fusion | flops 2149056512 | bytes 8388608 | tf_op jit(solution)/shard_map/tsr,src->tc/dot_general | solution.py:268
  286.5 5.4 %gather_fusion = bf16[1024,1024]{1,0:T(8,128)(2,1)} fusion(bf16[512,1024]{1,0:T(8,128)(2,1)S(1)} %fusion.5, s32[1024]{0:T(1024)S(1)} %broadcast_clamp_fusion), kind=kCustom, calls=%fused_computation | custom fusion | bytes 4198400 | tf_op jit(solution)/shard_map/gather | solution.py:275
  291.9 7.7 %all-to-all-start.2 = ((bf16[32,32,1024]{2,1,0:T(8,128)(2,1)}), bf16[32,32,1024]{2,1,0:T(8,128)(2,1)S(1)}, u32[]{:S(2)}, u32[]{:S(2)}) async-start(bf16[32,32,1024]{2,1,0:T(8,128)(2,1)} %bitcast.58), calls=%async_computation.2 | async-start | bytes 4194304 | tf_op jit(solution)/shard_map/all_to_all | solution.py:276
  299.6 28.3 %all-to-all-done.2 = bf16[32,32,1024]{2,1,0:T(8,128)(2,1)S(1)} async-done(((bf16[32,32,1024]{2,1,0:T(8,128)(2,1)}), bf16[32,32,1024]{2,1,0:T(8,128)(2,1)S(1)}, u32[]{:S(2)}, u32[]{:S(2)}) %all-to-all-start.2) | async-done | bytes 2097184 | tf_op jit(solution)/shard_map/all_to_all | solution.py:276
  327.9 2.8 gather_fusion.1
  (40 shorter events, 0.7 us)
Async XLA Ops:
  6.5 113.5 %copy-start = (bf16[4096,128]{1,0:T(8,128)(2,1)S(1)}, bf16[4096,128]{1,0:T(8,128)(2,1)}, u32[]{:S(2)}) copy-start(bf16[4096,128]{1,0:T(8,128)(2,1)} %param.13) | copy-start | bytes 3145732
  6.5 110.3 %all-gather.5.cloned.1.call-start = ((), (), s32[]{:S(2)}) async-start(), calls=%async_computation.3 | async-start | bytes 5242880 | tf_op jit(solution)/shard_map/all_gather | solution.py:224
  60.9 0.8 copy-start.1
  64.2 55.8 %copy-start.6 = (f32[4096]{0:T(1024)S(1)}, f32[4096]{0:T(1024)}, u32[]{:S(2)}) copy-start(f32[4096]{0:T(1024)} %param.11) | copy-start | bytes 49156
  71.2 101.2 %all-gather.9.cloned.1.call-start = ((), (), s32[]{:S(2)}) async-start(), calls=%async_computation.5 | async-start | bytes 4325376 | tf_op jit(solution)/shard_map/all_gather | solution.py:240
  116.8 3.4 %copy-start.2 = (bf16[512,4096]{1,0:T(8,128)(2,1)S(1)}, bf16[512,4096]{1,0:T(8,128)(2,1)}, u32[]{:S(2)}) copy-start(bf16[512,4096]{1,0:T(8,128)(2,1)} %all-gather.5.cloned.1.call-done) | copy-start | bytes 12582916
  120.2 2.5 copy-start.5
  125.0 95.4 %all-gather.7.cloned.1.call-start = ((), (), s32[]{:S(2)}) async-start(), calls=%async_computation.4 | async-start | bytes 4325376 | tf_op jit(solution)/shard_map/all_gather | solution.py:241
  138.5 11.5 %copy-start.4 = (s32[512]{0:T(512)S(1)}, s32[512]{0:T(512)}, u32[]{:S(2)}) copy-start(s32[512]{0:T(512)} %param.10) | copy-start | bytes 6148
  138.5 97.6 %all-to-all-start.1 = ((bf16[4,512,1024]{2,1,0:T(8,128)(2,1)}), bf16[4,512,1024]{2,1,0:T(8,128)(2,1)}, u32[]{:S(2)}, u32[]{:S(2)}) async-start(bf16[4,512,1024]{2,1,0:T(8,128)(2,1)} %bitcast.55), calls=%async_computation.1 | async-start | bytes 8388608 | tf_op jit(solution)/shard_map/all_to_all | solution.py:267
  143.5 137.8 %all-gather.11.cloned.1.call-start = ((), (), s32[]{:S(2)}) async-start(), calls=%async_computation.6 | async-start | bytes 2621440 | tf_op jit(solution)/shard_map/all_gather | solution.py:264
  220.4 61.0 %copy-start.3 = (bf16[512,1024]{1,0:T(8,128)(2,1)S(1)}, bf16[512,1024]{1,0:T(8,128)(2,1)}, u32[]{:S(2)}) copy-start(bf16[512,1024]{1,0:T(8,128)(2,1)} %scatter_custom_fusion.2) | copy-start | bytes 3145732
  291.9 36.0 %all-to-all-start.2 = ((bf16[32,32,1024]{2,1,0:T(8,128)(2,1)}), bf16[32,32,1024]{2,1,0:T(8,128)(2,1)S(1)}, u32[]{:S(2)}, u32[]{:S(2)}) async-start(bf16[32,32,1024]{2,1,0:T(8,128)(2,1)} %bitcast.58), calls=%async_computation.2 | async-start | bytes 4194304 | tf_op jit(solution)/shard_map/all_to_all | solution.py:276
Sparse Core Ops, SparseCore 0:
  71.3 45.4 all-gather.4
  125.1 47.2 all-gather.8
  174.7 45.6 all-gather.6
  236.2 45.0 all-gather.10

commit v15 on v13

--- a/solution.py
+++ b/solution.py
@@ -79,7 +79,7 @@
             sub = lax.broadcasted_iota(jnp.int32, (block, 1), 0)
             key_rows = key_first + (sub // part) * span_ref[4] + sub % part
             allowed = (key_rows >= start_ref[...]) & (key_rows <= row_ref[...])
-        for h in range(heads):
+        def one_head(h, carry):
             scores = jnp.dot(keys, q_ref[h], preferred_element_type=jnp.float32) * scale
             if masked:
                 scores = jnp.where(allowed, scores, -jnp.inf)
@@ -93,6 +93,9 @@
                 preferred_element_type=jnp.float32,
             )
             m_sc[h] = m_new
+            return carry
+
+        lax.fori_loop(0, heads, one_head, 0)
 
     @pl.when(active & whole)
     def _whole():

time: 333 us -> 339 us (1.018)
  waiting for transfers between devices: 176 us -> 181 us
    all_gather x1, waiting for transfers between devices: 48.7 us -> 54 us  [local(): context_all = lax.all_gather(context, 'mp', axis=1, tiled=True)]
where the time goes in v15:
time: 339 us; the launch traced here: 337 us
  waiting for transfers between devices  181 us (53%)
  local copies, waits for them, and re-layouts  42.4 us (13%)
  blocking collectives  40.9 us (12%)
  other arithmetic  17.3 us (5%)
  between operations  15.4 us (5%)
  matrix products  14.1 us (4%)
  Pallas kernels  13.9 us (4%)
  starting transfers between devices  13 us (4%)
    all_gather x1, waiting for transfers between devices, local(): context_all = lax.all_gather(context, 'mp', axis=1, tiled=True)  54 us
    all_gather x1, waiting for transfers between devices, local(): routed = lax.all_gather(routed_part, 'mp', axis=1, tiled=True)  45.4 us
    all_gather x1, waiting for transfers between devices, local(): lax.all_gather(kv_own[half:], ('chip', 'core'), axis=0, tiled=True)  41.3 us
    all_to_all x1, blocking collectives, local(): lax.all_to_all(wide.reshape(owners, capacity, columns + meta_width), ('ch...  40.9 us
    all_to_all x1, waiting for transfers between devices, local(): lax.all_to_all(backward, ('chip', 'core'), split_axis=0, concat_axis=0, t...  28.3 us
    pallas_call x2, Pallas kernels, flash_pass(): pl.pallas_call(functools.partial(flash_kernel, final), grid_spec=grid_spe...  13.9 us
    all_gather x1, waiting for transfers between devices, local(): kv_low = lax.all_gather(kv_own[:half], ('chip', 'core'), axis=0, tiled=True)  11 us
    all_to_all x1, starting transfers between devices, local(): lax.all_to_all(backward, ('chip', 'core'), split_axis=0, concat_axis=0, t...  7.7 us
  transfers between devices with their start and end apart: 6, of which 5 were waited for; matrix products, arithmetic and copies ran while one was open for 9% of the time, Pallas kernels for 4%

profile of v15, /device:TPU:1, one launch (start us, length us, event | category | flops | bytes accessed | tf_op | source)
XLA Modules:
  0.0 337.5 jit_solution(9760892979641615286)
XLA Ops:
  6.5 1.0 convert_reduce_fusion
  7.6 0.6 slice.57
  8.8 1.3 fusion.39
  10.2 0.7 add_select_fusion.2
  10.9 1.2 reduce-window.6
  12.0 0.2 slice_reduce_fusion
  12.4 2.4 scatter_custom_fusion.1
  15.7 0.2 copy.36
  15.9 3.9 %scatter_custom_fusion = bf16[1024,1024]{1,0:T(8,128)(2,1)S(1)} fusion(s32[512]{0:T(512)S(1)} %compare_select_fusion.2, bf16[512,1024]{1,0:T(8,128)(2,1)} %param.8, bf16[]{:T(256)} %constant.136.clone.1), kind=kCustom, calls=%fused_computation.18 | custom fusion | bytes 2097664 | tf_op jit(solution)/shard_map/scatter | solution.py:182
  19.8 0.2 fusion.4
  20.0 40.9 %all_to_all.15 = bf16[32,32,1152]{2,1,0:T(8,128)(2,1)S(1)} all-to-all(bf16[32,32,1152]{2,1,0:T(8,128)(2,1)S(1)} %bitcast.57), channel_id=1, replica_groups=mesh['chip'=16,'core'=2,'mp'=4] {'chip','core'}, dimensions={0} | all-to-all | bytes 4718592 | tf_op jit(solution)/shard_map/all_to_all | solution.py:207
  60.9 0.8 copy-done.1
  61.7 0.8 fusion.8
  62.6 1.7 slice.80
  64.3 6.9 %scatter_custom_fusion.2 = bf16[512,1024]{1,0:T(8,128)(2,1)} fusion(s32[1024]{0:T(1024)S(1)} %bitcast.64, bf16[1024,1024]{1,0:T(8,128)(2,1)} %bitcast.59, bf16[]{:T(256)} %constant.136.clone.1), kind=kCustom, calls=%fused_computation.26 | custom fusion | bytes 1049088 | tf_op jit(solution)/shard_map/scatter | solution.py:224
  71.2 0.2 all-gather.9.cloned.1.call-start
  71.4 45.4 %all-gather.5.cloned.1.call-done = bf16[512,4096]{1,0:T(8,128)(2,1)} async-done(((bf16[512,1024]{1,0:T(8,128)(2,1)}), bf16[512,4096]{1,0:T(8,128)(2,1)}) %all-gather.5.cloned.1.call-update) | async-done | bytes 4194320 | tf_op jit(solution)/shard_map/all_gather | solution.py:226
  116.8 3.2 fusion
  120.0 0.2 copy-done.2
  120.2 1.3 convolution_bitcast_fusion
  121.5 1.2 fusion.20
  122.8 1.3 convolution_convert_fusion
  124.2 0.7 fusion.38
  125.0 0.7 all-gather.7.cloned.1.call-update
  125.7 6.5 %copy.39 = bf16[512,4096]{0,1:T(8,128)(2,1)} copy(bf16[512,4096]{1,0:T(8,128)(2,1)} %param.15) | data formatting | bytes 8388608 | tf_op args[7]
  132.2 6.3 %copy.40 = bf16[512,4,1024]{2,0,1:T(8,128)(2,1)} copy(bf16[512,4,1024]{0,2,1:T(8,128)(2,1)} %bitcast.56) | data formatting | bytes 8388608 | tf_op jit(solution)/shard_map/reshape | solution.py:268
  138.5 5.0 %all-to-all-start.1 = ((bf16[4,512,1024]{2,1,0:T(8,128)(2,1)}), bf16[4,512,1024]{2,1,0:T(8,128)(2,1)}, u32[]{:S(2)}, u32[]{:S(2)}) async-start(bf16[4,512,1024]{2,1,0:T(8,128)(2,1)} %bitcast.55), calls=%async_computation.1 | async-start | bytes 8388608 | tf_op jit(solution)/shard_map/all_to_all | solution.py:269
  143.6 0.6 iota_add_fusion.refs_4_
  144.2 0.5 multiply_cosine_fusion.1
  144.7 2.2 compare_reduce_fusion
  146.9 1.7 fusion.24
  148.7 0.7 fusion.32
  150.0 1.7 fusion.37
  151.8 1.2 stack.42.span_ref
  152.9 1.2 stack.41.span_ref
  154.1 6.3 %fusion.35 = f32[512,512]{0,1:T(8,128)S(1)} fusion(bf16[4096,512]{1,0:T(8,128)(2,1)} %param.12, bf16[512,4096]{1,0:T(8,128)(2,1)} %all-gather.5.cloned.1.call-done, f32[4096]{0:T(1024)S(1)} %copy-done.6, f32[512]{0:T(512)S(1)} %add_rsqrt_fusion), kind=kOutput, calls=%fused_computation.88 | convolution fusion | flops 2155872256 | bytes 9455616 | tf_op jit(solution)/shard_map/dot_general | solution.py:231
  160.4 0.2 subtract_convert_fusion
  160.6 0.9 maximum_bitcast_fusion.refs_0_
  161.4 11.0 %all-gather.9.cloned.1.call-done.refs_1_.refs_2_ = bf16[8192,256]{1,0:T(8,128)(2,1)} async-done(((bf16[256,256]{1,0:T(8,128)(2,1)}), bf16[8192,256]{1,0:T(8,128)(2,1)}) %all-gather.9.cloned.1.call-update) | async-done | bytes 4194320 | tf_op jit(solution)/shard_map/all_gather | solution.py:242
  172.4 6.7 %shard_map.82 = (f32[4,1,512]{2,1,0:T(1,128)}, f32[4,1,512]{2,1,0:T(1,128)}, f32[4,128,512]{2,1,0:T(8,128)}) custom-call(s32[6]{0:T(128)} %stack.42.span_ref, bf16[4,128,512]{2,1,0:T(8,128)(2,1)} %maximum_bitcast_fusion.refs_0_, bf16[8192,256]{1,0:T(8,128)(2,1)} %all-gather.9.cloned.1.call-done.refs_1_.refs_2_, ...), custom_call_target="tpu_custom_call" | custom-call | flops 5368709120 | bytes 3670016 | tf_op jit(solution)/shard_map/pallas_call | solution.py:158
  179.1 41.3 %all-gather.7.cloned.1.call-done.refs_1_.refs_2_ = bf16[8192,256]{1,0:T(8,128)(2,1)} async-done(((bf16[256,256]{1,0:T(8,128)(2,1)}), bf16[8192,256]{1,0:T(8,128)(2,1)}) %all-gather.7.cloned.1.call-update) | async-done | bytes 4194320 | tf_op jit(solution)/shard_map/all_gather | solution.py:243
  220.4 7.2 %shard_map.83 = bf16[4,128,512]{2,1,0:T(8,128)(2,1)} custom-call(s32[6]{0:T(128)} %stack.41.span_ref, bf16[4,128,512]{2,1,0:T(8,128)(2,1)} %maximum_bitcast_fusion.refs_0_, bf16[8192,256]{1,0:T(8,128)(2,1)} %all-gather.7.cloned.1.call-done.refs_1_.refs_2_, bf16[8192,256]{1,0:T(8,128)(2,1)} %all-gather.7.cloned.1.call-done.refs_1_.refs_2_, ...), custom_call_target="tpu_custom_call" | custom-call | flops 5368709120 | bytes 3670016 | tf_op jit(solution)/shard_map/pallas_call | solution.py:158
  227.6 54.0 %all-gather.11.cloned.1.call-done = bf16[512,2048]{0,1:T(8,128)(2,1)} async-done(((bf16[512,512]{0,1:T(8,128)(2,1)}), bf16[512,2048]{0,1:T(8,128)(2,1)}) %all-gather.11.cloned.1.call-update) | async-done | bytes 2097168 | tf_op jit(solution)/shard_map/all_gather | solution.py:266
  281.6 5.2 %fusion.5 = bf16[512,1024]{1,0:T(8,128)(2,1)S(1)} fusion(bf16[512,1024]{1,0:T(8,128)(2,1)S(1)} %copy-done.3, bf16[512,4,512]{0,2,1:T(8,128)(2,1)} %bitcast.67, bf16[4,512,1024]{2,1,0:T(8,128)(2,1)} %all-to-all-done.1), kind=kOutput, calls=%fused_computation.14 | convolution fusion | flops 2149056512 | bytes 8388608 | tf_op jit(solution)/shard_map/tsr,src->tc/dot_general | solution.py:270
  286.8 5.4 %gather_fusion = bf16[1024,1024]{1,0:T(8,128)(2,1)} fusion(bf16[512,1024]{1,0:T(8,128)(2,1)S(1)} %fusion.5, s32[1024]{0:T(1024)S(1)} %broadcast_clamp_fusion), kind=kCustom, calls=%fused_computation | custom fusion | bytes 4198400 | tf_op jit(solution)/shard_map/gather | solution.py:277
  292.2 7.7 %all-to-all-start.2 = ((bf16[32,32,1024]{2,1,0:T(8,128)(2,1)}), bf16[32,32,1024]{2,1,0:T(8,128)(2,1)S(1)}, u32[]{:S(2)}, u32[]{:S(2)}) async-start(bf16[32,32,1024]{2,1,0:T(8,128)(2,1)} %bitcast.58), calls=%async_computation.2 | async-start | bytes 4194304 | tf_op jit(solution)/shard_map/all_to_all | solution.py:278
  299.9 28.3 %all-to-all-done.2 = bf16[32,32,1024]{2,1,0:T(8,128)(2,1)S(1)} async-done(((bf16[32,32,1024]{2,1,0:T(8,128)(2,1)}), bf16[32,32,1024]{2,1,0:T(8,128)(2,1)S(1)}, u32[]{:S(2)}, u32[]{:S(2)}) %all-to-all-start.2) | async-done | bytes 2097184 | tf_op jit(solution)/shard_map/all_to_all | solution.py:278
  328.2 2.8 gather_fusion.1
  (40 shorter events, 0.7 us)
Async XLA Ops:
  6.5 113.5 %copy-start = (bf16[4096,128]{1,0:T(8,128)(2,1)S(1)}, bf16[4096,128]{1,0:T(8,128)(2,1)}, u32[]{:S(2)}) copy-start(bf16[4096,128]{1,0:T(8,128)(2,1)} %param.13) | copy-start | bytes 3145732
  6.5 110.3 %all-gather.5.cloned.1.call-start = ((), (), s32[]{:S(2)}) async-start(), calls=%async_computation.3 | async-start | bytes 5242880 | tf_op jit(solution)/shard_map/all_gather | solution.py:226
  60.9 0.8 copy-start.1
  64.2 55.8 %copy-start.6 = (f32[4096]{0:T(1024)S(1)}, f32[4096]{0:T(1024)}, u32[]{:S(2)}) copy-start(f32[4096]{0:T(1024)} %param.11) | copy-start | bytes 49156
  71.2 101.2 %all-gather.9.cloned.1.call-start = ((), (), s32[]{:S(2)}) async-start(), calls=%async_computation.5 | async-start | bytes 4325376 | tf_op jit(solution)/shard_map/all_gather | solution.py:242
  116.8 3.4 %copy-start.2 = (bf16[512,4096]{1,0:T(8,128)(2,1)S(1)}, bf16[512,4096]{1,0:T(8,128)(2,1)}, u32[]{:S(2)}) copy-start(bf16[512,4096]{1,0:T(8,128)(2,1)} %all-gather.5.cloned.1.call-done) | copy-start | bytes 12582916
  120.2 2.5 copy-start.5
  125.0 95.4 %all-gather.7.cloned.1.call-start = ((), (), s32[]{:S(2)}) async-start(), calls=%async_computation.4 | async-start | bytes 4325376 | tf_op jit(solution)/shard_map/all_gather | solution.py:243
  138.5 11.5 %copy-start.4 = (s32[512]{0:T(512)S(1)}, s32[512]{0:T(512)}, u32[]{:S(2)}) copy-start(s32[512]{0:T(512)} %param.10) | copy-start | bytes 6148
  138.5 89.0 %all-to-all-start.1 = ((bf16[4,512,1024]{2,1,0:T(8,128)(2,1)}), bf16[4,512,1024]{2,1,0:T(8,128)(2,1)}, u32[]{:S(2)}, u32[]{:S(2)}) async-start(bf16[4,512,1024]{2,1,0:T(8,128)(2,1)} %bitcast.55), calls=%async_computation.1 | async-start | bytes 8388608 | tf_op jit(solution)/shard_map/all_to_all | solution.py:269
  143.5 138.1 %all-gather.11.cloned.1.call-start = ((), (), s32[]{:S(2)}) async-start(), calls=%async_computation.6 | async-start | bytes 2621440 | tf_op jit(solution)/shard_map/all_gather | solution.py:266
  220.4 61.2 %copy-start.3 = (bf16[512,1024]{1,0:T(8,128)(2,1)S(1)}, bf16[512,1024]{1,0:T(8,128)(2,1)}, u32[]{:S(2)}) copy-start(bf16[512,1024]{1,0:T(8,128)(2,1)} %scatter_custom_fusion.2) | copy-start | bytes 3145732
  292.2 36.0 %all-to-all-start.2 = ((bf16[32,32,1024]{2,1,0:T(8,128)(2,1)}), bf16[32,32,1024]{2,1,0:T(8,128)(2,1)S(1)}, u32[]{:S(2)}, u32[]{:S(2)}) async-start(bf16[32,32,1024]{2,1,0:T(8,128)(2,1)} %bitcast.58), calls=%async_computation.2 | async-start | bytes 4194304 | tf_op jit(solution)/shard_map/all_to_all | solution.py:278
Sparse Core Ops, SparseCore 0:
  71.3 45.4 all-gather.4
  125.1 47.2 all-gather.8
  174.6 45.6 all-gather.6
  227.7 53.8 all-gather.10

commit v16 on v13

--- a/solution.py
+++ b/solution.py
@@ -235,7 +235,7 @@
     keys_own = rotate(keys_own, angles).astype(jnp.bfloat16).reshape(tok_dev, kv_dev * HD)
     values_own = jnp.dot(normed, w_value, preferred_element_type=jnp.float32).astype(jnp.bfloat16)
     kv_own = jnp.concatenate([keys_own, values_own], axis=1)
-    half = tok_dev // 2
+    half = 5 * tok_dev // 8
     kv_low = lax.all_gather(kv_own[:half], ("chip", "core"), axis=0, tiled=True)
     kv_high = lax.all_gather(kv_own[half:], ("chip", "core"), axis=0, tiled=True)
 
@@ -256,7 +256,7 @@
         span_for(0), queries_t, kv_low, row_start[None, :], row_index[None, :], half, max_pairs, None
     )
     context_t = flash_pass(
-        span_for(half), queries_t, kv_high, row_start[None, :], row_index[None, :], half, max_pairs,
+        span_for(half), queries_t, kv_high, row_start[None, :], row_index[None, :], tok_dev - half, max_pairs,
         state,
     )
     context = jnp.transpose(context_t, (2, 0, 1)).reshape(tok_dev, heads_dev * HD)

time: 333 us -> 329 us (0.988)
  waiting for transfers between devices: 176 us -> 172 us
where the time goes in v16:
time: 329 us
  waiting for transfers between devices  172 us (52%)
  local copies, waits for them, and re-layouts  41.9 us (13%)
  blocking collectives  40.9 us (12%)
  other arithmetic  18.6 us (6%)
  between operations  15.5 us (5%)
  matrix products  14.1 us (4%)
  starting transfers between devices  13 us (4%)
  Pallas kernels  13 us (4%)
    all_gather x1, waiting for transfers between devices, local(): context_all = lax.all_gather(context, 'mp', axis=1, tiled=True)  46.9 us
    all_gather x1, waiting for transfers between devices, local(): routed = lax.all_gather(routed_part, 'mp', axis=1, tiled=True)  45.4 us
    all_to_all x1, blocking collectives, local(): lax.all_to_all(wide.reshape(owners, capacity, columns + meta_width), ('ch...  40.9 us
    all_gather x1, waiting for transfers between devices, local(): lax.all_gather(kv_own[half:], ('chip', 'core'), axis=0, tiled=True)  40 us
    all_to_all x1, waiting for transfers between devices, local(): lax.all_to_all(backward, ('chip', 'core'), split_axis=0, concat_axis=0, t...  28.3 us
    pallas_call x2, Pallas kernels, flash_pass(): pl.pallas_call(functools.partial(flash_kernel, final), grid_spec=grid_spe...  13 us
    all_gather x1, waiting for transfers between devices, local(): kv_low = lax.all_gather(kv_own[:half], ('chip', 'core'), axis=0, tiled=True)  11.7 us
    all_to_all x1, starting transfers between devices, local(): lax.all_to_all(backward, ('chip', 'core'), split_axis=0, concat_axis=0, t...  7.7 us
  transfers between devices with their start and end apart: 6, of which 5 were waited for; matrix products, arithmetic and copies ran while one was open for 9% of the time, Pallas kernels for 4%

profile of v16, /device:TPU:1, one launch (start us, length us, event | category | flops | bytes accessed | tf_op | source)
XLA Modules:
  0.0 329.4 jit_solution(8361579419703655516)
XLA Ops:
  6.5 1.4 fusion.38
  7.9 1.0 convert_reduce_fusion
  8.9 0.7 slice.57
  10.3 0.7 add_select_fusion.2
  11.0 1.2 reduce-window.6
  12.2 0.2 slice_reduce_fusion
  12.6 2.4 scatter_custom_fusion.1
  15.8 0.2 copy.36
  16.0 3.9 %scatter_custom_fusion = bf16[1024,1024]{1,0:T(8,128)(2,1)S(1)} fusion(s32[512]{0:T(512)S(1)} %compare_select_fusion.2, bf16[512,1024]{1,0:T(8,128)(2,1)} %param.8, bf16[]{:T(256)} %constant.136.clone.1), kind=kCustom, calls=%fused_computation.18 | custom fusion | bytes 2097664 | tf_op jit(solution)/shard_map/scatter | solution.py:179
  19.9 0.2 fusion.4
  20.2 40.9 %all_to_all.15 = bf16[32,32,1152]{2,1,0:T(8,128)(2,1)S(1)} all-to-all(bf16[32,32,1152]{2,1,0:T(8,128)(2,1)S(1)} %bitcast.57), channel_id=1, replica_groups=mesh['chip'=16,'core'=2,'mp'=4] {'chip','core'}, dimensions={0} | all-to-all | bytes 4718592 | tf_op jit(solution)/shard_map/all_to_all | solution.py:204
  61.1 0.8 copy-done.1
  61.9 0.8 fusion.8
  62.8 1.7 slice.80
  64.4 6.9 %scatter_custom_fusion.2 = bf16[512,1024]{1,0:T(8,128)(2,1)} fusion(s32[1024]{0:T(1024)S(1)} %bitcast.64, bf16[1024,1024]{1,0:T(8,128)(2,1)} %bitcast.59, bf16[]{:T(256)} %constant.136.clone.1), kind=kCustom, calls=%fused_computation.26 | custom fusion | bytes 1049088 | tf_op jit(solution)/shard_map/scatter | solution.py:221
  71.3 0.2 all-gather.9.cloned.1.call-start
  71.6 45.4 %all-gather.5.cloned.1.call-done = bf16[512,4096]{1,0:T(8,128)(2,1)} async-done(((bf16[512,1024]{1,0:T(8,128)(2,1)}), bf16[512,4096]{1,0:T(8,128)(2,1)}) %all-gather.5.cloned.1.call-update) | async-done | bytes 4194320 | tf_op jit(solution)/shard_map/all_gather | solution.py:223
  117.0 3.2 fusion
  120.2 0.2 copy-done.2
  120.4 1.3 convolution_bitcast_fusion
  121.7 1.2 fusion.20
  122.9 1.3 convolution_convert_fusion
  124.3 0.8 pad_maximum_fusion
  125.1 0.7 pad_maximum_fusion.2
  125.9 6.5 %copy.39 = bf16[512,4096]{0,1:T(8,128)(2,1)} copy(bf16[512,4096]{1,0:T(8,128)(2,1)} %param.15) | data formatting | bytes 8388608 | tf_op args[7]
  132.4 6.3 %copy.40 = bf16[512,4,1024]{2,0,1:T(8,128)(2,1)} copy(bf16[512,4,1024]{0,2,1:T(8,128)(2,1)} %bitcast.56) | data formatting | bytes 8388608 | tf_op jit(solution)/shard_map/reshape | solution.py:265
  138.7 5.0 %all-to-all-start.1 = ((bf16[4,512,1024]{2,1,0:T(8,128)(2,1)}), bf16[4,512,1024]{2,1,0:T(8,128)(2,1)}, u32[]{:S(2)}, u32[]{:S(2)}) async-start(bf16[4,512,1024]{2,1,0:T(8,128)(2,1)} %bitcast.55), calls=%async_computation.1 | async-start | bytes 8388608 | tf_op jit(solution)/shard_map/all_to_all | solution.py:266
  143.9 0.6 iota_add_fusion.refs_4_
  144.4 0.5 multiply_cosine_fusion.1
  145.0 2.2 compare_reduce_fusion
  147.2 1.7 fusion.24
  148.9 0.7 fusion.32
  150.3 1.8 fusion.37
  152.0 1.2 stack.41.span_ref
  153.3 1.2 stack.42.span_ref
  154.5 6.4 %fusion.35 = f32[512,512]{0,1:T(8,128)S(1)} fusion(bf16[4096,512]{1,0:T(8,128)(2,1)} %param.12, bf16[512,4096]{1,0:T(8,128)(2,1)} %all-gather.5.cloned.1.call-done, f32[4096]{0:T(1024)S(1)} %copy-done.6, f32[512]{0:T(512)S(1)} %add_rsqrt_fusion), kind=kOutput, calls=%fused_computation.90 | convolution fusion | flops 2155872256 | bytes 9455616 | tf_op jit(solution)/shard_map/dot_general | solution.py:228
  160.9 0.2 subtract_convert_fusion
  161.1 0.9 maximum_bitcast_fusion.refs_0_
  161.9 11.7 %all-gather.9.cloned.1.call-done.refs_1_.refs_2_ = bf16[10240,256]{1,0:T(8,128)(2,1)} async-done(((bf16[320,256]{1,0:T(8,128)(2,1)}), bf16[10240,256]{1,0:T(8,128)(2,1)}) %all-gather.9.cloned.1.call-update) | async-done | bytes 5242896 | tf_op jit(solution)/shard_map/all_gather | solution.py:239
  173.7 6.8 %shard_map.82 = (f32[4,1,512]{2,1,0:T(1,128)}, f32[4,1,512]{2,1,0:T(1,128)}, f32[4,128,512]{2,1,0:T(8,128)}) custom-call(s32[6]{0:T(128)} %stack.42.span_ref, bf16[4,128,512]{2,1,0:T(8,128)(2,1)} %maximum_bitcast_fusion.refs_0_, bf16[10240,256]{1,0:T(8,128)(2,1)} %all-gather.9.cloned.1.call-done.refs_1_.refs_2_, ...), custom_call_target="tpu_custom_call" | custom-call | flops 6710886400 | bytes 4325376 | tf_op jit(solution)/shard_map/pallas_call | solution.py:155
  180.5 40.0 %all-gather.7.cloned.1.call-done.refs_1_.refs_2_ = bf16[6144,256]{1,0:T(8,128)(2,1)} async-done(((bf16[192,256]{1,0:T(8,128)(2,1)}), bf16[6144,256]{1,0:T(8,128)(2,1)}) %all-gather.7.cloned.1.call-update) | async-done | bytes 3145744 | tf_op jit(solution)/shard_map/all_gather | solution.py:240
  220.5 6.2 %shard_map.83 = bf16[4,128,512]{2,1,0:T(8,128)(2,1)} custom-call(s32[6]{0:T(128)} %stack.41.span_ref, bf16[4,128,512]{2,1,0:T(8,128)(2,1)} %maximum_bitcast_fusion.refs_0_, bf16[6144,256]{1,0:T(8,128)(2,1)} %all-gather.7.cloned.1.call-done.refs_1_.refs_2_, bf16[6144,256]{1,0:T(8,128)(2,1)} %all-gather.7.cloned.1.call-done.refs_1_.refs_2_, ...), custom_call_target="tpu_custom_call" | custom-call | flops 4026531840 | bytes 3014656 | tf_op jit(solution)/shard_map/pallas_call | solution.py:155
  226.7 46.9 %all-gather.11.cloned.1.call-done = bf16[512,2048]{0,1:T(8,128)(2,1)} async-done(((bf16[512,512]{0,1:T(8,128)(2,1)}), bf16[512,2048]{0,1:T(8,128)(2,1)}) %all-gather.11.cloned.1.call-update) | async-done | bytes 2097168 | tf_op jit(solution)/shard_map/all_gather | solution.py:263
  273.6 5.2 %fusion.5 = bf16[512,1024]{1,0:T(8,128)(2,1)S(1)} fusion(bf16[512,1024]{1,0:T(8,128)(2,1)S(1)} %copy-done.3, bf16[512,4,512]{0,2,1:T(8,128)(2,1)} %bitcast.67, bf16[4,512,1024]{2,1,0:T(8,128)(2,1)} %all-to-all-done.1), kind=kOutput, calls=%fused_computation.14 | convolution fusion | flops 2149056512 | bytes 8388608 | tf_op jit(solution)/shard_map/tsr,src->tc/dot_general | solution.py:267
  278.7 5.4 %gather_fusion = bf16[1024,1024]{1,0:T(8,128)(2,1)} fusion(bf16[512,1024]{1,0:T(8,128)(2,1)S(1)} %fusion.5, s32[1024]{0:T(1024)S(1)} %broadcast_clamp_fusion), kind=kCustom, calls=%fused_computation | custom fusion | bytes 4198400 | tf_op jit(solution)/shard_map/gather | solution.py:274
  284.1 7.7 %all-to-all-start.2 = ((bf16[32,32,1024]{2,1,0:T(8,128)(2,1)}), bf16[32,32,1024]{2,1,0:T(8,128)(2,1)S(1)}, u32[]{:S(2)}, u32[]{:S(2)}) async-start(bf16[32,32,1024]{2,1,0:T(8,128)(2,1)} %bitcast.58), calls=%async_computation.2 | async-start | bytes 4194304 | tf_op jit(solution)/shard_map/all_to_all | solution.py:275
  291.8 28.3 %all-to-all-done.2 = bf16[32,32,1024]{2,1,0:T(8,128)(2,1)S(1)} async-done(((bf16[32,32,1024]{2,1,0:T(8,128)(2,1)}), bf16[32,32,1024]{2,1,0:T(8,128)(2,1)S(1)}, u32[]{:S(2)}, u32[]{:S(2)}) %all-to-all-start.2) | async-done | bytes 2097184 | tf_op jit(solution)/shard_map/all_to_all | solution.py:275
  320.1 2.8 gather_fusion.1
  (40 shorter events, 0.6 us)
Async XLA Ops:
  6.5 113.7 %copy-start = (bf16[4096,128]{1,0:T(8,128)(2,1)S(1)}, bf16[4096,128]{1,0:T(8,128)(2,1)}, u32[]{:S(2)}) copy-start(bf16[4096,128]{1,0:T(8,128)(2,1)} %param.13) | copy-start | bytes 3145732
  6.5 110.4 %all-gather.5.cloned.1.call-start = ((), (), s32[]{:S(2)}) async-start(), calls=%async_computation.3 | async-start | bytes 5242880 | tf_op jit(solution)/shard_map/all_gather | solution.py:223
  61.1 0.8 copy-start.1
  64.4 55.8 %copy-start.6 = (f32[4096]{0:T(1024)S(1)}, f32[4096]{0:T(1024)}, u32[]{:S(2)}) copy-start(f32[4096]{0:T(1024)} %param.11) | copy-start | bytes 49156
  71.3 102.3 %all-gather.9.cloned.1.call-start = ((), (), s32[]{:S(2)}) async-start(), calls=%async_computation.5 | async-start | bytes 5406720 | tf_op jit(solution)/shard_map/all_gather | solution.py:239
  117.0 3.4 %copy-start.2 = (bf16[512,4096]{1,0:T(8,128)(2,1)S(1)}, bf16[512,4096]{1,0:T(8,128)(2,1)}, u32[]{:S(2)}) copy-start(bf16[512,4096]{1,0:T(8,128)(2,1)} %all-gather.5.cloned.1.call-done) | copy-start | bytes 12582916
  120.4 2.5 copy-start.5
  125.1 95.4 %all-gather.7.cloned.1.call-start = ((), (), s32[]{:S(2)}) async-start(), calls=%async_computation.4 | async-start | bytes 3244032 | tf_op jit(solution)/shard_map/all_gather | solution.py:240
  138.7 11.5 %copy-start.4 = (s32[512]{0:T(512)S(1)}, s32[512]{0:T(512)}, u32[]{:S(2)}) copy-start(s32[512]{0:T(512)} %param.10) | copy-start | bytes 6148
  138.7 87.9 %all-to-all-start.1 = ((bf16[4,512,1024]{2,1,0:T(8,128)(2,1)}), bf16[4,512,1024]{2,1,0:T(8,128)(2,1)}, u32[]{:S(2)}, u32[]{:S(2)}) async-start(bf16[4,512,1024]{2,1,0:T(8,128)(2,1)} %bitcast.55), calls=%async_computation.1 | async-start | bytes 8388608 | tf_op jit(solution)/shard_map/all_to_all | solution.py:266
  143.8 129.8 %all-gather.11.cloned.1.call-start = ((), (), s32[]{:S(2)}) async-start(), calls=%async_computation.6 | async-start | bytes 2621440 | tf_op jit(solution)/shard_map/all_gather | solution.py:263
  220.5 53.1 %copy-start.3 = (bf16[512,1024]{1,0:T(8,128)(2,1)S(1)}, bf16[512,1024]{1,0:T(8,128)(2,1)}, u32[]{:S(2)}) copy-start(bf16[512,1024]{1,0:T(8,128)(2,1)} %scatter_custom_fusion.2) | copy-start | bytes 3145732
  284.1 36.0 %all-to-all-start.2 = ((bf16[32,32,1024]{2,1,0:T(8,128)(2,1)}), bf16[32,32,1024]{2,1,0:T(8,128)(2,1)S(1)}, u32[]{:S(2)}, u32[]{:S(2)}) async-start(bf16[32,32,1024]{2,1,0:T(8,128)(2,1)} %bitcast.58), calls=%async_computation.2 | async-start | bytes 4194304 | tf_op jit(solution)/shard_map/all_to_all | solution.py:275
Sparse Core Ops, SparseCore 0:
  71.5 45.4 all-gather.4
  125.2 48.4 all-gather.8
  175.9 44.4 all-gather.6
  226.8 46.7 all-gather.10

commit v17 on v16

--- a/solution.py
+++ b/solution.py
@@ -44,7 +44,7 @@
     return (wide_rows * inv_rms * norm_gain[None, :]).astype(jnp.bfloat16)
 
 
-def flash_kernel(final, span_ref, *refs):
+def flash_kernel(final, group, span_ref, *refs):
     if final:
         q_ref, k_ref, v_ref, start_ref, row_ref, m_in, l_in, acc_in, o_ref, m_sc, l_sc, acc_sc = refs
     else:
@@ -65,10 +65,10 @@
             l_sc[...] = jnp.zeros(l_sc.shape, jnp.float32)
             acc_sc[...] = jnp.zeros(acc_sc.shape, jnp.float32)
 
-    part = block // 2
-    pair = span_ref[0] // 2 + step
-    key_first = 2 * pair * span_ref[4] + span_ref[5]
-    key_last = (2 * pair + 1) * span_ref[4] + span_ref[5] + part - 1
+    part = block // group
+    pair = span_ref[0] // group + step
+    key_first = group * pair * span_ref[4] + span_ref[5]
+    key_last = (group * pair + group - 1) * span_ref[4] + span_ref[5] + part - 1
     active = step < span_ref[1]
     whole = (key_first >= span_ref[2]) & (key_last <= span_ref[3])
 
@@ -109,21 +109,21 @@
                 o_ref[h] = (acc_sc[h] / l_sc[h]).astype(o_ref.dtype)
 
 
-def flash_pass(span, queries_t, kv_part, row_start, row_index, block, max_blocks, state):
+def flash_pass(span, queries_t, kv_part, row_start, row_index, block, group, max_blocks, state):
     heads, _, rows = queries_t.shape
     final = state is not None
 
     def kv_map(column):
         def index_map(step, span_ref):
-            return (span_ref[0] // 2 + jnp.minimum(step, span_ref[1] - 1), column)
+            return (span_ref[0] // group + jnp.minimum(step, span_ref[1] - 1), column)
         return index_map
 
     fixed2 = lambda step, span_ref: (0, 0)
     fixed3 = lambda step, span_ref: (0, 0, 0)
     in_specs = [
         pl.BlockSpec((heads, HD, rows), fixed3),
-        pl.BlockSpec((2 * block, HD), kv_map(0)),
-        pl.BlockSpec((2 * block, HD), kv_map(1)),
+        pl.BlockSpec((group * block, HD), kv_map(0)),
+        pl.BlockSpec((group * block, HD), kv_map(1)),
         pl.BlockSpec((1, rows), fixed2),
         pl.BlockSpec((1, rows), fixed2),
     ]
@@ -151,16 +151,16 @@
         out_specs=out_specs,
         scratch_shapes=scratch,
     )
-    flops = 8 * heads * rows * block * HD * max_blocks
+    flops = 4 * group * heads * rows * block * HD * max_blocks
     return pl.pallas_call(
-        functools.partial(flash_kernel, final),
+        functools.partial(flash_kernel, final, group),
         grid_spec=grid_spec,
         out_shape=out_shape,
         compiler_params=pltpu.CompilerParams(dimension_semantics=("arbitrary",)),
         cost_estimate=pl.CostEstimate(
             flops=flops,
-            transcendentals=2 * heads * rows * block * max_blocks,
-            bytes_accessed=4 * block * HD * 2 * max_blocks + 2 * 2 * rows * heads * HD,
+            transcendentals=group * heads * rows * block * max_blocks,
+            bytes_accessed=2 * group * block * HD * 2 * max_blocks + 2 * 2 * rows * heads * HD,
         ),
     )(*operands)
 
@@ -243,20 +243,24 @@
     last_block = (block_first + tok_dev - 1) // block
     first_block = doc_low // block
     max_blocks = min((tok_dev - 1) // block + -(-(DOC_MAX - 1) // block) + 1, owners * tok_dev // block)
-    max_pairs = min(max_blocks // 2 + 1, owners * tok_dev // block // 2)
     max_start = jnp.max(row_start)
 
-    def span_for(offset):
+    def steps_for(group):
+        return min((max_blocks - 1) // group + 2, owners * tok_dev // block // group)
+
+    def span_for(offset, group):
         return jnp.stack(
-            [first_block, last_block // 2 - first_block // 2 + 1, max_start, block_first, block, offset]
+            [first_block, last_block // group - first_block // group + 1, max_start, block_first, block, offset]
         ).astype(jnp.int32)
 
     queries_t = jnp.transpose(queries.reshape(tok_dev, heads_dev, HD), (1, 2, 0))
     state = flash_pass(
-        span_for(0), queries_t, kv_low, row_start[None, :], row_index[None, :], half, max_pairs, None
+        span_for(0, 2), queries_t, kv_low, row_start[None, :], row_index[None, :], half, 2, steps_for(2),
+        None,
     )
     context_t = flash_pass(
-        span_for(half), queries_t, kv_high, row_start[None, :], row_index[None, :], tok_dev - half, max_pairs,
+        span_for(half, 4), queries_t, kv_high, row_start[None, :], row_index[None, :], tok_dev - half, 4,
+        steps_for(4),
         state,
     )
     context = jnp.transpose(context_t, (2, 0, 1)).reshape(tok_dev, heads_dev * HD)

time: 329 us -> 327 us (level)
  waiting for transfers between devices: 172 us -> 168 us
    all_gather x1, waiting for transfers between devices: 46.9 us -> 42.3 us  [local(): context_all = lax.all_gather(context, 'mp', axis=1, tiled=True)]
  transfers between devices with their start and end apart: 6 -> 6, of which waited for: 5 -> 5; matrix products, arithmetic and copies ran while one was open for 9% -> 10% of each run, Pallas kernels for 4% -> 4%
where the time goes in v17:
time: 327 us; the launch traced here: 326 us
  waiting for transfers between devices  168 us (51%)
  local copies, waits for them, and re-layouts  42 us (13%)
  blocking collectives  40.9 us (13%)
  other arithmetic  18.7 us (6%)
  between operations  15.5 us (5%)
  matrix products  14.1 us (4%)
  Pallas kernels  14 us (4%)
  starting transfers between devices  13 us (4%)
    all_gather x1, waiting for transfers between devices, local(): routed = lax.all_gather(routed_part, 'mp', axis=1, tiled=True)  45.4 us
    all_gather x1, waiting for transfers between devices, local(): context_all = lax.all_gather(context, 'mp', axis=1, tiled=True)  42.3 us
    all_to_all x1, blocking collectives, local(): lax.all_to_all(wide.reshape(owners, capacity, columns + meta_width), ('ch...  40.9 us
    all_gather x1, waiting for transfers between devices, local(): lax.all_gather(kv_own[half:], ('chip', 'core'), axis=0, tiled=True)  40 us
    all_to_all x1, waiting for transfers between devices, local(): lax.all_to_all(backward, ('chip', 'core'), split_axis=0, concat_axis=0, t...  28.3 us
    pallas_call x2, Pallas kernels, flash_pass(): pl.pallas_call(functools.partial(flash_kernel, final, group), grid_spec=g...  14 us
    all_gather x1, waiting for transfers between devices, local(): kv_low = lax.all_gather(kv_own[:half], ('chip', 'core'), axis=0, tiled=True)  11.6 us
    all_to_all x1, starting transfers between devices, local(): lax.all_to_all(backward, ('chip', 'core'), split_axis=0, concat_axis=0, t...  7.7 us
  transfers between devices with their start and end apart: 6, of which 5 were waited for; matrix products, arithmetic and copies ran while one was open for 10% of the time, Pallas kernels for 4%

profile of v17, /device:TPU:1, one launch (start us, length us, event | category | flops | bytes accessed | tf_op | source)
XLA Modules:
  0.0 325.8 jit_solution(13688368264145483433)
XLA Ops:
  6.5 1.4 fusion.38
  7.9 1.0 convert_reduce_fusion
  8.9 0.7 slice.57
  10.3 0.7 add_select_fusion.2
  11.0 1.2 reduce-window.6
  12.2 0.2 slice_reduce_fusion
  12.6 2.4 scatter_custom_fusion.1
  15.8 0.2 copy.36
  16.0 3.9 %scatter_custom_fusion = bf16[1024,1024]{1,0:T(8,128)(2,1)S(1)} fusion(s32[512]{0:T(512)S(1)} %compare_select_fusion.2, bf16[512,1024]{1,0:T(8,128)(2,1)} %param.8, bf16[]{:T(256)} %constant.148.clone.1), kind=kCustom, calls=%fused_computation.18 | custom fusion | bytes 2097664 | tf_op jit(solution)/shard_map/scatter | solution.py:179
  19.9 0.2 fusion.4
  20.2 40.9 %all_to_all.15 = bf16[32,32,1152]{2,1,0:T(8,128)(2,1)S(1)} all-to-all(bf16[32,32,1152]{2,1,0:T(8,128)(2,1)S(1)} %bitcast.58), channel_id=1, replica_groups=mesh['chip'=16,'core'=2,'mp'=4] {'chip','core'}, dimensions={0} | all-to-all | bytes 4718592 | tf_op jit(solution)/shard_map/all_to_all | solution.py:204
  61.1 0.8 copy-done.1
  61.9 0.8 fusion.8
  62.8 1.7 slice.80
  64.4 6.9 %scatter_custom_fusion.2 = bf16[512,1024]{1,0:T(8,128)(2,1)} fusion(s32[1024]{0:T(1024)S(1)} %bitcast.65, bf16[1024,1024]{1,0:T(8,128)(2,1)} %bitcast.60, bf16[]{:T(256)} %constant.148.clone.1), kind=kCustom, calls=%fused_computation.26 | custom fusion | bytes 1049088 | tf_op jit(solution)/shard_map/scatter | solution.py:221
  71.3 0.2 all-gather.9.cloned.1.call-start
  71.6 45.4 %all-gather.5.cloned.1.call-done = bf16[512,4096]{1,0:T(8,128)(2,1)} async-done(((bf16[512,1024]{1,0:T(8,128)(2,1)}), bf16[512,4096]{1,0:T(8,128)(2,1)}) %all-gather.5.cloned.1.call-update) | async-done | bytes 4194320 | tf_op jit(solution)/shard_map/all_gather | solution.py:223
  117.0 3.2 fusion
  120.2 0.2 copy-done.2
  120.4 1.3 convolution_bitcast_fusion
  121.7 1.2 fusion.20
  122.9 1.3 convolution_convert_fusion
  124.3 0.8 pad_maximum_fusion
  125.1 0.7 pad_maximum_fusion.2
  125.9 6.5 %copy.39 = bf16[512,4096]{0,1:T(8,128)(2,1)} copy(bf16[512,4096]{1,0:T(8,128)(2,1)} %param.15) | data formatting | bytes 8388608 | tf_op args[7]
  132.4 6.3 %copy.40 = bf16[512,4,1024]{2,0,1:T(8,128)(2,1)} copy(bf16[512,4,1024]{0,2,1:T(8,128)(2,1)} %bitcast.57) | data formatting | bytes 8388608 | tf_op jit(solution)/shard_map/reshape | solution.py:269
  138.7 5.0 %all-to-all-start.1 = ((bf16[4,512,1024]{2,1,0:T(8,128)(2,1)}), bf16[4,512,1024]{2,1,0:T(8,128)(2,1)}, u32[]{:S(2)}, u32[]{:S(2)}) async-start(bf16[4,512,1024]{2,1,0:T(8,128)(2,1)} %bitcast.56), calls=%async_computation.1 | async-start | bytes 8388608 | tf_op jit(solution)/shard_map/all_to_all | solution.py:270
  143.9 0.6 iota_add_fusion.refs_4_
  144.5 0.5 multiply_cosine_fusion.1
  145.0 2.2 compare_reduce_fusion
  147.2 1.7 fusion.24
  148.9 0.7 fusion.32
  150.3 1.8 fusion.37
  152.1 1.3 stack.43.span_ref
  153.4 1.3 stack.45.span_ref
  154.7 6.4 %fusion.35 = f32[512,512]{0,1:T(8,128)S(1)} fusion(bf16[4096,512]{1,0:T(8,128)(2,1)} %param.12, bf16[512,4096]{1,0:T(8,128)(2,1)} %all-gather.5.cloned.1.call-done, f32[4096]{0:T(1024)S(1)} %copy-done.6, f32[512]{0:T(512)S(1)} %add_rsqrt_fusion), kind=kOutput, calls=%fused_computation.90 | convolution fusion | flops 2155872256 | bytes 9455616 | tf_op jit(solution)/shard_map/dot_general | solution.py:228
  161.0 0.2 subtract_convert_fusion
  161.2 0.9 maximum_bitcast_fusion.refs_0_
  162.1 11.6 %all-gather.9.cloned.1.call-done.refs_1_.refs_2_ = bf16[10240,256]{1,0:T(8,128)(2,1)} async-done(((bf16[320,256]{1,0:T(8,128)(2,1)}), bf16[10240,256]{1,0:T(8,128)(2,1)}) %all-gather.9.cloned.1.call-update) | async-done | bytes 5242896 | tf_op jit(solution)/shard_map/all_gather | solution.py:239
  173.7 6.8 %shard_map.82 = (f32[4,1,512]{2,1,0:T(1,128)}, f32[4,1,512]{2,1,0:T(1,128)}, f32[4,128,512]{2,1,0:T(8,128)}) custom-call(s32[6]{0:T(128)} %stack.45.span_ref, bf16[4,128,512]{2,1,0:T(8,128)(2,1)} %maximum_bitcast_fusion.refs_0_, bf16[10240,256]{1,0:T(8,128)(2,1)} %all-gather.9.cloned.1.call-done.refs_1_.refs_2_, ...), custom_call_target="tpu_custom_call" | custom-call | flops 6710886400 | bytes 4325376 | tf_op jit(solution)/shard_map/pallas_call | solution.py:155
  180.5 40.0 %all-gather.7.cloned.1.call-done.refs_1_.refs_2_ = bf16[6144,256]{1,0:T(8,128)(2,1)} async-done(((bf16[192,256]{1,0:T(8,128)(2,1)}), bf16[6144,256]{1,0:T(8,128)(2,1)}) %all-gather.7.cloned.1.call-update) | async-done | bytes 3145744 | tf_op jit(solution)/shard_map/all_gather | solution.py:240
  220.5 7.2 %shard_map.83 = bf16[4,128,512]{2,1,0:T(8,128)(2,1)} custom-call(s32[6]{0:T(128)} %stack.43.span_ref, bf16[4,128,512]{2,1,0:T(8,128)(2,1)} %maximum_bitcast_fusion.refs_0_, bf16[6144,256]{1,0:T(8,128)(2,1)} %all-gather.7.cloned.1.call-done.refs_1_.refs_2_, bf16[6144,256]{1,0:T(8,128)(2,1)} %all-gather.7.cloned.1.call-done.refs_1_.refs_2_, ...), custom_call_target="tpu_custom_call" | custom-call | flops 4831838208 | bytes 3407872 | tf_op jit(solution)/shard_map/pallas_call | solution.py:155
  227.7 42.3 %all-gather.11.cloned.1.call-done = bf16[512,2048]{0,1:T(8,128)(2,1)} async-done(((bf16[512,512]{0,1:T(8,128)(2,1)}), bf16[512,2048]{0,1:T(8,128)(2,1)}) %all-gather.11.cloned.1.call-update) | async-done | bytes 2097168 | tf_op jit(solution)/shard_map/all_gather | solution.py:267
  270.0 5.2 %fusion.5 = bf16[512,1024]{1,0:T(8,128)(2,1)S(1)} fusion(bf16[512,1024]{1,0:T(8,128)(2,1)S(1)} %copy-done.3, bf16[512,4,512]{0,2,1:T(8,128)(2,1)} %bitcast.68, bf16[4,512,1024]{2,1,0:T(8,128)(2,1)} %all-to-all-done.1), kind=kOutput, calls=%fused_computation.14 | convolution fusion | flops 2149056512 | bytes 8388608 | tf_op jit(solution)/shard_map/tsr,src->tc/dot_general | solution.py:271
  275.1 5.4 %gather_fusion = bf16[1024,1024]{1,0:T(8,128)(2,1)} fusion(bf16[512,1024]{1,0:T(8,128)(2,1)S(1)} %fusion.5, s32[1024]{0:T(1024)S(1)} %broadcast_clamp_fusion), kind=kCustom, calls=%fused_computation | custom fusion | bytes 4198400 | tf_op jit(solution)/shard_map/gather | solution.py:278
  280.5 7.7 %all-to-all-start.2 = ((bf16[32,32,1024]{2,1,0:T(8,128)(2,1)}), bf16[32,32,1024]{2,1,0:T(8,128)(2,1)S(1)}, u32[]{:S(2)}, u32[]{:S(2)}) async-start(bf16[32,32,1024]{2,1,0:T(8,128)(2,1)} %bitcast.59), calls=%async_computation.2 | async-start | bytes 4194304 | tf_op jit(solution)/shard_map/all_to_all | solution.py:279
  288.2 28.3 %all-to-all-done.2 = bf16[32,32,1024]{2,1,0:T(8,128)(2,1)S(1)} async-done(((bf16[32,32,1024]{2,1,0:T(8,128)(2,1)}), bf16[32,32,1024]{2,1,0:T(8,128)(2,1)S(1)}, u32[]{:S(2)}, u32[]{:S(2)}) %all-to-all-start.2) | async-done | bytes 2097184 | tf_op jit(solution)/shard_map/all_to_all | solution.py:279
  316.5 2.8 gather_fusion.1
  (40 shorter events, 0.6 us)
Async XLA Ops:
  6.5 113.7 %copy-start = (bf16[4096,128]{1,0:T(8,128)(2,1)S(1)}, bf16[4096,128]{1,0:T(8,128)(2,1)}, u32[]{:S(2)}) copy-start(bf16[4096,128]{1,0:T(8,128)(2,1)} %param.13) | copy-start | bytes 3145732
  6.5 110.4 %all-gather.5.cloned.1.call-start = ((), (), s32[]{:S(2)}) async-start(), calls=%async_computation.3 | async-start | bytes 5242880 | tf_op jit(solution)/shard_map/all_gather | solution.py:223
  61.1 0.8 copy-start.1
  64.4 55.8 %copy-start.6 = (f32[4096]{0:T(1024)S(1)}, f32[4096]{0:T(1024)}, u32[]{:S(2)}) copy-start(f32[4096]{0:T(1024)} %param.11) | copy-start | bytes 49156
  71.3 102.3 %all-gather.9.cloned.1.call-start = ((), (), s32[]{:S(2)}) async-start(), calls=%async_computation.5 | async-start | bytes 5406720 | tf_op jit(solution)/shard_map/all_gather | solution.py:239
  117.0 3.4 %copy-start.2 = (bf16[512,4096]{1,0:T(8,128)(2,1)S(1)}, bf16[512,4096]{1,0:T(8,128)(2,1)}, u32[]{:S(2)}) copy-start(bf16[512,4096]{1,0:T(8,128)(2,1)} %all-gather.5.cloned.1.call-done) | copy-start | bytes 12582916
  120.4 2.5 copy-start.5
  125.1 95.4 %all-gather.7.cloned.1.call-start = ((), (), s32[]{:S(2)}) async-start(), calls=%async_computation.4 | async-start | bytes 3244032 | tf_op jit(solution)/shard_map/all_gather | solution.py:240
  138.7 11.5 %copy-start.4 = (s32[512]{0:T(512)S(1)}, s32[512]{0:T(512)}, u32[]{:S(2)}) copy-start(s32[512]{0:T(512)} %param.10) | copy-start | bytes 6148
  138.7 88.9 %all-to-all-start.1 = ((bf16[4,512,1024]{2,1,0:T(8,128)(2,1)}), bf16[4,512,1024]{2,1,0:T(8,128)(2,1)}, u32[]{:S(2)}, u32[]{:S(2)}) async-start(bf16[4,512,1024]{2,1,0:T(8,128)(2,1)} %bitcast.56), calls=%async_computation.1 | async-start | bytes 8388608 | tf_op jit(solution)/shard_map/all_to_all | solution.py:270
  143.8 126.2 %all-gather.11.cloned.1.call-start = ((), (), s32[]{:S(2)}) async-start(), calls=%async_computation.6 | async-start | bytes 2621440 | tf_op jit(solution)/shard_map/all_gather | solution.py:267
  220.5 49.5 %copy-start.3 = (bf16[512,1024]{1,0:T(8,128)(2,1)S(1)}, bf16[512,1024]{1,0:T(8,128)(2,1)}, u32[]{:S(2)}) copy-start(bf16[512,1024]{1,0:T(8,128)(2,1)} %scatter_custom_fusion.2) | copy-start | bytes 3145732
  280.5 36.0 %all-to-all-start.2 = ((bf16[32,32,1024]{2,1,0:T(8,128)(2,1)}), bf16[32,32,1024]{2,1,0:T(8,128)(2,1)S(1)}, u32[]{:S(2)}, u32[]{:S(2)}) async-start(bf16[32,32,1024]{2,1,0:T(8,128)(2,1)} %bitcast.59), calls=%async_computation.2 | async-start | bytes 4194304 | tf_op jit(solution)/shard_map/all_to_all | solution.py:279
Sparse Core Ops, SparseCore 0:
  71.5 45.4 all-gather.4
  125.2 48.4 all-gather.8
  175.9 44.4 all-gather.6
  227.8 42.1 all-gather.10

commit v18 on v17

--- a/solution.py
+++ b/solution.py
@@ -235,7 +235,7 @@
     keys_own = rotate(keys_own, angles).astype(jnp.bfloat16).reshape(tok_dev, kv_dev * HD)
     values_own = jnp.dot(normed, w_value, preferred_element_type=jnp.float32).astype(jnp.bfloat16)
     kv_own = jnp.concatenate([keys_own, values_own], axis=1)
-    half = 5 * tok_dev // 8
+    half = 21 * tok_dev // 32
     kv_low = lax.all_gather(kv_own[:half], ("chip", "core"), axis=0, tiled=True)
     kv_high = lax.all_gather(kv_own[half:], ("chip", "core"), axis=0, tiled=True)
 

time: 327 us -> 328 us (level)
  transfers between devices with their start and end apart: 6 -> 6, of which waited for: 5 -> 5; matrix products, arithmetic and copies ran while one was open for 10% -> 9% of each run, Pallas kernels for 4% -> 4%
where the time goes in v18:
time: 328 us
  waiting for transfers between devices  170 us (52%)
  local copies, waits for them, and re-layouts  42 us (13%)
  blocking collectives  40.9 us (12%)
  other arithmetic  18.6 us (6%)
  between operations  15.5 us (5%)
  matrix products  14.2 us (4%)
  Pallas kernels  14 us (4%)
  starting transfers between devices  13 us (4%)
    all_gather x1, waiting for transfers between devices, local(): routed = lax.all_gather(routed_part, 'mp', axis=1, tiled=True)  45.4 us
    all_gather x1, waiting for transfers between devices, local(): context_all = lax.all_gather(context, 'mp', axis=1, tiled=True)  44.2 us
    all_to_all x1, blocking collectives, local(): lax.all_to_all(wide.reshape(owners, capacity, columns + meta_width), ('ch...  40.9 us
    all_gather x1, waiting for transfers between devices, local(): lax.all_gather(kv_own[half:], ('chip', 'core'), axis=0, tiled=True)  39.5 us
    all_to_all x1, waiting for transfers between devices, local(): lax.all_to_all(backward, ('chip', 'core'), split_axis=0, concat_axis=0, t...  28.3 us
    pallas_call x2, Pallas kernels, flash_pass(): pl.pallas_call(functools.partial(flash_kernel, final, group), grid_spec=g...  14 us
    all_gather x1, waiting for transfers between devices, local(): kv_low = lax.all_gather(kv_own[:half], ('chip', 'core'), axis=0, tiled=True)  12 us
    all_to_all x1, starting transfers between devices, local(): lax.all_to_all(backward, ('chip', 'core'), split_axis=0, concat_axis=0, t...  7.7 us
  transfers between devices with their start and end apart: 6, of which 5 were waited for; matrix products, arithmetic and copies ran while one was open for 9% of the time, Pallas kernels for 4%

profile of v18, /device:TPU:1, one launch (start us, length us, event | category | flops | bytes accessed | tf_op | source)
XLA Modules:
  0.0 327.8 jit_solution(8528915373101486025)
XLA Ops:
  6.5 1.4 fusion.38
  7.9 1.0 convert_reduce_fusion
  8.9 0.7 slice.57
  10.3 0.7 add_select_fusion.2
  11.0 1.2 reduce-window.6
  12.2 0.2 slice_reduce_fusion
  12.6 2.4 scatter_custom_fusion.1
  15.8 0.2 copy.36
  16.0 3.9 %scatter_custom_fusion = bf16[1024,1024]{1,0:T(8,128)(2,1)S(1)} fusion(s32[512]{0:T(512)S(1)} %compare_select_fusion.2, bf16[512,1024]{1,0:T(8,128)(2,1)} %param.8, bf16[]{:T(256)} %constant.148.clone.1), kind=kCustom, calls=%fused_computation.18 | custom fusion | bytes 2097664 | tf_op jit(solution)/shard_map/scatter | solution.py:179
  19.9 0.2 fusion.4
  20.2 40.9 %all_to_all.15 = bf16[32,32,1152]{2,1,0:T(8,128)(2,1)S(1)} all-to-all(bf16[32,32,1152]{2,1,0:T(8,128)(2,1)S(1)} %bitcast.58), channel_id=1, replica_groups=mesh['chip'=16,'core'=2,'mp'=4] {'chip','core'}, dimensions={0} | all-to-all | bytes 4718592 | tf_op jit(solution)/shard_map/all_to_all | solution.py:204
  61.1 0.8 copy-done.1
  61.9 0.8 fusion.8
  62.8 1.7 slice.80
  64.4 6.9 %scatter_custom_fusion.2 = bf16[512,1024]{1,0:T(8,128)(2,1)} fusion(s32[1024]{0:T(1024)S(1)} %bitcast.65, bf16[1024,1024]{1,0:T(8,128)(2,1)} %bitcast.60, bf16[]{:T(256)} %constant.148.clone.1), kind=kCustom, calls=%fused_computation.26 | custom fusion | bytes 1049088 | tf_op jit(solution)/shard_map/scatter | solution.py:221
  71.3 0.2 all-gather.9.cloned.1.call-start
  71.6 45.4 %all-gather.5.cloned.1.call-done = bf16[512,4096]{1,0:T(8,128)(2,1)} async-done(((bf16[512,1024]{1,0:T(8,128)(2,1)}), bf16[512,4096]{1,0:T(8,128)(2,1)}) %all-gather.5.cloned.1.call-update) | async-done | bytes 4194320 | tf_op jit(solution)/shard_map/all_gather | solution.py:223
  117.0 3.2 fusion
  120.2 0.2 copy-done.2
  120.4 1.3 convolution_bitcast_fusion
  121.7 1.2 fusion.20
  122.9 1.3 convolution_convert_fusion
  124.3 0.8 pad_maximum_fusion
  125.1 0.7 pad_maximum_fusion.2
  125.9 6.5 %copy.39 = bf16[512,4096]{0,1:T(8,128)(2,1)} copy(bf16[512,4096]{1,0:T(8,128)(2,1)} %param.15) | data formatting | bytes 8388608 | tf_op args[7]
  132.4 6.3 %copy.40 = bf16[512,4,1024]{2,0,1:T(8,128)(2,1)} copy(bf16[512,4,1024]{0,2,1:T(8,128)(2,1)} %bitcast.57) | data formatting | bytes 8388608 | tf_op jit(solution)/shard_map/reshape | solution.py:269
  138.8 5.0 %all-to-all-start.1 = ((bf16[4,512,1024]{2,1,0:T(8,128)(2,1)}), bf16[4,512,1024]{2,1,0:T(8,128)(2,1)}, u32[]{:S(2)}, u32[]{:S(2)}) async-start(bf16[4,512,1024]{2,1,0:T(8,128)(2,1)} %bitcast.56), calls=%async_computation.1 | async-start | bytes 8388608 | tf_op jit(solution)/shard_map/all_to_all | solution.py:270
  143.9 0.6 iota_add_fusion.refs_4_
  144.5 0.5 multiply_cosine_fusion.1
  145.0 2.2 compare_reduce_fusion
  147.2 1.7 fusion.24
  148.9 0.7 fusion.32
  150.3 1.8 fusion.37
  152.1 1.3 stack.43.span_ref
  153.3 1.3 stack.45.span_ref
  154.6 6.4 %fusion.35 = f32[512,512]{0,1:T(8,128)S(1)} fusion(bf16[4096,512]{1,0:T(8,128)(2,1)} %param.12, bf16[512,4096]{1,0:T(8,128)(2,1)} %all-gather.5.cloned.1.call-done, f32[4096]{0:T(1024)S(1)} %copy-done.6, f32[512]{0:T(512)S(1)} %add_rsqrt_fusion), kind=kOutput, calls=%fused_computation.90 | convolution fusion | flops 2155872256 | bytes 9455616 | tf_op jit(solution)/shard_map/dot_general | solution.py:228
  161.0 0.2 subtract_convert_fusion
  161.2 0.8 maximum_bitcast_fusion.refs_0_
  162.0 12.0 %all-gather.9.cloned.1.call-done.refs_1_.refs_2_ = bf16[10752,256]{1,0:T(8,128)(2,1)} async-done(((bf16[336,256]{1,0:T(8,128)(2,1)}), bf16[10752,256]{1,0:T(8,128)(2,1)}) %all-gather.9.cloned.1.call-update) | async-done | bytes 5505040 | tf_op jit(solution)/shard_map/all_gather | solution.py:239
  174.1 7.0 %shard_map.82 = (f32[4,1,512]{2,1,0:T(1,128)}, f32[4,1,512]{2,1,0:T(1,128)}, f32[4,128,512]{2,1,0:T(8,128)}) custom-call(s32[6]{0:T(128)} %stack.45.span_ref, bf16[4,128,512]{2,1,0:T(8,128)(2,1)} %maximum_bitcast_fusion.refs_0_, bf16[10752,256]{1,0:T(8,128)(2,1)} %all-gather.9.cloned.1.call-done.refs_1_.refs_2_, ...), custom_call_target="tpu_custom_call" | custom-call | flops 7046430720 | bytes 4489216 | tf_op jit(solution)/shard_map/pallas_call | solution.py:155
  181.1 39.5 %all-gather.7.cloned.1.call-done.refs_1_.refs_2_ = bf16[5632,256]{1,0:T(8,128)(2,1)} async-done(((bf16[176,256]{1,0:T(8,128)(2,1)}), bf16[5632,256]{1,0:T(8,128)(2,1)}) %all-gather.7.cloned.1.call-update) | async-done | bytes 2883600 | tf_op jit(solution)/shard_map/all_gather | solution.py:240
  220.6 7.0 %shard_map.83 = bf16[4,128,512]{2,1,0:T(8,128)(2,1)} custom-call(s32[6]{0:T(128)} %stack.43.span_ref, bf16[4,128,512]{2,1,0:T(8,128)(2,1)} %maximum_bitcast_fusion.refs_0_, bf16[5632,256]{1,0:T(8,128)(2,1)} %all-gather.7.cloned.1.call-done.refs_1_.refs_2_, bf16[5632,256]{1,0:T(8,128)(2,1)} %all-gather.7.cloned.1.call-done.refs_1_.refs_2_, ...), custom_call_target="tpu_custom_call" | custom-call | flops 4429185024 | bytes 3211264 | tf_op jit(solution)/shard_map/pallas_call | solution.py:155
  227.7 44.2 %all-gather.11.cloned.1.call-done = bf16[512,2048]{0,1:T(8,128)(2,1)} async-done(((bf16[512,512]{0,1:T(8,128)(2,1)}), bf16[512,2048]{0,1:T(8,128)(2,1)}) %all-gather.11.cloned.1.call-update) | async-done | bytes 2097168 | tf_op jit(solution)/shard_map/all_gather | solution.py:267
  271.9 5.2 %fusion.5 = bf16[512,1024]{1,0:T(8,128)(2,1)S(1)} fusion(bf16[512,1024]{1,0:T(8,128)(2,1)S(1)} %copy-done.3, bf16[512,4,512]{0,2,1:T(8,128)(2,1)} %bitcast.68, bf16[4,512,1024]{2,1,0:T(8,128)(2,1)} %all-to-all-done.1), kind=kOutput, calls=%fused_computation.14 | convolution fusion | flops 2149056512 | bytes 8388608 | tf_op jit(solution)/shard_map/tsr,src->tc/dot_general | solution.py:271
  277.1 5.4 %gather_fusion = bf16[1024,1024]{1,0:T(8,128)(2,1)} fusion(bf16[512,1024]{1,0:T(8,128)(2,1)S(1)} %fusion.5, s32[1024]{0:T(1024)S(1)} %broadcast_clamp_fusion), kind=kCustom, calls=%fused_computation | custom fusion | bytes 4198400 | tf_op jit(solution)/shard_map/gather | solution.py:278
  282.5 7.7 %all-to-all-start.2 = ((bf16[32,32,1024]{2,1,0:T(8,128)(2,1)}), bf16[32,32,1024]{2,1,0:T(8,128)(2,1)S(1)}, u32[]{:S(2)}, u32[]{:S(2)}) async-start(bf16[32,32,1024]{2,1,0:T(8,128)(2,1)} %bitcast.59), calls=%async_computation.2 | async-start | bytes 4194304 | tf_op jit(solution)/shard_map/all_to_all | solution.py:279
  290.2 28.3 %all-to-all-done.2 = bf16[32,32,1024]{2,1,0:T(8,128)(2,1)S(1)} async-done(((bf16[32,32,1024]{2,1,0:T(8,128)(2,1)}), bf16[32,32,1024]{2,1,0:T(8,128)(2,1)S(1)}, u32[]{:S(2)}, u32[]{:S(2)}) %all-to-all-start.2) | async-done | bytes 2097184 | tf_op jit(solution)/shard_map/all_to_all | solution.py:279
  318.5 2.8 gather_fusion.1
  (40 shorter events, 0.6 us)
Async XLA Ops:
  6.5 113.7 %copy-start = (bf16[4096,128]{1,0:T(8,128)(2,1)S(1)}, bf16[4096,128]{1,0:T(8,128)(2,1)}, u32[]{:S(2)}) copy-start(bf16[4096,128]{1,0:T(8,128)(2,1)} %param.13) | copy-start | bytes 3145732
  6.5 110.4 %all-gather.5.cloned.1.call-start = ((), (), s32[]{:S(2)}) async-start(), calls=%async_computation.3 | async-start | bytes 5242880 | tf_op jit(solution)/shard_map/all_gather | solution.py:223
  61.1 0.8 copy-start.1
  64.4 55.8 %copy-start.6 = (f32[4096]{0:T(1024)S(1)}, f32[4096]{0:T(1024)}, u32[]{:S(2)}) copy-start(f32[4096]{0:T(1024)} %param.11) | copy-start | bytes 49156
  71.3 102.8 %all-gather.9.cloned.1.call-start = ((), (), s32[]{:S(2)}) async-start(), calls=%async_computation.5 | async-start | bytes 5677056 | tf_op jit(solution)/shard_map/all_gather | solution.py:239
  117.0 3.4 %copy-start.2 = (bf16[512,4096]{1,0:T(8,128)(2,1)S(1)}, bf16[512,4096]{1,0:T(8,128)(2,1)}, u32[]{:S(2)}) copy-start(bf16[512,4096]{1,0:T(8,128)(2,1)} %all-gather.5.cloned.1.call-done) | copy-start | bytes 12582916
  120.4 2.5 copy-start.5
  125.1 95.5 %all-gather.7.cloned.1.call-start = ((), (), s32[]{:S(2)}) async-start(), calls=%async_computation.4 | async-start | bytes 2973696 | tf_op jit(solution)/shard_map/all_gather | solution.py:240
  138.8 11.5 %copy-start.4 = (s32[512]{0:T(512)S(1)}, s32[512]{0:T(512)}, u32[]{:S(2)}) copy-start(s32[512]{0:T(512)} %param.10) | copy-start | bytes 6148
  138.8 88.9 %all-to-all-start.1 = ((bf16[4,512,1024]{2,1,0:T(8,128)(2,1)}), bf16[4,512,1024]{2,1,0:T(8,128)(2,1)}, u32[]{:S(2)}, u32[]{:S(2)}) async-start(bf16[4,512,1024]{2,1,0:T(8,128)(2,1)} %bitcast.56), calls=%async_computation.1 | async-start | bytes 8388608 | tf_op jit(solution)/shard_map/all_to_all | solution.py:270
  143.8 128.1 %all-gather.11.cloned.1.call-start = ((), (), s32[]{:S(2)}) async-start(), calls=%async_computation.6 | async-start | bytes 2621440 | tf_op jit(solution)/shard_map/all_gather | solution.py:267
  220.6 51.3 %copy-start.3 = (bf16[512,1024]{1,0:T(8,128)(2,1)S(1)}, bf16[512,1024]{1,0:T(8,128)(2,1)}, u32[]{:S(2)}) copy-start(bf16[512,1024]{1,0:T(8,128)(2,1)} %scatter_custom_fusion.2) | copy-start | bytes 3145732
  282.5 36.0 %all-to-all-start.2 = ((bf16[32,32,1024]{2,1,0:T(8,128)(2,1)}), bf16[32,32,1024]{2,1,0:T(8,128)(2,1)S(1)}, u32[]{:S(2)}, u32[]{:S(2)}) async-start(bf16[32,32,1024]{2,1,0:T(8,128)(2,1)} %bitcast.59), calls=%async_computation.2 | async-start | bytes 4194304 | tf_op jit(solution)/shard_map/all_to_all | solution.py:279
Sparse Core Ops, SparseCore 0:
  71.5 45.4 all-gather.4
  125.2 48.8 all-gather.8
  176.3 44.2 all-gather.6
  227.8 44.0 all-gather.10

commit v19 on v18

--- a/solution.py
+++ b/solution.py
@@ -235,7 +235,7 @@
     keys_own = rotate(keys_own, angles).astype(jnp.bfloat16).reshape(tok_dev, kv_dev * HD)
     values_own = jnp.dot(normed, w_value, preferred_element_type=jnp.float32).astype(jnp.bfloat16)
     kv_own = jnp.concatenate([keys_own, values_own], axis=1)
-    half = 21 * tok_dev // 32
+    half = 11 * tok_dev // 16
     kv_low = lax.all_gather(kv_own[:half], ("chip", "core"), axis=0, tiled=True)
     kv_high = lax.all_gather(kv_own[half:], ("chip", "core"), axis=0, tiled=True)
 

time: 328 us -> 326 us (level)
  no operation moved by 1% of the time
where the time goes in v19:
time: 326 us; the launch traced here: 327 us
  waiting for transfers between devices  169 us (52%)
  local copies, waits for them, and re-layouts  42 us (13%)
  blocking collectives  40.9 us (13%)
  other arithmetic  18.7 us (6%)
  between operations  15.5 us (5%)
  matrix products  14.2 us (4%)
  Pallas kernels  13.8 us (4%)
  starting transfers between devices  13 us (4%)
    all_gather x1, waiting for transfers between devices, local(): routed = lax.all_gather(routed_part, 'mp', axis=1, tiled=True)  45.4 us
    all_gather x1, waiting for transfers between devices, local(): context_all = lax.all_gather(context, 'mp', axis=1, tiled=True)  44.4 us
    all_to_all x1, blocking collectives, local(): lax.all_to_all(wide.reshape(owners, capacity, columns + meta_width), ('ch...  40.9 us
    all_gather x1, waiting for transfers between devices, local(): lax.all_gather(kv_own[half:], ('chip', 'core'), axis=0, tiled=True)  38.8 us
    all_to_all x1, waiting for transfers between devices, local(): lax.all_to_all(backward, ('chip', 'core'), split_axis=0, concat_axis=0, t...  28.3 us
    pallas_call x2, Pallas kernels, flash_pass(): pl.pallas_call(functools.partial(flash_kernel, final, group), grid_spec=g...  13.8 us
    all_gather x1, waiting for transfers between devices, local(): kv_low = lax.all_gather(kv_own[:half], ('chip', 'core'), axis=0, tiled=True)  12.5 us
    all_to_all x1, starting transfers between devices, local(): lax.all_to_all(backward, ('chip', 'core'), split_axis=0, concat_axis=0, t...  7.7 us
  transfers between devices with their start and end apart: 6, of which 5 were waited for; matrix products, arithmetic and copies ran while one was open for 9% of the time, Pallas kernels for 4%

profile of v19, /device:TPU:1, one launch (start us, length us, event | category | flops | bytes accessed | tf_op | source)
XLA Modules:
  0.0 327.5 jit_solution(6644696355335090130)
XLA Ops:
  6.5 1.4 fusion.38
  7.9 1.0 convert_reduce_fusion
  8.9 0.7 slice.57
  10.3 0.7 add_select_fusion.2
  11.0 1.2 reduce-window.6
  12.2 0.2 slice_reduce_fusion
  12.6 2.4 scatter_custom_fusion.1
  15.8 0.2 copy.36
  16.0 3.9 %scatter_custom_fusion = bf16[1024,1024]{1,0:T(8,128)(2,1)S(1)} fusion(s32[512]{0:T(512)S(1)} %compare_select_fusion.2, bf16[512,1024]{1,0:T(8,128)(2,1)} %param.8, bf16[]{:T(256)} %constant.148.clone.1), kind=kCustom, calls=%fused_computation.18 | custom fusion | bytes 2097664 | tf_op jit(solution)/shard_map/scatter | solution.py:179
  19.9 0.2 fusion.4
  20.2 40.9 %all_to_all.15 = bf16[32,32,1152]{2,1,0:T(8,128)(2,1)S(1)} all-to-all(bf16[32,32,1152]{2,1,0:T(8,128)(2,1)S(1)} %bitcast.58), channel_id=1, replica_groups=mesh['chip'=16,'core'=2,'mp'=4] {'chip','core'}, dimensions={0} | all-to-all | bytes 4718592 | tf_op jit(solution)/shard_map/all_to_all | solution.py:204
  61.1 0.8 copy-done.1
  61.9 0.8 fusion.8
  62.8 1.7 slice.80
  64.4 6.9 %scatter_custom_fusion.2 = bf16[512,1024]{1,0:T(8,128)(2,1)} fusion(s32[1024]{0:T(1024)S(1)} %bitcast.65, bf16[1024,1024]{1,0:T(8,128)(2,1)} %bitcast.60, bf16[]{:T(256)} %constant.148.clone.1), kind=kCustom, calls=%fused_computation.26 | custom fusion | bytes 1049088 | tf_op jit(solution)/shard_map/scatter | solution.py:221
  71.3 0.2 all-gather.9.cloned.1.call-start
  71.6 45.4 %all-gather.5.cloned.1.call-done = bf16[512,4096]{1,0:T(8,128)(2,1)} async-done(((bf16[512,1024]{1,0:T(8,128)(2,1)}), bf16[512,4096]{1,0:T(8,128)(2,1)}) %all-gather.5.cloned.1.call-update) | async-done | bytes 4194320 | tf_op jit(solution)/shard_map/all_gather | solution.py:223
  117.0 3.2 fusion
  120.2 0.2 copy-done.2
  120.4 1.3 convolution_bitcast_fusion
  121.7 1.2 fusion.20
  122.9 1.3 convolution_convert_fusion
  124.3 0.8 pad_maximum_fusion
  125.1 0.7 pad_maximum_fusion.2
  125.9 6.5 %copy.39 = bf16[512,4096]{0,1:T(8,128)(2,1)} copy(bf16[512,4096]{1,0:T(8,128)(2,1)} %param.15) | data formatting | bytes 8388608 | tf_op args[7]
  132.4 6.3 %copy.40 = bf16[512,4,1024]{2,0,1:T(8,128)(2,1)} copy(bf16[512,4,1024]{0,2,1:T(8,128)(2,1)} %bitcast.57) | data formatting | bytes 8388608 | tf_op jit(solution)/shard_map/reshape | solution.py:269
  138.7 5.0 %all-to-all-start.1 = ((bf16[4,512,1024]{2,1,0:T(8,128)(2,1)}), bf16[4,512,1024]{2,1,0:T(8,128)(2,1)}, u32[]{:S(2)}, u32[]{:S(2)}) async-start(bf16[4,512,1024]{2,1,0:T(8,128)(2,1)} %bitcast.56), calls=%async_computation.1 | async-start | bytes 8388608 | tf_op jit(solution)/shard_map/all_to_all | solution.py:270
  143.8 0.6 iota_add_fusion.refs_4_
  144.4 0.5 multiply_cosine_fusion.1
  144.9 2.2 compare_reduce_fusion
  147.1 1.7 fusion.24
  148.9 0.7 fusion.32
  150.2 1.8 fusion.37
  152.0 1.3 stack.43.span_ref
  153.3 1.3 stack.45.span_ref
  154.6 6.4 %fusion.35 = f32[512,512]{0,1:T(8,128)S(1)} fusion(bf16[4096,512]{1,0:T(8,128)(2,1)} %param.12, bf16[512,4096]{1,0:T(8,128)(2,1)} %all-gather.5.cloned.1.call-done, f32[4096]{0:T(1024)S(1)} %copy-done.6, f32[512]{0:T(512)S(1)} %add_rsqrt_fusion), kind=kOutput, calls=%fused_computation.90 | convolution fusion | flops 2155872256 | bytes 9455616 | tf_op jit(solution)/shard_map/dot_general | solution.py:228
  161.0 0.2 subtract_convert_fusion
  161.2 0.8 maximum_bitcast_fusion.refs_0_
  162.1 12.5 %all-gather.9.cloned.1.call-done.refs_1_.refs_2_ = bf16[11264,256]{1,0:T(8,128)(2,1)} async-done(((bf16[352,256]{1,0:T(8,128)(2,1)}), bf16[11264,256]{1,0:T(8,128)(2,1)}) %all-gather.9.cloned.1.call-update) | async-done | bytes 5767184 | tf_op jit(solution)/shard_map/all_gather | solution.py:239
  174.5 7.1 %shard_map.82 = (f32[4,1,512]{2,1,0:T(1,128)}, f32[4,1,512]{2,1,0:T(1,128)}, f32[4,128,512]{2,1,0:T(8,128)}) custom-call(s32[6]{0:T(128)} %stack.45.span_ref, bf16[4,128,512]{2,1,0:T(8,128)(2,1)} %maximum_bitcast_fusion.refs_0_, bf16[11264,256]{1,0:T(8,128)(2,1)} %all-gather.9.cloned.1.call-done.refs_1_.refs_2_, ...), custom_call_target="tpu_custom_call" | custom-call | flops 7381975040 | bytes 4653056 | tf_op jit(solution)/shard_map/pallas_call | solution.py:155
  181.6 38.8 %all-gather.7.cloned.1.call-done.refs_1_.refs_2_ = bf16[5120,256]{1,0:T(8,128)(2,1)} async-done(((bf16[160,256]{1,0:T(8,128)(2,1)}), bf16[5120,256]{1,0:T(8,128)(2,1)}) %all-gather.7.cloned.1.call-update) | async-done | bytes 2621456 | tf_op jit(solution)/shard_map/all_gather | solution.py:240
  220.4 6.7 %shard_map.83 = bf16[4,128,512]{2,1,0:T(8,128)(2,1)} custom-call(s32[6]{0:T(128)} %stack.43.span_ref, bf16[4,128,512]{2,1,0:T(8,128)(2,1)} %maximum_bitcast_fusion.refs_0_, bf16[5120,256]{1,0:T(8,128)(2,1)} %all-gather.7.cloned.1.call-done.refs_1_.refs_2_, bf16[5120,256]{1,0:T(8,128)(2,1)} %all-gather.7.cloned.1.call-done.refs_1_.refs_2_, ...), custom_call_target="tpu_custom_call" | custom-call | flops 4026531840 | bytes 3014656 | tf_op jit(solution)/shard_map/pallas_call | solution.py:155
  227.2 44.4 %all-gather.11.cloned.1.call-done = bf16[512,2048]{0,1:T(8,128)(2,1)} async-done(((bf16[512,512]{0,1:T(8,128)(2,1)}), bf16[512,2048]{0,1:T(8,128)(2,1)}) %all-gather.11.cloned.1.call-update) | async-done | bytes 2097168 | tf_op jit(solution)/shard_map/all_gather | solution.py:267
  271.6 5.2 %fusion.5 = bf16[512,1024]{1,0:T(8,128)(2,1)S(1)} fusion(bf16[512,1024]{1,0:T(8,128)(2,1)S(1)} %copy-done.3, bf16[512,4,512]{0,2,1:T(8,128)(2,1)} %bitcast.68, bf16[4,512,1024]{2,1,0:T(8,128)(2,1)} %all-to-all-done.1), kind=kOutput, calls=%fused_computation.14 | convolution fusion | flops 2149056512 | bytes 8388608 | tf_op jit(solution)/shard_map/tsr,src->tc/dot_general | solution.py:271
  276.8 5.4 %gather_fusion = bf16[1024,1024]{1,0:T(8,128)(2,1)} fusion(bf16[512,1024]{1,0:T(8,128)(2,1)S(1)} %fusion.5, s32[1024]{0:T(1024)S(1)} %broadcast_clamp_fusion), kind=kCustom, calls=%fused_computation | custom fusion | bytes 4198400 | tf_op jit(solution)/shard_map/gather | solution.py:278
  282.2 7.7 %all-to-all-start.2 = ((bf16[32,32,1024]{2,1,0:T(8,128)(2,1)}), bf16[32,32,1024]{2,1,0:T(8,128)(2,1)S(1)}, u32[]{:S(2)}, u32[]{:S(2)}) async-start(bf16[32,32,1024]{2,1,0:T(8,128)(2,1)} %bitcast.59), calls=%async_computation.2 | async-start | bytes 4194304 | tf_op jit(solution)/shard_map/all_to_all | solution.py:279
  289.9 28.3 %all-to-all-done.2 = bf16[32,32,1024]{2,1,0:T(8,128)(2,1)S(1)} async-done(((bf16[32,32,1024]{2,1,0:T(8,128)(2,1)}), bf16[32,32,1024]{2,1,0:T(8,128)(2,1)S(1)}, u32[]{:S(2)}, u32[]{:S(2)}) %all-to-all-start.2) | async-done | bytes 2097184 | tf_op jit(solution)/shard_map/all_to_all | solution.py:279
  318.2 2.8 gather_fusion.1
  (40 shorter events, 0.6 us)
Async XLA Ops:
  6.5 113.7 %copy-start = (bf16[4096,128]{1,0:T(8,128)(2,1)S(1)}, bf16[4096,128]{1,0:T(8,128)(2,1)}, u32[]{:S(2)}) copy-start(bf16[4096,128]{1,0:T(8,128)(2,1)} %param.13) | copy-start | bytes 3145732
  6.5 110.4 %all-gather.5.cloned.1.call-start = ((), (), s32[]{:S(2)}) async-start(), calls=%async_computation.3 | async-start | bytes 5242880 | tf_op jit(solution)/shard_map/all_gather | solution.py:223
  61.1 0.8 copy-start.1
  64.4 55.8 %copy-start.6 = (f32[4096]{0:T(1024)S(1)}, f32[4096]{0:T(1024)}, u32[]{:S(2)}) copy-start(f32[4096]{0:T(1024)} %param.11) | copy-start | bytes 49156
  71.3 103.2 %all-gather.9.cloned.1.call-start = ((), (), s32[]{:S(2)}) async-start(), calls=%async_computation.5 | async-start | bytes 5947392 | tf_op jit(solution)/shard_map/all_gather | solution.py:239
  117.0 3.4 %copy-start.2 = (bf16[512,4096]{1,0:T(8,128)(2,1)S(1)}, bf16[512,4096]{1,0:T(8,128)(2,1)}, u32[]{:S(2)}) copy-start(bf16[512,4096]{1,0:T(8,128)(2,1)} %all-gather.5.cloned.1.call-done) | copy-start | bytes 12582916
  120.4 2.5 copy-start.5
  125.1 95.4 %all-gather.7.cloned.1.call-start = ((), (), s32[]{:S(2)}) async-start(), calls=%async_computation.4 | async-start | bytes 2703360 | tf_op jit(solution)/shard_map/all_gather | solution.py:240
  138.7 11.5 %copy-start.4 = (s32[512]{0:T(512)S(1)}, s32[512]{0:T(512)}, u32[]{:S(2)}) copy-start(s32[512]{0:T(512)} %param.10) | copy-start | bytes 6148
  138.7 88.5 %all-to-all-start.1 = ((bf16[4,512,1024]{2,1,0:T(8,128)(2,1)}), bf16[4,512,1024]{2,1,0:T(8,128)(2,1)}, u32[]{:S(2)}, u32[]{:S(2)}) async-start(bf16[4,512,1024]{2,1,0:T(8,128)(2,1)} %bitcast.56), calls=%async_computation.1 | async-start | bytes 8388608 | tf_op jit(solution)/shard_map/all_to_all | solution.py:270
  143.7 127.9 %all-gather.11.cloned.1.call-start = ((), (), s32[]{:S(2)}) async-start(), calls=%async_computation.6 | async-start | bytes 2621440 | tf_op jit(solution)/shard_map/all_gather | solution.py:267
  220.4 51.2 %copy-start.3 = (bf16[512,1024]{1,0:T(8,128)(2,1)S(1)}, bf16[512,1024]{1,0:T(8,128)(2,1)}, u32[]{:S(2)}) copy-start(bf16[512,1024]{1,0:T(8,128)(2,1)} %scatter_custom_fusion.2) | copy-start | bytes 3145732
  282.2 36.0 %all-to-all-start.2 = ((bf16[32,32,1024]{2,1,0:T(8,128)(2,1)}), bf16[32,32,1024]{2,1,0:T(8,128)(2,1)S(1)}, u32[]{:S(2)}, u32[]{:S(2)}) async-start(bf16[32,32,1024]{2,1,0:T(8,128)(2,1)} %bitcast.59), calls=%async_computation.2 | async-start | bytes 4194304 | tf_op jit(solution)/shard_map/all_to_all | solution.py:279
Sparse Core Ops, SparseCore 0:
  71.5 45.4 all-gather.4
  125.2 49.2 all-gather.8
  176.8 43.6 all-gather.6
  227.3 44.2 all-gather.10
